TPU v7x, 32 devices: a whole 2x2x4 slice. The times are simulated.
32 devices in a mesh: grp: 4 (over z), gx: 4 (over y, core), gy: 2 (over x).
Axes of the slice: x: 2, y: 2, z: 4, core: 2. Of those that a mesh axis runs over, the one named last changes fastest.
Arguments:
- source: float32 [64, 32, 512], P('gx', 'gy', 'grp'), may hold values from -13 to 13
- conductance: float32 [64, 32, 512], P('gx', 'gy', 'grp'), may hold values from 0.2 to 5
- storage: float32 [64, 32, 512], P('gx', 'gy', 'grp'), may hold values from 0.05 to 1
- aggregate_ids: int32 [64, 32, 512], P('gx', 'gy', 'grp'), may hold values from 0 to 511, as said below
- coarse_values: float32 [256, 64, 256], P(('grp', 'gx', 'gy')), as said below
- coarse_columns: int32 [256, 4], P(('grp', 'gx', 'gy')), may hold values from 0 to 255, as said below
Outputs:
- solution: float32 [64, 32, 512], P('gx', 'gy', 'grp')
- coarse_error: float32 [16384], P(('grp', 'gx', 'gy'))
Inputs may be any that keep to these rules, and one draw needn't show every extreme that they name: `aggregate_ids`: on each device, every id names exactly the 64 cells of one aligned 4 x 4 x 4 box of the device's block, and different boxes have different ids. `coarse_columns`: entry 0 of block row b is b itself; every other entry names a block of a device whose gx and gy indices differ from those of row b's device by at most one. `coarse_values`: in every row of the coarse operator the diagonal entry of the first stored block exceeds the sum of the magnitudes of all other stored entries of that row.
All inputs are finite; a program needn't handle non-finite values.
Results may differ from a plain program's by a relative error of at most 0.0001.
Values sent between devices are 32-bit elements; how exact they have to be, the bound alone decides.
No kernel may reach another device: no remote copies, remote signals or barrier semaphores. Data moves between devices by JAX's collectives and lax.ppermute only.
A program may use at most 64 MiB of HBM per device.

v0:
```python
import jax
import jax.numpy as jnp
from jax import lax
from jax.sharding import PartitionSpec as P

NU = 2
CITER = 4


WEIGHT = 2.0 / 3.0
PAIRS = ((0, 1), (0, -1), (1, 1), (1, -1), (2, 1), (2, -1))


def padded_2(cells, sides, width):
    for axis, dim in sides:
        count = lax.axis_size(axis)
        ends = count - 1
        head = lax.slice_in_dim(cells, 0, width, axis=dim)
        tail = lax.slice_in_dim(cells, cells.shape[dim] - width, cells.shape[dim], axis=dim)
        cells = jnp.concatenate(
            [
                lax.ppermute(tail, axis, [(i, (i + 1) % count) for i in range(ends)]),
                cells,
                lax.ppermute(head, axis, [((i + 1) % count, i) for i in range(ends)]),
            ],
            axis=dim,
        )
    return cells


def shifted(padded, dimension, offset):
    window = [slice(1, -1), slice(1, -1), slice(1, -1)]
    window[dimension] = slice(1 + offset, padded.shape[dimension] - 1 + offset)
    return padded[tuple(window)]


def trimmed(array):
    return array[1:-1, 1:-1, 1:-1]


def apply_wide(padded_field, storage_part, face_part):
    center = trimmed(padded_field)
    summed = storage_part * center
    for position in range(6):
        dimension, offset = PAIRS[position]
        summed = summed + face_part[position] * (center - shifted(padded_field, dimension, offset))
    return summed


def face_terms(padded_cond):
    center = trimmed(padded_cond)
    return [0.5 * (center + shifted(padded_cond, dimension, offset)) for dimension, offset in PAIRS]


def add_faces(storage_part, face_part):
    running = storage_part
    for position in range(6):
        running = running + face_part[position]
    return running


def local(source, conductance, storage, aggregate_ids, coarse_values, coarse_columns):
    size_x, size_y, size_z = source.shape
    padded_cond = padded_2(conductance, (("grp", 2), ("gx", 0), ("gy", 1)), 1)
    face_list = face_terms(padded_cond)
    diagonal = add_faces(storage, face_list)

    def operate(field):
        padded = padded_2(field, (("grp", 2), ("gx", 0), ("gy", 1)), 1)
        return apply_wide(padded, storage, face_list)

    solution = WEIGHT * source / diagonal
    solution = solution + WEIGHT * (source - operate(solution)) / diagonal
    residual = source - operate(solution)
    smoothed = residual - WEIGHT * operate(residual / diagonal)
    box_labels = aggregate_ids[::4, ::4, ::4].reshape(-1)
    box_totals = (
        smoothed.reshape(size_x // 4, 4, size_y // 4, 4, size_z // 4, 4)
        .sum(axis=(1, 3, 5))
        .reshape(-1)
    )
    coarse_rhs = jnp.zeros(box_totals.shape, source.dtype).at[box_labels].set(box_totals)
    coarse_diag = jnp.diagonal(coarse_values[:, :, :64], axis1=1, axis2=2).reshape(-1)
    block_rows = coarse_values.shape[0]
    grid_x = lax.axis_size("gx")
    grid_y = lax.axis_size("gy")
    groups = lax.axis_size("grp")
    within_ids = coarse_columns % block_rows
    device_ids = coarse_columns // block_rows
    target_y = device_ids % grid_y
    target_x = device_ids // grid_y % grid_x
    member_ids = device_ids // (grid_y * grid_x)
    delta_x = target_x - lax.axis_index("gx") + 1
    delta_y = target_y - lax.axis_index("gy") + 1
    local_columns = ((delta_x * 3 + delta_y) * groups + member_ids) * block_rows + within_ids
    coarse_error = coarse_rhs / coarse_diag
    for sweep_number in range(CITER - 1):
        pooled = lax.all_gather(coarse_error, "grp", axis=0, tiled=True)
        beside_all = padded_2(pooled.reshape(1, 1, -1), (("gx", 0), ("gy", 1)), 1)
        blocks = beside_all.reshape(-1, 64)[local_columns]
        blocks = blocks.reshape(blocks.shape[0], -1)
        applied = jnp.einsum(
            "bim,bm->bi", coarse_values, blocks, precision=lax.Precision.HIGHEST
        ).reshape(-1)
        coarse_error = coarse_error + (coarse_rhs - applied) / coarse_diag
    small_field = coarse_error[box_labels].reshape(size_x // 4, size_y // 4, size_z // 4)
    lifted = jnp.repeat(jnp.repeat(jnp.repeat(small_field, 4, axis=0), 4, axis=1), 4, axis=2)
    solution = solution + (lifted - WEIGHT * operate(lifted) / diagonal)
    for sweep_number in range(NU):
        solution = solution + WEIGHT * (source - operate(solution)) / diagonal
    return (solution, coarse_error)


def solution(mesh):
    return jax.shard_map(
        local,
        mesh=mesh,
        in_specs=(
            P("gx", "gy", "grp"),
            P("gx", "gy", "grp"),
            P("gx", "gy", "grp"),
            P("gx", "gy", "grp"),
            P(("grp", "gx", "gy"), None, None),
            P(("grp", "gx", "gy"), None),
        ),
        out_specs=(P("gx", "gy", "grp"), P(("grp", "gx", "gy"))),
        check_vma=False,
    )
```

profile of v0, /device:TPU:0, one launch (start us, length us, event | category | flops | bytes accessed | tf_op | source)
XLA Modules:
  0.0 275.6 jit_solution(16824515326365919431)
XLA Ops:
  1.7 5.1 %collective-permute-start = (f32[16,16,1]{2,1,0:T(8,128)S(1)}, f32[16,16,1]{2,1,0:T(8,128)S(1)}, u32[]{:S(2)}, u32[]{:S(2)}) collective-permute-start(f32[16,16,1]{2,1,0:T(8,128)S(1)} %get-tuple-element.55), channel_id=1, source_target_pairs={{0,8},{8,16},{16,24},{1,9},{9,17},{17,25},{2,10},{10,18},{18,26},{... | collective-permute-start | bytes 3080 | tf_op jit(solution)/shard_map/ppermute | solution.py:22
  9.5 4.1 %collective-permute-done.1 = f32[16,16,1]{2,1,0:T(8,128)S(1)} collective-permute-done((f32[16,16,1]{2,1,0:T(8,128)S(1)}, f32[16,16,1]{2,1,0:T(8,128)S(1)}, u32[]{:S(2)}, u32[]{:S(2)}) %collective-permute-start.1) | collective-permute-done | bytes 1056 | tf_op jit(solution)/shard_map/ppermute | solution.py:24
  22.0 4.5 %collective-permute-start.5 = (f32[18,1,130]{2,1,0:T(1,128)S(1)}, f32[18,1,130]{2,1,0:T(1,128)S(1)}, u32[]{:S(2)}, u32[]{:S(2)}) collective-permute-start(f32[18,1,130]{2,1,0:T(1,128)S(1)} %get-tuple-element.29), channel_id=1, source_target_pairs={{0,1},{2,3},{4,5},{6,7},{8,9},{10,11},{12,13},{14,15},{16,17},{18,... | collective-permute-start | bytes 28088 | tf_op jit(solution)/shard_map/ppermute | solution.py:22
  30.2 3.5 %collective-permute-start.6 = (f32[16,16,1]{2,1,0:T(8,128)S(1)}, f32[16,16,1]{2,1,0:T(8,128)S(1)}, u32[]{:S(2)}, u32[]{:S(2)}) collective-permute-start(f32[16,16,1]{2,1,0:T(8,128)S(1)} %get-tuple-element.54), channel_id=1, source_target_pairs={{0,8},{8,16},{16,24},{1,9},{9,17},{17,25},{2,10},{10,18},{18,26},{... | collective-permute-start | bytes 3080 | tf_op jit(solution)/shard_map/ppermute | solution.py:22
  36.6 4.1 %collective-permute-done.7 = f32[16,16,1]{2,1,0:T(8,128)S(1)} collective-permute-done((f32[16,16,1]{2,1,0:T(8,128)S(1)}, f32[16,16,1]{2,1,0:T(8,128)S(1)}, u32[]{:S(2)}, u32[]{:S(2)}) %collective-permute-start.7) | collective-permute-done | bytes 1056 | tf_op jit(solution)/shard_map/ppermute | solution.py:24
  42.1 3.0 %collective-permute-start.9 = (f32[1,16,130]{2,1,0:T(8,128)S(1)}, f32[1,16,130]{2,1,0:T(8,128)S(1)}, u32[]{:S(2)}, u32[]{:S(2)}) collective-permute-start(f32[1,16,130]{2,1,0:T(8,128)S(1)} %get-tuple-element.41), channel_id=1, source_target_pairs={{0,2},{2,4},{4,6},{1,3},{3,5},{5,7},{8,10},{10,12},{12,14},{9,11},... | collective-permute-start | bytes 24968 | tf_op jit(solution)/shard_map/ppermute | solution.py:22
  47.4 4.5 %collective-permute-start.11 = (f32[18,1,130]{2,1,0:T(1,128)S(1)}, f32[18,1,130]{2,1,0:T(1,128)S(1)}, u32[]{:S(2)}, u32[]{:S(2)}) collective-permute-start(f32[18,1,130]{2,1,0:T(1,128)S(1)} %get-tuple-element.28), channel_id=1, source_target_pairs={{0,1},{2,3},{4,5},{6,7},{8,9},{10,11},{12,13},{14,15},{16,17},{18,... | collective-permute-start | bytes 28088 | tf_op jit(solution)/shard_map/ppermute | solution.py:22
  53.9 3.5 %collective-permute-start.12 = (f32[16,16,1]{2,1,0:T(8,128)S(1)}, f32[16,16,1]{2,1,0:T(8,128)S(1)}, u32[]{:S(2)}, u32[]{:S(2)}) collective-permute-start(f32[16,16,1]{2,1,0:T(8,128)S(1)} %get-tuple-element.52), channel_id=1, source_target_pairs={{0,8},{8,16},{16,24},{1,9},{9,17},{17,25},{2,10},{10,18},{18,26},{... | collective-permute-start | bytes 3080 | tf_op jit(solution)/shard_map/ppermute | solution.py:22
  60.6 4.7 %collective-permute-done.13 = f32[16,16,1]{2,1,0:T(8,128)S(1)} collective-permute-done((f32[16,16,1]{2,1,0:T(8,128)S(1)}, f32[16,16,1]{2,1,0:T(8,128)S(1)}, u32[]{:S(2)}, u32[]{:S(2)}) %collective-permute-start.13) | collective-permute-done | bytes 1056 | tf_op jit(solution)/shard_map/ppermute | solution.py:24
  72.1 4.5 %collective-permute-start.17 = (f32[18,1,130]{2,1,0:T(1,128)S(1)}, f32[18,1,130]{2,1,0:T(1,128)S(1)}, u32[]{:S(2)}, u32[]{:S(2)}) collective-permute-start(f32[18,1,130]{2,1,0:T(1,128)S(1)} %get-tuple-element.26), channel_id=1, source_target_pairs={{0,1},{2,3},{4,5},{6,7},{8,9},{10,11},{12,13},{14,15},{16,17},{18,... | collective-permute-start | bytes 28088 | tf_op jit(solution)/shard_map/ppermute | solution.py:22
  84.1 4.1 %collective-permute-done.19 = f32[16,16,1]{2,1,0:T(8,128)S(1)} collective-permute-done((f32[16,16,1]{2,1,0:T(8,128)S(1)}, f32[16,16,1]{2,1,0:T(8,128)S(1)}, u32[]{:S(2)}, u32[]{:S(2)}) %collective-permute-start.19) | collective-permute-done | bytes 1056 | tf_op jit(solution)/shard_map/ppermute | solution.py:24
  89.5 3.3 %collective-permute-start.21 = (f32[1,16,130]{2,1,0:T(8,128)S(1)}, f32[1,16,130]{2,1,0:T(8,128)S(1)}, u32[]{:S(2)}, u32[]{:S(2)}) collective-permute-start(f32[1,16,130]{2,1,0:T(8,128)S(1)} %get-tuple-element.37), channel_id=1, source_target_pairs={{0,2},{2,4},{4,6},{1,3},{3,5},{5,7},{8,10},{10,12},{12,14},{9,11},... | collective-permute-start | bytes 24968 | tf_op jit(solution)/shard_map/ppermute | solution.py:22
  95.1 4.5 %collective-permute-start.23 = (f32[18,1,130]{2,1,0:T(1,128)S(1)}, f32[18,1,130]{2,1,0:T(1,128)S(1)}, u32[]{:S(2)}, u32[]{:S(2)}) collective-permute-start(f32[18,1,130]{2,1,0:T(1,128)S(1)} %get-tuple-element.24), channel_id=1, source_target_pairs={{0,1},{2,3},{4,5},{6,7},{8,9},{10,11},{12,13},{14,15},{16,17},{18,... | collective-permute-start | bytes 28088 | tf_op jit(solution)/shard_map/ppermute | solution.py:22
  103.9 5.7 %reshape.93 = f32[4,4,4,4,32,4]{5,4,3,2,1,0:T(8,128)} reshape(f32[16,16,128]{2,1,0:T(8,128)S(1)} %fusion.70) | data formatting | bytes 262144 | tf_op jit(solution)/shard_map/reshape | solution.py:78
  114.8 11.9 %all-gather = f32[4,1,512]{2,1,0:T(1,128)S(1)} all-gather(f32[1,1,512]{2,1,0:T(1,128)S(1)} %bitcast.42), channel_id=1, replica_groups=mesh['grp'=4,'gx'=4,'gy'=2] {'grp'}, dimensions={0}, use_global_device_ids=true | all-gather | bytes 10240 | tf_op jit(solution)/shard_map/all_gather | solution.py:98
  126.7 3.1 %collective-permute-start.24 = (f32[1,1,2048]{2,1,0:T(1,128)S(1)}, f32[1,1,2048]{2,1,0:T(1,128)S(1)}, u32[]{:S(2)}, u32[]{:S(2)}) collective-permute-start(f32[1,1,2048]{2,1,0:T(1,128)S(1)} %bitcast.29), channel_id=1, source_target_pairs={{0,2},{2,4},{4,6},{1,3},{3,5},{5,7},{8,10},{10,12},{12,14},{9,11},... | collective-permute-start | bytes 24584 | tf_op jit(solution)/shard_map/ppermute | solution.py:22
  131.4 6.5 %collective-permute-done.25 = f32[1,1,2048]{2,1,0:T(1,128)S(1)} collective-permute-done((f32[1,1,2048]{2,1,0:T(1,128)S(1)}, f32[1,1,2048]{2,1,0:T(1,128)S(1)}, u32[]{:S(2)}, u32[]{:S(2)}) %collective-permute-start.25) | collective-permute-done | bytes 8224 | tf_op jit(solution)/shard_map/ppermute | solution.py:24
  141.4 4.2 %collective-permute-done.27 = f32[3,1,2048]{2,1,0:T(1,128)S(1)} collective-permute-done((f32[3,1,2048]{2,1,0:T(1,128)S(1)}, f32[3,1,2048]{2,1,0:T(1,128)S(1)}, u32[]{:S(2)}, u32[]{:S(2)}) %collective-permute-start.27) | collective-permute-done | bytes 24608 | tf_op jit(solution)/shard_map/ppermute | solution.py:24
  147.1 11.9 %all-gather.1 = f32[4,1,512]{2,1,0:T(1,128)S(1)} all-gather(f32[1,1,512]{2,1,0:T(1,128)S(1)} %bitcast.44), channel_id=1, replica_groups=mesh['grp'=4,'gx'=4,'gy'=2] {'grp'}, dimensions={0}, use_global_device_ids=true | all-gather | bytes 10240 | tf_op jit(solution)/shard_map/all_gather | solution.py:98
  161.6 4.3 %collective-permute-done.29 = f32[1,1,2048]{2,1,0:T(1,128)S(1)} collective-permute-done((f32[1,1,2048]{2,1,0:T(1,128)S(1)}, f32[1,1,2048]{2,1,0:T(1,128)S(1)}, u32[]{:S(2)}, u32[]{:S(2)}) %collective-permute-start.29) | collective-permute-done | bytes 8224 | tf_op jit(solution)/shard_map/ppermute | solution.py:24
  169.1 4.2 %collective-permute-done.31 = f32[3,1,2048]{2,1,0:T(1,128)S(1)} collective-permute-done((f32[3,1,2048]{2,1,0:T(1,128)S(1)}, f32[3,1,2048]{2,1,0:T(1,128)S(1)}, u32[]{:S(2)}, u32[]{:S(2)}) %collective-permute-start.31) | collective-permute-done | bytes 24608 | tf_op jit(solution)/shard_map/ppermute | solution.py:24
  174.8 11.9 %all-gather.2 = f32[4,1,512]{2,1,0:T(1,128)S(1)} all-gather(f32[1,1,512]{2,1,0:T(1,128)S(1)} %bitcast.43), channel_id=1, replica_groups=mesh['grp'=4,'gx'=4,'gy'=2] {'grp'}, dimensions={0}, use_global_device_ids=true | all-gather | bytes 10240 | tf_op jit(solution)/shard_map/all_gather | solution.py:98
  189.3 4.3 %collective-permute-done.33 = f32[1,1,2048]{2,1,0:T(1,128)S(1)} collective-permute-done((f32[1,1,2048]{2,1,0:T(1,128)S(1)}, f32[1,1,2048]{2,1,0:T(1,128)S(1)}, u32[]{:S(2)}, u32[]{:S(2)}) %collective-permute-start.33) | collective-permute-done | bytes 8224 | tf_op jit(solution)/shard_map/ppermute | solution.py:24
  196.7 4.2 %collective-permute-done.35 = f32[3,1,2048]{2,1,0:T(1,128)S(1)} collective-permute-done((f32[3,1,2048]{2,1,0:T(1,128)S(1)}, f32[3,1,2048]{2,1,0:T(1,128)S(1)}, u32[]{:S(2)}, u32[]{:S(2)}) %collective-permute-start.35) | collective-permute-done | bytes 24608 | tf_op jit(solution)/shard_map/ppermute | solution.py:24
  202.4 3.5 %gather_fusion.4 = f32[512]{0:T(512)S(1)} fusion(f32[512]{0:T(512)S(1)} %divide_add_fusion, s32[1024]{0:T(1024)S(1)} %pad_clamp_fusion), kind=kCustom, calls=%fused_computation.4 | custom fusion | bytes 6144 | tf_op jit(solution)/shard_map/gather | solution.py:106
  209.7 3.6 %collective-permute-done.37 = f32[16,16,1]{1,0,2:T(8,128)S(1)} collective-permute-done((f32[16,16,1]{1,0,2:T(8,128)S(1)}, f32[16,16,1]{1,0,2:T(8,128)S(1)}, u32[]{:S(2)}, u32[]{:S(2)}) %collective-permute-start.37) | collective-permute-done | bytes 1056 | tf_op jit(solution)/shard_map/ppermute | solution.py:24
  220.2 4.5 %collective-permute-start.41 = (f32[18,1,130]{2,1,0:T(1,128)S(1)}, f32[18,1,130]{2,1,0:T(1,128)S(1)}, u32[]{:S(2)}, u32[]{:S(2)}) collective-permute-start(f32[18,1,130]{2,1,0:T(1,128)S(1)} %get-tuple-element.22), channel_id=1, source_target_pairs={{0,1},{2,3},{4,5},{6,7},{8,9},{10,11},{12,13},{14,15},{16,17},{18,... | collective-permute-start | bytes 28088 | tf_op jit(solution)/shard_map/ppermute | solution.py:22
  226.7 3.8 %collective-permute-start.42 = (f32[16,16,1]{2,1,0:T(8,128)S(1)}, f32[16,16,1]{2,1,0:T(8,128)S(1)}, u32[]{:S(2)}, u32[]{:S(2)}) collective-permute-start(f32[16,16,1]{2,1,0:T(8,128)S(1)} %get-tuple-element.48), channel_id=1, source_target_pairs={{0,8},{8,16},{16,24},{1,9},{9,17},{17,25},{2,10},{10,18},{18,26},{... | collective-permute-start | bytes 3080 | tf_op jit(solution)/shard_map/ppermute | solution.py:22
  234.3 4.1 %collective-permute-done.43 = f32[16,16,1]{2,1,0:T(8,128)S(1)} collective-permute-done((f32[16,16,1]{2,1,0:T(8,128)S(1)}, f32[16,16,1]{2,1,0:T(8,128)S(1)}, u32[]{:S(2)}, u32[]{:S(2)}) %collective-permute-start.43) | collective-permute-done | bytes 1056 | tf_op jit(solution)/shard_map/ppermute | solution.py:24
  245.1 4.5 %collective-permute-start.47 = (f32[18,1,130]{2,1,0:T(1,128)S(1)}, f32[18,1,130]{2,1,0:T(1,128)S(1)}, u32[]{:S(2)}, u32[]{:S(2)}) collective-permute-start(f32[18,1,130]{2,1,0:T(1,128)S(1)} %get-tuple-element.20), channel_id=1, source_target_pairs={{0,1},{2,3},{4,5},{6,7},{8,9},{10,11},{12,13},{14,15},{16,17},{18,... | collective-permute-start | bytes 28088 | tf_op jit(solution)/shard_map/ppermute | solution.py:22
  257.3 4.6 %collective-permute-done.49 = f32[16,16,1]{2,1,0:T(8,128)S(1)} collective-permute-done((f32[16,16,1]{2,1,0:T(8,128)S(1)}, f32[16,16,1]{2,1,0:T(8,128)S(1)}, u32[]{:S(2)}, u32[]{:S(2)}) %collective-permute-start.49) | collective-permute-done | bytes 1056 | tf_op jit(solution)/shard_map/ppermute | solution.py:24
  268.6 4.5 %collective-permute-start.53 = (f32[18,1,130]{2,1,0:T(1,128)S(1)}, f32[18,1,130]{2,1,0:T(1,128)S(1)}, u32[]{:S(2)}, u32[]{:S(2)}) collective-permute-start(f32[18,1,130]{2,1,0:T(1,128)S(1)} %get-tuple-element.18), channel_id=1, source_target_pairs={{0,1},{2,3},{4,5},{6,7},{8,9},{10,11},{12,13},{14,15},{16,17},{18,... | collective-permute-start | bytes 28088 | tf_op jit(solution)/shard_map/ppermute | solution.py:22
  (171 shorter events, 115.0 us)
Async XLA Ops:
  1.7 7.8 %collective-permute-start = (f32[16,16,1]{2,1,0:T(8,128)S(1)}, f32[16,16,1]{2,1,0:T(8,128)S(1)}, u32[]{:S(2)}, u32[]{:S(2)}) collective-permute-start(f32[16,16,1]{2,1,0:T(8,128)S(1)} %get-tuple-element.55), channel_id=1, source_target_pairs={{0,8},{8,16},{16,24},{1,9},{9,17},{17,25},{2,10},{10,18},{18,26},{... | collective-permute-start | bytes 3080 | tf_op jit(solution)/shard_map/ppermute | solution.py:22
  6.8 6.9 %collective-permute-start.1 = (f32[16,16,1]{2,1,0:T(8,128)S(1)}, f32[16,16,1]{2,1,0:T(8,128)S(1)}, u32[]{:S(2)}, u32[]{:S(2)}) collective-permute-start(f32[16,16,1]{2,1,0:T(8,128)S(1)} %get-tuple-element.56), channel_id=1, source_target_pairs={{8,0},{16,8},{24,16},{9,1},{17,9},{25,17},{10,2},{18,10},{26,18},{... | collective-permute-start | bytes 3080 | tf_op jit(solution)/shard_map/ppermute | solution.py:24
  20.7 5.9 %collective-permute-start.4 = (f32[18,1,130]{2,1,0:T(1,128)S(1)}, f32[18,1,130]{2,1,0:T(1,128)S(1)}, u32[]{:S(2)}, u32[]{:S(2)}) collective-permute-start(f32[18,1,130]{2,1,0:T(1,128)S(1)} %get-tuple-element.30), channel_id=1, source_target_pairs={{1,0},{3,2},{5,4},{7,6},{9,8},{11,10},{13,12},{15,14},{17,16},{19,... | collective-permute-start | bytes 28088 | tf_op jit(solution)/shard_map/ppermute | solution.py:24
  22.0 6.0 %collective-permute-start.5 = (f32[18,1,130]{2,1,0:T(1,128)S(1)}, f32[18,1,130]{2,1,0:T(1,128)S(1)}, u32[]{:S(2)}, u32[]{:S(2)}) collective-permute-start(f32[18,1,130]{2,1,0:T(1,128)S(1)} %get-tuple-element.29), channel_id=1, source_target_pairs={{0,1},{2,3},{4,5},{6,7},{8,9},{10,11},{12,13},{14,15},{16,17},{18,... | collective-permute-start | bytes 28088 | tf_op jit(solution)/shard_map/ppermute | solution.py:22
  30.2 6.4 %collective-permute-start.6 = (f32[16,16,1]{2,1,0:T(8,128)S(1)}, f32[16,16,1]{2,1,0:T(8,128)S(1)}, u32[]{:S(2)}, u32[]{:S(2)}) collective-permute-start(f32[16,16,1]{2,1,0:T(8,128)S(1)} %get-tuple-element.54), channel_id=1, source_target_pairs={{0,8},{8,16},{16,24},{1,9},{9,17},{17,25},{2,10},{10,18},{18,26},{... | collective-permute-start | bytes 3080 | tf_op jit(solution)/shard_map/ppermute | solution.py:22
  33.6 7.0 %collective-permute-start.7 = (f32[16,16,1]{2,1,0:T(8,128)S(1)}, f32[16,16,1]{2,1,0:T(8,128)S(1)}, u32[]{:S(2)}, u32[]{:S(2)}) collective-permute-start(f32[16,16,1]{2,1,0:T(8,128)S(1)} %get-tuple-element.53), channel_id=1, source_target_pairs={{8,0},{16,8},{24,16},{9,1},{17,9},{25,17},{10,2},{18,10},{26,18},{... | collective-permute-start | bytes 3080 | tf_op jit(solution)/shard_map/ppermute | solution.py:24
  46.1 5.9 %collective-permute-start.10 = (f32[18,1,130]{2,1,0:T(1,128)S(1)}, f32[18,1,130]{2,1,0:T(1,128)S(1)}, u32[]{:S(2)}, u32[]{:S(2)}) collective-permute-start(f32[18,1,130]{2,1,0:T(1,128)S(1)} %get-tuple-element.27), channel_id=1, source_target_pairs={{1,0},{3,2},{5,4},{7,6},{9,8},{11,10},{13,12},{15,14},{17,16},{19,... | collective-permute-start | bytes 28088 | tf_op jit(solution)/shard_map/ppermute | solution.py:24
  47.4 6.0 %collective-permute-start.11 = (f32[18,1,130]{2,1,0:T(1,128)S(1)}, f32[18,1,130]{2,1,0:T(1,128)S(1)}, u32[]{:S(2)}, u32[]{:S(2)}) collective-permute-start(f32[18,1,130]{2,1,0:T(1,128)S(1)} %get-tuple-element.28), channel_id=1, source_target_pairs={{0,1},{2,3},{4,5},{6,7},{8,9},{10,11},{12,13},{14,15},{16,17},{18,... | collective-permute-start | bytes 28088 | tf_op jit(solution)/shard_map/ppermute | solution.py:22
  53.9 6.7 %collective-permute-start.12 = (f32[16,16,1]{2,1,0:T(8,128)S(1)}, f32[16,16,1]{2,1,0:T(8,128)S(1)}, u32[]{:S(2)}, u32[]{:S(2)}) collective-permute-start(f32[16,16,1]{2,1,0:T(8,128)S(1)} %get-tuple-element.52), channel_id=1, source_target_pairs={{0,8},{8,16},{16,24},{1,9},{9,17},{17,25},{2,10},{10,18},{18,26},{... | collective-permute-start | bytes 3080 | tf_op jit(solution)/shard_map/ppermute | solution.py:22
  57.4 7.9 %collective-permute-start.13 = (f32[16,16,1]{2,1,0:T(8,128)S(1)}, f32[16,16,1]{2,1,0:T(8,128)S(1)}, u32[]{:S(2)}, u32[]{:S(2)}) collective-permute-start(f32[16,16,1]{2,1,0:T(8,128)S(1)} %get-tuple-element.51), channel_id=1, source_target_pairs={{8,0},{16,8},{24,16},{9,1},{17,9},{25,17},{10,2},{18,10},{26,18},{... | collective-permute-start | bytes 3080 | tf_op jit(solution)/shard_map/ppermute | solution.py:24
  70.8 5.9 %collective-permute-start.16 = (f32[18,1,130]{2,1,0:T(1,128)S(1)}, f32[18,1,130]{2,1,0:T(1,128)S(1)}, u32[]{:S(2)}, u32[]{:S(2)}) collective-permute-start(f32[18,1,130]{2,1,0:T(1,128)S(1)} %get-tuple-element.25), channel_id=1, source_target_pairs={{1,0},{3,2},{5,4},{7,6},{9,8},{11,10},{13,12},{15,14},{17,16},{19,... | collective-permute-start | bytes 28088 | tf_op jit(solution)/shard_map/ppermute | solution.py:24
  72.1 6.0 %collective-permute-start.17 = (f32[18,1,130]{2,1,0:T(1,128)S(1)}, f32[18,1,130]{2,1,0:T(1,128)S(1)}, u32[]{:S(2)}, u32[]{:S(2)}) collective-permute-start(f32[18,1,130]{2,1,0:T(1,128)S(1)} %get-tuple-element.26), channel_id=1, source_target_pairs={{0,1},{2,3},{4,5},{6,7},{8,9},{10,11},{12,13},{14,15},{16,17},{18,... | collective-permute-start | bytes 28088 | tf_op jit(solution)/shard_map/ppermute | solution.py:22
  80.8 7.4 %collective-permute-start.19 = (f32[16,16,1]{2,1,0:T(8,128)S(1)}, f32[16,16,1]{2,1,0:T(8,128)S(1)}, u32[]{:S(2)}, u32[]{:S(2)}) collective-permute-start(f32[16,16,1]{2,1,0:T(8,128)S(1)} %get-tuple-element.49), channel_id=1, source_target_pairs={{8,0},{16,8},{24,16},{9,1},{17,9},{25,17},{10,2},{18,10},{26,18},{... | collective-permute-start | bytes 3080 | tf_op jit(solution)/shard_map/ppermute | solution.py:24
  93.8 9.5 %collective-permute-start.22 = (f32[18,1,130]{2,1,0:T(1,128)S(1)}, f32[18,1,130]{2,1,0:T(1,128)S(1)}, u32[]{:S(2)}, u32[]{:S(2)}) collective-permute-start(f32[18,1,130]{2,1,0:T(1,128)S(1)} %get-tuple-element.23), channel_id=1, source_target_pairs={{1,0},{3,2},{5,4},{7,6},{9,8},{11,10},{13,12},{15,14},{17,16},{19,... | collective-permute-start | bytes 28088 | tf_op jit(solution)/shard_map/ppermute | solution.py:24
  95.1 8.2 %collective-permute-start.23 = (f32[18,1,130]{2,1,0:T(1,128)S(1)}, f32[18,1,130]{2,1,0:T(1,128)S(1)}, u32[]{:S(2)}, u32[]{:S(2)}) collective-permute-start(f32[18,1,130]{2,1,0:T(1,128)S(1)} %get-tuple-element.24), channel_id=1, source_target_pairs={{0,1},{2,3},{4,5},{6,7},{8,9},{10,11},{12,13},{14,15},{16,17},{18,... | collective-permute-start | bytes 28088 | tf_op jit(solution)/shard_map/ppermute | solution.py:22
  129.8 8.0 %collective-permute-start.25 = (f32[1,1,2048]{2,1,0:T(1,128)S(1)}, f32[1,1,2048]{2,1,0:T(1,128)S(1)}, u32[]{:S(2)}, u32[]{:S(2)}) collective-permute-start(f32[1,1,2048]{2,1,0:T(1,128)S(1)} %bitcast.30), channel_id=1, source_target_pairs={{2,0},{4,2},{6,4},{3,1},{5,3},{7,5},{10,8},{12,10},{14,12},{11,9},... | collective-permute-start | bytes 24584 | tf_op jit(solution)/shard_map/ppermute | solution.py:24
  139.9 5.7 %collective-permute-start.27 = (f32[3,1,2048]{2,1,0:T(1,128)S(1)}, f32[3,1,2048]{2,1,0:T(1,128)S(1)}, u32[]{:S(2)}, u32[]{:S(2)}) collective-permute-start(f32[3,1,2048]{2,1,0:T(1,128)S(1)} %pad_maximum_fusion.129), channel_id=1, source_target_pairs={{1,0},{3,2},{5,4},{7,6},{9,8},{11,10},{13,12},{15,14},{17,16},{19,... | collective-permute-start | bytes 73736 | tf_op jit(solution)/shard_map/ppermute | solution.py:24
  160.3 5.6 %collective-permute-start.29 = (f32[1,1,2048]{2,1,0:T(1,128)S(1)}, f32[1,1,2048]{2,1,0:T(1,128)S(1)}, u32[]{:S(2)}, u32[]{:S(2)}) collective-permute-start(f32[1,1,2048]{2,1,0:T(1,128)S(1)} %bitcast.38), channel_id=1, source_target_pairs={{2,0},{4,2},{6,4},{3,1},{5,3},{7,5},{10,8},{12,10},{14,12},{11,9},... | collective-permute-start | bytes 24584 | tf_op jit(solution)/shard_map/ppermute | solution.py:24
  167.6 5.7 %collective-permute-start.31 = (f32[3,1,2048]{2,1,0:T(1,128)S(1)}, f32[3,1,2048]{2,1,0:T(1,128)S(1)}, u32[]{:S(2)}, u32[]{:S(2)}) collective-permute-start(f32[3,1,2048]{2,1,0:T(1,128)S(1)} %pad_maximum_fusion.130), channel_id=1, source_target_pairs={{1,0},{3,2},{5,4},{7,6},{9,8},{11,10},{13,12},{15,14},{17,16},{19,... | collective-permute-start | bytes 73736 | tf_op jit(solution)/shard_map/ppermute | solution.py:24
  188.0 5.6 %collective-permute-start.33 = (f32[1,1,2048]{2,1,0:T(1,128)S(1)}, f32[1,1,2048]{2,1,0:T(1,128)S(1)}, u32[]{:S(2)}, u32[]{:S(2)}) collective-permute-start(f32[1,1,2048]{2,1,0:T(1,128)S(1)} %bitcast.34), channel_id=1, source_target_pairs={{2,0},{4,2},{6,4},{3,1},{5,3},{7,5},{10,8},{12,10},{14,12},{11,9},... | collective-permute-start | bytes 24584 | tf_op jit(solution)/shard_map/ppermute | solution.py:24
  195.2 5.7 %collective-permute-start.35 = (f32[3,1,2048]{2,1,0:T(1,128)S(1)}, f32[3,1,2048]{2,1,0:T(1,128)S(1)}, u32[]{:S(2)}, u32[]{:S(2)}) collective-permute-start(f32[3,1,2048]{2,1,0:T(1,128)S(1)} %pad_maximum_fusion.131), channel_id=1, source_target_pairs={{1,0},{3,2},{5,4},{7,6},{9,8},{11,10},{13,12},{15,14},{17,16},{19,... | collective-permute-start | bytes 73736 | tf_op jit(solution)/shard_map/ppermute | solution.py:24
  207.6 5.7 %collective-permute-start.37 = (f32[16,16,1]{1,0,2:T(8,128)S(1)}, f32[16,16,1]{1,0,2:T(8,128)S(1)}, u32[]{:S(2)}, u32[]{:S(2)}) collective-permute-start(f32[16,16,1]{1,0,2:T(8,128)S(1)} %get-tuple-element.15), channel_id=1, source_target_pairs={{8,0},{16,8},{24,16},{9,1},{17,9},{25,17},{10,2},{18,10},{26,18},{... | collective-permute-start | bytes 3080 | tf_op jit(solution)/shard_map/ppermute | solution.py:24
  218.9 5.9 %collective-permute-start.40 = (f32[18,1,130]{2,1,0:T(1,128)S(1)}, f32[18,1,130]{2,1,0:T(1,128)S(1)}, u32[]{:S(2)}, u32[]{:S(2)}) collective-permute-start(f32[18,1,130]{2,1,0:T(1,128)S(1)} %get-tuple-element.21), channel_id=1, source_target_pairs={{1,0},{3,2},{5,4},{7,6},{9,8},{11,10},{13,12},{15,14},{17,16},{19,... | collective-permute-start | bytes 28088 | tf_op jit(solution)/shard_map/ppermute | solution.py:24
  220.2 6.0 %collective-permute-start.41 = (f32[18,1,130]{2,1,0:T(1,128)S(1)}, f32[18,1,130]{2,1,0:T(1,128)S(1)}, u32[]{:S(2)}, u32[]{:S(2)}) collective-permute-start(f32[18,1,130]{2,1,0:T(1,128)S(1)} %get-tuple-element.22), channel_id=1, source_target_pairs={{0,1},{2,3},{4,5},{6,7},{8,9},{10,11},{12,13},{14,15},{16,17},{18,... | collective-permute-start | bytes 28088 | tf_op jit(solution)/shard_map/ppermute | solution.py:22
  226.7 7.6 %collective-permute-start.42 = (f32[16,16,1]{2,1,0:T(8,128)S(1)}, f32[16,16,1]{2,1,0:T(8,128)S(1)}, u32[]{:S(2)}, u32[]{:S(2)}) collective-permute-start(f32[16,16,1]{2,1,0:T(8,128)S(1)} %get-tuple-element.48), channel_id=1, source_target_pairs={{0,8},{8,16},{16,24},{1,9},{9,17},{17,25},{2,10},{10,18},{18,26},{... | collective-permute-start | bytes 3080 | tf_op jit(solution)/shard_map/ppermute | solution.py:22
  230.6 7.9 %collective-permute-start.43 = (f32[16,16,1]{2,1,0:T(8,128)S(1)}, f32[16,16,1]{2,1,0:T(8,128)S(1)}, u32[]{:S(2)}, u32[]{:S(2)}) collective-permute-start(f32[16,16,1]{2,1,0:T(8,128)S(1)} %get-tuple-element.47), channel_id=1, source_target_pairs={{8,0},{16,8},{24,16},{9,1},{17,9},{25,17},{10,2},{18,10},{26,18},{... | collective-permute-start | bytes 3080 | tf_op jit(solution)/shard_map/ppermute | solution.py:24
  243.8 5.9 %collective-permute-start.46 = (f32[18,1,130]{2,1,0:T(1,128)S(1)}, f32[18,1,130]{2,1,0:T(1,128)S(1)}, u32[]{:S(2)}, u32[]{:S(2)}) collective-permute-start(f32[18,1,130]{2,1,0:T(1,128)S(1)} %get-tuple-element.19), channel_id=1, source_target_pairs={{1,0},{3,2},{5,4},{7,6},{9,8},{11,10},{13,12},{15,14},{17,16},{19,... | collective-permute-start | bytes 28088 | tf_op jit(solution)/shard_map/ppermute | solution.py:24
  245.1 6.0 %collective-permute-start.47 = (f32[18,1,130]{2,1,0:T(1,128)S(1)}, f32[18,1,130]{2,1,0:T(1,128)S(1)}, u32[]{:S(2)}, u32[]{:S(2)}) collective-permute-start(f32[18,1,130]{2,1,0:T(1,128)S(1)} %get-tuple-element.20), channel_id=1, source_target_pairs={{0,1},{2,3},{4,5},{6,7},{8,9},{10,11},{12,13},{14,15},{16,17},{18,... | collective-permute-start | bytes 28088 | tf_op jit(solution)/shard_map/ppermute | solution.py:22
  251.6 5.7 %collective-permute-start.48 = (f32[16,16,1]{2,1,0:T(8,128)S(1)}, f32[16,16,1]{2,1,0:T(8,128)S(1)}, u32[]{:S(2)}, u32[]{:S(2)}) collective-permute-start(f32[16,16,1]{2,1,0:T(8,128)S(1)} %get-tuple-element.46), channel_id=1, source_target_pairs={{0,8},{8,16},{16,24},{1,9},{9,17},{17,25},{2,10},{10,18},{18,26},{... | collective-permute-start | bytes 3080 | tf_op jit(solution)/shard_map/ppermute | solution.py:22
  253.8 8.1 %collective-permute-start.49 = (f32[16,16,1]{2,1,0:T(8,128)S(1)}, f32[16,16,1]{2,1,0:T(8,128)S(1)}, u32[]{:S(2)}, u32[]{:S(2)}) collective-permute-start(f32[16,16,1]{2,1,0:T(8,128)S(1)} %get-tuple-element.45), channel_id=1, source_target_pairs={{8,0},{16,8},{24,16},{9,1},{17,9},{25,17},{10,2},{18,10},{26,18},{... | collective-permute-start | bytes 3080 | tf_op jit(solution)/shard_map/ppermute | solution.py:24
  267.3 5.9 %collective-permute-start.52 = (f32[18,1,130]{2,1,0:T(1,128)S(1)}, f32[18,1,130]{2,1,0:T(1,128)S(1)}, u32[]{:S(2)}, u32[]{:S(2)}) collective-permute-start(f32[18,1,130]{2,1,0:T(1,128)S(1)} %get-tuple-element.17), channel_id=1, source_target_pairs={{1,0},{3,2},{5,4},{7,6},{9,8},{11,10},{13,12},{15,14},{17,16},{19,... | collective-permute-start | bytes 28088 | tf_op jit(solution)/shard_map/ppermute | solution.py:24
  268.6 6.0 %collective-permute-start.53 = (f32[18,1,130]{2,1,0:T(1,128)S(1)}, f32[18,1,130]{2,1,0:T(1,128)S(1)}, u32[]{:S(2)}, u32[]{:S(2)}) collective-permute-start(f32[18,1,130]{2,1,0:T(1,128)S(1)} %get-tuple-element.18), channel_id=1, source_target_pairs={{0,1},{2,3},{4,5},{6,7},{8,9},{10,11},{12,13},{14,15},{16,17},{18,... | collective-permute-start | bytes 28088 | tf_op jit(solution)/shard_map/ppermute | solution.py:22
  (28 other events, 289.6 us)
where the time goes:
time: 280 us; the launch traced here: 276 us
  starting transfers between devices  121 us (43%)
  waiting for transfers between devices  81.6 us (29%)
  blocking collectives  35.7 us (13%)
  local copies, waits for them, and re-layouts  22.8 us (8%)
  other arithmetic  11.5 us (4%)
    ppermute x27, starting transfers between devices, padded_2(): lax.ppermute(tail, axis, [(i, (i + 1) % count) for i in range(ends)])  85.8 us
    ppermute x27, waiting for transfers between devices, padded_2(): lax.ppermute(head, axis, [((i + 1) % count, i) for i in range(ends)])  57.2 us
    all_gather x3, blocking collectives, local(): pooled = lax.all_gather(coarse_error, 'grp', axis=0, tiled=True)  35.7 us
    ppermute x27, starting transfers between devices, padded_2(): lax.ppermute(head, axis, [((i + 1) % count, i) for i in range(ends)])  35.2 us
    ppermute x27, waiting for transfers between devices, padded_2(): lax.ppermute(tail, axis, [(i, (i + 1) % count) for i in range(ends)])  24.5 us
    reshape x1, local copies, waits for them, and re-layouts, local(): smoothed.reshape(size_x // 4, 4, size_y // 4, 4, size_z // 4, 4)  5.72 us
  transfers between devices with their start and end apart: 54, of which 34 were waited for; matrix products, arithmetic and copies ran while one was open for 2% of the time, Pallas kernels for 0%

commit v1 on v0

v1 whole, which is shorter than its diff:
```python
import jax
import jax.numpy as jnp
from jax import lax
from jax.sharding import PartitionSpec as P

NU = 2
CITER = 4
BOX = 4
HALO = 4

WEIGHT = 2.0 / 3.0
PAIRS = ((0, 1), (0, -1), (1, 1), (1, -1), (2, 1), (2, -1))
ALL_AXES = ("grp", "gx", "gy")


def exchange(cells, sides, width):
    for axis, dim in sides:
        count = lax.axis_size(axis)
        size = cells.shape[dim]
        head = lax.slice_in_dim(cells, 0, width, axis=dim)
        tail = lax.slice_in_dim(cells, size - width, size, axis=dim)
        if count == 1:
            before = jnp.zeros_like(tail)
            after = jnp.zeros_like(head)
        elif count == 2:
            index = lax.axis_index(axis)
            sent = jnp.where(index == 0, tail, head)
            got = lax.ppermute(sent, axis, [(0, 1), (1, 0)])
            before = jnp.where(index == 1, got, 0.0)
            after = jnp.where(index == 0, got, 0.0)
        else:
            before = lax.ppermute(tail, axis, [(i, i + 1) for i in range(count - 1)])
            after = lax.ppermute(head, axis, [(i + 1, i) for i in range(count - 1)])
        cells = jnp.concatenate([before, cells, after], axis=dim)
    return cells


def shifted(padded, dimension, offset):
    window = [slice(1, -1), slice(1, -1), slice(1, -1)]
    window[dimension] = slice(1 + offset, padded.shape[dimension] - 1 + offset)
    return padded[tuple(window)]


def face_terms(conductance):
    padded = jnp.pad(conductance, 1)
    return [0.5 * (conductance + shifted(padded, dimension, offset)) for dimension, offset in PAIRS]


def operate(field, storage, face_list):
    padded = jnp.pad(field, 1)
    summed = storage * field
    for position in range(6):
        dimension, offset = PAIRS[position]
        summed = summed + face_list[position] * (field - shifted(padded, dimension, offset))
    return summed


def inside_mask(shape):
    mask = None
    for dim, axis in ((0, "gx"), (1, "gy"), (2, "grp")):
        block = shape[dim] - 2 * HALO
        start = lax.axis_index(axis) * block - HALO
        coords = start + lax.broadcasted_iota(jnp.int32, shape, dim)
        ok = (coords >= 0) & (coords < block * lax.axis_size(axis))
        mask = ok if mask is None else mask & ok
    return mask


def trimmed(array):
    return array[HALO:-HALO, HALO:-HALO, HALO:-HALO]


def local(source, conductance, storage, aggregate_ids, coarse_values, coarse_columns):
    size_x, size_y, size_z = source.shape
    stacked = jnp.stack([source, conductance, storage])
    wide = exchange(stacked, (("grp", 3), ("gx", 1), ("gy", 2)), HALO)
    src, cond, stor = wide[0], wide[1], wide[2]
    mask = inside_mask(src.shape)
    face_list = face_terms(cond)
    diagonal = stor
    for position in range(6):
        diagonal = diagonal + face_list[position]

    def op(field):
        return operate(field, stor, face_list)

    solution = jnp.where(mask, WEIGHT * src / diagonal, 0.0)
    for sweep_number in range(NU - 1):
        solution = jnp.where(mask, solution + WEIGHT * (src - op(solution)) / diagonal, 0.0)
    residual = src - op(solution)
    scaled = jnp.where(mask, residual / diagonal, 0.0)
    smoothed = trimmed(residual - WEIGHT * op(scaled))

    box_labels = aggregate_ids[::BOX, ::BOX, ::BOX].reshape(-1)
    box_totals = (
        smoothed.reshape(size_x // BOX, BOX, size_y // BOX, BOX, size_z // BOX, BOX)
        .sum(axis=(1, 3, 5))
        .reshape(-1)
    )
    coarse_rhs = jnp.zeros(box_totals.shape, source.dtype).at[box_labels].set(box_totals)
    coarse_diag = jnp.diagonal(coarse_values[:, :, :64], axis1=1, axis2=2).reshape(-1)
    block_rows = coarse_values.shape[0]
    coarse_error = coarse_rhs / coarse_diag
    for sweep_number in range(CITER - 1):
        pooled = lax.all_gather(coarse_error, ALL_AXES, axis=0, tiled=True)
        blocks = pooled.reshape(-1, 64)[coarse_columns]
        blocks = blocks.reshape(block_rows, -1)
        applied = jnp.einsum(
            "bim,bm->bi", coarse_values, blocks, precision=lax.Precision.HIGHEST
        ).reshape(-1)
        coarse_error = coarse_error + (coarse_rhs - applied) / coarse_diag

    bx, by, bz = size_x // BOX, size_y // BOX, size_z // BOX
    groups = lax.axis_size("grp")
    grid_x = lax.axis_size("gx")
    grid_y = lax.axis_size("gy")
    small = coarse_error[box_labels]
    every = lax.all_gather(small, ALL_AXES, axis=0, tiled=True)
    every = every.reshape(groups, grid_x, grid_y, bx, by, bz)
    boxes = every.transpose(1, 3, 2, 4, 0, 5).reshape(grid_x * bx, grid_y * by, groups * bz)
    boxes = jnp.pad(boxes, 1)
    window = lax.dynamic_slice(
        boxes,
        (lax.axis_index("gx") * bx, lax.axis_index("gy") * by, lax.axis_index("grp") * bz),
        (bx + 2, by + 2, bz + 2),
    )
    lifted = jnp.repeat(jnp.repeat(jnp.repeat(window, BOX, axis=0), BOX, axis=1), BOX, axis=2)
    solution = jnp.where(mask, solution + (lifted - WEIGHT * op(lifted) / diagonal), 0.0)
    for sweep_number in range(NU):
        solution = jnp.where(mask, solution + WEIGHT * (src - op(solution)) / diagonal, 0.0)
    return (trimmed(solution), coarse_error)


def solution(mesh):
    return jax.shard_map(
        local,
        mesh=mesh,
        in_specs=(
            P("gx", "gy", "grp"),
            P("gx", "gy", "grp"),
            P("gx", "gy", "grp"),
            P("gx", "gy", "grp"),
            P(("grp", "gx", "gy"), None, None),
            P(("grp", "gx", "gy"), None),
        ),
        out_specs=(P("gx", "gy", "grp"), P(("grp", "gx", "gy"))),
        check_vma=False,
    )
```

time: 280 us -> 397 us (1.42)
  blocking collectives: 35.7 us -> 260 us
  starting transfers between devices: 121 us -> 10.3 us
  waiting for transfers between devices: 81.6 us -> 10.8 us
  other arithmetic: 11.5 us -> 66.8 us
  local copies, waits for them, and re-layouts: 22.8 us -> 42.6 us
    all_gather x3 -> x4, blocking collectives: 35.7 us -> 260 us  [the longest x3 194 us: local(): pooled = lax.all_gather(coarse_error, ALL_AXES, axis=0, tiled=True)]
    ppermute x54 -> x5, starting transfers between devices: 121 us -> 10.3 us  [the longest x2 6.25 us: exchange(): before = lax.ppermute(tail, axis, [(i, i + 1) for i in range(count - 1)])]
    ppermute x54 -> x5, waiting for transfers between devices: 81.6 us -> 10.8 us  [the longest x2 7.88 us: exchange(): after = lax.ppermute(head, axis, [(i + 1, i) for i in range(count - 1)])]
    select_n x1 -> x9, other arithmetic: 0.04 us -> 34.9 us  [the longest x3 14.6 us: local(): jnp.where(mask, solution + WEIGHT * (src - op(solution)) / diagonal, 0.0)]
    select_n x1 -> x3, local copies, waits for them, and re-layouts: 0.08 us -> 7.36 us  [the longest x1 3.65 us: exchange(): after = jnp.where(index == 0, got, 0.0)]
    sub x1, other arithmetic: 0.63 us -> 6.69 us  [local(): smoothed = trimmed(residual - WEIGHT * op(scaled))]
    concatenate x14 -> x2, other arithmetic: 2.59 us -> 8.38 us  [exchange(): cells = jnp.concatenate([before, cells, after], axis=dim)]
    add x4 -> x2, other arithmetic: 2.08 us -> 6.92 us  [operate(): summed + face_list[position] * (field - shifted(padded, dimension, offset))]
  transfers between devices with their start and end apart: 54 -> 5, of which waited for: 34 -> 3; matrix products, arithmetic and copies ran while one was open for 2% -> 3% of each run, Pallas kernels for 0% -> 0%
where the time goes in v1:
time: 397 us; the launch traced here: 396 us
  blocking collectives  260 us (65%)
  other arithmetic  66.8 us (17%)
  local copies, waits for them, and re-layouts  42.6 us (11%)
  waiting for transfers between devices  10.8 us (3%)
  starting transfers between devices  10.3 us (3%)
  matrix products  4.67 us (1%)
    all_gather x3, blocking collectives, local(): pooled = lax.all_gather(coarse_error, ALL_AXES, axis=0, tiled=True)  194 us
    all_gather x1, blocking collectives, local(): every = lax.all_gather(small, ALL_AXES, axis=0, tiled=True)  65.9 us
    select_n x3, other arithmetic, local(): jnp.where(mask, solution + WEIGHT * (src - op(solution)) / diagonal, 0.0)  14.6 us
    select_n x1, other arithmetic, local(): jnp.where(mask, solution + (lifted - WEIGHT * op(lifted) / diagonal), 0.0)  11.7 us
    concatenate x2, other arithmetic, exchange(): cells = jnp.concatenate([before, cells, after], axis=dim)  8.38 us
  transfers between devices with their start and end apart: 5, of which 3 were waited for; matrix products, arithmetic and copies ran while one was open for 3% of the time, Pallas kernels for 0%

profile of v1, /device:TPU:0, one launch (start us, length us, event | category | flops | bytes accessed | tf_op | source)
XLA Modules:
  0.0 396.2 jit_solution(6078403444874472616)
XLA Ops:
  2.0 5.0 %collective-permute-start = (f32[3,16,16,4]{3,2,1,0:T(8,128)S(1)}, f32[3,16,16,4]{3,2,1,0:T(8,128)S(1)}, u32[]{:S(2)}, u32[]{:S(2)}) collective-permute-start(f32[3,16,16,4]{3,2,1,0:T(8,128)S(1)} %get-tuple-element.35), channel_id=1, source_target_pairs={{0,8},{8,16},{16,24},{1,9},{9,17},{17,25},{2,10},{10,18},{18,26},{... | collective-permute-start | bytes 36872 | tf_op jit(solution)/shard_map/ppermute | solution.py:32
  8.3 1.9 slice.186
  12.4 2.9 collective-permute-done
  15.3 4.1 %collective-permute-done.1 = f32[3,16,16,4]{3,2,1,0:T(8,128)S(1)} collective-permute-done((f32[3,16,16,4]{3,2,1,0:T(8,128)S(1)}, f32[3,16,16,4]{3,2,1,0:T(8,128)S(1)}, u32[]{:S(2)}, u32[]{:S(2)}) %collective-permute-start.1) | collective-permute-done | bytes 12320 | tf_op jit(solution)/shard_map/ppermute | solution.py:33
  22.3 3.7 collective-permute-done.3
  31.8 3.5 copy.65
  36.3 3.6 copy.64
  39.9 3.7 copy.66
  43.6 8.0 %pad_maximum_fusion = f32[3,24,24,136]{2,1,3,0:T(8,128)S(1)} fusion(f32[3,24,4,136]{2,1,3,0:T(8,128)} %copy.66, f32[3,24,16,136]{2,1,3,0:T(8,128)} %copy.65, f32[3,24,4,136]{2,1,3,0:T(8,128)} %copy.64), kind=kLoop, calls=%fused_computation.14 | loop fusion | flops 470016 | bytes 1880064 | tf_op jit(solution)/shard_map/concatenate | solution.py:34
  51.6 1.6 slice_bitcast_fusion.2
  53.2 2.8 divide_select_fusion.1
  56.0 3.1 fusion.118
  59.1 4.0 %divide_select_fusion = (f32[24,24,136]{1,0,2:T(8,128)S(1)}, f32[24,24,136]{1,0,2:T(8,128)}) fusion(f32[24,24,136]{1,0,2:T(8,128)S(1)} %get-tuple-element.15, pred[136]{0:T(512)(128)(4,1)S(1)} %copy-done.22, pred[24]{0:T(512)(128)(4,1)S(1)} %get-tuple-element.39, pred[24]{0:T(512)(128)(4,1)S(1)} %get-tuple-element.40, ...), kind=kLoop, calls=%fused_computation.177 | loop fusion | flops 1880064 | bytes 3760312 | tf_op jit(solution)/shard_map/jit(_where)/select_n | solution.py:91
  63.1 3.6 fusion.56
  66.7 6.7 %slice_subtract_fusion.1 = f32[16,16,128]{1,0,2:T(8,128)} fusion(f32[24,24,136]{1,0,2:T(8,128)S(1)} %copy-done.14, f32[24,24,136]{1,0,2:T(8,128)S(1)} %get-tuple-element.21, f32[24,24,136]{1,0,2:T(8,128)} %get-tuple-element.29, f32[24,24,136]{1,0,2:T(8,128)S(1)} %get-tuple-element.20, f32[24,24,136]{1,0,2:T(8,128)} %get-tuple-element.30, ...), kind=kLoop, calls=%fused_computation.190 | loop fusion | flops 360448 | bytes 1441792 | tf_op jit(solution)/shard_map/sub | solution.py:92
  73.4 1.6 copy.67
  75.0 5.7 %reshape.87 = f32[4,4,4,4,32,4]{5,4,3,2,1,0:T(8,128)} reshape(f32[16,16,128]{2,1,0:T(8,128)S(1)} %copy.67) | data formatting | bytes 262144 | tf_op jit(solution)/shard_map/reshape | solution.py:96
  80.7 2.6 reduce_sum.9
  83.4 2.6 scatter_custom_fusion
  86.0 64.4 %all-gather.1 = f32[32,1,512]{2,1,0:T(1,128)S(1)} all-gather(f32[1,1,512]{2,1,0:T(1,128)S(1)} %bitcast.128), channel_id=1, replica_groups=mesh['grp'=4,'gx'=4,'gy'=2] {'grp','gx','gy'}, dimensions={0}, use_global_device_ids=true | all-gather | bytes 67584 | tf_op jit(solution)/shard_map/all_gather | solution.py:105
  153.6 65.7 %all-gather.2 = f32[32,1,512]{2,1,0:T(1,128)S(1)} all-gather(f32[1,1,512]{2,1,0:T(1,128)S(1)} %bitcast.127), channel_id=1, replica_groups=mesh['grp'=4,'gx'=4,'gy'=2] {'grp','gx','gy'}, dimensions={0}, use_global_device_ids=true | all-gather | bytes 67584 | tf_op jit(solution)/shard_map/all_gather | solution.py:105
  222.5 63.9 %all-gather.3 = f32[32,1,512]{2,1,0:T(1,128)S(1)} all-gather(f32[1,1,512]{2,1,0:T(1,128)S(1)} %bitcast.126), channel_id=1, replica_groups=mesh['grp'=4,'gx'=4,'gy'=2] {'grp','gx','gy'}, dimensions={0}, use_global_device_ids=true | all-gather | bytes 67584 | tf_op jit(solution)/shard_map/all_gather | solution.py:105
  287.4 1.6 fusion.138
  289.7 3.6 gather_fusion.4
  293.3 65.9 %all-gather.4 = f32[32,1,512]{2,1,0:T(1,128)S(1)} all-gather(f32[1,1,512]{2,1,0:T(1,128)S(1)} %bitcast.134), channel_id=2, replica_groups=mesh['grp'=4,'gx'=4,'gy'=2] {'grp','gx','gy'}, dimensions={0}, use_global_device_ids=true | all-gather | bytes 67584 | tf_op jit(solution)/shard_map/all_gather | solution.py:118
  360.3 1.8 copy.71
  364.1 2.0 copy.73
  366.1 2.3 broadcast_in_dim.43
  368.4 11.7 %fusion.116 = f32[24,24,136]{1,0,2:T(8,128)} fusion(f32[24,24,136]{1,0,2:T(8,128)} %copy-done.12, f32[24,24,136]{1,0,2:T(8,128)} %copy-done.10, f32[24,24,136]{1,0,2:T(8,128)} %copy-done.8, f32[24,24,136]{1,0,2:T(8,128)} %bitcast.112, f32[24,24,136]{1,0,2:T(8,128)} %copy-done.6, f32[24,24,136]{1,0,2:T(8,128)} %copy-done.4, f32[24,24,136]{1,0,2:T(8,128)} %copy-done.2, ...), kind=kLoop, calls=%fused_computation.173 | loop fusion | flops 2036736 | bytes 3525304 | tf_op jit(solution)/shard_map/jit(_where)/select_n | solution.py:128
  380.1 9.8 %fusion.117 = f32[24,24,136]{1,0,2:T(8,128)S(1)} fusion(f32[24,24,136]{1,0,2:T(8,128)} %fusion.116, f32[24,24,136]{1,0,2:T(8,128)} %copy-done.10, f32[24,24,136]{1,0,2:T(8,128)} %copy-done.8, f32[24,24,136]{1,0,2:T(8,128)} %copy-done.6, f32[24,24,136]{1,0,2:T(8,128)} %copy-done.4, f32[24,24,136]{1,0,2:T(8,128)} %copy-done.2, ...), kind=kLoop, calls=%fused_computation.181 | loop fusion | flops 2036736 | bytes 3446968 | tf_op jit(solution)/shard_map/jit(_where)/select_n | solution.py:130
  390.0 3.4 fusion.90
  393.4 1.7 fusion.119
  (116 shorter events, 26.8 us)
Async XLA Ops:
  0.6 18.8 %copy-start.17 = (f32[16,16,128]{2,1,0:T(8,128)S(1)}, f32[16,16,128]{2,1,0:T(8,128)}, u32[]{:S(2)}) copy-start(f32[16,16,128]{2,1,0:T(8,128)} %param.6) | copy-start | bytes 393220
  0.6 18.8 %copy-start.16 = (f32[16,16,128]{2,1,0:T(8,128)S(1)}, f32[16,16,128]{2,1,0:T(8,128)}, u32[]{:S(2)}) copy-start(f32[16,16,128]{2,1,0:T(8,128)} %param.7) | copy-start | bytes 393220
  0.7 18.8 %copy-start.15 = (f32[16,16,128]{2,1,0:T(8,128)S(1)}, f32[16,16,128]{2,1,0:T(8,128)}, u32[]{:S(2)}) copy-start(f32[16,16,128]{2,1,0:T(8,128)} %param.8) | copy-start | bytes 393220
  0.7 11.5 %copy-start.27 = (s32[8,4]{0,1:T(4,128)S(1)}, s32[8,4]{0,1:T(4,128)}, u32[]{:S(2)}) copy-start(s32[8,4]{0,1:T(4,128)} %param.11) | copy-start | bytes 388
  2.0 13.3 %collective-permute-start = (f32[3,16,16,4]{3,2,1,0:T(8,128)S(1)}, f32[3,16,16,4]{3,2,1,0:T(8,128)S(1)}, u32[]{:S(2)}, u32[]{:S(2)}) collective-permute-start(f32[3,16,16,4]{3,2,1,0:T(8,128)S(1)} %get-tuple-element.35), channel_id=1, source_target_pairs={{0,8},{8,16},{16,24},{1,9},{9,17},{17,25},{2,10},{10,18},{18,26},{... | collective-permute-start | bytes 36872 | tf_op jit(solution)/shard_map/ppermute | solution.py:32
  6.9 12.5 %collective-permute-start.1 = (f32[3,16,16,4]{3,2,1,0:T(8,128)S(1)}, f32[3,16,16,4]{3,2,1,0:T(8,128)S(1)}, u32[]{:S(2)}, u32[]{:S(2)}) collective-permute-start(f32[3,16,16,4]{3,2,1,0:T(8,128)S(1)} %get-tuple-element.36), channel_id=1, source_target_pairs={{8,0},{16,8},{24,16},{9,1},{17,9},{25,17},{10,2},{18,10},{26,18},{... | collective-permute-start | bytes 36872 | tf_op jit(solution)/shard_map/ppermute | solution.py:33
  8.3 14.0 %copy-start.21 = (pred[136]{0:T(512)(128)(4,1)}, pred[136]{0:T(512)(128)(4,1)S(1)}, u32[]{:S(2)}) copy-start(pred[136]{0:T(512)(128)(4,1)S(1)} %compare_and_fusion) | copy-start | bytes 412
  10.8 48.3 %copy-start.19 = (pred[24]{0:T(512)(128)(4,1)}, pred[24]{0:T(512)(128)(4,1)S(1)}, u32[]{:S(2)}) copy-start(pred[24]{0:T(512)(128)(4,1)S(1)} %get-tuple-element.40) | copy-start | bytes 76
  19.6 2.6 collective-permute-start.2
  21.0 5.1 %collective-permute-start.3 = (f32[3,4,16,136]{3,2,1,0:T(8,128)S(1)}, f32[3,4,16,136]{3,2,1,0:T(8,128)S(1)}, u32[]{:S(2)}, u32[]{:S(2)}) collective-permute-start(f32[3,4,16,136]{3,2,1,0:T(8,128)S(1)} %get-tuple-element.34), channel_id=1, source_target_pairs={{2,0},{4,2},{6,4},{3,1},{5,3},{7,5},{10,8},{12,10},{14,12},{11,9},... | collective-permute-start | bytes 313352 | tf_op jit(solution)/shard_map/ppermute | solution.py:33
  27.3 8.0 %collective-permute-start.4 = (f32[3,24,4,136]{3,1,2,0:T(8,128)}, f32[3,24,4,136]{3,1,2,0:T(8,128)}, u32[]{:S(2)}, u32[]{:S(2)}) collective-permute-start(f32[3,24,4,136]{3,1,2,0:T(8,128)} %copy_select_fusion), channel_id=1, source_target_pairs={{0,1},{1,0},{2,3},{3,2},{4,5},{5,4},{6,7},{7,6},{8,9},{9,8},{10,11... | collective-permute-start | bytes 470024 | tf_op jit(solution)/shard_map/ppermute | solution.py:28
  51.6 11.5 %copy-start.1 = (f32[3,24,24,136]{2,1,3,0:T(8,128)}, f32[3,24,24,136]{2,1,3,0:T(8,128)S(1)}, u32[]{:S(2)}) copy-start(f32[3,24,24,136]{2,1,3,0:T(8,128)S(1)} %pad_maximum_fusion) | copy-start | bytes 2820100
  56.0 3.1 copy-start.10
  56.0 7.1 %copy-start.2 = (f32[24,24,136]{1,0,2:T(8,128)}, f32[24,24,136]{1,0,2:T(8,128)S(1)}, u32[]{:S(2)}) copy-start(f32[24,24,136]{1,0,2:T(8,128)S(1)} %get-tuple-element.18) | copy-start | bytes 940036
  56.0 10.7 %copy-start.4 = (f32[24,24,136]{1,0,2:T(8,128)}, f32[24,24,136]{1,0,2:T(8,128)S(1)}, u32[]{:S(2)}) copy-start(f32[24,24,136]{1,0,2:T(8,128)S(1)} %get-tuple-element.19) | copy-start | bytes 940036
  56.0 10.7 %copy-start.6 = (f32[24,24,136]{1,0,2:T(8,128)}, f32[24,24,136]{1,0,2:T(8,128)S(1)}, u32[]{:S(2)}) copy-start(f32[24,24,136]{1,0,2:T(8,128)S(1)} %get-tuple-element.20) | copy-start | bytes 940036
  56.0 10.7 %copy-start.8 = (f32[24,24,136]{1,0,2:T(8,128)}, f32[24,24,136]{1,0,2:T(8,128)S(1)}, u32[]{:S(2)}) copy-start(f32[24,24,136]{1,0,2:T(8,128)S(1)} %get-tuple-element.21) | copy-start | bytes 940036
  59.1 4.0 %copy-start.12 = (f32[24,24,136]{1,0,2:T(8,128)}, f32[24,24,136]{1,0,2:T(8,128)S(1)}, u32[]{:S(2)}) copy-start(f32[24,24,136]{1,0,2:T(8,128)S(1)} %fusion.118) | copy-start | bytes 940036
  63.1 3.6 copy-start.14
  86.0 64.4 %copy-start.26 = (f32[512]{0:T(512)}, f32[512]{0:T(512)S(1)}, u32[]{:S(2)}) copy-start(f32[512]{0:T(512)S(1)} %div.33) | copy-start | bytes 6148
  153.6 65.7 %copy-start.25 = (f32[512]{0:T(512)}, f32[512]{0:T(512)S(1)}, u32[]{:S(2)}) copy-start(f32[512]{0:T(512)S(1)} %divide_add_fusion.2) | copy-start | bytes 6148
  222.5 63.9 %copy-start.24 = (f32[512]{0:T(512)}, f32[512]{0:T(512)S(1)}, u32[]{:S(2)}) copy-start(f32[512]{0:T(512)S(1)} %divide_add_fusion.1) | copy-start | bytes 6148
  289.7 73.5 %copy-start = (f32[512]{0:T(512)}, f32[512]{0:T(512)S(1)}, u32[]{:S(2)}) copy-start(f32[512]{0:T(512)S(1)} %divide_add_fusion) | copy-start | bytes 6148
  363.3 5.1 %copy-start.20 = (pred[24]{0:T(512)(128)(4,1)S(1)}, pred[24]{0:T(512)(128)(4,1)}, u32[]{:S(2)}) copy-start(pred[24]{0:T(512)(128)(4,1)} %copy-done.19) | copy-start | bytes 76
  363.3 5.1 %copy-start.23 = (pred[136]{0:T(512)(128)(4,1)S(1)}, pred[136]{0:T(512)(128)(4,1)}, u32[]{:S(2)}) copy-start(pred[136]{0:T(512)(128)(4,1)} %copy-done.21) | copy-start | bytes 412
  380.1 9.8 %copy-start.3 = (f32[24,24,136]{1,0,2:T(8,128)S(1)}, f32[24,24,136]{1,0,2:T(8,128)}, u32[]{:S(2)}) copy-start(f32[24,24,136]{1,0,2:T(8,128)} %copy-done.2) | copy-start | bytes 940036
  380.1 9.9 %copy-start.5 = (f32[24,24,136]{1,0,2:T(8,128)S(1)}, f32[24,24,136]{1,0,2:T(8,128)}, u32[]{:S(2)}) copy-start(f32[24,24,136]{1,0,2:T(8,128)} %copy-done.4) | copy-start | bytes 940036
  380.1 9.9 %copy-start.7 = (f32[24,24,136]{1,0,2:T(8,128)S(1)}, f32[24,24,136]{1,0,2:T(8,128)}, u32[]{:S(2)}) copy-start(f32[24,24,136]{1,0,2:T(8,128)} %copy-done.6) | copy-start | bytes 940036
  380.1 9.9 %copy-start.9 = (f32[24,24,136]{1,0,2:T(8,128)S(1)}, f32[24,24,136]{1,0,2:T(8,128)}, u32[]{:S(2)}) copy-start(f32[24,24,136]{1,0,2:T(8,128)} %copy-done.8) | copy-start | bytes 940036
  390.0 3.4 copy-start.11
  390.0 3.4 copy-start.13
  390.0 3.4 copy-start.18
  (2 other events, 4.0 us)

commit v2 on v1

v2 whole, which is shorter than its diff:
```python
import jax
import jax.numpy as jnp
from jax import lax
from jax.sharding import PartitionSpec as P

NU = 2
CITER = 4
BOX = 4
HALO = 4

WEIGHT = 2.0 / 3.0
PAIRS = ((0, 1), (0, -1), (1, 1), (1, -1), (2, 1), (2, -1))


def exchange(cells, sides, width):
    for axis, dim in sides:
        count = lax.axis_size(axis)
        size = cells.shape[dim]
        head = lax.slice_in_dim(cells, 0, width, axis=dim)
        tail = lax.slice_in_dim(cells, size - width, size, axis=dim)
        if count == 1:
            before = jnp.zeros_like(tail)
            after = jnp.zeros_like(head)
        elif count == 2:
            index = lax.axis_index(axis)
            sent = jnp.where(index == 0, tail, head)
            got = lax.ppermute(sent, axis, [(0, 1), (1, 0)])
            before = jnp.where(index == 1, got, 0.0)
            after = jnp.where(index == 0, got, 0.0)
        else:
            before = lax.ppermute(tail, axis, [(i, i + 1) for i in range(count - 1)])
            after = lax.ppermute(head, axis, [(i + 1, i) for i in range(count - 1)])
        cells = jnp.concatenate([before, cells, after], axis=dim)
    return cells


def flat_shift(padded, rows, width, stride, dx, dy, dz):
    lead = stride + dy * stride + dz
    return padded[1 + dx:1 + dx + rows, lead:lead + width]


def neighbours(field, stride):
    rows, width = field.shape
    padded = jnp.pad(field, ((1, 1), (stride, stride)))
    steps = ((1, 0, 0), (-1, 0, 0), (0, 1, 0), (0, -1, 0), (0, 0, 1), (0, 0, -1))
    return [flat_shift(padded, rows, width, stride, *step) for step in steps]


def face_terms(conductance, stride):
    return [0.5 * (conductance + other) for other in neighbours(conductance, stride)]


def operate(field, storage, face_list, stride):
    summed = storage * field
    for face, other in zip(face_list, neighbours(field, stride)):
        summed = summed + face * (field - other)
    return summed


def inside_mask(rows, span_y, span_z):
    shape = (rows, span_y * span_z)
    column = lax.broadcasted_iota(jnp.int32, shape, 1)
    coords = (
        (lax.broadcasted_iota(jnp.int32, shape, 0), rows, "gx"),
        (column // span_z, span_y, "gy"),
        (column % span_z, span_z, "grp"),
    )
    mask = None
    for local_index, span, axis in coords:
        block = span - 2 * HALO
        where = lax.axis_index(axis) * block - HALO + local_index
        ok = (where >= 0) & (where < block * lax.axis_size(axis))
        mask = ok if mask is None else mask & ok
    return mask


def trimmed(flat, span_y, span_z):
    cube = flat.reshape(flat.shape[0], span_y, span_z)
    return cube[HALO:-HALO, HALO:-HALO, HALO:-HALO]


def grp_pool(vector):
    groups = lax.axis_size("grp")
    index = lax.axis_index("grp")
    parts = [vector]
    for step in range(1, groups):
        parts.append(lax.ppermute(vector, "grp", [(i, (i + step) % groups) for i in range(groups)]))
    stacked = jnp.stack(parts)
    order = (index - jnp.arange(groups)) % groups
    return jnp.take(stacked, order, axis=0)


def local(source, conductance, storage, aggregate_ids, coarse_values, coarse_columns):
    size_x, size_y, size_z = source.shape
    assert HALO == BOX and HALO >= 2 * NU and HALO >= NU + 2
    stacked = jnp.stack([source, conductance, storage])
    wide = exchange(stacked, (("gx", 1), ("gy", 2), ("grp", 3)), HALO)
    rows, span_y, span_z = wide.shape[1:]
    stride = span_z
    wide = wide.reshape(3, rows, span_y * span_z)
    src, cond, stor = wide[0], wide[1], wide[2]
    mask = inside_mask(rows, span_y, span_z)
    face_list = face_terms(cond, stride)
    diagonal = stor
    for position in range(6):
        diagonal = diagonal + face_list[position]

    def op(field):
        return operate(field, stor, face_list, stride)

    solution = jnp.where(mask, WEIGHT * src / diagonal, 0.0)
    for sweep_number in range(NU - 1):
        solution = jnp.where(mask, solution + WEIGHT * (src - op(solution)) / diagonal, 0.0)
    residual = src - op(solution)
    scaled = jnp.where(mask, residual / diagonal, 0.0)
    smoothed = trimmed(residual - WEIGHT * op(scaled), span_y, span_z)

    box_labels = aggregate_ids[::BOX, ::BOX, ::BOX].reshape(-1)
    box_totals = (
        smoothed.reshape(size_x // BOX, BOX, size_y // BOX, BOX, size_z // BOX, BOX)
        .sum(axis=(1, 3, 5))
        .reshape(-1)
    )
    coarse_rhs = jnp.zeros(box_totals.shape, source.dtype).at[box_labels].set(box_totals)
    coarse_diag = jnp.diagonal(coarse_values[:, :, :64], axis1=1, axis2=2).reshape(-1)
    block_rows = coarse_values.shape[0]
    grid_x = lax.axis_size("gx")
    grid_y = lax.axis_size("gy")
    groups = lax.axis_size("grp")
    within_ids = coarse_columns % block_rows
    device_ids = coarse_columns // block_rows
    target_y = device_ids % grid_y
    target_x = device_ids // grid_y % grid_x
    member_ids = device_ids // (grid_y * grid_x)
    delta_x = target_x - lax.axis_index("gx") + 1
    delta_y = target_y - lax.axis_index("gy") + 1
    local_columns = ((delta_x * 3 + delta_y) * groups + member_ids) * block_rows + within_ids
    coarse_error = coarse_rhs / coarse_diag
    for sweep_number in range(CITER - 1):
        pooled = grp_pool(coarse_error)
        beside_all = exchange(pooled.reshape(1, 1, -1), (("gx", 0), ("gy", 1)), 1)
        blocks = beside_all.reshape(-1, 64)[local_columns]
        blocks = blocks.reshape(blocks.shape[0], -1)
        applied = jnp.einsum(
            "bim,bm->bi", coarse_values, blocks, precision=lax.Precision.HIGHEST
        ).reshape(-1)
        coarse_error = coarse_error + (coarse_rhs - applied) / coarse_diag

    bx, by, bz = size_x // BOX, size_y // BOX, size_z // BOX
    small = coarse_error[box_labels].reshape(bx, by, bz)
    window = exchange(small, (("gx", 0), ("gy", 1), ("grp", 2)), 1)
    lifted = jnp.repeat(jnp.repeat(jnp.repeat(window, BOX, axis=0), BOX, axis=1), BOX, axis=2)
    lifted = lifted.reshape(rows, span_y * span_z)
    solution = jnp.where(mask, solution + (lifted - WEIGHT * op(lifted) / diagonal), 0.0)
    for sweep_number in range(NU):
        solution = jnp.where(mask, solution + WEIGHT * (src - op(solution)) / diagonal, 0.0)
    return (trimmed(solution, span_y, span_z), coarse_error)


def solution(mesh):
    return jax.shard_map(
        local,
        mesh=mesh,
        in_specs=(
            P("gx", "gy", "grp"),
            P("gx", "gy", "grp"),
            P("gx", "gy", "grp"),
            P("gx", "gy", "grp"),
            P(("grp", "gx", "gy"), None, None),
            P(("grp", "gx", "gy"), None),
        ),
        out_specs=(P("gx", "gy", "grp"), P(("grp", "gx", "gy"))),
        check_vma=False,
    )
```

time: 397 us -> 170 us (0.43)
  blocking collectives: 260 us -> 0 us
  other arithmetic: 66.8 us -> 22.1 us
  starting transfers between devices: 10.3 us -> 49.5 us
  waiting for transfers between devices: 10.8 us -> 38.1 us
  local copies, waits for them, and re-layouts: 42.6 us -> 56.4 us
    all_gather x4 -> x0, blocking collectives: 260 us -> none  [the longest x3 194 us: local(): pooled = lax.all_gather(coarse_error, ALL_AXES, axis=0, tiled=True)]
    ppermute x0 -> x9, starting transfers between devices: none -> 14.3 us  [grp_pool(): lax.ppermute(vector, 'grp', [(i, (i + step) % groups) for i in range(grou...]
    select_n x3, other arithmetic: 14.6 us -> 1.77 us  [local(): jnp.where(mask, solution + WEIGHT * (src - op(solution)) / diagonal, 0.0)]
    ppermute x2 -> x7, waiting for transfers between devices: 7.88 us -> 20.6 us  [exchange(): after = lax.ppermute(head, axis, [(i + 1, i) for i in range(count - 1)])]
    ppermute x2 -> x7, starting transfers between devices: 6.25 us -> 18.2 us  [exchange(): before = lax.ppermute(tail, axis, [(i, i + 1) for i in range(count - 1)])]
    ppermute x1 -> x5, waiting for transfers between devices: 0.01 us -> 9.34 us  [exchange(): got = lax.ppermute(sent, axis, [(0, 1), (1, 0)])]
    select_n x1, other arithmetic: 11.7 us -> 2.78 us  [local(): jnp.where(mask, solution + (lifted - WEIGHT * op(lifted) / diagonal), 0.0)]
    ppermute x0 -> x9, waiting for transfers between devices: none -> 7.92 us  [grp_pool(): lax.ppermute(vector, 'grp', [(i, (i + step) % groups) for i in range(grou...]
  transfers between devices with their start and end apart: 5 -> 28, of which waited for: 3 -> 18; matrix products, arithmetic and copies ran while one was open for 3% -> 7% of each run, Pallas kernels for 0% -> 0%
where the time goes in v2:
time: 170 us; the launch traced here: 169 us
  local copies, waits for them, and re-layouts  56.4 us (33%)
  starting transfers between devices  49.5 us (29%)
  waiting for transfers between devices  38.1 us (22%)
  other arithmetic  22.1 us (13%)
    ppermute x7, waiting for transfers between devices, exchange(): after = lax.ppermute(head, axis, [(i + 1, i) for i in range(count - 1)])  20.6 us
    ppermute x7, starting transfers between devices, exchange(): before = lax.ppermute(tail, axis, [(i, i + 1) for i in range(count - 1)])  18.2 us
    ppermute x9, starting transfers between devices, grp_pool(): lax.ppermute(vector, 'grp', [(i, (i + step) % groups) for i in range(grou...  14.3 us
    concatenate x8, other arithmetic, exchange(): cells = jnp.concatenate([before, cells, after], axis=dim)  11.7 us
    ppermute x7, starting transfers between devices, exchange(): after = lax.ppermute(head, axis, [(i + 1, i) for i in range(count - 1)])  9.43 us
    ppermute x5, waiting for transfers between devices, exchange(): got = lax.ppermute(sent, axis, [(0, 1), (1, 0)])  9.34 us
    ppermute x9, waiting for transfers between devices, grp_pool(): lax.ppermute(vector, 'grp', [(i, (i + step) % groups) for i in range(grou...  7.92 us
    ppermute x5, starting transfers between devices, exchange(): got = lax.ppermute(sent, axis, [(0, 1), (1, 0)])  7.58 us
  transfers between devices with their start and end apart: 28, of which 18 were waited for; matrix products, arithmetic and copies ran while one was open for 7% of the time, Pallas kernels for 0%

profile of v2, /device:TPU:0, one launch (start us, length us, event | category | flops | bytes accessed | tf_op | source)
XLA Modules:
  0.0 168.9 jit_solution(6102556477736813619)
XLA Ops:
  1.5 2.4 %collective-permute-start = (f32[3,4,16,128]{3,2,1,0:T(8,128)S(1)}, f32[3,4,16,128]{3,2,1,0:T(8,128)S(1)}, u32[]{:S(2)}, u32[]{:S(2)}) collective-permute-start(f32[3,4,16,128]{3,2,1,0:T(8,128)S(1)} %get-tuple-element.17), channel_id=1, source_target_pairs={{0,2},{2,4},{4,6},{1,3},{3,5},{5,7},{8,10},{10,12},{12,14},{9,11},... | collective-permute-start | bytes 294920 | tf_op jit(solution)/shard_map/ppermute | solution.py:31
  5.2 1.9 %slice.229 = s32[4,4,32]{2,1,0:T(4,128)S(1)} slice(s32[16,16,128]{2,1,0:T(8,128)} %param.11), slice={[0:16:4], [0:16:4], [0:128:4]} | slice | bytes 4096 | tf_op jit(solution)/shard_map/slice | solution.py:118
  7.2 2.0 %collective-permute-done.1 = f32[3,4,16,128]{3,2,1,0:T(8,128)S(1)} collective-permute-done((f32[3,4,16,128]{3,2,1,0:T(8,128)S(1)}, f32[3,4,16,128]{3,2,1,0:T(8,128)S(1)}, u32[]{:S(2)}, u32[]{:S(2)}) %collective-permute-start.1) | collective-permute-done | bytes 98336 | tf_op jit(solution)/shard_map/ppermute | solution.py:32
  11.9 3.4 %copy.82 = f32[3,24,16,128]{2,1,3,0:T(8,128)} copy(f32[3,24,16,128]{3,2,1,0:T(8,128)S(1)} %pad_maximum_fusion.2) | data formatting | bytes 1179648 | tf_op jit(solution)/shard_map/concatenate | solution.py:33
  15.6 3.4 %copy.81 = f32[3,24,4,128]{2,1,3,0:T(8,128)} copy(f32[3,24,4,128]{3,1,2,0:T(8,128)S(1)} %get-tuple-element.19) | data formatting | bytes 294912 | tf_op jit(solution)/shard_map/jit(_where)/select_n | solution.py:28
  18.9 3.4 %copy.83 = f32[3,24,4,128]{2,1,3,0:T(8,128)} copy(f32[3,24,4,128]{3,1,2,0:T(8,128)S(1)} %get-tuple-element.20) | data formatting | bytes 294912 | tf_op jit(solution)/shard_map/jit(_where)/select_n | solution.py:29
  22.3 7.6 %pad_maximum_fusion = f32[3,24,24,128]{2,1,3,0:T(8,128)S(1)} fusion(f32[3,24,4,128]{2,1,3,0:T(8,128)} %copy.83, f32[3,24,16,128]{2,1,3,0:T(8,128)} %copy.82, f32[3,24,4,128]{2,1,3,0:T(8,128)} %copy.81), kind=kLoop, calls=%fused_computation.9 | loop fusion | flops 442368 | bytes 1769472 | tf_op jit(solution)/shard_map/concatenate | solution.py:33
  30.0 2.1 %copy-done.1 = f32[3,24,24,128]{2,1,3,0:T(8,128)} copy-done((f32[3,24,24,128]{2,1,3,0:T(8,128)}, f32[3,24,24,128]{2,1,3,0:T(8,128)S(1)}, u32[]{:S(2)}) %copy-start.1) | copy-done | bytes 884760
  32.1 3.5 %collective-permute-start.3 = (f32[3,24,24,4]{2,1,3,0:T(8,128)S(1)}, f32[3,24,24,4]{2,1,3,0:T(8,128)S(1)}, u32[]{:S(2)}, u32[]{:S(2)}) collective-permute-start(f32[3,24,24,4]{2,1,3,0:T(8,128)S(1)} %get-tuple-element.10), channel_id=1, source_target_pairs={{0,8},{8,16},{16,24},{1,9},{9,17},{17,25},{2,10},{10,18},{18,26},{... | collective-permute-start | bytes 82952 | tf_op jit(solution)/shard_map/ppermute | solution.py:31
  38.8 3.7 %copy.85 = f32[3,24,24,128]{3,2,1,0:T(8,128)S(1)} copy(f32[3,24,24,128]{2,1,3,0:T(8,128)} %copy-done.1) | data formatting | bytes 1769472 | tf_op jit(solution)/shard_map/concatenate | solution.py:33
  50.6 6.5 %reshape.127 = f32[4,4,4,4,32,4]{5,4,3,2,1,0:T(8,128)} reshape(f32[16,16,128]{2,1,0:T(8,128)} %slice.294) | data formatting | bytes 262144 | tf_op jit(solution)/shard_map/reshape | solution.py:120
  57.1 2.6 %reduce_sum.9 = f32[4,4,32]{2,1,0:T(4,128)S(1)} reduce(f32[4,4,4,4,32,4]{5,4,3,2,1,0:T(8,128)} %reshape.127, f32[]{:T(128)} %constant.145.clone.1), dimensions={1,3,5}, to_apply=%region_0.1 | reduce | flops 32256 | bytes 133124 | tf_op jit(solution)/shard_map/reduce_sum | solution.py:121
  59.9 2.4 %scatter_custom_fusion = f32[512]{0:T(512)S(1)} fusion(s32[512]{0:T(512)S(1)} %bitcast.56, f32[512]{0:T(512)S(1)} %reshape.212, f32[]{:T(128)} %constant.145.clone.1), kind=kCustom, calls=%fused_computation.306 | custom fusion | bytes 2052 | tf_op jit(solution)/shard_map/scatter | solution.py:124
  62.3 2.7 %collective-permute-start.5 = (f32[512]{0:T(512)S(1)}, f32[512]{0:T(512)S(1)}, u32[]{:S(2)}, u32[]{:S(2)}) collective-permute-start(f32[512]{0:T(512)S(1)} %div.69), channel_id=1, source_target_pairs={{0,8},{8,16},{16,24},{24,0},{1,9},{9,17},{17,25},{25,1},{2,10},{10... | collective-permute-start | bytes 6152 | tf_op jit(solution)/shard_map/ppermute | solution.py:87
  65.0 2.6 %collective-permute-start.6 = (f32[512]{0:T(512)S(1)}, f32[512]{0:T(512)S(1)}, u32[]{:S(2)}, u32[]{:S(2)}) collective-permute-start(f32[512]{0:T(512)S(1)} %div.69), channel_id=1, source_target_pairs={{0,16},{8,24},{16,0},{24,8},{1,17},{9,25},{17,1},{25,9},{2,18},{10... | collective-permute-start | bytes 6152 | tf_op jit(solution)/shard_map/ppermute | solution.py:87
  71.9 2.4 %collective-permute-start.8 = (f32[1,1,2048]{2,1,0:T(1,128)S(1)}, f32[1,1,2048]{2,1,0:T(1,128)S(1)}, u32[]{:S(2)}, u32[]{:S(2)}) collective-permute-start(f32[1,1,2048]{2,1,0:T(1,128)S(1)} %reshape.130), channel_id=1, source_target_pairs={{0,2},{2,4},{4,6},{1,3},{3,5},{5,7},{8,10},{10,12},{12,14},{9,11},... | collective-permute-start | bytes 24584 | tf_op jit(solution)/shard_map/ppermute | solution.py:31
  75.8 3.9 %collective-permute-done.9 = f32[1,1,2048]{2,1,0:T(1,128)S(1)} collective-permute-done((f32[1,1,2048]{2,1,0:T(1,128)S(1)}, f32[1,1,2048]{2,1,0:T(1,128)S(1)}, u32[]{:S(2)}, u32[]{:S(2)}) %collective-permute-start.9) | collective-permute-done | bytes 8224 | tf_op jit(solution)/shard_map/ppermute | solution.py:32
  81.2 2.3 %collective-permute-done.10 = f32[3,1,2048]{2,1,0:T(1,128)S(1)} collective-permute-done((f32[3,1,2048]{2,1,0:T(1,128)S(1)}, f32[3,1,2048]{2,1,0:T(1,128)S(1)}, u32[]{:S(2)}, u32[]{:S(2)}) %collective-permute-start.10) | collective-permute-done | bytes 24608 | tf_op jit(solution)/shard_map/ppermute | solution.py:27
  88.2 3.6 %collective-permute-start.12 = (f32[512]{0:T(512)S(1)}, f32[512]{0:T(512)S(1)}, u32[]{:S(2)}, u32[]{:S(2)}) collective-permute-start(f32[512]{0:T(512)S(1)} %divide_add_fusion.2), channel_id=1, source_target_pairs={{0,16},{8,24},{16,0},{24,8},{1,17},{9,25},{17,1},{25,9},{2,18},{10... | collective-permute-start | bytes 6152 | tf_op jit(solution)/shard_map/ppermute | solution.py:87
  93.6 1.9 %collective-permute-done.13 = f32[512]{0:T(512)S(1)} collective-permute-done((f32[512]{0:T(512)S(1)}, f32[512]{0:T(512)S(1)}, u32[]{:S(2)}, u32[]{:S(2)}) %collective-permute-start.13) | collective-permute-done | bytes 2080 | tf_op jit(solution)/shard_map/ppermute | solution.py:87
  98.9 4.1 %collective-permute-done.15 = f32[1,1,2048]{2,1,0:T(1,128)S(1)} collective-permute-done((f32[1,1,2048]{2,1,0:T(1,128)S(1)}, f32[1,1,2048]{2,1,0:T(1,128)S(1)}, u32[]{:S(2)}, u32[]{:S(2)}) %collective-permute-start.15) | collective-permute-done | bytes 8224 | tf_op jit(solution)/shard_map/ppermute | solution.py:32
  104.6 2.3 %collective-permute-done.16 = f32[3,1,2048]{2,1,0:T(1,128)S(1)} collective-permute-done((f32[3,1,2048]{2,1,0:T(1,128)S(1)}, f32[3,1,2048]{2,1,0:T(1,128)S(1)}, u32[]{:S(2)}, u32[]{:S(2)}) %collective-permute-start.16) | collective-permute-done | bytes 24608 | tf_op jit(solution)/shard_map/ppermute | solution.py:27
  121.4 3.8 %collective-permute-done.21 = f32[1,1,2048]{2,1,0:T(1,128)S(1)} collective-permute-done((f32[1,1,2048]{2,1,0:T(1,128)S(1)}, f32[1,1,2048]{2,1,0:T(1,128)S(1)}, u32[]{:S(2)}, u32[]{:S(2)}) %collective-permute-start.21) | collective-permute-done | bytes 8224 | tf_op jit(solution)/shard_map/ppermute | solution.py:32
  126.7 2.3 %collective-permute-done.22 = f32[3,1,2048]{2,1,0:T(1,128)S(1)} collective-permute-done((f32[3,1,2048]{2,1,0:T(1,128)S(1)}, f32[3,1,2048]{2,1,0:T(1,128)S(1)}, u32[]{:S(2)}, u32[]{:S(2)}) %collective-permute-start.22) | collective-permute-done | bytes 24608 | tf_op jit(solution)/shard_map/ppermute | solution.py:27
  133.6 3.5 %gather_fusion.4 = f32[512]{0:T(512)S(1)} fusion(f32[512]{0:T(512)S(1)} %divide_add_fusion, s32[1024]{0:T(1024)S(1)} %pad_clamp_fusion), kind=kCustom, calls=%fused_computation.7 | custom fusion | bytes 6144 | tf_op jit(solution)/shard_map/gather | solution.py:150
  137.2 3.1 %collective-permute-start.23 = (f32[1,4,32]{2,1,0:T(4,128)S(1)}, f32[1,4,32]{2,1,0:T(4,128)S(1)}, u32[]{:S(2)}, u32[]{:S(2)}) collective-permute-start(f32[1,4,32]{2,1,0:T(4,128)S(1)} %slice.245), channel_id=1, source_target_pairs={{0,2},{2,4},{4,6},{1,3},{3,5},{5,7},{8,10},{10,12},{12,14},{9,11},... | collective-permute-start | bytes 1544 | tf_op jit(solution)/shard_map/ppermute | solution.py:31
  141.9 2.4 %collective-permute-done.24 = f32[1,4,32]{2,1,0:T(4,128)S(1)} collective-permute-done((f32[1,4,32]{2,1,0:T(4,128)S(1)}, f32[1,4,32]{2,1,0:T(4,128)S(1)}, u32[]{:S(2)}, u32[]{:S(2)}) %collective-permute-start.24) | collective-permute-done | bytes 544 | tf_op jit(solution)/shard_map/ppermute | solution.py:32
  145.9 2.1 %collective-permute-done.25 = f32[6,1,32]{2,1,0:T(1,128)S(1)} collective-permute-done((f32[6,1,32]{2,1,0:T(1,128)S(1)}, f32[6,1,32]{2,1,0:T(1,128)S(1)}, u32[]{:S(2)}, u32[]{:S(2)}) %collective-permute-start.25) | collective-permute-done | bytes 800 | tf_op jit(solution)/shard_map/ppermute | solution.py:27
  148.1 3.8 %collective-permute-start.26 = (f32[6,6,1]{2,1,0:T(8,128)S(1)}, f32[6,6,1]{2,1,0:T(8,128)S(1)}, u32[]{:S(2)}, u32[]{:S(2)}) collective-permute-start(f32[6,6,1]{2,1,0:T(8,128)S(1)} %get-tuple-element.21), channel_id=1, source_target_pairs={{0,8},{8,16},{16,24},{1,9},{9,17},{17,25},{2,10},{10,18},{18,26},{... | collective-permute-start | bytes 440 | tf_op jit(solution)/shard_map/ppermute | solution.py:31
  153.4 4.4 %collective-permute-done.27 = f32[6,6,1]{2,1,0:T(8,128)S(1)} collective-permute-done((f32[6,6,1]{2,1,0:T(8,128)S(1)}, f32[6,6,1]{2,1,0:T(8,128)S(1)}, u32[]{:S(2)}, u32[]{:S(2)}) %collective-permute-start.27) | collective-permute-done | bytes 176 | tf_op jit(solution)/shard_map/ppermute | solution.py:32
  161.2 2.6 %copy.100 = f32[24,3264]{1,0:T(8,128)} copy(f32[24,3264]{0,1:T(8,128)} %bitcast.40) | data formatting | bytes 626688 | tf_op jit(solution)/shard_map/reshape;reshape | solution.py:153
  163.8 2.8 %fusion.149 = f32[24,3264]{1,0:T(8,128)S(1)} fusion(f32[24,3264]{1,0:T(8,128)S(1)} %fusion.150, f32[24,3264]{1,0:T(8,128)} %copy.100, f32[24,3264]{1,0:T(8,128)S(1)} %get-tuple-element.9, f32[24,3264]{1,0:T(8,128)S(1)} %get-tuple-element.8, f32[24,3264]{1,0:T(8,128)S(1)} %get-tuple-element.7, f32[24,3264]{1,0:T(8,128)S(1)} %get-tuple-element.6, ...), kind=kLoop, calls=%fused_computation.210 | loop fusion | flops 3290112 | bytes 3192224 | tf_op jit(solution)/shard_map/jit(_where)/select_n | solution.py:154
  (152 shorter events, 66.0 us)
Async XLA Ops:
  1.5 5.7 %collective-permute-start = (f32[3,4,16,128]{3,2,1,0:T(8,128)S(1)}, f32[3,4,16,128]{3,2,1,0:T(8,128)S(1)}, u32[]{:S(2)}, u32[]{:S(2)}) collective-permute-start(f32[3,4,16,128]{3,2,1,0:T(8,128)S(1)} %get-tuple-element.17), channel_id=1, source_target_pairs={{0,2},{2,4},{4,6},{1,3},{3,5},{5,7},{8,10},{10,12},{12,14},{9,11},... | collective-permute-start | bytes 294920 | tf_op jit(solution)/shard_map/ppermute | solution.py:31
  3.9 5.3 %collective-permute-start.1 = (f32[3,4,16,128]{3,2,1,0:T(8,128)S(1)}, f32[3,4,16,128]{3,2,1,0:T(8,128)S(1)}, u32[]{:S(2)}, u32[]{:S(2)}) collective-permute-start(f32[3,4,16,128]{3,2,1,0:T(8,128)S(1)} %get-tuple-element.18), channel_id=1, source_target_pairs={{2,0},{4,2},{6,4},{3,1},{5,3},{7,5},{10,8},{12,10},{14,12},{11,9},... | collective-permute-start | bytes 294920 | tf_op jit(solution)/shard_map/ppermute | solution.py:32
  10.4 5.2 %collective-permute-start.2 = (f32[3,24,4,128]{3,1,2,0:T(8,128)S(1)}, f32[3,24,4,128]{3,1,2,0:T(8,128)S(1)}, u32[]{:S(2)}, u32[]{:S(2)}) collective-permute-start(f32[3,24,4,128]{3,1,2,0:T(8,128)S(1)} %copy_select_fusion), channel_id=1, source_target_pairs={{0,1},{1,0},{2,3},{3,2},{4,5},{5,4},{6,7},{7,6},{8,9},{9,8},{10,11... | collective-permute-start | bytes 442376 | tf_op jit(solution)/shard_map/ppermute | solution.py:27
  22.3 14.8 %slice-start = ((f32[8,64,256]{2,1,0:T(8,128)}), f32[8,64,64]{2,1,0:T(8,128)S(1)}, s32[]{:S(2)}) async-start(f32[8,64,256]{2,1,0:T(8,128)} %param.12), calls=%async_computation | async-start | bytes 524288 | tf_op jit(solution)/shard_map/slice | solution.py:125
  32.1 10.4 %collective-permute-start.3 = (f32[3,24,24,4]{2,1,3,0:T(8,128)S(1)}, f32[3,24,24,4]{2,1,3,0:T(8,128)S(1)}, u32[]{:S(2)}, u32[]{:S(2)}) collective-permute-start(f32[3,24,24,4]{2,1,3,0:T(8,128)S(1)} %get-tuple-element.10), channel_id=1, source_target_pairs={{0,8},{8,16},{16,24},{1,9},{9,17},{17,25},{2,10},{10,18},{18,26},{... | collective-permute-start | bytes 82952 | tf_op jit(solution)/shard_map/ppermute | solution.py:31
  35.6 7.4 %collective-permute-start.4 = (f32[3,24,24,4]{2,1,3,0:T(8,128)S(1)}, f32[3,24,24,4]{2,1,3,0:T(8,128)S(1)}, u32[]{:S(2)}, u32[]{:S(2)}) collective-permute-start(f32[3,24,24,4]{2,1,3,0:T(8,128)S(1)} %get-tuple-element.11), channel_id=1, source_target_pairs={{8,0},{16,8},{24,16},{9,1},{17,9},{25,17},{10,2},{18,10},{26,18},{... | collective-permute-start | bytes 82952 | tf_op jit(solution)/shard_map/ppermute | solution.py:32
  47.6 26.6 %copy-start.3 = (s32[8,4]{0,1:T(4,128)S(1)}, s32[8,4]{0,1:T(4,128)}, u32[]{:S(2)}) copy-start(s32[8,4]{0,1:T(4,128)} %param.13) | copy-start | bytes 388
  50.6 36.9 %copy-start.2 = (f32[8,64,256]{2,1,0:T(8,128)S(1)}, f32[8,64,256]{2,1,0:T(8,128)}, u32[]{:S(2)}) copy-start(f32[8,64,256]{2,1,0:T(8,128)} %param.12) | copy-start | bytes 1572868
  62.3 6.6 %collective-permute-start.5 = (f32[512]{0:T(512)S(1)}, f32[512]{0:T(512)S(1)}, u32[]{:S(2)}, u32[]{:S(2)}) collective-permute-start(f32[512]{0:T(512)S(1)} %div.69), channel_id=1, source_target_pairs={{0,8},{8,16},{16,24},{24,0},{1,9},{9,17},{17,25},{25,1},{2,10},{10... | collective-permute-start | bytes 6152 | tf_op jit(solution)/shard_map/ppermute | solution.py:87
  65.0 4.5 %collective-permute-start.6 = (f32[512]{0:T(512)S(1)}, f32[512]{0:T(512)S(1)}, u32[]{:S(2)}, u32[]{:S(2)}) collective-permute-start(f32[512]{0:T(512)S(1)} %div.69), channel_id=1, source_target_pairs={{0,16},{8,24},{16,0},{24,8},{1,17},{9,25},{17,1},{25,9},{2,18},{10... | collective-permute-start | bytes 6152 | tf_op jit(solution)/shard_map/ppermute | solution.py:87
  67.6 3.6 %collective-permute-start.7 = (f32[512]{0:T(512)S(1)}, f32[512]{0:T(512)S(1)}, u32[]{:S(2)}, u32[]{:S(2)}) collective-permute-start(f32[512]{0:T(512)S(1)} %div.69), channel_id=1, source_target_pairs={{0,24},{8,0},{16,8},{24,16},{1,25},{9,1},{17,9},{25,17},{2,26},{10... | collective-permute-start | bytes 6152 | tf_op jit(solution)/shard_map/ppermute | solution.py:87
  71.9 3.9 %collective-permute-start.8 = (f32[1,1,2048]{2,1,0:T(1,128)S(1)}, f32[1,1,2048]{2,1,0:T(1,128)S(1)}, u32[]{:S(2)}, u32[]{:S(2)}) collective-permute-start(f32[1,1,2048]{2,1,0:T(1,128)S(1)} %reshape.130), channel_id=1, source_target_pairs={{0,2},{2,4},{4,6},{1,3},{3,5},{5,7},{8,10},{10,12},{12,14},{9,11},... | collective-permute-start | bytes 24584 | tf_op jit(solution)/shard_map/ppermute | solution.py:31
  74.4 5.3 %collective-permute-start.9 = (f32[1,1,2048]{2,1,0:T(1,128)S(1)}, f32[1,1,2048]{2,1,0:T(1,128)S(1)}, u32[]{:S(2)}, u32[]{:S(2)}) collective-permute-start(f32[1,1,2048]{2,1,0:T(1,128)S(1)} %reshape.130), channel_id=1, source_target_pairs={{2,0},{4,2},{6,4},{3,1},{5,3},{7,5},{10,8},{12,10},{14,12},{11,9},... | collective-permute-start | bytes 24584 | tf_op jit(solution)/shard_map/ppermute | solution.py:32
  79.7 3.8 %collective-permute-start.10 = (f32[3,1,2048]{2,1,0:T(1,128)S(1)}, f32[3,1,2048]{2,1,0:T(1,128)S(1)}, u32[]{:S(2)}, u32[]{:S(2)}) collective-permute-start(f32[3,1,2048]{2,1,0:T(1,128)S(1)} %constant_dynamic-update-slice_fusion), channel_id=1, source_target_pairs={{0,1},{1,0},{2,3},{3,2},{4,5},{5,4},{6,7},{7,6},{8,9},{9,8},{10,11... | collective-permute-start | bytes 73736 | tf_op jit(solution)/shard_map/ppermute | solution.py:27
  88.1 5.4 %collective-permute-start.11 = (f32[512]{0:T(512)S(1)}, f32[512]{0:T(512)S(1)}, u32[]{:S(2)}, u32[]{:S(2)}) collective-permute-start(f32[512]{0:T(512)S(1)} %divide_add_fusion.2), channel_id=1, source_target_pairs={{0,8},{8,16},{16,24},{24,0},{1,9},{9,17},{17,25},{25,1},{2,10},{10... | collective-permute-start | bytes 6152 | tf_op jit(solution)/shard_map/ppermute | solution.py:87
  88.2 5.3 %collective-permute-start.12 = (f32[512]{0:T(512)S(1)}, f32[512]{0:T(512)S(1)}, u32[]{:S(2)}, u32[]{:S(2)}) collective-permute-start(f32[512]{0:T(512)S(1)} %divide_add_fusion.2), channel_id=1, source_target_pairs={{0,16},{8,24},{16,0},{24,8},{1,17},{9,25},{17,1},{25,9},{2,18},{10... | collective-permute-start | bytes 6152 | tf_op jit(solution)/shard_map/ppermute | solution.py:87
  91.9 3.6 %collective-permute-start.13 = (f32[512]{0:T(512)S(1)}, f32[512]{0:T(512)S(1)}, u32[]{:S(2)}, u32[]{:S(2)}) collective-permute-start(f32[512]{0:T(512)S(1)} %divide_add_fusion.2), channel_id=1, source_target_pairs={{0,24},{8,0},{16,8},{24,16},{1,25},{9,1},{17,9},{25,17},{2,26},{10... | collective-permute-start | bytes 6152 | tf_op jit(solution)/shard_map/ppermute | solution.py:87
  96.1 2.8 %collective-permute-start.14 = (f32[1,1,2048]{2,1,0:T(1,128)S(1)}, f32[1,1,2048]{2,1,0:T(1,128)S(1)}, u32[]{:S(2)}, u32[]{:S(2)}) collective-permute-start(f32[1,1,2048]{2,1,0:T(1,128)S(1)} %reshape.134), channel_id=1, source_target_pairs={{0,2},{2,4},{4,6},{1,3},{3,5},{5,7},{8,10},{10,12},{12,14},{9,11},... | collective-permute-start | bytes 24584 | tf_op jit(solution)/shard_map/ppermute | solution.py:31
  97.6 5.5 %collective-permute-start.15 = (f32[1,1,2048]{2,1,0:T(1,128)S(1)}, f32[1,1,2048]{2,1,0:T(1,128)S(1)}, u32[]{:S(2)}, u32[]{:S(2)}) collective-permute-start(f32[1,1,2048]{2,1,0:T(1,128)S(1)} %reshape.134), channel_id=1, source_target_pairs={{2,0},{4,2},{6,4},{3,1},{5,3},{7,5},{10,8},{12,10},{14,12},{11,9},... | collective-permute-start | bytes 24584 | tf_op jit(solution)/shard_map/ppermute | solution.py:32
  103.1 3.8 %collective-permute-start.16 = (f32[3,1,2048]{2,1,0:T(1,128)S(1)}, f32[3,1,2048]{2,1,0:T(1,128)S(1)}, u32[]{:S(2)}, u32[]{:S(2)}) collective-permute-start(f32[3,1,2048]{2,1,0:T(1,128)S(1)} %constant_dynamic-update-slice_fusion.3), channel_id=1, source_target_pairs={{0,1},{1,0},{2,3},{3,2},{4,5},{5,4},{6,7},{7,6},{8,9},{9,8},{10,11... | collective-permute-start | bytes 73736 | tf_op jit(solution)/shard_map/ppermute | solution.py:27
  111.5 5.4 %collective-permute-start.17 = (f32[512]{0:T(512)S(1)}, f32[512]{0:T(512)S(1)}, u32[]{:S(2)}, u32[]{:S(2)}) collective-permute-start(f32[512]{0:T(512)S(1)} %divide_add_fusion.1), channel_id=1, source_target_pairs={{0,8},{8,16},{16,24},{24,0},{1,9},{9,17},{17,25},{25,1},{2,10},{10... | collective-permute-start | bytes 6152 | tf_op jit(solution)/shard_map/ppermute | solution.py:87
  112.2 4.7 %collective-permute-start.18 = (f32[512]{0:T(512)S(1)}, f32[512]{0:T(512)S(1)}, u32[]{:S(2)}, u32[]{:S(2)}) collective-permute-start(f32[512]{0:T(512)S(1)} %divide_add_fusion.1), channel_id=1, source_target_pairs={{0,16},{8,24},{16,0},{24,8},{1,17},{9,25},{17,1},{25,9},{2,18},{10... | collective-permute-start | bytes 6152 | tf_op jit(solution)/shard_map/ppermute | solution.py:87
  114.0 3.6 %collective-permute-start.19 = (f32[512]{0:T(512)S(1)}, f32[512]{0:T(512)S(1)}, u32[]{:S(2)}, u32[]{:S(2)}) collective-permute-start(f32[512]{0:T(512)S(1)} %divide_add_fusion.1), channel_id=1, source_target_pairs={{0,24},{8,0},{16,8},{24,16},{1,25},{9,1},{17,9},{25,17},{2,26},{10... | collective-permute-start | bytes 6152 | tf_op jit(solution)/shard_map/ppermute | solution.py:87
  118.3 3.1 %collective-permute-start.20 = (f32[1,1,2048]{2,1,0:T(1,128)S(1)}, f32[1,1,2048]{2,1,0:T(1,128)S(1)}, u32[]{:S(2)}, u32[]{:S(2)}) collective-permute-start(f32[1,1,2048]{2,1,0:T(1,128)S(1)} %reshape.138), channel_id=1, source_target_pairs={{0,2},{2,4},{4,6},{1,3},{3,5},{5,7},{8,10},{10,12},{12,14},{9,11},... | collective-permute-start | bytes 24584 | tf_op jit(solution)/shard_map/ppermute | solution.py:31
  119.9 5.3 %collective-permute-start.21 = (f32[1,1,2048]{2,1,0:T(1,128)S(1)}, f32[1,1,2048]{2,1,0:T(1,128)S(1)}, u32[]{:S(2)}, u32[]{:S(2)}) collective-permute-start(f32[1,1,2048]{2,1,0:T(1,128)S(1)} %reshape.138), channel_id=1, source_target_pairs={{2,0},{4,2},{6,4},{3,1},{5,3},{7,5},{10,8},{12,10},{14,12},{11,9},... | collective-permute-start | bytes 24584 | tf_op jit(solution)/shard_map/ppermute | solution.py:32
  125.2 3.8 %collective-permute-start.22 = (f32[3,1,2048]{2,1,0:T(1,128)S(1)}, f32[3,1,2048]{2,1,0:T(1,128)S(1)}, u32[]{:S(2)}, u32[]{:S(2)}) collective-permute-start(f32[3,1,2048]{2,1,0:T(1,128)S(1)} %constant_dynamic-update-slice_fusion.6), channel_id=1, source_target_pairs={{0,1},{1,0},{2,3},{3,2},{4,5},{5,4},{6,7},{7,6},{8,9},{9,8},{10,11... | collective-permute-start | bytes 73736 | tf_op jit(solution)/shard_map/ppermute | solution.py:27
  133.6 32.9 %copy-start = (f32[512]{0:T(512)}, f32[512]{0:T(512)S(1)}, u32[]{:S(2)}) copy-start(f32[512]{0:T(512)S(1)} %divide_add_fusion) | copy-start | bytes 6148
  137.2 4.6 %collective-permute-start.23 = (f32[1,4,32]{2,1,0:T(4,128)S(1)}, f32[1,4,32]{2,1,0:T(4,128)S(1)}, u32[]{:S(2)}, u32[]{:S(2)}) collective-permute-start(f32[1,4,32]{2,1,0:T(4,128)S(1)} %slice.245), channel_id=1, source_target_pairs={{0,2},{2,4},{4,6},{1,3},{3,5},{5,7},{8,10},{10,12},{12,14},{9,11},... | collective-permute-start | bytes 1544 | tf_op jit(solution)/shard_map/ppermute | solution.py:31
  140.6 3.7 %collective-permute-start.24 = (f32[1,4,32]{2,1,0:T(4,128)S(1)}, f32[1,4,32]{2,1,0:T(4,128)S(1)}, u32[]{:S(2)}, u32[]{:S(2)}) collective-permute-start(f32[1,4,32]{2,1,0:T(4,128)S(1)} %slice.247), channel_id=1, source_target_pairs={{2,0},{4,2},{6,4},{3,1},{5,3},{7,5},{10,8},{12,10},{14,12},{11,9},... | collective-permute-start | bytes 1544 | tf_op jit(solution)/shard_map/ppermute | solution.py:32
  144.3 3.7 %collective-permute-start.25 = (f32[6,1,32]{2,1,0:T(1,128)S(1)}, f32[6,1,32]{2,1,0:T(1,128)S(1)}, u32[]{:S(2)}, u32[]{:S(2)}) collective-permute-start(f32[6,1,32]{2,1,0:T(1,128)S(1)} %broadcast_select_fusion.9), channel_id=1, source_target_pairs={{0,1},{1,0},{2,3},{3,2},{4,5},{5,4},{6,7},{7,6},{8,9},{9,8},{10,11... | collective-permute-start | bytes 2312 | tf_op jit(solution)/shard_map/ppermute | solution.py:27
  148.1 5.3 %collective-permute-start.26 = (f32[6,6,1]{2,1,0:T(8,128)S(1)}, f32[6,6,1]{2,1,0:T(8,128)S(1)}, u32[]{:S(2)}, u32[]{:S(2)}) collective-permute-start(f32[6,6,1]{2,1,0:T(8,128)S(1)} %get-tuple-element.21), channel_id=1, source_target_pairs={{0,8},{8,16},{16,24},{1,9},{9,17},{17,25},{2,10},{10,18},{18,26},{... | collective-permute-start | bytes 440 | tf_op jit(solution)/shard_map/ppermute | solution.py:31
  151.9 5.9 %collective-permute-start.27 = (f32[6,6,1]{2,1,0:T(8,128)S(1)}, f32[6,6,1]{2,1,0:T(8,128)S(1)}, u32[]{:S(2)}, u32[]{:S(2)}) collective-permute-start(f32[6,6,1]{2,1,0:T(8,128)S(1)} %get-tuple-element.22), channel_id=1, source_target_pairs={{8,0},{16,8},{24,16},{9,1},{17,9},{25,17},{10,2},{18,10},{26,18},{... | collective-permute-start | bytes 440 | tf_op jit(solution)/shard_map/ppermute | solution.py:32
  (1 other events, 2.1 us)

commit v3 on v2

--- a/solution.py
+++ b/solution.py
@@ -90,14 +90,35 @@
     return jnp.take(stacked, order, axis=0)
 
 
+def dot(left, right):
+    return jnp.dot(left, right, precision=lax.Precision.HIGHEST)
+
+
+def box_matrix(boxes, cells, stride, offset, live, inner=None):
+    box = lax.broadcasted_iota(jnp.int32, (boxes, cells), 0)
+    cell = lax.broadcasted_iota(jnp.int32, (boxes, cells), 1)
+    if inner is None:
+        hit = (cell - offset >= box * BOX) & (cell - offset < box * BOX + BOX)
+    else:
+        outer_cell, inner_cell = cell // stride - offset, cell % stride - offset
+        outer_box, inner_box = box // inner, box % inner
+        hit = (outer_cell >= outer_box * BOX) & (outer_cell < outer_box * BOX + BOX)
+        hit = hit & (inner_cell >= inner_box * BOX) & (inner_cell < inner_box * BOX + BOX)
+    return (hit & live).astype(jnp.float32)
+
+
 def local(source, conductance, storage, aggregate_ids, coarse_values, coarse_columns):
     size_x, size_y, size_z = source.shape
     assert HALO == BOX and HALO >= 2 * NU and HALO >= NU + 2
     stacked = jnp.stack([source, conductance, storage])
-    wide = exchange(stacked, (("gx", 1), ("gy", 2), ("grp", 3)), HALO)
-    rows, span_y, span_z = wide.shape[1:]
+    wide = exchange(stacked, (("grp", 3),), HALO)
+    span_z = wide.shape[3]
     stride = span_z
-    wide = wide.reshape(3, rows, span_y * span_z)
+    wide = wide.reshape(3, size_x, size_y * span_z)
+    wide = exchange(wide, (("gy", 2),), HALO * span_z)
+    wide = exchange(wide, (("gx", 1),), HALO)
+    rows = wide.shape[1]
+    span_y = wide.shape[2] // span_z
     src, cond, stor = wide[0], wide[1], wide[2]
     mask = inside_mask(rows, span_y, span_z)
     face_list = face_terms(cond, stride)
@@ -113,15 +134,18 @@
         solution = jnp.where(mask, solution + WEIGHT * (src - op(solution)) / diagonal, 0.0)
     residual = src - op(solution)
     scaled = jnp.where(mask, residual / diagonal, 0.0)
-    smoothed = trimmed(residual - WEIGHT * op(scaled), span_y, span_z)
+    smoothed = residual - WEIGHT * op(scaled)
 
+    bx, by, bz = size_x // BOX, size_y // BOX, size_z // BOX
+    live = lax.axis_index("grp") >= 0
+    pick_x = box_matrix(bx, rows, 1, HALO, live)
+    pick_yz = box_matrix(by * bz, span_y * span_z, span_z, HALO, live, bz).T
+    box_totals = dot(pick_x, dot(smoothed, pick_yz)).reshape(-1)
     box_labels = aggregate_ids[::BOX, ::BOX, ::BOX].reshape(-1)
-    box_totals = (
-        smoothed.reshape(size_x // BOX, BOX, size_y // BOX, BOX, size_z // BOX, BOX)
-        .sum(axis=(1, 3, 5))
-        .reshape(-1)
-    )
-    coarse_rhs = jnp.zeros(box_totals.shape, source.dtype).at[box_labels].set(box_totals)
+    placed = (
+        box_labels[:, None] == lax.broadcasted_iota(jnp.int32, (box_labels.shape[0],) * 2, 1)
+    ).astype(source.dtype)
+    coarse_rhs = dot(box_totals[None, :], placed)[0]
     coarse_diag = jnp.diagonal(coarse_values[:, :, :64], axis1=1, axis2=2).reshape(-1)
     block_rows = coarse_values.shape[0]
     grid_x = lax.axis_size("gx")
@@ -146,11 +170,12 @@
         ).reshape(-1)
         coarse_error = coarse_error + (coarse_rhs - applied) / coarse_diag
 
-    bx, by, bz = size_x // BOX, size_y // BOX, size_z // BOX
-    small = coarse_error[box_labels].reshape(bx, by, bz)
+    small = dot(placed, coarse_error[:, None]).reshape(bx, by, bz)
     window = exchange(small, (("gx", 0), ("gy", 1), ("grp", 2)), 1)
-    lifted = jnp.repeat(jnp.repeat(jnp.repeat(window, BOX, axis=0), BOX, axis=1), BOX, axis=2)
-    lifted = lifted.reshape(rows, span_y * span_z)
+    window = window.reshape(bx + 2, (by + 2) * (bz + 2))
+    spread_x = box_matrix(bx + 2, rows, 1, 0, live).T
+    spread_yz = box_matrix((by + 2) * (bz + 2), span_y * span_z, span_z, 0, live, bz + 2)
+    lifted = dot(spread_x, dot(window, spread_yz))
     solution = jnp.where(mask, solution + (lifted - WEIGHT * op(lifted) / diagonal), 0.0)
     for sweep_number in range(NU):
         solution = jnp.where(mask, solution + WEIGHT * (src - op(solution)) / diagonal, 0.0)

time: 170 us -> 136 us (0.80)
  local copies, waits for them, and re-layouts: 56.4 us -> 20.1 us
  waiting for transfers between devices: 38.1 us -> 55.7 us
  other arithmetic: 22.1 us -> 7.9 us
  starting transfers between devices: 49.5 us -> 43.1 us
  matrix products: 1.56 us -> 7.34 us
    concatenate x8 -> x7, other arithmetic: 11.7 us -> 2.77 us  [exchange(): cells = jnp.concatenate([before, cells, after], axis=dim)]
    reshape x5 -> x3, local copies, waits for them, and re-layouts: 7.56 us -> 0.56 us  [the longest x1 0.41 us: local(): wide = wide.reshape(3, size_x, size_y * span_z)]
    concatenate x7 -> x5, local copies, waits for them, and re-layouts: 7.14 us -> 0.29 us  [exchange(): cells = jnp.concatenate([before, cells, after], axis=dim)]
    select_n x2 -> x0, local copies, waits for them, and re-layouts: 6.72 us -> none  [the longest x1 3.36 us: exchange(): after = jnp.where(index == 0, got, 0.0)]
    ppermute x7, waiting for transfers between devices: 0.22 us -> 6.91 us  [exchange(): before = lax.ppermute(tail, axis, [(i, i + 1) for i in range(count - 1)])]
    dot_general x0 -> x6, matrix products: none -> 5.79 us  [dot(): return jnp.dot(left, right, precision=lax.Precision.HIGHEST)]
    ppermute x9, starting transfers between devices: 14.3 us -> 8.7 us  [grp_pool(): lax.ppermute(vector, 'grp', [(i, (i + step) % groups) for i in range(grou...]
    ppermute x9, waiting for transfers between devices: 7.92 us -> 13.1 us  [grp_pool(): lax.ppermute(vector, 'grp', [(i, (i + step) % groups) for i in range(grou...]
  transfers between devices with their start and end apart: 28 -> 28, of which waited for: 18 -> 20; matrix products, arithmetic and copies ran while one was open for 7% -> 5% of each run, Pallas kernels for 0% -> 0%
where the time goes in v3:
time: 136 us; the launch traced here: 135 us
  waiting for transfers between devices  55.7 us (41%)
  starting transfers between devices  43.1 us (32%)
  local copies, waits for them, and re-layouts  20.1 us (15%)
  other arithmetic  7.9 us (6%)
  matrix products  7.34 us (5%)
    ppermute x7, waiting for transfers between devices, exchange(): after = lax.ppermute(head, axis, [(i + 1, i) for i in range(count - 1)])  23.3 us
    ppermute x7, starting transfers between devices, exchange(): before = lax.ppermute(tail, axis, [(i, i + 1) for i in range(count - 1)])  17.6 us
    ppermute x9, waiting for transfers between devices, grp_pool(): lax.ppermute(vector, 'grp', [(i, (i + step) % groups) for i in range(grou...  13.1 us
    ppermute x5, waiting for transfers between devices, exchange(): got = lax.ppermute(sent, axis, [(0, 1), (1, 0)])  12.5 us
    ppermute x7, starting transfers between devices, exchange(): after = lax.ppermute(head, axis, [(i + 1, i) for i in range(count - 1)])  9.21 us
    ppermute x9, starting transfers between devices, grp_pool(): lax.ppermute(vector, 'grp', [(i, (i + step) % groups) for i in range(grou...  8.7 us
    ppermute x5, starting transfers between devices, exchange(): got = lax.ppermute(sent, axis, [(0, 1), (1, 0)])  7.58 us
    ppermute x7, waiting for transfers between devices, exchange(): before = lax.ppermute(tail, axis, [(i, i + 1) for i in range(count - 1)])  6.91 us
  transfers between devices with their start and end apart: 28, of which 20 were waited for; matrix products, arithmetic and copies ran while one was open for 5% of the time, Pallas kernels for 0%

profile of v3, /device:TPU:0, one launch (start us, length us, event | category | flops | bytes accessed | tf_op | source)
XLA Modules:
  0.0 135.4 jit_solution(1765429566868795863)
XLA Ops:
  1.9 5.0 %collective-permute-start = (f32[3,16,16,4]{3,2,1,0:T(8,128)S(1)}, f32[3,16,16,4]{3,2,1,0:T(8,128)S(1)}, u32[]{:S(2)}, u32[]{:S(2)}) collective-permute-start(f32[3,16,16,4]{3,2,1,0:T(8,128)S(1)} %get-tuple-element.12), channel_id=1, source_target_pairs={{0,8},{8,16},{16,24},{1,9},{9,17},{17,25},{2,10},{10,18},{18,26},{... | collective-permute-start | bytes 36872 | tf_op jit(solution)/shard_map/ppermute | solution.py:31
  8.4 6.9 %collective-permute-done = f32[3,16,16,4]{3,2,1,0:T(8,128)S(1)} collective-permute-done((f32[3,16,16,4]{3,2,1,0:T(8,128)S(1)}, f32[3,16,16,4]{3,2,1,0:T(8,128)S(1)}, u32[]{:S(2)}, u32[]{:S(2)}) %collective-permute-start) | collective-permute-done | bytes 12320 | tf_op jit(solution)/shard_map/ppermute | solution.py:31
  15.2 4.1 %collective-permute-done.1 = f32[3,16,16,4]{3,2,1,0:T(8,128)S(1)} collective-permute-done((f32[3,16,16,4]{3,2,1,0:T(8,128)S(1)}, f32[3,16,16,4]{3,2,1,0:T(8,128)S(1)}, u32[]{:S(2)}, u32[]{:S(2)}) %collective-permute-start.1) | collective-permute-done | bytes 12320 | tf_op jit(solution)/shard_map/ppermute | solution.py:32
  20.3 1.6 %collective-permute-start.2 = (f32[3,16,544]{2,1,0:T(8,128)S(1)}, f32[3,16,544]{2,1,0:T(8,128)S(1)}, u32[]{:S(2)}, u32[]{:S(2)}) collective-permute-start(f32[3,16,544]{2,1,0:T(8,128)S(1)} %slice_select_fusion), channel_id=1, source_target_pairs={{0,1},{1,0},{2,3},{3,2},{4,5},{5,4},{6,7},{7,6},{8,9},{9,8},{10,11... | collective-permute-start | bytes 313352 | tf_op jit(solution)/shard_map/ppermute | solution.py:27
  21.9 3.4 %collective-permute-done.2 = f32[3,16,544]{2,1,0:T(8,128)S(1)} collective-permute-done((f32[3,16,544]{2,1,0:T(8,128)S(1)}, f32[3,16,544]{2,1,0:T(8,128)S(1)}, u32[]{:S(2)}, u32[]{:S(2)}) %collective-permute-start.2) | collective-permute-done | bytes 104480 | tf_op jit(solution)/shard_map/ppermute | solution.py:27
  28.2 1.9 %slice.223 = s32[4,4,32]{2,1,0:T(4,128)S(1)} slice(s32[16,16,128]{2,1,0:T(8,128)} %param.11), slice={[0:16:4], [0:16:4], [0:128:4]} | slice | bytes 4096 | tf_op jit(solution)/shard_map/slice | solution.py:144
  30.2 2.0 %copy.10 = f32[8,64,64]{0,2,1:T(8,128)} copy(f32[8,64,64]{2,1,0:T(8,128)S(1)} %slice-done) | data formatting | bytes 262144 | tf_op jit(solution)/shard_map/slice | solution.py:149
  35.7 2.2 %fusion.12 = f32[24,128]{1,0:T(8,128)S(1)} fusion(s32[128]{0:T(128)S(1)} %get-tuple-element.37, s32[128]{0:T(128)S(1)} %get-tuple-element.38, s32[3264]{0:T(1024)S(1)} %get-tuple-element.29, s32[3264]{0:T(1024)S(1)} %get-tuple-element.30, s32[128]{0:T(128)S(1)} %get-tuple-element.36, s32[128]{0:T(128)S(1)} %get-tuple-element.39, ...), kind=kOutput, calls=%fused_computation.30 | convolution fusion | flops 131056128 | bytes 3283969 | tf_op jit(solution)/shard_map/dot_general | solution.py:94
  38.6 1.6 %collective-permute-start.7 = (f32[512]{0:T(512)S(1)}, f32[512]{0:T(512)S(1)}, u32[]{:S(2)}, u32[]{:S(2)}) collective-permute-start(f32[512]{0:T(512)S(1)} %div.97), channel_id=1, source_target_pairs={{0,24},{8,0},{16,8},{24,16},{1,25},{9,1},{17,9},{25,17},{2,26},{10... | collective-permute-start | bytes 6152 | tf_op jit(solution)/shard_map/ppermute | solution.py:87
  41.6 1.6 %collective-permute-start.5 = (f32[512]{0:T(512)S(1)}, f32[512]{0:T(512)S(1)}, u32[]{:S(2)}, u32[]{:S(2)}) collective-permute-start(f32[512]{0:T(512)S(1)} %div.97), channel_id=1, source_target_pairs={{0,8},{8,16},{16,24},{24,0},{1,9},{9,17},{17,25},{25,1},{2,10},{10... | collective-permute-start | bytes 6152 | tf_op jit(solution)/shard_map/ppermute | solution.py:87
  44.6 2.4 %collective-permute-done.5 = f32[512]{0:T(512)S(1)} collective-permute-done((f32[512]{0:T(512)S(1)}, f32[512]{0:T(512)S(1)}, u32[]{:S(2)}, u32[]{:S(2)}) %collective-permute-start.5) | collective-permute-done | bytes 2080 | tf_op jit(solution)/shard_map/ppermute | solution.py:87
  47.7 3.1 %collective-permute-start.8 = (f32[1,1,2048]{2,1,0:T(1,128)S(1)}, f32[1,1,2048]{2,1,0:T(1,128)S(1)}, u32[]{:S(2)}, u32[]{:S(2)}) collective-permute-start(f32[1,1,2048]{2,1,0:T(1,128)S(1)} %reshape.92), channel_id=1, source_target_pairs={{0,2},{2,4},{4,6},{1,3},{3,5},{5,7},{8,10},{10,12},{12,14},{9,11},... | collective-permute-start | bytes 24584 | tf_op jit(solution)/shard_map/ppermute | solution.py:31
  52.3 4.7 %collective-permute-done.9 = f32[1,1,2048]{2,1,0:T(1,128)S(1)} collective-permute-done((f32[1,1,2048]{2,1,0:T(1,128)S(1)}, f32[1,1,2048]{2,1,0:T(1,128)S(1)}, u32[]{:S(2)}, u32[]{:S(2)}) %collective-permute-start.9) | collective-permute-done | bytes 8224 | tf_op jit(solution)/shard_map/ppermute | solution.py:32
  58.5 2.3 %collective-permute-done.10 = f32[3,1,2048]{2,1,0:T(1,128)S(1)} collective-permute-done((f32[3,1,2048]{2,1,0:T(1,128)S(1)}, f32[3,1,2048]{2,1,0:T(1,128)S(1)}, u32[]{:S(2)}, u32[]{:S(2)}) %collective-permute-start.10) | collective-permute-done | bytes 24608 | tf_op jit(solution)/shard_map/ppermute | solution.py:27
  61.6 1.7 %reshape.93 = f32[288,64]{1,0:T(8,128)} reshape(f32[3,3,2048]{2,1,0:T(4,128)} %pad_maximum_fusion.3) | data formatting | bytes 147456 | tf_op jit(solution)/shard_map/reshape | solution.py:166
  67.5 1.6 %collective-permute-done.13 = f32[512]{0:T(512)S(1)} collective-permute-done((f32[512]{0:T(512)S(1)}, f32[512]{0:T(512)S(1)}, u32[]{:S(2)}, u32[]{:S(2)}) %collective-permute-start.13) | collective-permute-done | bytes 2080 | tf_op jit(solution)/shard_map/ppermute | solution.py:87
  70.0 2.0 %collective-permute-done.11 = f32[512]{0:T(512)S(1)} collective-permute-done((f32[512]{0:T(512)S(1)}, f32[512]{0:T(512)S(1)}, u32[]{:S(2)}, u32[]{:S(2)}) %collective-permute-start.11) | collective-permute-done | bytes 2080 | tf_op jit(solution)/shard_map/ppermute | solution.py:87
  75.5 4.1 %collective-permute-done.15 = f32[1,1,2048]{2,1,0:T(1,128)S(1)} collective-permute-done((f32[1,1,2048]{2,1,0:T(1,128)S(1)}, f32[1,1,2048]{2,1,0:T(1,128)S(1)}, u32[]{:S(2)}, u32[]{:S(2)}) %collective-permute-start.15) | collective-permute-done | bytes 8224 | tf_op jit(solution)/shard_map/ppermute | solution.py:32
  81.2 2.3 %collective-permute-done.16 = f32[3,1,2048]{2,1,0:T(1,128)S(1)} collective-permute-done((f32[3,1,2048]{2,1,0:T(1,128)S(1)}, f32[3,1,2048]{2,1,0:T(1,128)S(1)}, u32[]{:S(2)}, u32[]{:S(2)}) %collective-permute-start.16) | collective-permute-done | bytes 24608 | tf_op jit(solution)/shard_map/ppermute | solution.py:27
  84.3 1.7 %reshape.97 = f32[288,64]{1,0:T(8,128)} reshape(f32[3,3,2048]{2,1,0:T(4,128)} %pad_maximum_fusion.4) | data formatting | bytes 147456 | tf_op jit(solution)/shard_map/reshape | solution.py:166
  90.2 1.6 %collective-permute-done.19 = f32[512]{0:T(512)S(1)} collective-permute-done((f32[512]{0:T(512)S(1)}, f32[512]{0:T(512)S(1)}, u32[]{:S(2)}, u32[]{:S(2)}) %collective-permute-start.19) | collective-permute-done | bytes 2080 | tf_op jit(solution)/shard_map/ppermute | solution.py:87
  91.7 2.3 %collective-permute-done.18 = f32[512]{0:T(512)S(1)} collective-permute-done((f32[512]{0:T(512)S(1)}, f32[512]{0:T(512)S(1)}, u32[]{:S(2)}, u32[]{:S(2)}) %collective-permute-start.18) | collective-permute-done | bytes 2080 | tf_op jit(solution)/shard_map/ppermute | solution.py:87
  95.6 2.0 %collective-permute-start.20 = (f32[1,1,2048]{2,1,0:T(1,128)S(1)}, f32[1,1,2048]{2,1,0:T(1,128)S(1)}, u32[]{:S(2)}, u32[]{:S(2)}) collective-permute-start(f32[1,1,2048]{2,1,0:T(1,128)S(1)} %reshape.100), channel_id=1, source_target_pairs={{0,2},{2,4},{4,6},{1,3},{3,5},{5,7},{8,10},{10,12},{12,14},{9,11},... | collective-permute-start | bytes 24584 | tf_op jit(solution)/shard_map/ppermute | solution.py:31
  98.9 3.5 %collective-permute-done.21 = f32[1,1,2048]{2,1,0:T(1,128)S(1)} collective-permute-done((f32[1,1,2048]{2,1,0:T(1,128)S(1)}, f32[1,1,2048]{2,1,0:T(1,128)S(1)}, u32[]{:S(2)}, u32[]{:S(2)}) %collective-permute-start.21) | collective-permute-done | bytes 8224 | tf_op jit(solution)/shard_map/ppermute | solution.py:32
  104.0 2.3 %collective-permute-done.22 = f32[3,1,2048]{2,1,0:T(1,128)S(1)} collective-permute-done((f32[3,1,2048]{2,1,0:T(1,128)S(1)}, f32[3,1,2048]{2,1,0:T(1,128)S(1)}, u32[]{:S(2)}, u32[]{:S(2)}) %collective-permute-start.22) | collective-permute-done | bytes 24608 | tf_op jit(solution)/shard_map/ppermute | solution.py:27
  107.1 1.7 %reshape.101 = f32[288,64]{1,0:T(8,128)} reshape(f32[3,3,2048]{2,1,0:T(4,128)} %pad_maximum_fusion.5) | data formatting | bytes 147456 | tf_op jit(solution)/shard_map/reshape | solution.py:166
  111.7 3.2 %collective-permute-start.23 = (f32[1,4,32]{2,1,0:T(4,128)S(1)}, f32[1,4,32]{2,1,0:T(4,128)S(1)}, u32[]{:S(2)}, u32[]{:S(2)}) collective-permute-start(f32[1,4,32]{2,1,0:T(4,128)S(1)} %slice.238), channel_id=1, source_target_pairs={{0,2},{2,4},{4,6},{1,3},{3,5},{5,7},{8,10},{10,12},{12,14},{9,11},... | collective-permute-start | bytes 1544 | tf_op jit(solution)/shard_map/ppermute | solution.py:31
  116.3 2.4 %collective-permute-done.24 = f32[1,4,32]{2,1,0:T(4,128)S(1)} collective-permute-done((f32[1,4,32]{2,1,0:T(4,128)S(1)}, f32[1,4,32]{2,1,0:T(4,128)S(1)}, u32[]{:S(2)}, u32[]{:S(2)}) %collective-permute-start.24) | collective-permute-done | bytes 544 | tf_op jit(solution)/shard_map/ppermute | solution.py:32
  120.3 2.1 %collective-permute-done.25 = f32[6,1,32]{2,1,0:T(1,128)S(1)} collective-permute-done((f32[6,1,32]{2,1,0:T(1,128)S(1)}, f32[6,1,32]{2,1,0:T(1,128)S(1)}, u32[]{:S(2)}, u32[]{:S(2)}) %collective-permute-start.25) | collective-permute-done | bytes 800 | tf_op jit(solution)/shard_map/ppermute | solution.py:27
  122.5 1.7 %collective-permute-start.26 = (f32[6,6,1]{2,1,0:T(8,128)S(1)}, f32[6,6,1]{2,1,0:T(8,128)S(1)}, u32[]{:S(2)}, u32[]{:S(2)}) collective-permute-start(f32[6,6,1]{2,1,0:T(8,128)S(1)} %get-tuple-element.16), channel_id=1, source_target_pairs={{0,8},{8,16},{16,24},{1,9},{9,17},{17,25},{2,10},{10,18},{18,26},{... | collective-permute-start | bytes 440 | tf_op jit(solution)/shard_map/ppermute | solution.py:31
  125.7 4.3 %collective-permute-done.27 = f32[6,6,1]{2,1,0:T(8,128)S(1)} collective-permute-done((f32[6,6,1]{2,1,0:T(8,128)S(1)}, f32[6,6,1]{2,1,0:T(8,128)S(1)}, u32[]{:S(2)}, u32[]{:S(2)}) %collective-permute-start.27) | collective-permute-done | bytes 176 | tf_op jit(solution)/shard_map/ppermute | solution.py:32
  130.2 1.8 %fusion.4 = f32[6,3264]{1,0:T(8,128)S(1)} fusion(f32[6,204]{1,0:T(8,128)S(1)} %reshape.105, s32[204]{0:T(256)S(1)} %get-tuple-element.43, s32[204]{0:T(256)S(1)} %get-tuple-element.46, s32[3264]{0:T(1024)S(1)} %get-tuple-element.29, s32[3264]{0:T(1024)S(1)} %get-tuple-element.30, s32[204]{0:T(256)S(1)} %get-tuple-element.42, s32[204]{0:T(256)S(1)} %get-tuple-element.47, ...), kind=kOutput, calls=%fused_computation.17 | convolution fusion | flops 58595328 | bytes 145657 | tf_op jit(solution)/shard_map/dot_general | solution.py:94
  (152 shorter events, 49.3 us)
Async XLA Ops:
  0.6 18.8 %copy-start.3 = (f32[16,16,128]{2,1,0:T(8,128)S(1)}, f32[16,16,128]{2,1,0:T(8,128)}, u32[]{:S(2)}) copy-start(f32[16,16,128]{2,1,0:T(8,128)} %param.10) | copy-start | bytes 393220
  0.6 18.7 %copy-start.4 = (f32[16,16,128]{2,1,0:T(8,128)S(1)}, f32[16,16,128]{2,1,0:T(8,128)}, u32[]{:S(2)}) copy-start(f32[16,16,128]{2,1,0:T(8,128)} %param.9) | copy-start | bytes 393220
  1.9 13.3 %collective-permute-start = (f32[3,16,16,4]{3,2,1,0:T(8,128)S(1)}, f32[3,16,16,4]{3,2,1,0:T(8,128)S(1)}, u32[]{:S(2)}, u32[]{:S(2)}) collective-permute-start(f32[3,16,16,4]{3,2,1,0:T(8,128)S(1)} %get-tuple-element.12), channel_id=1, source_target_pairs={{0,8},{8,16},{16,24},{1,9},{9,17},{17,25},{2,10},{10,18},{18,26},{... | collective-permute-start | bytes 36872 | tf_op jit(solution)/shard_map/ppermute | solution.py:31
  6.9 12.5 %collective-permute-start.1 = (f32[3,16,16,4]{3,2,1,0:T(8,128)S(1)}, f32[3,16,16,4]{3,2,1,0:T(8,128)S(1)}, u32[]{:S(2)}, u32[]{:S(2)}) collective-permute-start(f32[3,16,16,4]{3,2,1,0:T(8,128)S(1)} %get-tuple-element.13), channel_id=1, source_target_pairs={{8,0},{16,8},{24,16},{9,1},{17,9},{25,17},{10,2},{18,10},{26,18},{... | collective-permute-start | bytes 36872 | tf_op jit(solution)/shard_map/ppermute | solution.py:32
  20.3 4.9 %collective-permute-start.2 = (f32[3,16,544]{2,1,0:T(8,128)S(1)}, f32[3,16,544]{2,1,0:T(8,128)S(1)}, u32[]{:S(2)}, u32[]{:S(2)}) collective-permute-start(f32[3,16,544]{2,1,0:T(8,128)S(1)} %slice_select_fusion), channel_id=1, source_target_pairs={{0,1},{1,0},{2,3},{3,2},{4,5},{5,4},{6,7},{7,6},{8,9},{9,8},{10,11... | collective-permute-start | bytes 313352 | tf_op jit(solution)/shard_map/ppermute | solution.py:27
  25.6 8.2 %collective-permute-start.3 = (f32[3,4,3264]{2,1,0:T(4,128)S(1)}, f32[3,4,3264]{2,1,0:T(4,128)S(1)}, u32[]{:S(2)}, u32[]{:S(2)}) collective-permute-start(f32[3,4,3264]{2,1,0:T(4,128)S(1)} %get-tuple-element.10), channel_id=1, source_target_pairs={{0,2},{2,4},{4,6},{1,3},{3,5},{5,7},{8,10},{10,12},{12,14},{9,11},... | collective-permute-start | bytes 470024 | tf_op jit(solution)/shard_map/ppermute | solution.py:31
  26.9 6.9 %collective-permute-start.4 = (f32[3,4,3264]{2,1,0:T(4,128)S(1)}, f32[3,4,3264]{2,1,0:T(4,128)S(1)}, u32[]{:S(2)}, u32[]{:S(2)}) collective-permute-start(f32[3,4,3264]{2,1,0:T(4,128)S(1)} %get-tuple-element.11), channel_id=1, source_target_pairs={{2,0},{4,2},{6,4},{3,1},{5,3},{7,5},{10,8},{12,10},{14,12},{11,9},... | collective-permute-start | bytes 470024 | tf_op jit(solution)/shard_map/ppermute | solution.py:32
  35.7 29.2 %copy-start = (f32[8,64,256]{2,1,0:T(8,128)S(1)}, f32[8,64,256]{2,1,0:T(8,128)}, u32[]{:S(2)}) copy-start(f32[8,64,256]{2,1,0:T(8,128)} %param.12) | copy-start | bytes 1572868
  38.6 4.6 %collective-permute-start.7 = (f32[512]{0:T(512)S(1)}, f32[512]{0:T(512)S(1)}, u32[]{:S(2)}, u32[]{:S(2)}) collective-permute-start(f32[512]{0:T(512)S(1)} %div.97), channel_id=1, source_target_pairs={{0,24},{8,0},{16,8},{24,16},{1,25},{9,1},{17,9},{25,17},{2,26},{10... | collective-permute-start | bytes 6152 | tf_op jit(solution)/shard_map/ppermute | solution.py:87
  40.1 4.5 %collective-permute-start.6 = (f32[512]{0:T(512)S(1)}, f32[512]{0:T(512)S(1)}, u32[]{:S(2)}, u32[]{:S(2)}) collective-permute-start(f32[512]{0:T(512)S(1)} %div.97), channel_id=1, source_target_pairs={{0,16},{8,24},{16,0},{24,8},{1,17},{9,25},{17,1},{25,9},{2,18},{10... | collective-permute-start | bytes 6152 | tf_op jit(solution)/shard_map/ppermute | solution.py:87
  41.6 5.4 %collective-permute-start.5 = (f32[512]{0:T(512)S(1)}, f32[512]{0:T(512)S(1)}, u32[]{:S(2)}, u32[]{:S(2)}) collective-permute-start(f32[512]{0:T(512)S(1)} %div.97), channel_id=1, source_target_pairs={{0,8},{8,16},{16,24},{24,0},{1,9},{9,17},{17,25},{25,1},{2,10},{10... | collective-permute-start | bytes 6152 | tf_op jit(solution)/shard_map/ppermute | solution.py:87
  47.7 4.6 %collective-permute-start.8 = (f32[1,1,2048]{2,1,0:T(1,128)S(1)}, f32[1,1,2048]{2,1,0:T(1,128)S(1)}, u32[]{:S(2)}, u32[]{:S(2)}) collective-permute-start(f32[1,1,2048]{2,1,0:T(1,128)S(1)} %reshape.92), channel_id=1, source_target_pairs={{0,2},{2,4},{4,6},{1,3},{3,5},{5,7},{8,10},{10,12},{12,14},{9,11},... | collective-permute-start | bytes 24584 | tf_op jit(solution)/shard_map/ppermute | solution.py:31
  51.0 6.0 %collective-permute-start.9 = (f32[1,1,2048]{2,1,0:T(1,128)S(1)}, f32[1,1,2048]{2,1,0:T(1,128)S(1)}, u32[]{:S(2)}, u32[]{:S(2)}) collective-permute-start(f32[1,1,2048]{2,1,0:T(1,128)S(1)} %reshape.92), channel_id=1, source_target_pairs={{2,0},{4,2},{6,4},{3,1},{5,3},{7,5},{10,8},{12,10},{14,12},{11,9},... | collective-permute-start | bytes 24584 | tf_op jit(solution)/shard_map/ppermute | solution.py:32
  57.0 3.8 %collective-permute-start.10 = (f32[3,1,2048]{2,1,0:T(1,128)S(1)}, f32[3,1,2048]{2,1,0:T(1,128)S(1)}, u32[]{:S(2)}, u32[]{:S(2)}) collective-permute-start(f32[3,1,2048]{2,1,0:T(1,128)S(1)} %constant_dynamic-update-slice_fusion), channel_id=1, source_target_pairs={{0,1},{1,0},{2,3},{3,2},{4,5},{5,4},{6,7},{7,6},{8,9},{9,8},{10,11... | collective-permute-start | bytes 73736 | tf_op jit(solution)/shard_map/ppermute | solution.py:27
  65.4 3.6 %collective-permute-start.13 = (f32[512]{0:T(512)S(1)}, f32[512]{0:T(512)S(1)}, u32[]{:S(2)}, u32[]{:S(2)}) collective-permute-start(f32[512]{0:T(512)S(1)} %divide_add_fusion.2), channel_id=1, source_target_pairs={{0,24},{8,0},{16,8},{24,16},{1,25},{9,1},{17,9},{25,17},{2,26},{10... | collective-permute-start | bytes 6152 | tf_op jit(solution)/shard_map/ppermute | solution.py:87
  65.6 4.5 %collective-permute-start.12 = (f32[512]{0:T(512)S(1)}, f32[512]{0:T(512)S(1)}, u32[]{:S(2)}, u32[]{:S(2)}) collective-permute-start(f32[512]{0:T(512)S(1)} %divide_add_fusion.2), channel_id=1, source_target_pairs={{0,16},{8,24},{16,0},{24,8},{1,17},{9,25},{17,1},{25,9},{2,18},{10... | collective-permute-start | bytes 6152 | tf_op jit(solution)/shard_map/ppermute | solution.py:87
  66.7 5.4 %collective-permute-start.11 = (f32[512]{0:T(512)S(1)}, f32[512]{0:T(512)S(1)}, u32[]{:S(2)}, u32[]{:S(2)}) collective-permute-start(f32[512]{0:T(512)S(1)} %divide_add_fusion.2), channel_id=1, source_target_pairs={{0,8},{8,16},{16,24},{24,0},{1,9},{9,17},{17,25},{25,1},{2,10},{10... | collective-permute-start | bytes 6152 | tf_op jit(solution)/shard_map/ppermute | solution.py:87
  72.8 2.8 %collective-permute-start.14 = (f32[1,1,2048]{2,1,0:T(1,128)S(1)}, f32[1,1,2048]{2,1,0:T(1,128)S(1)}, u32[]{:S(2)}, u32[]{:S(2)}) collective-permute-start(f32[1,1,2048]{2,1,0:T(1,128)S(1)} %reshape.96), channel_id=1, source_target_pairs={{0,2},{2,4},{4,6},{1,3},{3,5},{5,7},{8,10},{10,12},{12,14},{9,11},... | collective-permute-start | bytes 24584 | tf_op jit(solution)/shard_map/ppermute | solution.py:31
  74.2 5.5 %collective-permute-start.15 = (f32[1,1,2048]{2,1,0:T(1,128)S(1)}, f32[1,1,2048]{2,1,0:T(1,128)S(1)}, u32[]{:S(2)}, u32[]{:S(2)}) collective-permute-start(f32[1,1,2048]{2,1,0:T(1,128)S(1)} %reshape.96), channel_id=1, source_target_pairs={{2,0},{4,2},{6,4},{3,1},{5,3},{7,5},{10,8},{12,10},{14,12},{11,9},... | collective-permute-start | bytes 24584 | tf_op jit(solution)/shard_map/ppermute | solution.py:32
  79.7 3.8 %collective-permute-start.16 = (f32[3,1,2048]{2,1,0:T(1,128)S(1)}, f32[3,1,2048]{2,1,0:T(1,128)S(1)}, u32[]{:S(2)}, u32[]{:S(2)}) collective-permute-start(f32[3,1,2048]{2,1,0:T(1,128)S(1)} %constant_dynamic-update-slice_fusion.3), channel_id=1, source_target_pairs={{0,1},{1,0},{2,3},{3,2},{4,5},{5,4},{6,7},{7,6},{8,9},{9,8},{10,11... | collective-permute-start | bytes 73736 | tf_op jit(solution)/shard_map/ppermute | solution.py:27
  88.1 3.6 %collective-permute-start.19 = (f32[512]{0:T(512)S(1)}, f32[512]{0:T(512)S(1)}, u32[]{:S(2)}, u32[]{:S(2)}) collective-permute-start(f32[512]{0:T(512)S(1)} %divide_add_fusion.1), channel_id=1, source_target_pairs={{0,24},{8,0},{16,8},{24,16},{1,25},{9,1},{17,9},{25,17},{2,26},{10... | collective-permute-start | bytes 6152 | tf_op jit(solution)/shard_map/ppermute | solution.py:87
  89.5 4.5 %collective-permute-start.18 = (f32[512]{0:T(512)S(1)}, f32[512]{0:T(512)S(1)}, u32[]{:S(2)}, u32[]{:S(2)}) collective-permute-start(f32[512]{0:T(512)S(1)} %divide_add_fusion.1), channel_id=1, source_target_pairs={{0,16},{8,24},{16,0},{24,8},{1,17},{9,25},{17,1},{25,9},{2,18},{10... | collective-permute-start | bytes 6152 | tf_op jit(solution)/shard_map/ppermute | solution.py:87
  89.5 5.4 %collective-permute-start.17 = (f32[512]{0:T(512)S(1)}, f32[512]{0:T(512)S(1)}, u32[]{:S(2)}, u32[]{:S(2)}) collective-permute-start(f32[512]{0:T(512)S(1)} %divide_add_fusion.1), channel_id=1, source_target_pairs={{0,8},{8,16},{16,24},{24,0},{1,9},{9,17},{17,25},{25,1},{2,10},{10... | collective-permute-start | bytes 6152 | tf_op jit(solution)/shard_map/ppermute | solution.py:87
  95.6 3.3 %collective-permute-start.20 = (f32[1,1,2048]{2,1,0:T(1,128)S(1)}, f32[1,1,2048]{2,1,0:T(1,128)S(1)}, u32[]{:S(2)}, u32[]{:S(2)}) collective-permute-start(f32[1,1,2048]{2,1,0:T(1,128)S(1)} %reshape.100), channel_id=1, source_target_pairs={{0,2},{2,4},{4,6},{1,3},{3,5},{5,7},{8,10},{10,12},{12,14},{9,11},... | collective-permute-start | bytes 24584 | tf_op jit(solution)/shard_map/ppermute | solution.py:31
  97.6 4.9 %collective-permute-start.21 = (f32[1,1,2048]{2,1,0:T(1,128)S(1)}, f32[1,1,2048]{2,1,0:T(1,128)S(1)}, u32[]{:S(2)}, u32[]{:S(2)}) collective-permute-start(f32[1,1,2048]{2,1,0:T(1,128)S(1)} %reshape.100), channel_id=1, source_target_pairs={{2,0},{4,2},{6,4},{3,1},{5,3},{7,5},{10,8},{12,10},{14,12},{11,9},... | collective-permute-start | bytes 24584 | tf_op jit(solution)/shard_map/ppermute | solution.py:32
  102.5 3.8 %collective-permute-start.22 = (f32[3,1,2048]{2,1,0:T(1,128)S(1)}, f32[3,1,2048]{2,1,0:T(1,128)S(1)}, u32[]{:S(2)}, u32[]{:S(2)}) collective-permute-start(f32[3,1,2048]{2,1,0:T(1,128)S(1)} %constant_dynamic-update-slice_fusion.6), channel_id=1, source_target_pairs={{0,1},{1,0},{2,3},{3,2},{4,5},{5,4},{6,7},{7,6},{8,9},{9,8},{10,11... | collective-permute-start | bytes 73736 | tf_op jit(solution)/shard_map/ppermute | solution.py:27
  110.9 21.1 %copy-start.6 = (f32[512]{0:T(512)}, f32[512]{0:T(512)S(1)}, u32[]{:S(2)}) copy-start(f32[512]{0:T(512)S(1)} %divide_add_fusion) | copy-start | bytes 6148
  111.7 4.6 %collective-permute-start.23 = (f32[1,4,32]{2,1,0:T(4,128)S(1)}, f32[1,4,32]{2,1,0:T(4,128)S(1)}, u32[]{:S(2)}, u32[]{:S(2)}) collective-permute-start(f32[1,4,32]{2,1,0:T(4,128)S(1)} %slice.238), channel_id=1, source_target_pairs={{0,2},{2,4},{4,6},{1,3},{3,5},{5,7},{8,10},{10,12},{12,14},{9,11},... | collective-permute-start | bytes 1544 | tf_op jit(solution)/shard_map/ppermute | solution.py:31
  115.0 3.7 %collective-permute-start.24 = (f32[1,4,32]{2,1,0:T(4,128)S(1)}, f32[1,4,32]{2,1,0:T(4,128)S(1)}, u32[]{:S(2)}, u32[]{:S(2)}) collective-permute-start(f32[1,4,32]{2,1,0:T(4,128)S(1)} %slice.240), channel_id=1, source_target_pairs={{2,0},{4,2},{6,4},{3,1},{5,3},{7,5},{10,8},{12,10},{14,12},{11,9},... | collective-permute-start | bytes 1544 | tf_op jit(solution)/shard_map/ppermute | solution.py:32
  118.8 3.7 %collective-permute-start.25 = (f32[6,1,32]{2,1,0:T(1,128)S(1)}, f32[6,1,32]{2,1,0:T(1,128)S(1)}, u32[]{:S(2)}, u32[]{:S(2)}) collective-permute-start(f32[6,1,32]{2,1,0:T(1,128)S(1)} %broadcast_select_fusion.9), channel_id=1, source_target_pairs={{0,1},{1,0},{2,3},{3,2},{4,5},{5,4},{6,7},{7,6},{8,9},{9,8},{10,11... | collective-permute-start | bytes 2312 | tf_op jit(solution)/shard_map/ppermute | solution.py:27
  122.5 3.2 %collective-permute-start.26 = (f32[6,6,1]{2,1,0:T(8,128)S(1)}, f32[6,6,1]{2,1,0:T(8,128)S(1)}, u32[]{:S(2)}, u32[]{:S(2)}) collective-permute-start(f32[6,6,1]{2,1,0:T(8,128)S(1)} %get-tuple-element.16), channel_id=1, source_target_pairs={{0,8},{8,16},{16,24},{1,9},{9,17},{17,25},{2,10},{10,18},{18,26},{... | collective-permute-start | bytes 440 | tf_op jit(solution)/shard_map/ppermute | solution.py:31
  124.2 5.9 %collective-permute-start.27 = (f32[6,6,1]{2,1,0:T(8,128)S(1)}, f32[6,6,1]{2,1,0:T(8,128)S(1)}, u32[]{:S(2)}, u32[]{:S(2)}) collective-permute-start(f32[6,6,1]{2,1,0:T(8,128)S(1)} %get-tuple-element.17), channel_id=1, source_target_pairs={{8,0},{16,8},{24,16},{9,1},{17,9},{25,17},{10,2},{18,10},{26,18},{... | collective-permute-start | bytes 440 | tf_op jit(solution)/shard_map/ppermute | solution.py:32
  (5 other events, 48.9 us)

commit v4 on v3

--- a/solution.py
+++ b/solution.py
@@ -105,6 +105,38 @@
         hit = (outer_cell >= outer_box * BOX) & (outer_cell < outer_box * BOX + BOX)
         hit = hit & (inner_cell >= inner_box * BOX) & (inner_cell < inner_box * BOX + BOX)
     return (hit & live).astype(jnp.float32)
+
+
+def neighbourhood(block):
+    size_x, size_y = lax.axis_size("gx"), lax.axis_size("gy")
+    index_y = lax.axis_index("gy")
+    axes = ("gx", "gy")
+
+    def pairs_for(dx, dy_of):
+        pairs = []
+        for x in range(size_x):
+            for y in range(size_y):
+                sx, sy = x + dx, dy_of(y)
+                if 0 <= sx < size_x and 0 <= sy < size_y:
+                    pairs.append((sx * size_y + sy, x * size_y + y))
+        return pairs
+
+    def sent(pairs):
+        return lax.ppermute(block, axes, pairs) if pairs else jnp.zeros_like(block)
+
+    slots = {(0, 0): block}
+    for dx in (-1, 0, 1):
+        if size_y == 2:
+            got = sent(pairs_for(dx, lambda y: 1 - y))
+            slots[(dx, 1)] = jnp.where(index_y == 0, got, 0.0)
+            slots[(dx, -1)] = jnp.where(index_y == 1, got, 0.0)
+            if dx != 0:
+                slots[(dx, 0)] = sent(pairs_for(dx, lambda y: y))
+        else:
+            for dy in (-1, 0, 1):
+                if (dx, dy) != (0, 0):
+                    slots[(dx, dy)] = sent(pairs_for(dx, lambda y, dy=dy: y + dy))
+    return jnp.stack([jnp.stack([slots[(dx, dy)] for dy in (-1, 0, 1)]) for dx in (-1, 0, 1)])
 
 
 def local(source, conductance, storage, aggregate_ids, coarse_values, coarse_columns):
@@ -159,19 +191,27 @@
     delta_x = target_x - lax.axis_index("gx") + 1
     delta_y = target_y - lax.axis_index("gy") + 1
     local_columns = ((delta_x * 3 + delta_y) * groups + member_ids) * block_rows + within_ids
-    coarse_error = coarse_rhs / coarse_diag
+    rhs_blocks = coarse_rhs.reshape(block_rows, 64)
+    diag_blocks = coarse_diag.reshape(block_rows, 64)
+    tables = 9 * groups * block_rows
+    pick = (
+        local_columns.reshape(-1, 1) == lax.broadcasted_iota(jnp.int32, (local_columns.size, tables), 1)
+    ).astype(source.dtype)
+    error_blocks = rhs_blocks / diag_blocks
     for sweep_number in range(CITER - 1):
-        pooled = grp_pool(coarse_error)
-        beside_all = exchange(pooled.reshape(1, 1, -1), (("gx", 0), ("gy", 1)), 1)
-        blocks = beside_all.reshape(-1, 64)[local_columns]
-        blocks = blocks.reshape(blocks.shape[0], -1)
+        pooled = grp_pool(error_blocks)
+        table = neighbourhood(pooled).reshape(tables, 64)
+        blocks = dot(pick, table).reshape(block_rows, -1)
         applied = jnp.einsum(
             "bim,bm->bi", coarse_values, blocks, precision=lax.Precision.HIGHEST
-        ).reshape(-1)
-        coarse_error = coarse_error + (coarse_rhs - applied) / coarse_diag
+        )
+        error_blocks = error_blocks + (rhs_blocks - applied) / diag_blocks
+    coarse_error = error_blocks.reshape(-1)
 
     small = dot(placed, coarse_error[:, None]).reshape(bx, by, bz)
-    window = exchange(small, (("gx", 0), ("gy", 1), ("grp", 2)), 1)
+    small = exchange(small, (("grp", 2),), 1)
+    around = neighbourhood(small).transpose(0, 2, 1, 3, 4).reshape(3 * bx, 3 * by, bz + 2)
+    window = around[bx - 1:2 * bx + 1, by - 1:2 * by + 1]
     window = window.reshape(bx + 2, (by + 2) * (bz + 2))
     spread_x = box_matrix(bx + 2, rows, 1, 0, live).T
     spread_yz = box_matrix((by + 2) * (bz + 2), span_y * span_z, span_z, 0, live, bz + 2)

time: 136 us -> 169 us (1.24); the launches traced: 135 us -> 166 us
  starting transfers between devices: 43.1 us -> 77.2 us
  waiting for transfers between devices: 55.7 us -> 26.8 us
  other arithmetic: 7.9 us -> 19.4 us
  matrix products: 7.34 us -> 14.4 us
  local copies, waits for them, and re-layouts: 20.1 us -> 26.9 us
    ppermute x0 -> x20, starting transfers between devices: none -> 50.9 us  [sent(): return lax.ppermute(block, axes, pairs) if pairs else jnp.zeros_like(block)]
    ppermute x7 -> x3, waiting for transfers between devices: 23.3 us -> 8.33 us  [exchange(): after = lax.ppermute(head, axis, [(i + 1, i) for i in range(count - 1)])]
    another operation x0 -> x14, local copies, waits for them, and re-layouts: none -> 10.6 us  [the longest x12 9.84 us: grp_pool(): stacked = jnp.stack(parts)]
    ppermute x5 -> x1, waiting for transfers between devices: 12.5 us -> 3.38 us  [exchange(): got = lax.ppermute(sent, axis, [(0, 1), (1, 0)])]
    ppermute x7 -> x3, starting transfers between devices: 17.6 us -> 8.53 us  [exchange(): before = lax.ppermute(tail, axis, [(i, i + 1) for i in range(count - 1)])]
    ppermute x9, waiting for transfers between devices: 13.1 us -> 4.63 us  [grp_pool(): lax.ppermute(vector, 'grp', [(i, (i + step) % groups) for i in range(grou...]
    ppermute x5 -> x1, starting transfers between devices: 7.58 us -> 1.56 us  [exchange(): got = lax.ppermute(sent, axis, [(0, 1), (1, 0)])]
    ppermute x7 -> x3, starting transfers between devices: 9.21 us -> 3.88 us  [exchange(): after = lax.ppermute(head, axis, [(i + 1, i) for i in range(count - 1)])]
  transfers between devices with their start and end apart: 28 -> 36, of which waited for: 20 -> 12; matrix products, arithmetic and copies ran while one was open for 5% -> 12% of each run, Pallas kernels for 0% -> 0%
where the time goes in v4:
time: 169 us; the launch traced here: 166 us
  starting transfers between devices  77.2 us (46%)
  local copies, waits for them, and re-layouts  26.9 us (16%)
  waiting for transfers between devices  26.8 us (16%)
  other arithmetic  19.4 us (11%)
  matrix products  14.4 us (9%)
    ppermute x20, starting transfers between devices, sent(): return lax.ppermute(block, axes, pairs) if pairs else jnp.zeros_like(block)  50.9 us
    ppermute x9, starting transfers between devices, grp_pool(): lax.ppermute(vector, 'grp', [(i, (i + step) % groups) for i in range(grou...  12.3 us
    dot_general x9, matrix products, dot(): return jnp.dot(left, right, precision=lax.Precision.HIGHEST)  10.7 us
    another operation x12, local copies, waits for them, and re-layouts, grp_pool(): stacked = jnp.stack(parts)  9.84 us
    ppermute x3, starting transfers between devices, exchange(): before = lax.ppermute(tail, axis, [(i, i + 1) for i in range(count - 1)])  8.53 us
    ppermute x3, waiting for transfers between devices, exchange(): after = lax.ppermute(head, axis, [(i + 1, i) for i in range(count - 1)])  8.33 us
    ppermute x20, waiting for transfers between devices, sent(): return lax.ppermute(block, axes, pairs) if pairs else jnp.zeros_like(block)  5.29 us
    ppermute x3, waiting for transfers between devices, exchange(): before = lax.ppermute(tail, axis, [(i, i + 1) for i in range(count - 1)])  5.14 us
  transfers between devices with their start and end apart: 36, of which 12 were waited for; matrix products, arithmetic and copies ran while one was open for 12% of the time, Pallas kernels for 0%

profile of v4, /device:TPU:0, one launch (start us, length us, event | category | flops | bytes accessed | tf_op | source)
XLA Modules:
  0.0 166.2 jit_solution(7547521340216440722)
XLA Ops:
  2.0 5.0 %collective-permute-start = (f32[3,16,16,4]{3,2,1,0:T(8,128)S(1)}, f32[3,16,16,4]{3,2,1,0:T(8,128)S(1)}, u32[]{:S(2)}, u32[]{:S(2)}) collective-permute-start(f32[3,16,16,4]{3,2,1,0:T(8,128)S(1)} %get-tuple-element.12), channel_id=1, source_target_pairs={{0,8},{8,16},{16,24},{1,9},{9,17},{17,25},{2,10},{10,18},{18,26},{... | collective-permute-start | bytes 36872 | tf_op jit(solution)/shard_map/ppermute | solution.py:31
  10.2 5.1 %collective-permute-done = f32[3,16,16,4]{3,2,1,0:T(8,128)S(1)} collective-permute-done((f32[3,16,16,4]{3,2,1,0:T(8,128)S(1)}, f32[3,16,16,4]{3,2,1,0:T(8,128)S(1)}, u32[]{:S(2)}, u32[]{:S(2)}) %collective-permute-start) | collective-permute-done | bytes 12320 | tf_op jit(solution)/shard_map/ppermute | solution.py:31
  15.3 4.1 %collective-permute-done.1 = f32[3,16,16,4]{3,2,1,0:T(8,128)S(1)} collective-permute-done((f32[3,16,16,4]{3,2,1,0:T(8,128)S(1)}, f32[3,16,16,4]{3,2,1,0:T(8,128)S(1)}, u32[]{:S(2)}, u32[]{:S(2)}) %collective-permute-start.1) | collective-permute-done | bytes 12320 | tf_op jit(solution)/shard_map/ppermute | solution.py:32
  20.3 1.6 collective-permute-start.2
  21.9 3.4 %collective-permute-done.2 = f32[3,16,544]{2,1,0:T(8,128)S(1)} collective-permute-done((f32[3,16,544]{2,1,0:T(8,128)S(1)}, f32[3,16,544]{2,1,0:T(8,128)S(1)}, u32[]{:S(2)}, u32[]{:S(2)}) %collective-permute-start.2) | collective-permute-done | bytes 104480 | tf_op jit(solution)/shard_map/ppermute | solution.py:27
  28.3 1.9 %slice.192 = s32[4,4,32]{2,1,0:T(4,128)S(1)} slice(s32[16,16,128]{2,1,0:T(8,128)} %param.11), slice={[0:16:4], [0:16:4], [0:128:4]} | slice | bytes 4096 | tf_op jit(solution)/shard_map/slice | solution.py:176
  30.2 2.0 %copy.20 = f32[8,64,64]{0,2,1:T(8,128)} copy(f32[8,64,64]{2,1,0:T(8,128)S(1)} %slice-done) | data formatting | bytes 262144 | tf_op jit(solution)/shard_map/slice | solution.py:181
  32.2 1.5 gather_fusion
  35.5 2.2 %fusion.12 = f32[24,128]{1,0:T(8,128)S(1)} fusion(s32[128]{0:T(128)S(1)} %get-tuple-element.53, s32[128]{0:T(128)S(1)} %get-tuple-element.54, s32[3264]{0:T(1024)S(1)} %get-tuple-element.45, s32[3264]{0:T(1024)S(1)} %get-tuple-element.46, s32[128]{0:T(128)S(1)} %get-tuple-element.52, s32[128]{0:T(128)S(1)} %get-tuple-element.55, ...), kind=kOutput, calls=%fused_computation.27 | convolution fusion | flops 131056128 | bytes 3283969 | tf_op jit(solution)/shard_map/dot_general | solution.py:94
  39.5 2.6 %collective-permute-start.6 = (f32[8,64]{0,1:T(8,128)}, f32[8,64]{0,1:T(8,128)}, u32[]{:S(2)}, u32[]{:S(2)}) collective-permute-start(f32[8,64]{0,1:T(8,128)} %get-tuple-element.17), channel_id=1, source_target_pairs={{0,16},{8,24},{16,0},{24,8},{1,17},{9,25},{17,1},{25,9},{2,18},{10... | collective-permute-start | bytes 6152 | tf_op jit(solution)/shard_map/ppermute | solution.py:87
  42.1 3.8 %collective-permute-start.7 = (f32[8,64]{0,1:T(8,128)}, f32[8,64]{0,1:T(8,128)}, u32[]{:S(2)}, u32[]{:S(2)}) collective-permute-start(f32[8,64]{0,1:T(8,128)} %get-tuple-element.17), channel_id=1, source_target_pairs={{0,24},{8,0},{16,8},{24,16},{1,25},{9,1},{17,9},{25,17},{2,26},{10... | collective-permute-start | bytes 6152 | tf_op jit(solution)/shard_map/ppermute | solution.py:87
  56.5 1.6 collective-permute-start.10
  58.1 4.9 %collective-permute-start.9 = (f32[4,8,64]{2,1,0:T(8,128)S(1)}, f32[4,8,64]{2,1,0:T(8,128)S(1)}, u32[]{:S(2)}, u32[]{:S(2)}) collective-permute-start(f32[4,8,64]{2,1,0:T(8,128)S(1)} %broadcast_select_fusion.4), channel_id=1, source_target_pairs={{0,2},{1,3},{2,4},{3,5},{4,6},{5,7},{8,10},{9,11},{10,12},{11,13},... | collective-permute-start | bytes 24584 | tf_op jit(solution)/shard_map/ppermute | solution.py:125
  63.0 5.0 %collective-permute-start.8 = (f32[4,8,64]{2,1,0:T(8,128)S(1)}, f32[4,8,64]{2,1,0:T(8,128)S(1)}, u32[]{:S(2)}, u32[]{:S(2)}) collective-permute-start(f32[4,8,64]{2,1,0:T(8,128)S(1)} %broadcast_select_fusion.4), channel_id=1, source_target_pairs={{1,2},{0,3},{3,4},{2,5},{5,6},{4,7},{9,10},{8,11},{11,12},{10,13},... | collective-permute-start | bytes 24584 | tf_op jit(solution)/shard_map/ppermute | solution.py:125
  74.4 2.2 %collective-permute-start.15 = (f32[8,64]{0,1:T(8,128)}, f32[8,64]{0,1:T(8,128)}, u32[]{:S(2)}, u32[]{:S(2)}) collective-permute-start(f32[8,64]{0,1:T(8,128)} %fusion.212), channel_id=1, source_target_pairs={{0,24},{8,0},{16,8},{24,16},{1,25},{9,1},{17,9},{25,17},{2,26},{10... | collective-permute-start | bytes 6152 | tf_op jit(solution)/shard_map/ppermute | solution.py:87
  79.4 2.3 %collective-permute-done.14 = f32[8,64]{0,1:T(8,128)} collective-permute-done((f32[8,64]{0,1:T(8,128)}, f32[8,64]{0,1:T(8,128)}, u32[]{:S(2)}, u32[]{:S(2)}) %collective-permute-start.14) | collective-permute-done | bytes 2080 | tf_op jit(solution)/shard_map/ppermute | solution.py:87
  84.0 1.4 gather_fusion.2
  89.5 1.5 collective-permute-start.18
  91.0 3.5 %collective-permute-start.17 = (f32[4,8,64]{2,1,0:T(8,128)S(1)}, f32[4,8,64]{2,1,0:T(8,128)S(1)}, u32[]{:S(2)}, u32[]{:S(2)}) collective-permute-start(f32[4,8,64]{2,1,0:T(8,128)S(1)} %broadcast_select_fusion.3), channel_id=1, source_target_pairs={{0,2},{1,3},{2,4},{3,5},{4,6},{5,7},{8,10},{9,11},{10,12},{11,13},... | collective-permute-start | bytes 24584 | tf_op jit(solution)/shard_map/ppermute | solution.py:125
  94.5 5.0 %collective-permute-start.16 = (f32[4,8,64]{2,1,0:T(8,128)S(1)}, f32[4,8,64]{2,1,0:T(8,128)S(1)}, u32[]{:S(2)}, u32[]{:S(2)}) collective-permute-start(f32[4,8,64]{2,1,0:T(8,128)S(1)} %broadcast_select_fusion.3), channel_id=1, source_target_pairs={{1,2},{0,3},{3,4},{2,5},{5,6},{4,7},{9,10},{8,11},{11,12},{10,13},... | collective-permute-start | bytes 24584 | tf_op jit(solution)/shard_map/ppermute | solution.py:125
  104.5 1.4 fusion.210
  106.0 2.0 %collective-permute-start.23 = (f32[8,64]{0,1:T(8,128)}, f32[8,64]{0,1:T(8,128)}, u32[]{:S(2)}, u32[]{:S(2)}) collective-permute-start(f32[8,64]{0,1:T(8,128)} %fusion.210), channel_id=1, source_target_pairs={{0,24},{8,0},{16,8},{24,16},{1,25},{9,1},{17,9},{25,17},{2,26},{10... | collective-permute-start | bytes 6152 | tf_op jit(solution)/shard_map/ppermute | solution.py:87
  111.3 2.1 %collective-permute-done.22 = f32[8,64]{0,1:T(8,128)} collective-permute-done((f32[8,64]{0,1:T(8,128)}, f32[8,64]{0,1:T(8,128)}, u32[]{:S(2)}, u32[]{:S(2)}) %collective-permute-start.22) | collective-permute-done | bytes 2080 | tf_op jit(solution)/shard_map/ppermute | solution.py:87
  121.8 4.4 %collective-permute-start.25 = (f32[4,8,64]{2,1,0:T(8,128)S(1)}, f32[4,8,64]{2,1,0:T(8,128)S(1)}, u32[]{:S(2)}, u32[]{:S(2)}) collective-permute-start(f32[4,8,64]{2,1,0:T(8,128)S(1)} %broadcast_select_fusion.2), channel_id=1, source_target_pairs={{0,2},{1,3},{2,4},{3,5},{4,6},{5,7},{8,10},{9,11},{10,12},{11,13},... | collective-permute-start | bytes 24584 | tf_op jit(solution)/shard_map/ppermute | solution.py:125
  126.2 4.1 %collective-permute-start.24 = (f32[4,8,64]{2,1,0:T(8,128)S(1)}, f32[4,8,64]{2,1,0:T(8,128)S(1)}, u32[]{:S(2)}, u32[]{:S(2)}) collective-permute-start(f32[4,8,64]{2,1,0:T(8,128)S(1)} %broadcast_select_fusion.2), channel_id=1, source_target_pairs={{1,2},{0,3},{3,4},{2,5},{5,6},{4,7},{9,10},{8,11},{11,12},{10,13},... | collective-permute-start | bytes 24584 | tf_op jit(solution)/shard_map/ppermute | solution.py:125
  136.3 1.9 %fusion.31 = f32[1,4,4,32]{3,0,2,1:T(1,128)S(1)} fusion(s32[4,4,32]{2,1,0:T(4,128)} %copy-done.6, f32[512,1,1,1]{0,1,2,3:T(1,128)S(1)} %reshape.153), kind=kOutput, calls=%fused_computation.46 | convolution fusion | flops 3407872 | bytes 6144 | tf_op jit(solution)/shard_map/dot_general | solution.py:94
  138.3 2.3 %collective-permute-start.29 = (f32[4,4,1]{2,1,0:T(4,128)S(1)}, f32[4,4,1]{2,1,0:T(4,128)S(1)}, u32[]{:S(2)}, u32[]{:S(2)}) collective-permute-start(f32[4,4,1]{2,1,0:T(4,128)S(1)} %get-tuple-element.42), channel_id=1, source_target_pairs={{0,8},{8,16},{16,24},{1,9},{9,17},{17,25},{2,10},{10,18},{18,26},{... | collective-permute-start | bytes 200 | tf_op jit(solution)/shard_map/ppermute | solution.py:31
  141.9 4.2 %collective-permute-done.30 = f32[4,4,1]{2,1,0:T(4,128)S(1)} collective-permute-done((f32[4,4,1]{2,1,0:T(4,128)S(1)}, f32[4,4,1]{2,1,0:T(4,128)S(1)}, u32[]{:S(2)}, u32[]{:S(2)}) %collective-permute-start.30) | collective-permute-done | bytes 96 | tf_op jit(solution)/shard_map/ppermute | solution.py:32
  148.8 1.5 collective-permute-start.33
  150.2 3.6 %collective-permute-start.32 = (f32[4,4,34]{2,1,0:T(4,128)S(1)}, f32[4,4,34]{2,1,0:T(4,128)S(1)}, u32[]{:S(2)}, u32[]{:S(2)}) collective-permute-start(f32[4,4,34]{2,1,0:T(4,128)S(1)} %pad_maximum_fusion.9), channel_id=1, source_target_pairs={{0,2},{1,3},{2,4},{3,5},{4,6},{5,7},{8,10},{9,11},{10,12},{11,13},... | collective-permute-start | bytes 6536 | tf_op jit(solution)/shard_map/ppermute | solution.py:125
  153.8 4.9 %collective-permute-start.31 = (f32[4,4,34]{2,1,0:T(4,128)S(1)}, f32[4,4,34]{2,1,0:T(4,128)S(1)}, u32[]{:S(2)}, u32[]{:S(2)}) collective-permute-start(f32[4,4,34]{2,1,0:T(4,128)S(1)} %pad_maximum_fusion.9), channel_id=1, source_target_pairs={{1,2},{0,3},{3,4},{2,5},{5,6},{4,7},{9,10},{8,11},{11,12},{10,13},... | collective-permute-start | bytes 6536 | tf_op jit(solution)/shard_map/ppermute | solution.py:125
  160.4 2.5 %fusion.4 = f32[6,3264]{1,0:T(8,128)S(1)} fusion(f32[6,204]{1,0:T(8,128)S(1)} %reshape.104, s32[204]{0:T(256)} %get-tuple-element.59, s32[204]{0:T(256)S(1)} %copy-done.10, s32[3264]{0:T(1024)S(1)} %get-tuple-element.45, s32[3264]{0:T(1024)S(1)} %get-tuple-element.46, s32[204]{0:T(256)S(1)} %copy-done.12, s32[204]{0:T(256)S(1)} %copy-done.11, ...), kind=kOutput, calls=%fused_computation.14 | convolution fusion | flops 58595328 | bytes 145657 | tf_op jit(solution)/shard_map/dot_general | solution.py:94
  (198 shorter events, 69.4 us)
Async XLA Ops:
  2.0 13.3 %collective-permute-start = (f32[3,16,16,4]{3,2,1,0:T(8,128)S(1)}, f32[3,16,16,4]{3,2,1,0:T(8,128)S(1)}, u32[]{:S(2)}, u32[]{:S(2)}) collective-permute-start(f32[3,16,16,4]{3,2,1,0:T(8,128)S(1)} %get-tuple-element.12), channel_id=1, source_target_pairs={{0,8},{8,16},{16,24},{1,9},{9,17},{17,25},{2,10},{10,18},{18,26},{... | collective-permute-start | bytes 36872 | tf_op jit(solution)/shard_map/ppermute | solution.py:31
  6.9 12.5 %collective-permute-start.1 = (f32[3,16,16,4]{3,2,1,0:T(8,128)S(1)}, f32[3,16,16,4]{3,2,1,0:T(8,128)S(1)}, u32[]{:S(2)}, u32[]{:S(2)}) collective-permute-start(f32[3,16,16,4]{3,2,1,0:T(8,128)S(1)} %get-tuple-element.13), channel_id=1, source_target_pairs={{8,0},{16,8},{24,16},{9,1},{17,9},{25,17},{10,2},{18,10},{26,18},{... | collective-permute-start | bytes 36872 | tf_op jit(solution)/shard_map/ppermute | solution.py:32
  25.6 8.1 %collective-permute-start.3 = (f32[3,4,3264]{2,1,0:T(4,128)S(1)}, f32[3,4,3264]{2,1,0:T(4,128)S(1)}, u32[]{:S(2)}, u32[]{:S(2)}) collective-permute-start(f32[3,4,3264]{2,1,0:T(4,128)S(1)} %get-tuple-element.10), channel_id=1, source_target_pairs={{0,2},{2,4},{4,6},{1,3},{3,5},{5,7},{8,10},{10,12},{12,14},{9,11},... | collective-permute-start | bytes 470024 | tf_op jit(solution)/shard_map/ppermute | solution.py:31
  26.9 6.8 %collective-permute-start.4 = (f32[3,4,3264]{2,1,0:T(4,128)S(1)}, f32[3,4,3264]{2,1,0:T(4,128)S(1)}, u32[]{:S(2)}, u32[]{:S(2)}) collective-permute-start(f32[3,4,3264]{2,1,0:T(4,128)S(1)} %get-tuple-element.11), channel_id=1, source_target_pairs={{2,0},{4,2},{6,4},{3,1},{5,3},{7,5},{10,8},{12,10},{14,12},{11,9},... | collective-permute-start | bytes 470024 | tf_op jit(solution)/shard_map/ppermute | solution.py:32
  39.5 8.5 %collective-permute-start.6 = (f32[8,64]{0,1:T(8,128)}, f32[8,64]{0,1:T(8,128)}, u32[]{:S(2)}, u32[]{:S(2)}) collective-permute-start(f32[8,64]{0,1:T(8,128)} %get-tuple-element.17), channel_id=1, source_target_pairs={{0,16},{8,24},{16,0},{24,8},{1,17},{9,25},{17,1},{25,9},{2,18},{10... | collective-permute-start | bytes 6152 | tf_op jit(solution)/shard_map/ppermute | solution.py:87
  42.1 6.8 %collective-permute-start.5 = (f32[8,64]{0,1:T(8,128)}, f32[8,64]{0,1:T(8,128)}, u32[]{:S(2)}, u32[]{:S(2)}) collective-permute-start(f32[8,64]{0,1:T(8,128)} %get-tuple-element.17), channel_id=1, source_target_pairs={{0,8},{8,16},{16,24},{24,0},{1,9},{9,17},{17,25},{25,1},{2,10},{10... | collective-permute-start | bytes 6152 | tf_op jit(solution)/shard_map/ppermute | solution.py:87
  42.1 7.6 %collective-permute-start.7 = (f32[8,64]{0,1:T(8,128)}, f32[8,64]{0,1:T(8,128)}, u32[]{:S(2)}, u32[]{:S(2)}) collective-permute-start(f32[8,64]{0,1:T(8,128)} %get-tuple-element.17), channel_id=1, source_target_pairs={{0,24},{8,0},{16,8},{24,16},{1,25},{9,1},{17,9},{25,17},{2,26},{10... | collective-permute-start | bytes 6152 | tf_op jit(solution)/shard_map/ppermute | solution.py:87
  53.2 14.8 %collective-permute-start.11 = (f32[4,8,64]{2,1,0:T(8,128)S(1)}, f32[4,8,64]{2,1,0:T(8,128)S(1)}, u32[]{:S(2)}, u32[]{:S(2)}) collective-permute-start(f32[4,8,64]{2,1,0:T(8,128)S(1)} %broadcast_select_fusion.4), channel_id=1, source_target_pairs={{3,0},{2,1},{5,2},{4,3},{7,4},{6,5},{11,8},{10,9},{13,10},{12,11},... | collective-permute-start | bytes 24584 | tf_op jit(solution)/shard_map/ppermute | solution.py:125
  55.2 12.8 %collective-permute-start.12 = (f32[4,8,64]{2,1,0:T(8,128)S(1)}, f32[4,8,64]{2,1,0:T(8,128)S(1)}, u32[]{:S(2)}, u32[]{:S(2)}) collective-permute-start(f32[4,8,64]{2,1,0:T(8,128)S(1)} %broadcast_select_fusion.4), channel_id=1, source_target_pairs={{2,0},{3,1},{4,2},{5,3},{6,4},{7,5},{10,8},{11,9},{12,10},{13,11},... | collective-permute-start | bytes 24584 | tf_op jit(solution)/shard_map/ppermute | solution.py:125
  56.5 11.5 %collective-permute-start.10 = (f32[4,8,64]{2,1,0:T(8,128)S(1)}, f32[4,8,64]{2,1,0:T(8,128)S(1)}, u32[]{:S(2)}, u32[]{:S(2)}) collective-permute-start(f32[4,8,64]{2,1,0:T(8,128)S(1)} %broadcast_select_fusion.4), channel_id=1, source_target_pairs={{1,0},{0,1},{3,2},{2,3},{5,4},{4,5},{7,6},{6,7},{9,8},{8,9},{11,10... | collective-permute-start | bytes 24584 | tf_op jit(solution)/shard_map/ppermute | solution.py:125
  58.1 11.4 %collective-permute-start.9 = (f32[4,8,64]{2,1,0:T(8,128)S(1)}, f32[4,8,64]{2,1,0:T(8,128)S(1)}, u32[]{:S(2)}, u32[]{:S(2)}) collective-permute-start(f32[4,8,64]{2,1,0:T(8,128)S(1)} %broadcast_select_fusion.4), channel_id=1, source_target_pairs={{0,2},{1,3},{2,4},{3,5},{4,6},{5,7},{8,10},{9,11},{10,12},{11,13},... | collective-permute-start | bytes 24584 | tf_op jit(solution)/shard_map/ppermute | solution.py:125
  63.0 6.4 %collective-permute-start.8 = (f32[4,8,64]{2,1,0:T(8,128)S(1)}, f32[4,8,64]{2,1,0:T(8,128)S(1)}, u32[]{:S(2)}, u32[]{:S(2)}) collective-permute-start(f32[4,8,64]{2,1,0:T(8,128)S(1)} %broadcast_select_fusion.4), channel_id=1, source_target_pairs={{1,2},{0,3},{3,4},{2,5},{5,6},{4,7},{9,10},{8,11},{11,12},{10,13},... | collective-permute-start | bytes 24584 | tf_op jit(solution)/shard_map/ppermute | solution.py:125
  76.6 5.1 %collective-permute-start.14 = (f32[8,64]{0,1:T(8,128)}, f32[8,64]{0,1:T(8,128)}, u32[]{:S(2)}, u32[]{:S(2)}) collective-permute-start(f32[8,64]{0,1:T(8,128)} %fusion.212), channel_id=1, source_target_pairs={{0,16},{8,24},{16,0},{24,8},{1,17},{9,25},{17,1},{25,9},{2,18},{10... | collective-permute-start | bytes 6152 | tf_op jit(solution)/shard_map/ppermute | solution.py:87
  76.6 6.0 %collective-permute-start.13 = (f32[8,64]{0,1:T(8,128)}, f32[8,64]{0,1:T(8,128)}, u32[]{:S(2)}, u32[]{:S(2)}) collective-permute-start(f32[8,64]{0,1:T(8,128)} %fusion.212), channel_id=1, source_target_pairs={{0,8},{8,16},{16,24},{24,0},{1,9},{9,17},{17,25},{25,1},{2,10},{10... | collective-permute-start | bytes 6152 | tf_op jit(solution)/shard_map/ppermute | solution.py:87
  86.2 13.4 %collective-permute-start.19 = (f32[4,8,64]{2,1,0:T(8,128)S(1)}, f32[4,8,64]{2,1,0:T(8,128)S(1)}, u32[]{:S(2)}, u32[]{:S(2)}) collective-permute-start(f32[4,8,64]{2,1,0:T(8,128)S(1)} %broadcast_select_fusion.3), channel_id=1, source_target_pairs={{3,0},{2,1},{5,2},{4,3},{7,4},{6,5},{11,8},{10,9},{13,10},{12,11},... | collective-permute-start | bytes 24584 | tf_op jit(solution)/shard_map/ppermute | solution.py:125
  88.2 11.4 %collective-permute-start.20 = (f32[4,8,64]{2,1,0:T(8,128)S(1)}, f32[4,8,64]{2,1,0:T(8,128)S(1)}, u32[]{:S(2)}, u32[]{:S(2)}) collective-permute-start(f32[4,8,64]{2,1,0:T(8,128)S(1)} %broadcast_select_fusion.3), channel_id=1, source_target_pairs={{2,0},{3,1},{4,2},{5,3},{6,4},{7,5},{10,8},{11,9},{12,10},{13,11},... | collective-permute-start | bytes 24584 | tf_op jit(solution)/shard_map/ppermute | solution.py:125
  89.5 10.1 %collective-permute-start.18 = (f32[4,8,64]{2,1,0:T(8,128)S(1)}, f32[4,8,64]{2,1,0:T(8,128)S(1)}, u32[]{:S(2)}, u32[]{:S(2)}) collective-permute-start(f32[4,8,64]{2,1,0:T(8,128)S(1)} %broadcast_select_fusion.3), channel_id=1, source_target_pairs={{1,0},{0,1},{3,2},{2,3},{5,4},{4,5},{7,6},{6,7},{9,8},{8,9},{11,10... | collective-permute-start | bytes 24584 | tf_op jit(solution)/shard_map/ppermute | solution.py:125
  91.0 10.0 %collective-permute-start.17 = (f32[4,8,64]{2,1,0:T(8,128)S(1)}, f32[4,8,64]{2,1,0:T(8,128)S(1)}, u32[]{:S(2)}, u32[]{:S(2)}) collective-permute-start(f32[4,8,64]{2,1,0:T(8,128)S(1)} %broadcast_select_fusion.3), channel_id=1, source_target_pairs={{0,2},{1,3},{2,4},{3,5},{4,6},{5,7},{8,10},{9,11},{10,12},{11,13},... | collective-permute-start | bytes 24584 | tf_op jit(solution)/shard_map/ppermute | solution.py:125
  94.5 6.4 %collective-permute-start.16 = (f32[4,8,64]{2,1,0:T(8,128)S(1)}, f32[4,8,64]{2,1,0:T(8,128)S(1)}, u32[]{:S(2)}, u32[]{:S(2)}) collective-permute-start(f32[4,8,64]{2,1,0:T(8,128)S(1)} %broadcast_select_fusion.3), channel_id=1, source_target_pairs={{1,2},{0,3},{3,4},{2,5},{5,6},{4,7},{9,10},{8,11},{11,12},{10,13},... | collective-permute-start | bytes 24584 | tf_op jit(solution)/shard_map/ppermute | solution.py:125
  108.0 5.5 %collective-permute-start.22 = (f32[8,64]{0,1:T(8,128)}, f32[8,64]{0,1:T(8,128)}, u32[]{:S(2)}, u32[]{:S(2)}) collective-permute-start(f32[8,64]{0,1:T(8,128)} %fusion.210), channel_id=1, source_target_pairs={{0,16},{8,24},{16,0},{24,8},{1,17},{9,25},{17,1},{25,9},{2,18},{10... | collective-permute-start | bytes 6152 | tf_op jit(solution)/shard_map/ppermute | solution.py:87
  108.0 6.3 %collective-permute-start.21 = (f32[8,64]{0,1:T(8,128)}, f32[8,64]{0,1:T(8,128)}, u32[]{:S(2)}, u32[]{:S(2)}) collective-permute-start(f32[8,64]{0,1:T(8,128)} %fusion.210), channel_id=1, source_target_pairs={{0,8},{8,16},{16,24},{24,0},{1,9},{9,17},{17,25},{25,1},{2,10},{10... | collective-permute-start | bytes 6152 | tf_op jit(solution)/shard_map/ppermute | solution.py:87
  117.8 12.5 %collective-permute-start.27 = (f32[4,8,64]{2,1,0:T(8,128)S(1)}, f32[4,8,64]{2,1,0:T(8,128)S(1)}, u32[]{:S(2)}, u32[]{:S(2)}) collective-permute-start(f32[4,8,64]{2,1,0:T(8,128)S(1)} %broadcast_select_fusion.2), channel_id=1, source_target_pairs={{3,0},{2,1},{5,2},{4,3},{7,4},{6,5},{11,8},{10,9},{13,10},{12,11},... | collective-permute-start | bytes 24584 | tf_op jit(solution)/shard_map/ppermute | solution.py:125
  119.8 10.5 %collective-permute-start.28 = (f32[4,8,64]{2,1,0:T(8,128)S(1)}, f32[4,8,64]{2,1,0:T(8,128)S(1)}, u32[]{:S(2)}, u32[]{:S(2)}) collective-permute-start(f32[4,8,64]{2,1,0:T(8,128)S(1)} %broadcast_select_fusion.2), channel_id=1, source_target_pairs={{2,0},{3,1},{4,2},{5,3},{6,4},{7,5},{10,8},{11,9},{12,10},{13,11},... | collective-permute-start | bytes 24584 | tf_op jit(solution)/shard_map/ppermute | solution.py:125
  121.1 9.2 %collective-permute-start.26 = (f32[4,8,64]{2,1,0:T(8,128)S(1)}, f32[4,8,64]{2,1,0:T(8,128)S(1)}, u32[]{:S(2)}, u32[]{:S(2)}) collective-permute-start(f32[4,8,64]{2,1,0:T(8,128)S(1)} %broadcast_select_fusion.2), channel_id=1, source_target_pairs={{1,0},{0,1},{3,2},{2,3},{5,4},{4,5},{7,6},{6,7},{9,8},{8,9},{11,10... | collective-permute-start | bytes 24584 | tf_op jit(solution)/shard_map/ppermute | solution.py:125
  121.8 10.0 %collective-permute-start.25 = (f32[4,8,64]{2,1,0:T(8,128)S(1)}, f32[4,8,64]{2,1,0:T(8,128)S(1)}, u32[]{:S(2)}, u32[]{:S(2)}) collective-permute-start(f32[4,8,64]{2,1,0:T(8,128)S(1)} %broadcast_select_fusion.2), channel_id=1, source_target_pairs={{0,2},{1,3},{2,4},{3,5},{4,6},{5,7},{8,10},{9,11},{10,12},{11,13},... | collective-permute-start | bytes 24584 | tf_op jit(solution)/shard_map/ppermute | solution.py:125
  126.2 5.5 %collective-permute-start.24 = (f32[4,8,64]{2,1,0:T(8,128)S(1)}, f32[4,8,64]{2,1,0:T(8,128)S(1)}, u32[]{:S(2)}, u32[]{:S(2)}) collective-permute-start(f32[4,8,64]{2,1,0:T(8,128)S(1)} %broadcast_select_fusion.2), channel_id=1, source_target_pairs={{1,2},{0,3},{3,4},{2,5},{5,6},{4,7},{9,10},{8,11},{11,12},{10,13},... | collective-permute-start | bytes 24584 | tf_op jit(solution)/shard_map/ppermute | solution.py:125
  140.5 5.5 %collective-permute-start.30 = (f32[4,4,1]{2,1,0:T(4,128)S(1)}, f32[4,4,1]{2,1,0:T(4,128)S(1)}, u32[]{:S(2)}, u32[]{:S(2)}) collective-permute-start(f32[4,4,1]{2,1,0:T(4,128)S(1)} %get-tuple-element.43), channel_id=1, source_target_pairs={{8,0},{16,8},{24,16},{9,1},{17,9},{25,17},{10,2},{18,10},{26,18},{... | collective-permute-start | bytes 200 | tf_op jit(solution)/shard_map/ppermute | solution.py:32
  146.2 12.7 %collective-permute-start.34 = (f32[4,4,34]{2,1,0:T(4,128)S(1)}, f32[4,4,34]{2,1,0:T(4,128)S(1)}, u32[]{:S(2)}, u32[]{:S(2)}) collective-permute-start(f32[4,4,34]{2,1,0:T(4,128)S(1)} %pad_maximum_fusion.9), channel_id=1, source_target_pairs={{3,0},{2,1},{5,2},{4,3},{7,4},{6,5},{11,8},{10,9},{13,10},{12,11},... | collective-permute-start | bytes 6536 | tf_op jit(solution)/shard_map/ppermute | solution.py:125
  147.5 11.4 %collective-permute-start.35 = (f32[4,4,34]{2,1,0:T(4,128)S(1)}, f32[4,4,34]{2,1,0:T(4,128)S(1)}, u32[]{:S(2)}, u32[]{:S(2)}) collective-permute-start(f32[4,4,34]{2,1,0:T(4,128)S(1)} %pad_maximum_fusion.9), channel_id=1, source_target_pairs={{2,0},{3,1},{4,2},{5,3},{6,4},{7,5},{10,8},{11,9},{12,10},{13,11},... | collective-permute-start | bytes 6536 | tf_op jit(solution)/shard_map/ppermute | solution.py:125
  148.8 10.1 %collective-permute-start.33 = (f32[4,4,34]{2,1,0:T(4,128)S(1)}, f32[4,4,34]{2,1,0:T(4,128)S(1)}, u32[]{:S(2)}, u32[]{:S(2)}) collective-permute-start(f32[4,4,34]{2,1,0:T(4,128)S(1)} %pad_maximum_fusion.9), channel_id=1, source_target_pairs={{1,0},{0,1},{3,2},{2,3},{5,4},{4,5},{7,6},{6,7},{9,8},{8,9},{11,10... | collective-permute-start | bytes 6536 | tf_op jit(solution)/shard_map/ppermute | solution.py:125
  150.2 9.9 %collective-permute-start.32 = (f32[4,4,34]{2,1,0:T(4,128)S(1)}, f32[4,4,34]{2,1,0:T(4,128)S(1)}, u32[]{:S(2)}, u32[]{:S(2)}) collective-permute-start(f32[4,4,34]{2,1,0:T(4,128)S(1)} %pad_maximum_fusion.9), channel_id=1, source_target_pairs={{0,2},{1,3},{2,4},{3,5},{4,6},{5,7},{8,10},{9,11},{10,12},{11,13},... | collective-permute-start | bytes 6536 | tf_op jit(solution)/shard_map/ppermute | solution.py:125
  153.8 6.3 %collective-permute-start.31 = (f32[4,4,34]{2,1,0:T(4,128)S(1)}, f32[4,4,34]{2,1,0:T(4,128)S(1)}, u32[]{:S(2)}, u32[]{:S(2)}) collective-permute-start(f32[4,4,34]{2,1,0:T(4,128)S(1)} %pad_maximum_fusion.9), channel_id=1, source_target_pairs={{1,2},{0,3},{3,4},{2,5},{5,6},{4,7},{9,10},{8,11},{11,12},{10,13},... | collective-permute-start | bytes 6536 | tf_op jit(solution)/shard_map/ppermute | solution.py:125
  (20 other events, 229.9 us)

commit v5 on v3

--- a/solution.py
+++ b/solution.py
@@ -9,6 +9,7 @@
 HALO = 4
 
 WEIGHT = 2.0 / 3.0
+ALL_AXES = ("grp", "gx", "gy")
 PAIRS = ((0, 1), (0, -1), (1, 1), (1, -1), (2, 1), (2, -1))
 
 
@@ -107,6 +108,12 @@
     return (hit & live).astype(jnp.float32)
 
 
+def everyone(vector):
+    count = lax.axis_size(ALL_AXES)
+    copies = jnp.broadcast_to(vector[None], (count,) + vector.shape)
+    return lax.all_to_all(copies, ALL_AXES, 0, 0, tiled=True).reshape(-1)
+
+
 def local(source, conductance, storage, aggregate_ids, coarse_values, coarse_columns):
     size_x, size_y, size_z = source.shape
     assert HALO == BOX and HALO >= 2 * NU and HALO >= NU + 2
@@ -151,27 +158,25 @@
     grid_x = lax.axis_size("gx")
     grid_y = lax.axis_size("gy")
     groups = lax.axis_size("grp")
-    within_ids = coarse_columns % block_rows
-    device_ids = coarse_columns // block_rows
-    target_y = device_ids % grid_y
-    target_x = device_ids // grid_y % grid_x
-    member_ids = device_ids // (grid_y * grid_x)
-    delta_x = target_x - lax.axis_index("gx") + 1
-    delta_y = target_y - lax.axis_index("gy") + 1
-    local_columns = ((delta_x * 3 + delta_y) * groups + member_ids) * block_rows + within_ids
     coarse_error = coarse_rhs / coarse_diag
     for sweep_number in range(CITER - 1):
-        pooled = grp_pool(coarse_error)
-        beside_all = exchange(pooled.reshape(1, 1, -1), (("gx", 0), ("gy", 1)), 1)
-        blocks = beside_all.reshape(-1, 64)[local_columns]
-        blocks = blocks.reshape(blocks.shape[0], -1)
+        pooled = everyone(coarse_error)
+        blocks = pooled.reshape(-1, 64)[coarse_columns]
+        blocks = blocks.reshape(block_rows, -1)
         applied = jnp.einsum(
             "bim,bm->bi", coarse_values, blocks, precision=lax.Precision.HIGHEST
         ).reshape(-1)
         coarse_error = coarse_error + (coarse_rhs - applied) / coarse_diag
 
-    small = dot(placed, coarse_error[:, None]).reshape(bx, by, bz)
-    window = exchange(small, (("gx", 0), ("gy", 1), ("grp", 2)), 1)
+    small = dot(placed, coarse_error[:, None]).reshape(-1)
+    every = everyone(small).reshape(groups, grid_x, grid_y, bx, by, bz)
+    boxes = every.transpose(1, 3, 2, 4, 0, 5).reshape(grid_x * bx, grid_y * by, groups * bz)
+    boxes = jnp.pad(boxes, 1)
+    window = lax.dynamic_slice(
+        boxes,
+        (lax.axis_index("gx") * bx, lax.axis_index("gy") * by, lax.axis_index("grp") * bz),
+        (bx + 2, by + 2, bz + 2),
+    )
     window = window.reshape(bx + 2, (by + 2) * (bz + 2))
     spread_x = box_matrix(bx + 2, rows, 1, 0, live).T
     spread_yz = box_matrix((by + 2) * (bz + 2), span_y * span_z, span_z, 0, live, bz + 2)

time: 136 us -> 110 us (0.81)
  waiting for transfers between devices: 55.7 us -> 35.6 us
  starting transfers between devices: 43.1 us -> 24.3 us
  blocking collectives: 0 us -> 9.96 us
  other arithmetic: 7.9 us -> 11.6 us
  local copies, waits for them, and re-layouts: 20.1 us -> 18.3 us
    all_to_all x0 -> x3, waiting for transfers between devices: none -> 21.2 us  [everyone(): return lax.all_to_all(copies, ALL_AXES, 0, 0, tiled=True).reshape(-1)]
    ppermute x7 -> x2, waiting for transfers between devices: 23.3 us -> 4.14 us  [exchange(): after = lax.ppermute(head, axis, [(i + 1, i) for i in range(count - 1)])]
    all_to_all x0 -> x3, starting transfers between devices: none -> 13.9 us  [everyone(): return lax.all_to_all(copies, ALL_AXES, 0, 0, tiled=True).reshape(-1)]
    ppermute x9 -> x0, waiting for transfers between devices: 13.1 us -> none  [grp_pool(): lax.ppermute(vector, 'grp', [(i, (i + step) % groups) for i in range(grou...]
    ppermute x7 -> x2, starting transfers between devices: 17.6 us -> 6.25 us  [exchange(): before = lax.ppermute(tail, axis, [(i, i + 1) for i in range(count - 1)])]
    all_to_all x0 -> x1, blocking collectives: none -> 9.96 us  [everyone(): return lax.all_to_all(copies, ALL_AXES, 0, 0, tiled=True).reshape(-1)]
    ppermute x5 -> x1, waiting for transfers between devices: 12.5 us -> 3.38 us  [exchange(): got = lax.ppermute(sent, axis, [(0, 1), (1, 0)])]
    ppermute x9 -> x0, starting transfers between devices: 8.7 us -> none  [grp_pool(): lax.ppermute(vector, 'grp', [(i, (i + step) % groups) for i in range(grou...]
  transfers between devices with their start and end apart: 28 -> 8, of which waited for: 20 -> 6; matrix products, arithmetic and copies ran while one was open for 5% -> 6% of each run, Pallas kernels for 0% -> 0%
where the time goes in v5:
time: 110 us; the launch traced here: 109 us
  waiting for transfers between devices  35.6 us (32%)
  starting transfers between devices  24.3 us (22%)
  local copies, waits for them, and re-layouts  18.3 us (17%)
  other arithmetic  11.6 us (11%)
  blocking collectives  9.96 us (9%)
  matrix products  7.98 us (7%)
    all_to_all x3, waiting for transfers between devices, everyone(): return lax.all_to_all(copies, ALL_AXES, 0, 0, tiled=True).reshape(-1)  21.2 us
    all_to_all x3, starting transfers between devices, everyone(): return lax.all_to_all(copies, ALL_AXES, 0, 0, tiled=True).reshape(-1)  13.9 us
    all_to_all x1, blocking collectives, everyone(): return lax.all_to_all(copies, ALL_AXES, 0, 0, tiled=True).reshape(-1)  9.96 us
    ppermute x2, waiting for transfers between devices, exchange(): before = lax.ppermute(tail, axis, [(i, i + 1) for i in range(count - 1)])  6.93 us
    dot_general x6, matrix products, dot(): return jnp.dot(left, right, precision=lax.Precision.HIGHEST)  6.43 us
    ppermute x2, starting transfers between devices, exchange(): before = lax.ppermute(tail, axis, [(i, i + 1) for i in range(count - 1)])  6.25 us
    gather x3, local copies, waits for them, and re-layouts, local(): blocks = pooled.reshape(-1, 64)[coarse_columns]  4.43 us
    ppermute x2, waiting for transfers between devices, exchange(): after = lax.ppermute(head, axis, [(i + 1, i) for i in range(count - 1)])  4.14 us
  transfers between devices with their start and end apart: 8, of which 6 were waited for; matrix products, arithmetic and copies ran while one was open for 6% of the time, Pallas kernels for 0%

profile of v5, /device:TPU:0, one launch (start us, length us, event | category | flops | bytes accessed | tf_op | source)
XLA Modules:
  0.0 108.9 jit_solution(6168557967872233762)
XLA Ops:
  0.7 1.1 %pad_maximum_fusion.2 = f32[3,16,16,128]{3,2,1,0:T(8,128)S(1)} fusion(f32[1,16,16,128]{3,2,1,0:T(8,128)} %bitcast.76, f32[1,16,16,128]{3,2,1,0:T(8,128)} %bitcast.78, f32[1,16,16,128]{3,2,1,0:T(8,128)} %bitcast.80), kind=kLoop, calls=%fused_computation.106 | loop fusion | flops 196608 | bytes 786432 | tf_op jit(solution)/shard_map/stack | solution.py:120
  1.9 5.0 %collective-permute-start = (f32[3,16,16,4]{3,2,1,0:T(8,128)S(1)}, f32[3,16,16,4]{3,2,1,0:T(8,128)S(1)}, u32[]{:S(2)}, u32[]{:S(2)}) collective-permute-start(f32[3,16,16,4]{3,2,1,0:T(8,128)S(1)} %get-tuple-element.11), channel_id=1, source_target_pairs={{0,8},{8,16},{16,24},{1,9},{9,17},{17,25},{2,10},{10,18},{18,26},{... | collective-permute-start | bytes 36872 | tf_op jit(solution)/shard_map/ppermute | solution.py:32
  6.9 1.3 %collective-permute-start.1 = (f32[3,16,16,4]{3,2,1,0:T(8,128)S(1)}, f32[3,16,16,4]{3,2,1,0:T(8,128)S(1)}, u32[]{:S(2)}, u32[]{:S(2)}) collective-permute-start(f32[3,16,16,4]{3,2,1,0:T(8,128)S(1)} %get-tuple-element.12), channel_id=1, source_target_pairs={{8,0},{16,8},{24,16},{9,1},{17,9},{25,17},{10,2},{18,10},{26,18},{... | collective-permute-start | bytes 36872 | tf_op jit(solution)/shard_map/ppermute | solution.py:33
  8.3 6.9 %collective-permute-done = f32[3,16,16,4]{3,2,1,0:T(8,128)S(1)} collective-permute-done((f32[3,16,16,4]{3,2,1,0:T(8,128)S(1)}, f32[3,16,16,4]{3,2,1,0:T(8,128)S(1)}, u32[]{:S(2)}, u32[]{:S(2)}) %collective-permute-start) | collective-permute-done | bytes 12320 | tf_op jit(solution)/shard_map/ppermute | solution.py:32
  15.2 4.1 %collective-permute-done.1 = f32[3,16,16,4]{3,2,1,0:T(8,128)S(1)} collective-permute-done((f32[3,16,16,4]{3,2,1,0:T(8,128)S(1)}, f32[3,16,16,4]{3,2,1,0:T(8,128)S(1)}, u32[]{:S(2)}, u32[]{:S(2)}) %collective-permute-start.1) | collective-permute-done | bytes 12320 | tf_op jit(solution)/shard_map/ppermute | solution.py:33
  20.3 1.6 %collective-permute-start.2 = (f32[3,16,544]{2,1,0:T(8,128)S(1)}, f32[3,16,544]{2,1,0:T(8,128)S(1)}, u32[]{:S(2)}, u32[]{:S(2)}) collective-permute-start(f32[3,16,544]{2,1,0:T(8,128)S(1)} %slice_select_fusion), channel_id=1, source_target_pairs={{0,1},{1,0},{2,3},{3,2},{4,5},{5,4},{6,7},{7,6},{8,9},{9,8},{10,11... | collective-permute-start | bytes 313352 | tf_op jit(solution)/shard_map/ppermute | solution.py:28
  21.9 3.4 %collective-permute-done.2 = f32[3,16,544]{2,1,0:T(8,128)S(1)} collective-permute-done((f32[3,16,544]{2,1,0:T(8,128)S(1)}, f32[3,16,544]{2,1,0:T(8,128)S(1)}, u32[]{:S(2)}, u32[]{:S(2)}) %collective-permute-start.2) | collective-permute-done | bytes 104480 | tf_op jit(solution)/shard_map/ppermute | solution.py:28
  25.6 1.3 %collective-permute-start.3 = (f32[3,4,3264]{2,1,0:T(4,128)S(1)}, f32[3,4,3264]{2,1,0:T(4,128)S(1)}, u32[]{:S(2)}, u32[]{:S(2)}) collective-permute-start(f32[3,4,3264]{2,1,0:T(4,128)S(1)} %get-tuple-element.9), channel_id=1, source_target_pairs={{0,2},{2,4},{4,6},{1,3},{3,5},{5,7},{8,10},{10,12},{12,14},{9,11},... | collective-permute-start | bytes 470024 | tf_op jit(solution)/shard_map/ppermute | solution.py:32
  26.9 1.3 %collective-permute-start.4 = (f32[3,4,3264]{2,1,0:T(4,128)S(1)}, f32[3,4,3264]{2,1,0:T(4,128)S(1)}, u32[]{:S(2)}, u32[]{:S(2)}) collective-permute-start(f32[3,4,3264]{2,1,0:T(4,128)S(1)} %get-tuple-element.10), channel_id=1, source_target_pairs={{2,0},{4,2},{6,4},{3,1},{5,3},{7,5},{10,8},{12,10},{14,12},{11,9},... | collective-permute-start | bytes 470024 | tf_op jit(solution)/shard_map/ppermute | solution.py:33
  28.2 1.9 %slice.183 = s32[4,4,32]{2,1,0:T(4,128)S(1)} slice(s32[16,16,128]{2,1,0:T(8,128)} %param.9), slice={[0:16:4], [0:16:4], [0:128:4]} | slice | bytes 4096 | tf_op jit(solution)/shard_map/slice | solution.py:151
  30.2 2.0 %copy.17 = f32[8,64,64]{0,2,1:T(8,128)} copy(f32[8,64,64]{2,1,0:T(8,128)S(1)} %slice-done) | data formatting | bytes 262144 | tf_op jit(solution)/shard_map/slice | solution.py:156
  32.2 1.5 %gather_fusion = f32[64,8]{1,0:T(8,128)S(1)} fusion(f32[8,64,64]{0,2,1:T(8,128)} %copy.17, s32[64]{0:T(128)S(1)} %or_bitcast_fusion), kind=kCustom, calls=%fused_computation | custom fusion | bytes 4608 | tf_op jit(solution)/shard_map/jit(diagonal)/gather | solution.py:156
  35.7 2.2 %fusion.12 = f32[24,128]{1,0:T(8,128)S(1)} fusion(s32[128]{0:T(128)S(1)} %get-tuple-element.24, s32[128]{0:T(128)S(1)} %get-tuple-element.25, s32[3264]{0:T(1024)S(1)} %get-tuple-element.16, s32[3264]{0:T(1024)S(1)} %get-tuple-element.17, s32[128]{0:T(128)S(1)} %get-tuple-element.23, s32[128]{0:T(128)S(1)} %get-tuple-element.26, ...), kind=kOutput, calls=%fused_computation.27 | convolution fusion | flops 131056128 | bytes 3283969 | tf_op jit(solution)/shard_map/dot_general | solution.py:95
  39.3 7.9 %all-to-all-start = ((f32[32,1,512]{2,1,0:T(1,128)}), f32[32,1,512]{2,1,0:T(1,128)}, u32[]{:S(2)}, u32[]{:S(2)}) async-start(f32[32,1,512]{2,1,0:T(1,128)} %broadcast_in_dim.49), calls=%async_computation | async-start | bytes 131072 | tf_op jit(solution)/shard_map/all_to_all | solution.py:114
  47.4 7.4 %all-to-all-done = f32[32,1,512]{2,1,0:T(1,128)} async-done(((f32[32,1,512]{2,1,0:T(1,128)}), f32[32,1,512]{2,1,0:T(1,128)}, u32[]{:S(2)}, u32[]{:S(2)}) %all-to-all-start) | async-done | bytes 65568 | tf_op jit(solution)/shard_map/all_to_all | solution.py:114
  54.8 1.0 reduce
  55.8 0.7 reshape_reshape.12
  56.5 1.5 %gather_fusion.1 = f32[32,64]{1,0:T(8,128)S(1)} fusion(f32[256,64]{1,0:T(8,128)} %reshape_reshape.12, s32[1024]{0:T(1024)S(1)} %pad_clamp_fusion), kind=kCustom, calls=%fused_computation.1 | custom fusion | bytes 16512 | tf_op jit(solution)/shard_map/gather | solution.py:164
  60.0 10.0 %all_to_all.24 = f32[32,1,512]{2,1,0:T(1,128)} all-to-all(f32[32,1,512]{2,1,0:T(1,128)S(1)} %broadcast_in_dim.51), channel_id=1, replica_groups=mesh['grp'=4,'gx'=4,'gy'=2] {'grp','gx','gy'}, dimensions={0} | all-to-all | bytes 131072 | tf_op jit(solution)/shard_map/all_to_all | solution.py:114
  69.9 1.0 reduce.1
  70.9 0.7 reshape_reshape.13
  71.7 1.5 %gather_fusion.2 = f32[32,64]{1,0:T(8,128)S(1)} fusion(f32[256,64]{1,0:T(8,128)} %reshape_reshape.13, s32[1024]{0:T(1024)S(1)} %pad_clamp_fusion), kind=kCustom, calls=%fused_computation.2 | custom fusion | bytes 16512 | tf_op jit(solution)/shard_map/gather | solution.py:164
  75.2 3.3 %all-to-all-start.2 = ((f32[32,1,512]{2,1,0:T(1,128)}), f32[32,1,512]{2,1,0:T(1,128)}, u32[]{:S(2)}, u32[]{:S(2)}) async-start(f32[32,1,512]{2,1,0:T(1,128)} %broadcast_in_dim.52), calls=%async_computation.2 | async-start | bytes 131072 | tf_op jit(solution)/shard_map/all_to_all | solution.py:114
  79.7 6.4 %all-to-all-done.2 = f32[32,1,512]{2,1,0:T(1,128)} async-done(((f32[32,1,512]{2,1,0:T(1,128)}), f32[32,1,512]{2,1,0:T(1,128)}, u32[]{:S(2)}, u32[]{:S(2)}) %all-to-all-start.2) | async-done | bytes 65568 | tf_op jit(solution)/shard_map/all_to_all | solution.py:114
  86.1 1.0 reduce.2
  87.1 0.7 reshape_reshape.14
  87.8 1.5 %gather_fusion.3 = f32[32,64]{1,0:T(8,128)S(1)} fusion(f32[256,64]{1,0:T(8,128)} %reshape_reshape.14, s32[1024]{0:T(1024)S(1)} %pad_clamp_fusion), kind=kCustom, calls=%fused_computation.3 | custom fusion | bytes 16512 | tf_op jit(solution)/shard_map/gather | solution.py:164
  90.7 1.3 %fusion.28 = f32[1,512]{1,0:T(1,128)S(1)} fusion(f32[512,1]{0,1:T(1,128)S(1)} %bitcast.90, s32[512]{0:T(512)} %copy-done.9), kind=kOutput, calls=%fused_computation.43 | convolution fusion | flops 3407872 | bytes 6144 | tf_op jit(solution)/shard_map/dot_general | solution.py:95
  92.7 2.8 %all-to-all-start.3 = ((f32[32,1,512]{2,1,0:T(1,128)}), f32[32,1,512]{2,1,0:T(1,128)S(1)}, u32[]{:S(2)}, u32[]{:S(2)}) async-start(f32[32,1,512]{2,1,0:T(1,128)} %broadcast_in_dim.53), calls=%async_computation.3 | async-start | bytes 131072 | tf_op jit(solution)/shard_map/all_to_all | solution.py:114
  95.5 7.4 %all-to-all-done.3 = f32[32,1,512]{2,1,0:T(1,128)S(1)} async-done(((f32[32,1,512]{2,1,0:T(1,128)}), f32[32,1,512]{2,1,0:T(1,128)S(1)}, u32[]{:S(2)}, u32[]{:S(2)}) %all-to-all-start.3) | async-done | bytes 65568 | tf_op jit(solution)/shard_map/all_to_all | solution.py:114
  103.8 1.8 %fusion.4 = f32[6,3264]{1,0:T(8,128)S(1)} fusion(f32[6,204]{1,0:T(8,128)S(1)} %reshape.86, s32[204]{0:T(256)S(1)} %get-tuple-element.30, s32[204]{0:T(256)S(1)} %copy-done.12, s32[3264]{0:T(1024)S(1)} %get-tuple-element.16, s32[3264]{0:T(1024)S(1)} %get-tuple-element.17, s32[204]{0:T(256)S(1)} %get-tuple-element.29, s32[204]{0:T(256)S(1)} %copy-done.13, ...), kind=kOutput, calls=%fused_computation.14 | convolution fusion | flops 58595328 | bytes 145657 | tf_op jit(solution)/shard_map/dot_general | solution.py:95
  108.1 0.8 slice.233
  (99 shorter events, 15.7 us)
Async XLA Ops:
  0.6 18.8 %copy-start.3 = (f32[16,16,128]{2,1,0:T(8,128)S(1)}, f32[16,16,128]{2,1,0:T(8,128)}, u32[]{:S(2)}) copy-start(f32[16,16,128]{2,1,0:T(8,128)} %param.8) | copy-start | bytes 393220
  0.6 18.7 %copy-start.4 = (f32[16,16,128]{2,1,0:T(8,128)S(1)}, f32[16,16,128]{2,1,0:T(8,128)}, u32[]{:S(2)}) copy-start(f32[16,16,128]{2,1,0:T(8,128)} %param.7) | copy-start | bytes 393220
  0.6 18.7 %copy-start.5 = (f32[16,16,128]{2,1,0:T(8,128)S(1)}, f32[16,16,128]{2,1,0:T(8,128)}, u32[]{:S(2)}) copy-start(f32[16,16,128]{2,1,0:T(8,128)} %param.6) | copy-start | bytes 393220
  1.9 13.3 %collective-permute-start = (f32[3,16,16,4]{3,2,1,0:T(8,128)S(1)}, f32[3,16,16,4]{3,2,1,0:T(8,128)S(1)}, u32[]{:S(2)}, u32[]{:S(2)}) collective-permute-start(f32[3,16,16,4]{3,2,1,0:T(8,128)S(1)} %get-tuple-element.11), channel_id=1, source_target_pairs={{0,8},{8,16},{16,24},{1,9},{9,17},{17,25},{2,10},{10,18},{18,26},{... | collective-permute-start | bytes 36872 | tf_op jit(solution)/shard_map/ppermute | solution.py:32
  6.9 12.5 %collective-permute-start.1 = (f32[3,16,16,4]{3,2,1,0:T(8,128)S(1)}, f32[3,16,16,4]{3,2,1,0:T(8,128)S(1)}, u32[]{:S(2)}, u32[]{:S(2)}) collective-permute-start(f32[3,16,16,4]{3,2,1,0:T(8,128)S(1)} %get-tuple-element.12), channel_id=1, source_target_pairs={{8,0},{16,8},{24,16},{9,1},{17,9},{25,17},{10,2},{18,10},{26,18},{... | collective-permute-start | bytes 36872 | tf_op jit(solution)/shard_map/ppermute | solution.py:33
  20.2 10.0 %slice-start = ((f32[8,64,256]{2,1,0:T(8,128)}), f32[8,64,64]{2,1,0:T(8,128)S(1)}, s32[]{:S(2)}) async-start(f32[8,64,256]{2,1,0:T(8,128)} %param.10), calls=%async_computation.4 | async-start | bytes 524288 | tf_op jit(solution)/shard_map/slice | solution.py:156
  20.3 4.9 %collective-permute-start.2 = (f32[3,16,544]{2,1,0:T(8,128)S(1)}, f32[3,16,544]{2,1,0:T(8,128)S(1)}, u32[]{:S(2)}, u32[]{:S(2)}) collective-permute-start(f32[3,16,544]{2,1,0:T(8,128)S(1)} %slice_select_fusion), channel_id=1, source_target_pairs={{0,1},{1,0},{2,3},{3,2},{4,5},{5,4},{6,7},{7,6},{8,9},{9,8},{10,11... | collective-permute-start | bytes 313352 | tf_op jit(solution)/shard_map/ppermute | solution.py:28
  25.6 8.3 %collective-permute-start.3 = (f32[3,4,3264]{2,1,0:T(4,128)S(1)}, f32[3,4,3264]{2,1,0:T(4,128)S(1)}, u32[]{:S(2)}, u32[]{:S(2)}) collective-permute-start(f32[3,4,3264]{2,1,0:T(4,128)S(1)} %get-tuple-element.9), channel_id=1, source_target_pairs={{0,2},{2,4},{4,6},{1,3},{3,5},{5,7},{8,10},{10,12},{12,14},{9,11},... | collective-permute-start | bytes 470024 | tf_op jit(solution)/shard_map/ppermute | solution.py:32
  26.9 7.0 %collective-permute-start.4 = (f32[3,4,3264]{2,1,0:T(4,128)S(1)}, f32[3,4,3264]{2,1,0:T(4,128)S(1)}, u32[]{:S(2)}, u32[]{:S(2)}) collective-permute-start(f32[3,4,3264]{2,1,0:T(4,128)S(1)} %get-tuple-element.10), channel_id=1, source_target_pairs={{2,0},{4,2},{6,4},{3,1},{5,3},{7,5},{10,8},{12,10},{14,12},{11,9},... | collective-permute-start | bytes 470024 | tf_op jit(solution)/shard_map/ppermute | solution.py:33
  30.2 7.9 %copy-start.9 = (s32[512]{0:T(512)}, s32[512]{0:T(512)S(1)}, u32[]{:S(2)}) copy-start(s32[512]{0:T(512)S(1)} %eq.27) | copy-start | bytes 6148
  35.1 2.8 %copy-start.1 = (f32[24,3264]{1,0:T(8,128)}, f32[24,3264]{1,0:T(8,128)S(1)}, u32[]{:S(2)}) copy-start(f32[24,3264]{1,0:T(8,128)S(1)} %fusion.198) | copy-start | bytes 940036
  35.7 11.5 %copy-start.11 = (s32[8,4]{0,1:T(4,128)S(1)}, s32[8,4]{0,1:T(4,128)}, u32[]{:S(2)}) copy-start(s32[8,4]{0,1:T(4,128)} %param.11) | copy-start | bytes 388
  35.7 22.4 %copy-start = (f32[8,64,256]{2,1,0:T(8,128)S(1)}, f32[8,64,256]{2,1,0:T(8,128)}, u32[]{:S(2)}) copy-start(f32[8,64,256]{2,1,0:T(8,128)} %param.10) | copy-start | bytes 1572868
  38.6 8.7 %copy-start.7 = (f32[512]{0:T(512)}, f32[512]{0:T(512)S(1)}, u32[]{:S(2)}) copy-start(f32[512]{0:T(512)S(1)} %div.69) | copy-start | bytes 6148
  39.3 15.5 %all-to-all-start = ((f32[32,1,512]{2,1,0:T(1,128)}), f32[32,1,512]{2,1,0:T(1,128)}, u32[]{:S(2)}, u32[]{:S(2)}) async-start(f32[32,1,512]{2,1,0:T(1,128)} %broadcast_in_dim.49), calls=%async_computation | async-start | bytes 131072 | tf_op jit(solution)/shard_map/all_to_all | solution.py:114
  59.4 0.6 copy-start.8
  74.5 5.1 %copy-start.6 = (f32[512]{0:T(512)}, f32[512]{0:T(512)S(1)}, u32[]{:S(2)}) copy-start(f32[512]{0:T(512)S(1)} %divide_add_fusion.1) | copy-start | bytes 6148
  75.2 10.9 %all-to-all-start.2 = ((f32[32,1,512]{2,1,0:T(1,128)}), f32[32,1,512]{2,1,0:T(1,128)}, u32[]{:S(2)}, u32[]{:S(2)}) async-start(f32[32,1,512]{2,1,0:T(1,128)} %broadcast_in_dim.52), calls=%async_computation.2 | async-start | bytes 131072 | tf_op jit(solution)/shard_map/all_to_all | solution.py:114
  87.8 15.9 %copy-start.12 = (s32[204]{0:T(256)S(1)}, s32[204]{0:T(256)}, u32[]{:S(2)}) copy-start(s32[204]{0:T(256)} %get-tuple-element.33) | copy-start | bytes 2452
  87.8 15.9 %copy-start.13 = (s32[204]{0:T(256)S(1)}, s32[204]{0:T(256)}, u32[]{:S(2)}) copy-start(s32[204]{0:T(256)} %get-tuple-element.34) | copy-start | bytes 2452
  90.7 14.9 %copy-start.10 = (f32[512]{0:T(512)}, f32[512]{0:T(512)S(1)}, u32[]{:S(2)}) copy-start(f32[512]{0:T(512)S(1)} %divide_add_fusion) | copy-start | bytes 6148
  92.7 10.2 %all-to-all-start.3 = ((f32[32,1,512]{2,1,0:T(1,128)}), f32[32,1,512]{2,1,0:T(1,128)S(1)}, u32[]{:S(2)}, u32[]{:S(2)}) async-start(f32[32,1,512]{2,1,0:T(1,128)} %broadcast_in_dim.53), calls=%async_computation.3 | async-start | bytes 131072 | tf_op jit(solution)/shard_map/all_to_all | solution.py:114
  103.7 1.8 %copy-start.14 = (s32[6]{0:T(128)S(1)}, s32[6]{0:T(128)}, u32[]{:S(2)}) copy-start(s32[6]{0:T(128)} %get-tuple-element.35) | copy-start | bytes 76
  103.7 1.8 %copy-start.15 = (s32[6]{0:T(128)S(1)}, s32[6]{0:T(128)}, u32[]{:S(2)}) copy-start(s32[6]{0:T(128)} %get-tuple-element.36) | copy-start | bytes 76
  103.8 2.3 %copy-start.2 = (f32[24,3264]{1,0:T(8,128)S(1)}, f32[24,3264]{1,0:T(8,128)}, u32[]{:S(2)}) copy-start(f32[24,3264]{1,0:T(8,128)} %copy-done.1) | copy-start | bytes 940036

commit v6 on v5

--- a/solution.py
+++ b/solution.py
@@ -111,7 +111,7 @@
 def everyone(vector):
     count = lax.axis_size(ALL_AXES)
     copies = jnp.broadcast_to(vector[None], (count,) + vector.shape)
-    return lax.all_to_all(copies, ALL_AXES, 0, 0, tiled=True).reshape(-1)
+    return lax.all_to_all(copies, ALL_AXES, 0, 0, tiled=True)
 
 
 def local(source, conductance, storage, aggregate_ids, coarse_values, coarse_columns):
@@ -153,22 +153,29 @@
         box_labels[:, None] == lax.broadcasted_iota(jnp.int32, (box_labels.shape[0],) * 2, 1)
     ).astype(source.dtype)
     coarse_rhs = dot(box_totals[None, :], placed)[0]
-    coarse_diag = jnp.diagonal(coarse_values[:, :, :64], axis1=1, axis2=2).reshape(-1)
     block_rows = coarse_values.shape[0]
+    leading = coarse_values[:, :, :64]
+    eye = lax.broadcasted_iota(jnp.int32, (64, 64), 0) == lax.broadcasted_iota(jnp.int32, (64, 64), 1)
+    diag_blocks = jnp.sum(jnp.where(eye[None], leading, 0.0), axis=2)
+    rhs_blocks = coarse_rhs.reshape(block_rows, 64)
     grid_x = lax.axis_size("gx")
     grid_y = lax.axis_size("gy")
     groups = lax.axis_size("grp")
-    coarse_error = coarse_rhs / coarse_diag
+    tables = groups * grid_x * grid_y * block_rows
+    pick = (
+        coarse_columns.reshape(-1, 1) == lax.broadcasted_iota(jnp.int32, (coarse_columns.size, tables), 1)
+    ).astype(source.dtype)
+    error_blocks = rhs_blocks / diag_blocks
     for sweep_number in range(CITER - 1):
-        pooled = everyone(coarse_error)
-        blocks = pooled.reshape(-1, 64)[coarse_columns]
-        blocks = blocks.reshape(block_rows, -1)
+        table = everyone(error_blocks).reshape(tables, 64)
+        blocks = dot(pick, table).reshape(block_rows, -1)
         applied = jnp.einsum(
             "bim,bm->bi", coarse_values, blocks, precision=lax.Precision.HIGHEST
-        ).reshape(-1)
-        coarse_error = coarse_error + (coarse_rhs - applied) / coarse_diag
-
-    small = dot(placed, coarse_error[:, None]).reshape(-1)
+        )
+        error_blocks = error_blocks + (rhs_blocks - applied) / diag_blocks
+    coarse_error = error_blocks.reshape(-1)
+
+    small = dot(placed, coarse_error[:, None]).reshape(bx * by, bz)
     every = everyone(small).reshape(groups, grid_x, grid_y, bx, by, bz)
     boxes = every.transpose(1, 3, 2, 4, 0, 5).reshape(grid_x * bx, grid_y * by, groups * bz)
     boxes = jnp.pad(boxes, 1)

time: 110 us -> 113 us (1.027)
  matrix products: 7.98 us -> 12.3 us
    unnamed x32 -> x35, local copies, waits for them, and re-layouts: 0.61 us -> 9.05 us
    gather x5 -> x0, local copies, waits for them, and re-layouts: 5.98 us -> none  [the longest x3 4.43 us: local(): blocks = pooled.reshape(-1, 64)[coarse_columns]]
    dot_general x6 -> x9, matrix products: 6.43 us -> 10.7 us  [dot(): return jnp.dot(left, right, precision=lax.Precision.HIGHEST)]
    all_to_all x4, other arithmetic: 3.15 us -> 5.56 us  [everyone(): return lax.all_to_all(copies, ALL_AXES, 0, 0, tiled=True)]
    add x3, other arithmetic: 2.1 us -> 0.03 us  [local(): error_blocks = error_blocks + (rhs_blocks - applied) / diag_blocks]
    slice x3 -> x0, local copies, waits for them, and re-layouts: 2.01 us -> none  [local(): coarse_values[:, :, :64]]
    all_to_all x3, waiting for transfers between devices: 21.2 us -> 19.4 us  [everyone(): return lax.all_to_all(copies, ALL_AXES, 0, 0, tiled=True)]
    another operation x4 -> x2, local copies, waits for them, and re-layouts: 2.4 us -> 0.73 us  [the longest x3 2.22 us: local(): blocks = pooled.reshape(-1, 64)[coarse_columns]]
  transfers between devices with their start and end apart: 8 -> 8, of which waited for: 6 -> 7; matrix products, arithmetic and copies ran while one was open for 6% -> 5% of each run, Pallas kernels for 0% -> 0%
where the time goes in v6:
time: 113 us; the launch traced here: 112 us
  waiting for transfers between devices  35.4 us (31%)
  starting transfers between devices  23.7 us (21%)
  local copies, waits for them, and re-layouts  17.8 us (16%)
  matrix products  12.3 us (11%)
  other arithmetic  12 us (11%)
  blocking collectives  9.98 us (9%)
    all_to_all x3, waiting for transfers between devices, everyone(): return lax.all_to_all(copies, ALL_AXES, 0, 0, tiled=True)  19.4 us
    all_to_all x3, starting transfers between devices, everyone(): return lax.all_to_all(copies, ALL_AXES, 0, 0, tiled=True)  13.3 us
    dot_general x9, matrix products, dot(): return jnp.dot(left, right, precision=lax.Precision.HIGHEST)  10.7 us
    all_to_all x1, blocking collectives, everyone(): return lax.all_to_all(copies, ALL_AXES, 0, 0, tiled=True)  9.98 us
    unnamed x35, local copies, waits for them, and re-layouts  9.05 us
    ppermute x2, waiting for transfers between devices, exchange(): before = lax.ppermute(tail, axis, [(i, i + 1) for i in range(count - 1)])  6.89 us
    ppermute x2, starting transfers between devices, exchange(): before = lax.ppermute(tail, axis, [(i, i + 1) for i in range(count - 1)])  6.25 us
    ppermute x2, waiting for transfers between devices, exchange(): after = lax.ppermute(head, axis, [(i + 1, i) for i in range(count - 1)])  5.69 us
  transfers between devices with their start and end apart: 8, of which 7 were waited for; matrix products, arithmetic and copies ran while one was open for 5% of the time, Pallas kernels for 0%

profile of v6, /device:TPU:0, one launch (start us, length us, event | category | flops | bytes accessed | tf_op | source)
XLA Modules:
  0.0 112.2 jit_solution(15612005937969308176)
XLA Ops:
  0.6 1.1 pad_maximum_fusion.2
  1.9 5.0 %collective-permute-start = (f32[3,16,16,4]{3,2,1,0:T(8,128)S(1)}, f32[3,16,16,4]{3,2,1,0:T(8,128)S(1)}, u32[]{:S(2)}, u32[]{:S(2)}) collective-permute-start(f32[3,16,16,4]{3,2,1,0:T(8,128)S(1)} %get-tuple-element.11), channel_id=1, source_target_pairs={{0,8},{8,16},{16,24},{1,9},{9,17},{17,25},{2,10},{10,18},{18,26},{... | collective-permute-start | bytes 36872 | tf_op jit(solution)/shard_map/ppermute | solution.py:32
  6.9 1.3 %collective-permute-start.1 = (f32[3,16,16,4]{3,2,1,0:T(8,128)S(1)}, f32[3,16,16,4]{3,2,1,0:T(8,128)S(1)}, u32[]{:S(2)}, u32[]{:S(2)}) collective-permute-start(f32[3,16,16,4]{3,2,1,0:T(8,128)S(1)} %get-tuple-element.12), channel_id=1, source_target_pairs={{8,0},{16,8},{24,16},{9,1},{17,9},{25,17},{10,2},{18,10},{26,18},{... | collective-permute-start | bytes 36872 | tf_op jit(solution)/shard_map/ppermute | solution.py:33
  8.3 6.9 %collective-permute-done = f32[3,16,16,4]{3,2,1,0:T(8,128)S(1)} collective-permute-done((f32[3,16,16,4]{3,2,1,0:T(8,128)S(1)}, f32[3,16,16,4]{3,2,1,0:T(8,128)S(1)}, u32[]{:S(2)}, u32[]{:S(2)}) %collective-permute-start) | collective-permute-done | bytes 12320 | tf_op jit(solution)/shard_map/ppermute | solution.py:32
  15.2 4.1 %collective-permute-done.1 = f32[3,16,16,4]{3,2,1,0:T(8,128)S(1)} collective-permute-done((f32[3,16,16,4]{3,2,1,0:T(8,128)S(1)}, f32[3,16,16,4]{3,2,1,0:T(8,128)S(1)}, u32[]{:S(2)}, u32[]{:S(2)}) %collective-permute-start.1) | collective-permute-done | bytes 12320 | tf_op jit(solution)/shard_map/ppermute | solution.py:33
  20.2 1.6 %collective-permute-start.2 = (f32[3,16,544]{2,1,0:T(8,128)S(1)}, f32[3,16,544]{2,1,0:T(8,128)S(1)}, u32[]{:S(2)}, u32[]{:S(2)}) collective-permute-start(f32[3,16,544]{2,1,0:T(8,128)S(1)} %slice_select_fusion), channel_id=1, source_target_pairs={{0,1},{1,0},{2,3},{3,2},{4,5},{5,4},{6,7},{7,6},{8,9},{9,8},{10,11... | collective-permute-start | bytes 313352 | tf_op jit(solution)/shard_map/ppermute | solution.py:28
  21.8 3.4 %collective-permute-done.2 = f32[3,16,544]{2,1,0:T(8,128)S(1)} collective-permute-done((f32[3,16,544]{2,1,0:T(8,128)S(1)}, f32[3,16,544]{2,1,0:T(8,128)S(1)}, u32[]{:S(2)}, u32[]{:S(2)}) %collective-permute-start.2) | collective-permute-done | bytes 104480 | tf_op jit(solution)/shard_map/ppermute | solution.py:28
  25.6 1.3 %collective-permute-start.3 = (f32[3,4,3264]{2,1,0:T(4,128)S(1)}, f32[3,4,3264]{2,1,0:T(4,128)S(1)}, u32[]{:S(2)}, u32[]{:S(2)}) collective-permute-start(f32[3,4,3264]{2,1,0:T(4,128)S(1)} %get-tuple-element.9), channel_id=1, source_target_pairs={{0,2},{2,4},{4,6},{1,3},{3,5},{5,7},{8,10},{10,12},{12,14},{9,11},... | collective-permute-start | bytes 470024 | tf_op jit(solution)/shard_map/ppermute | solution.py:32
  26.9 1.3 %collective-permute-start.4 = (f32[3,4,3264]{2,1,0:T(4,128)S(1)}, f32[3,4,3264]{2,1,0:T(4,128)S(1)}, u32[]{:S(2)}, u32[]{:S(2)}) collective-permute-start(f32[3,4,3264]{2,1,0:T(4,128)S(1)} %get-tuple-element.10), channel_id=1, source_target_pairs={{2,0},{4,2},{6,4},{3,1},{5,3},{7,5},{10,8},{12,10},{14,12},{11,9},... | collective-permute-start | bytes 470024 | tf_op jit(solution)/shard_map/ppermute | solution.py:33
  28.2 1.9 %slice.183 = s32[4,4,32]{2,1,0:T(4,128)S(1)} slice(s32[16,16,128]{2,1,0:T(8,128)} %param.9), slice={[0:16:4], [0:16:4], [0:128:4]} | slice | bytes 4096 | tf_op jit(solution)/shard_map/slice | solution.py:151
  30.3 1.6 %collective-permute-done.4 = f32[3,4,3264]{2,1,0:T(4,128)S(1)} collective-permute-done((f32[3,4,3264]{2,1,0:T(4,128)S(1)}, f32[3,4,3264]{2,1,0:T(4,128)S(1)}, u32[]{:S(2)}, u32[]{:S(2)}) %collective-permute-start.4) | collective-permute-done | bytes 156704 | tf_op jit(solution)/shard_map/ppermute | solution.py:33
  33.8 2.2 %fusion.12 = f32[24,128]{1,0:T(8,128)S(1)} fusion(s32[128]{0:T(128)S(1)} %get-tuple-element.24, s32[128]{0:T(128)S(1)} %get-tuple-element.25, s32[3264]{0:T(1024)S(1)} %get-tuple-element.16, s32[3264]{0:T(1024)S(1)} %get-tuple-element.17, s32[128]{0:T(128)S(1)} %get-tuple-element.23, s32[128]{0:T(128)S(1)} %get-tuple-element.26, ...), kind=kOutput, calls=%fused_computation.23 | convolution fusion | flops 131056128 | bytes 3283969 | tf_op jit(solution)/shard_map/dot_general | solution.py:95
  36.2 0.8 fusion.29
  37.7 1.7 %reshape.137 = f32[32,1,512]{2,1,0:T(1,128)} reshape(f32[32,8,64]{2,1,0:T(8,128)} %broadcast_in_dim.54) | data formatting | bytes 131072
  39.4 7.3 %all-to-all-start = ((f32[32,1,512]{2,1,0:T(1,128)}), f32[32,1,512]{2,1,0:T(1,128)S(1)}, u32[]{:S(2)}, u32[]{:S(2)}) async-start(f32[32,1,512]{2,1,0:T(1,128)} %reshape.137), calls=%async_computation | async-start | bytes 131072 | tf_op jit(solution)/shard_map/all_to_all | solution.py:114
  48.0 6.3 %all-to-all-done = f32[32,1,512]{2,1,0:T(1,128)S(1)} async-done(((f32[32,1,512]{2,1,0:T(1,128)}), f32[32,1,512]{2,1,0:T(1,128)S(1)}, u32[]{:S(2)}, u32[]{:S(2)}) %all-to-all-start) | async-done | bytes 65568 | tf_op jit(solution)/shard_map/all_to_all | solution.py:114
  55.4 1.6 %reduce = f32[32,512]{1,0:T(8,128)S(1)} reduce(f32[32,1,512]{2,1,0:T(1,128)} %copy-done.6, f32[]{:T(128)} %broadcast.320), dimensions={1}, to_apply=%all_to_all.12.reduce_sub_computation | reduce | bytes 131076 | tf_op jit(solution)/shard_map/all_to_all | solution.py:114
  57.8 1.1 fusion.208
  60.2 1.0 reshape.139
  61.3 10.0 %all_to_all.20 = f32[32,1,512]{2,1,0:T(1,128)} all-to-all(f32[32,1,512]{2,1,0:T(1,128)S(1)} %reshape.139), channel_id=1, replica_groups=mesh['grp'=4,'gx'=4,'gy'=2] {'grp','gx','gy'}, dimensions={0} | all-to-all | bytes 131072 | tf_op jit(solution)/shard_map/all_to_all | solution.py:114
  71.2 1.6 %reduce.1 = f32[32,512]{1,0:T(8,128)S(1)} reduce(f32[32,1,512]{2,1,0:T(1,128)} %all_to_all.20, f32[]{:T(128)} %broadcast.320), dimensions={1}, to_apply=%all_to_all.13.reduce_sub_computation | reduce | bytes 131076 | tf_op jit(solution)/shard_map/all_to_all | solution.py:114
  73.6 1.1 fusion.206
  76.0 1.7 %reshape.141 = f32[32,1,512]{2,1,0:T(1,128)} reshape(f32[32,8,64]{2,1,0:T(8,128)} %broadcast_in_dim.56) | data formatting | bytes 131072
  77.7 3.3 %all-to-all-start.2 = ((f32[32,1,512]{2,1,0:T(1,128)}), f32[32,1,512]{2,1,0:T(1,128)}, u32[]{:S(2)}, u32[]{:S(2)}) async-start(f32[32,1,512]{2,1,0:T(1,128)} %reshape.141), calls=%async_computation.2 | async-start | bytes 131072 | tf_op jit(solution)/shard_map/all_to_all | solution.py:114
  82.1 6.4 %all-to-all-done.2 = f32[32,1,512]{2,1,0:T(1,128)} async-done(((f32[32,1,512]{2,1,0:T(1,128)}), f32[32,1,512]{2,1,0:T(1,128)}, u32[]{:S(2)}, u32[]{:S(2)}) %all-to-all-start.2) | async-done | bytes 65568 | tf_op jit(solution)/shard_map/all_to_all | solution.py:114
  88.5 1.6 %reduce.2 = f32[32,512]{1,0:T(8,128)S(1)} reduce(f32[32,1,512]{2,1,0:T(1,128)} %all-to-all-done.2, f32[]{:T(128)} %broadcast.320), dimensions={1}, to_apply=%all_to_all.14.reduce_sub_computation | reduce | bytes 131076 | tf_op jit(solution)/shard_map/all_to_all | solution.py:114
  90.9 1.1 fusion.204
  92.7 1.9 %fusion.31 = f32[1,16,32]{2,0,1:T(1,128)S(1)} fusion(f32[512,1,1]{0,1,2:T(1,128)S(1)} %reshape.128, s32[16,32]{1,0:T(8,128)} %bitcast.99), kind=kOutput, calls=%fused_computation.42 | convolution fusion | flops 3407872 | bytes 6144 | tf_op jit(solution)/shard_map/dot_general | solution.py:95
  94.7 0.8 reshape.143
  95.5 2.8 %all-to-all-start.3 = ((f32[32,1,512]{2,1,0:T(1,128)}), f32[32,1,512]{2,1,0:T(1,128)S(1)}, u32[]{:S(2)}, u32[]{:S(2)}) async-start(f32[32,1,512]{2,1,0:T(1,128)} %reshape.143), calls=%async_computation.3 | async-start | bytes 131072 | tf_op jit(solution)/shard_map/all_to_all | solution.py:114
  98.9 6.7 %all-to-all-done.3 = f32[32,1,512]{2,1,0:T(1,128)S(1)} async-done(((f32[32,1,512]{2,1,0:T(1,128)}), f32[32,1,512]{2,1,0:T(1,128)S(1)}, u32[]{:S(2)}, u32[]{:S(2)}) %all-to-all-start.3) | async-done | bytes 65568 | tf_op jit(solution)/shard_map/all_to_all | solution.py:114
  107.1 1.8 %fusion.4 = f32[6,3264]{1,0:T(8,128)S(1)} fusion(f32[6,204]{1,0:T(8,128)S(1)} %reshape.118, s32[204]{0:T(256)S(1)} %copy-done.10, s32[204]{0:T(256)S(1)} %get-tuple-element.33, s32[3264]{0:T(1024)S(1)} %get-tuple-element.16, s32[3264]{0:T(1024)S(1)} %get-tuple-element.17, s32[204]{0:T(256)S(1)} %get-tuple-element.29, s32[204]{0:T(256)S(1)} %get-tuple-element.34, ...), kind=kOutput, calls=%fused_computation.10 | convolution fusion | flops 58595328 | bytes 145657 | tf_op jit(solution)/shard_map/dot_general | solution.py:95
  (91 shorter events, 19.2 us)
Async XLA Ops:
  1.7 17.6 %copy-start.3 = (f32[16,16,128]{2,1,0:T(8,128)S(1)}, f32[16,16,128]{2,1,0:T(8,128)}, u32[]{:S(2)}) copy-start(f32[16,16,128]{2,1,0:T(8,128)} %param.8) | copy-start | bytes 393220
  1.7 17.6 %copy-start.4 = (f32[16,16,128]{2,1,0:T(8,128)S(1)}, f32[16,16,128]{2,1,0:T(8,128)}, u32[]{:S(2)}) copy-start(f32[16,16,128]{2,1,0:T(8,128)} %param.7) | copy-start | bytes 393220
  1.7 17.6 %copy-start.5 = (f32[16,16,128]{2,1,0:T(8,128)S(1)}, f32[16,16,128]{2,1,0:T(8,128)}, u32[]{:S(2)}) copy-start(f32[16,16,128]{2,1,0:T(8,128)} %param.6) | copy-start | bytes 393220
  1.9 13.3 %collective-permute-start = (f32[3,16,16,4]{3,2,1,0:T(8,128)S(1)}, f32[3,16,16,4]{3,2,1,0:T(8,128)S(1)}, u32[]{:S(2)}, u32[]{:S(2)}) collective-permute-start(f32[3,16,16,4]{3,2,1,0:T(8,128)S(1)} %get-tuple-element.11), channel_id=1, source_target_pairs={{0,8},{8,16},{16,24},{1,9},{9,17},{17,25},{2,10},{10,18},{18,26},{... | collective-permute-start | bytes 36872 | tf_op jit(solution)/shard_map/ppermute | solution.py:32
  6.9 12.5 %collective-permute-start.1 = (f32[3,16,16,4]{3,2,1,0:T(8,128)S(1)}, f32[3,16,16,4]{3,2,1,0:T(8,128)S(1)}, u32[]{:S(2)}, u32[]{:S(2)}) collective-permute-start(f32[3,16,16,4]{3,2,1,0:T(8,128)S(1)} %get-tuple-element.12), channel_id=1, source_target_pairs={{8,0},{16,8},{24,16},{9,1},{17,9},{25,17},{10,2},{18,10},{26,18},{... | collective-permute-start | bytes 36872 | tf_op jit(solution)/shard_map/ppermute | solution.py:33
  20.2 4.9 %collective-permute-start.2 = (f32[3,16,544]{2,1,0:T(8,128)S(1)}, f32[3,16,544]{2,1,0:T(8,128)S(1)}, u32[]{:S(2)}, u32[]{:S(2)}) collective-permute-start(f32[3,16,544]{2,1,0:T(8,128)S(1)} %slice_select_fusion), channel_id=1, source_target_pairs={{0,1},{1,0},{2,3},{3,2},{4,5},{5,4},{6,7},{7,6},{8,9},{9,8},{10,11... | collective-permute-start | bytes 313352 | tf_op jit(solution)/shard_map/ppermute | solution.py:28
  25.2 5.0 %copy-start = (f32[8,64,256]{2,1,0:T(8,128)S(1)}, f32[8,64,256]{2,1,0:T(8,128)}, u32[]{:S(2)}) copy-start(f32[8,64,256]{2,1,0:T(8,128)} %param.10) | copy-start | bytes 1572868
  25.6 4.8 %collective-permute-start.3 = (f32[3,4,3264]{2,1,0:T(4,128)S(1)}, f32[3,4,3264]{2,1,0:T(4,128)S(1)}, u32[]{:S(2)}, u32[]{:S(2)}) collective-permute-start(f32[3,4,3264]{2,1,0:T(4,128)S(1)} %get-tuple-element.9), channel_id=1, source_target_pairs={{0,2},{2,4},{4,6},{1,3},{3,5},{5,7},{8,10},{10,12},{12,14},{9,11},... | collective-permute-start | bytes 470024 | tf_op jit(solution)/shard_map/ppermute | solution.py:32
  26.9 5.0 %collective-permute-start.4 = (f32[3,4,3264]{2,1,0:T(4,128)S(1)}, f32[3,4,3264]{2,1,0:T(4,128)S(1)}, u32[]{:S(2)}, u32[]{:S(2)}) collective-permute-start(f32[3,4,3264]{2,1,0:T(4,128)S(1)} %get-tuple-element.10), channel_id=1, source_target_pairs={{2,0},{4,2},{6,4},{3,1},{5,3},{7,5},{10,8},{12,10},{14,12},{11,9},... | collective-permute-start | bytes 470024 | tf_op jit(solution)/shard_map/ppermute | solution.py:33
  28.2 4.9 %copy-start.8 = (pred[24]{0:T(512)(128)(4,1)}, pred[24]{0:T(512)(128)(4,1)S(1)}, u32[]{:S(2)}) copy-start(pred[24]{0:T(512)(128)(4,1)S(1)} %compare_and_fusion.4) | copy-start | bytes 76
  30.1 1.9 %copy-start.7 = (s32[4,4,32]{2,1,0:T(4,128)}, s32[4,4,32]{2,1,0:T(4,128)S(1)}, u32[]{:S(2)}) copy-start(s32[4,4,32]{2,1,0:T(4,128)S(1)} %slice.183) | copy-start | bytes 6148
  33.1 0.7 copy-start.1
  39.4 14.9 %all-to-all-start = ((f32[32,1,512]{2,1,0:T(1,128)}), f32[32,1,512]{2,1,0:T(1,128)S(1)}, u32[]{:S(2)}, u32[]{:S(2)}) async-start(f32[32,1,512]{2,1,0:T(1,128)} %reshape.137), calls=%async_computation | async-start | bytes 131072 | tf_op jit(solution)/shard_map/all_to_all | solution.py:114
  54.3 0.6 copy-start.6
  77.7 10.9 %all-to-all-start.2 = ((f32[32,1,512]{2,1,0:T(1,128)}), f32[32,1,512]{2,1,0:T(1,128)}, u32[]{:S(2)}, u32[]{:S(2)}) async-start(f32[32,1,512]{2,1,0:T(1,128)} %reshape.141), calls=%async_computation.2 | async-start | bytes 131072 | tf_op jit(solution)/shard_map/all_to_all | solution.py:114
  94.6 12.4 %copy-start.10 = (s32[204]{0:T(256)S(1)}, s32[204]{0:T(256)}, u32[]{:S(2)}) copy-start(s32[204]{0:T(256)} %get-tuple-element.30) | copy-start | bytes 2452
  94.6 12.4 %copy-start.11 = (pred[204]{0:T(512)(128)(4,1)S(1)}, pred[204]{0:T(512)(128)(4,1)}, u32[]{:S(2)}) copy-start(pred[204]{0:T(512)(128)(4,1)} %get-tuple-element.31) | copy-start | bytes 616
  94.7 12.4 %copy-start.12 = (pred[204]{0:T(512)(128)(4,1)S(1)}, pred[204]{0:T(512)(128)(4,1)}, u32[]{:S(2)}) copy-start(pred[204]{0:T(512)(128)(4,1)} %get-tuple-element.32) | copy-start | bytes 616
  95.5 10.2 %all-to-all-start.3 = ((f32[32,1,512]{2,1,0:T(1,128)}), f32[32,1,512]{2,1,0:T(1,128)S(1)}, u32[]{:S(2)}, u32[]{:S(2)}) async-start(f32[32,1,512]{2,1,0:T(1,128)} %reshape.143), calls=%async_computation.3 | async-start | bytes 131072 | tf_op jit(solution)/shard_map/all_to_all | solution.py:114
  107.1 2.3 %copy-start.2 = (f32[24,3264]{1,0:T(8,128)S(1)}, f32[24,3264]{1,0:T(8,128)}, u32[]{:S(2)}) copy-start(f32[24,3264]{1,0:T(8,128)} %copy-done.1) | copy-start | bytes 940036
  107.1 2.3 %copy-start.9 = (pred[24]{0:T(512)(128)(4,1)S(1)}, pred[24]{0:T(512)(128)(4,1)}, u32[]{:S(2)}) copy-start(pred[24]{0:T(512)(128)(4,1)} %copy-done.8) | copy-start | bytes 76

commit v7 on v5

--- a/solution.py
+++ b/solution.py
@@ -153,15 +153,20 @@
         box_labels[:, None] == lax.broadcasted_iota(jnp.int32, (box_labels.shape[0],) * 2, 1)
     ).astype(source.dtype)
     coarse_rhs = dot(box_totals[None, :], placed)[0]
-    coarse_diag = jnp.diagonal(coarse_values[:, :, :64], axis1=1, axis2=2).reshape(-1)
+    eye = lax.broadcasted_iota(jnp.int32, (64, 64), 0) == lax.broadcasted_iota(jnp.int32, (64, 64), 1)
+    coarse_diag = jnp.sum(jnp.where(eye[None], coarse_values[:, :, :64], 0.0), axis=2).reshape(-1)
     block_rows = coarse_values.shape[0]
     grid_x = lax.axis_size("gx")
     grid_y = lax.axis_size("gy")
     groups = lax.axis_size("grp")
+    tables = groups * grid_x * grid_y * block_rows
+    pick = (
+        coarse_columns.reshape(-1, 1) == lax.broadcasted_iota(jnp.int32, (coarse_columns.size, tables), 1)
+    ).astype(source.dtype)
     coarse_error = coarse_rhs / coarse_diag
     for sweep_number in range(CITER - 1):
         pooled = everyone(coarse_error)
-        blocks = pooled.reshape(-1, 64)[coarse_columns]
+        blocks = dot(pick, pooled.reshape(tables, 64))
         blocks = blocks.reshape(block_rows, -1)
         applied = jnp.einsum(
             "bim,bm->bi", coarse_values, blocks, precision=lax.Precision.HIGHEST

time: 110 us -> 105 us (0.955)
  local copies, waits for them, and re-layouts: 18.3 us -> 11.1 us
  matrix products: 7.98 us -> 11.3 us
  other arithmetic: 11.6 us -> 10.3 us
    gather x5 -> x0, local copies, waits for them, and re-layouts: 5.98 us -> none  [the longest x3 4.43 us: local(): blocks = pooled.reshape(-1, 64)[coarse_columns]]
    dot_general x6 -> x9, matrix products: 6.43 us -> 9.74 us  [dot(): return jnp.dot(left, right, precision=lax.Precision.HIGHEST)]
    slice x3 -> x0, local copies, waits for them, and re-layouts: 2.01 us -> none  [local(): coarse_values[:, :, :64]]
    ppermute x2, waiting for transfers between devices: 4.14 us -> 5.77 us  [exchange(): after = lax.ppermute(head, axis, [(i + 1, i) for i in range(count - 1)])]
    add x3, other arithmetic: 2.1 us -> 0.72 us  [local(): coarse_error = coarse_error + (coarse_rhs - applied) / coarse_diag]
  transfers between devices with their start and end apart: 8 -> 8, of which waited for: 6 -> 7; matrix products, arithmetic and copies ran while one was open for 6% -> 4% of each run, Pallas kernels for 0% -> 0%
where the time goes in v7:
time: 105 us; the launch traced here: 104 us
  waiting for transfers between devices  36.6 us (35%)
  starting transfers between devices  24 us (23%)
  matrix products  11.3 us (11%)
  local copies, waits for them, and re-layouts  11.1 us (11%)
  other arithmetic  10.3 us (10%)
  blocking collectives  9.96 us (9%)
  between operations  1.07 us (1%)
    all_to_all x3, waiting for transfers between devices, everyone(): return lax.all_to_all(copies, ALL_AXES, 0, 0, tiled=True).reshape(-1)  20.7 us
    all_to_all x3, starting transfers between devices, everyone(): return lax.all_to_all(copies, ALL_AXES, 0, 0, tiled=True).reshape(-1)  13.4 us
    all_to_all x1, blocking collectives, everyone(): return lax.all_to_all(copies, ALL_AXES, 0, 0, tiled=True).reshape(-1)  9.96 us
    dot_general x9, matrix products, dot(): return jnp.dot(left, right, precision=lax.Precision.HIGHEST)  9.74 us
    ppermute x2, waiting for transfers between devices, exchange(): before = lax.ppermute(tail, axis, [(i, i + 1) for i in range(count - 1)])  6.77 us
    ppermute x2, starting transfers between devices, exchange(): before = lax.ppermute(tail, axis, [(i, i + 1) for i in range(count - 1)])  6.38 us
    ppermute x2, waiting for transfers between devices, exchange(): after = lax.ppermute(head, axis, [(i + 1, i) for i in range(count - 1)])  5.77 us
    ppermute x1, waiting for transfers between devices, exchange(): got = lax.ppermute(sent, axis, [(0, 1), (1, 0)])  3.38 us
  transfers between devices with their start and end apart: 8, of which 7 were waited for; matrix products, arithmetic and copies ran while one was open for 4% of the time, Pallas kernels for 0%

profile of v7, /device:TPU:0, one launch (start us, length us, event | category | flops | bytes accessed | tf_op | source)
XLA Modules:
  0.0 104.2 jit_solution(2101918741723864685)
XLA Ops:
  0.6 1.1 %pad_maximum_fusion.2 = f32[3,16,16,128]{3,2,1,0:T(8,128)S(1)} fusion(f32[1,16,16,128]{3,2,1,0:T(8,128)} %bitcast.76, f32[1,16,16,128]{3,2,1,0:T(8,128)} %bitcast.78, f32[1,16,16,128]{3,2,1,0:T(8,128)} %bitcast.80), kind=kLoop, calls=%fused_computation.102 | loop fusion | flops 196608 | bytes 786432 | tf_op jit(solution)/shard_map/stack | solution.py:120
  1.9 5.1 %collective-permute-start = (f32[3,16,16,4]{3,2,1,0:T(8,128)S(1)}, f32[3,16,16,4]{3,2,1,0:T(8,128)S(1)}, u32[]{:S(2)}, u32[]{:S(2)}) collective-permute-start(f32[3,16,16,4]{3,2,1,0:T(8,128)S(1)} %get-tuple-element.11), channel_id=1, source_target_pairs={{0,8},{8,16},{16,24},{1,9},{9,17},{17,25},{2,10},{10,18},{18,26},{... | collective-permute-start | bytes 36872 | tf_op jit(solution)/shard_map/ppermute | solution.py:32
  7.0 1.3 %collective-permute-start.1 = (f32[3,16,16,4]{3,2,1,0:T(8,128)S(1)}, f32[3,16,16,4]{3,2,1,0:T(8,128)S(1)}, u32[]{:S(2)}, u32[]{:S(2)}) collective-permute-start(f32[3,16,16,4]{3,2,1,0:T(8,128)S(1)} %get-tuple-element.12), channel_id=1, source_target_pairs={{8,0},{16,8},{24,16},{9,1},{17,9},{25,17},{10,2},{18,10},{26,18},{... | collective-permute-start | bytes 36872 | tf_op jit(solution)/shard_map/ppermute | solution.py:33
  8.6 6.8 %collective-permute-done = f32[3,16,16,4]{3,2,1,0:T(8,128)S(1)} collective-permute-done((f32[3,16,16,4]{3,2,1,0:T(8,128)S(1)}, f32[3,16,16,4]{3,2,1,0:T(8,128)S(1)}, u32[]{:S(2)}, u32[]{:S(2)}) %collective-permute-start) | collective-permute-done | bytes 12320 | tf_op jit(solution)/shard_map/ppermute | solution.py:32
  15.3 4.1 %collective-permute-done.1 = f32[3,16,16,4]{3,2,1,0:T(8,128)S(1)} collective-permute-done((f32[3,16,16,4]{3,2,1,0:T(8,128)S(1)}, f32[3,16,16,4]{3,2,1,0:T(8,128)S(1)}, u32[]{:S(2)}, u32[]{:S(2)}) %collective-permute-start.1) | collective-permute-done | bytes 12320 | tf_op jit(solution)/shard_map/ppermute | solution.py:33
  20.4 1.6 %collective-permute-start.2 = (f32[3,16,544]{2,1,0:T(8,128)S(1)}, f32[3,16,544]{2,1,0:T(8,128)S(1)}, u32[]{:S(2)}, u32[]{:S(2)}) collective-permute-start(f32[3,16,544]{2,1,0:T(8,128)S(1)} %slice_select_fusion), channel_id=1, source_target_pairs={{0,1},{1,0},{2,3},{3,2},{4,5},{5,4},{6,7},{7,6},{8,9},{9,8},{10,11... | collective-permute-start | bytes 313352 | tf_op jit(solution)/shard_map/ppermute | solution.py:28
  21.9 3.4 %collective-permute-done.2 = f32[3,16,544]{2,1,0:T(8,128)S(1)} collective-permute-done((f32[3,16,544]{2,1,0:T(8,128)S(1)}, f32[3,16,544]{2,1,0:T(8,128)S(1)}, u32[]{:S(2)}, u32[]{:S(2)}) %collective-permute-start.2) | collective-permute-done | bytes 104480 | tf_op jit(solution)/shard_map/ppermute | solution.py:28
  25.7 1.3 %collective-permute-start.3 = (f32[3,4,3264]{2,1,0:T(4,128)S(1)}, f32[3,4,3264]{2,1,0:T(4,128)S(1)}, u32[]{:S(2)}, u32[]{:S(2)}) collective-permute-start(f32[3,4,3264]{2,1,0:T(4,128)S(1)} %get-tuple-element.9), channel_id=1, source_target_pairs={{0,2},{2,4},{4,6},{1,3},{3,5},{5,7},{8,10},{10,12},{12,14},{9,11},... | collective-permute-start | bytes 470024 | tf_op jit(solution)/shard_map/ppermute | solution.py:32
  27.0 1.3 %collective-permute-start.4 = (f32[3,4,3264]{2,1,0:T(4,128)S(1)}, f32[3,4,3264]{2,1,0:T(4,128)S(1)}, u32[]{:S(2)}, u32[]{:S(2)}) collective-permute-start(f32[3,4,3264]{2,1,0:T(4,128)S(1)} %get-tuple-element.10), channel_id=1, source_target_pairs={{2,0},{4,2},{6,4},{3,1},{5,3},{7,5},{10,8},{12,10},{14,12},{11,9},... | collective-permute-start | bytes 470024 | tf_op jit(solution)/shard_map/ppermute | solution.py:33
  28.3 1.9 %slice.183 = s32[4,4,32]{2,1,0:T(4,128)S(1)} slice(s32[16,16,128]{2,1,0:T(8,128)} %param.9), slice={[0:16:4], [0:16:4], [0:128:4]} | slice | bytes 4096 | tf_op jit(solution)/shard_map/slice | solution.py:151
  30.4 1.6 %collective-permute-done.4 = f32[3,4,3264]{2,1,0:T(4,128)S(1)} collective-permute-done((f32[3,4,3264]{2,1,0:T(4,128)S(1)}, f32[3,4,3264]{2,1,0:T(4,128)S(1)}, u32[]{:S(2)}, u32[]{:S(2)}) %collective-permute-start.4) | collective-permute-done | bytes 156704 | tf_op jit(solution)/shard_map/ppermute | solution.py:33
  34.0 2.2 %fusion.12 = f32[24,128]{1,0:T(8,128)S(1)} fusion(s32[128]{0:T(128)S(1)} %get-tuple-element.24, s32[128]{0:T(128)S(1)} %get-tuple-element.25, s32[3264]{0:T(1024)S(1)} %get-tuple-element.16, s32[3264]{0:T(1024)S(1)} %get-tuple-element.17, s32[128]{0:T(128)S(1)} %get-tuple-element.23, s32[128]{0:T(128)S(1)} %get-tuple-element.26, ...), kind=kOutput, calls=%fused_computation.23 | convolution fusion | flops 131056128 | bytes 3283969 | tf_op jit(solution)/shard_map/dot_general | solution.py:95
  37.5 7.4 %all-to-all-start = ((f32[32,1,512]{2,1,0:T(1,128)}), f32[32,1,512]{2,1,0:T(1,128)}, u32[]{:S(2)}, u32[]{:S(2)}) async-start(f32[32,1,512]{2,1,0:T(1,128)} %broadcast_in_dim.55), calls=%async_computation | async-start | bytes 131072 | tf_op jit(solution)/shard_map/all_to_all | solution.py:114
  45.7 6.8 %all-to-all-done = f32[32,1,512]{2,1,0:T(1,128)} async-done(((f32[32,1,512]{2,1,0:T(1,128)}), f32[32,1,512]{2,1,0:T(1,128)}, u32[]{:S(2)}, u32[]{:S(2)}) %all-to-all-start) | async-done | bytes 65568 | tf_op jit(solution)/shard_map/all_to_all | solution.py:114
  52.5 1.0 reduce
  53.5 0.7 reshape_reshape.12
  54.3 1.1 %fusion.202 = f32[32,64]{1,0:T(8,128)S(1)} fusion(f32[256,64]{1,0:T(8,128)} %reshape_reshape.12, s32[32]{0:T(128)} %eq.48), kind=kOutput, calls=%fused_computation.273 | convolution fusion | flops 6299648 | bytes 73856 | tf_op jit(solution)/shard_map/dot_general | solution.py:95
  56.7 10.0 %all_to_all.24 = f32[32,1,512]{2,1,0:T(1,128)} all-to-all(f32[32,1,512]{2,1,0:T(1,128)S(1)} %broadcast_in_dim.56), channel_id=1, replica_groups=mesh['grp'=4,'gx'=4,'gy'=2] {'grp','gx','gy'}, dimensions={0} | all-to-all | bytes 131072 | tf_op jit(solution)/shard_map/all_to_all | solution.py:114
  66.6 1.0 reduce.1
  67.6 0.7 reshape_reshape.13
  68.4 1.1 %fusion.201 = f32[32,64]{1,0:T(8,128)S(1)} fusion(f32[256,64]{1,0:T(8,128)} %reshape_reshape.13, s32[32]{0:T(128)} %eq.48), kind=kOutput, calls=%fused_computation.272 | convolution fusion | flops 6299648 | bytes 73856 | tf_op jit(solution)/shard_map/dot_general | solution.py:95
  70.2 0.7 divide_add_fusion.1
  71.6 3.3 %all-to-all-start.2 = ((f32[32,1,512]{2,1,0:T(1,128)}), f32[32,1,512]{2,1,0:T(1,128)}, u32[]{:S(2)}, u32[]{:S(2)}) async-start(f32[32,1,512]{2,1,0:T(1,128)} %broadcast_in_dim.57), calls=%async_computation.2 | async-start | bytes 131072 | tf_op jit(solution)/shard_map/all_to_all | solution.py:114
  76.0 6.4 %all-to-all-done.2 = f32[32,1,512]{2,1,0:T(1,128)} async-done(((f32[32,1,512]{2,1,0:T(1,128)}), f32[32,1,512]{2,1,0:T(1,128)}, u32[]{:S(2)}, u32[]{:S(2)}) %all-to-all-start.2) | async-done | bytes 65568 | tf_op jit(solution)/shard_map/all_to_all | solution.py:114
  82.4 1.0 reduce.2
  83.4 0.7 reshape_reshape.14
  84.2 1.1 %fusion.200 = f32[32,64]{1,0:T(8,128)S(1)} fusion(f32[256,64]{1,0:T(8,128)} %reshape_reshape.14, s32[32]{0:T(128)} %eq.48), kind=kOutput, calls=%fused_computation.271 | convolution fusion | flops 6299648 | bytes 73856 | tf_op jit(solution)/shard_map/dot_general | solution.py:95
  86.0 1.3 %fusion.28 = f32[1,512]{1,0:T(1,128)S(1)} fusion(f32[512,1]{0,1:T(1,128)S(1)} %bitcast.89, s32[512]{0:T(512)} %copy-done.8), kind=kOutput, calls=%fused_computation.39 | convolution fusion | flops 3407872 | bytes 6144 | tf_op jit(solution)/shard_map/dot_general | solution.py:95
  88.0 2.8 %all-to-all-start.3 = ((f32[32,1,512]{2,1,0:T(1,128)}), f32[32,1,512]{2,1,0:T(1,128)S(1)}, u32[]{:S(2)}, u32[]{:S(2)}) async-start(f32[32,1,512]{2,1,0:T(1,128)} %broadcast_in_dim.58), calls=%async_computation.3 | async-start | bytes 131072 | tf_op jit(solution)/shard_map/all_to_all | solution.py:114
  90.8 7.4 %all-to-all-done.3 = f32[32,1,512]{2,1,0:T(1,128)S(1)} async-done(((f32[32,1,512]{2,1,0:T(1,128)}), f32[32,1,512]{2,1,0:T(1,128)S(1)}, u32[]{:S(2)}, u32[]{:S(2)}) %all-to-all-start.3) | async-done | bytes 65568 | tf_op jit(solution)/shard_map/all_to_all | solution.py:114
  99.1 1.8 %fusion.4 = f32[6,3264]{1,0:T(8,128)S(1)} fusion(f32[6,204]{1,0:T(8,128)S(1)} %reshape.95, s32[204]{0:T(256)S(1)} %copy-done.11, s32[204]{0:T(256)S(1)} %get-tuple-element.33, s32[3264]{0:T(1024)S(1)} %get-tuple-element.16, s32[3264]{0:T(1024)S(1)} %get-tuple-element.17, s32[204]{0:T(256)S(1)} %copy-done.10, s32[204]{0:T(256)S(1)} %get-tuple-element.34, ...), kind=kOutput, calls=%fused_computation.10 | convolution fusion | flops 58595328 | bytes 145657 | tf_op jit(solution)/shard_map/dot_general | solution.py:95
  103.5 0.8 slice.225
  (89 shorter events, 14.5 us)
Async XLA Ops:
  1.7 6.7 %copy-start = (f32[8,64,256]{2,1,0:T(8,128)S(1)}, f32[8,64,256]{2,1,0:T(8,128)}, u32[]{:S(2)}) copy-start(f32[8,64,256]{2,1,0:T(8,128)} %param.10) | copy-start | bytes 1572868
  1.7 17.8 %copy-start.3 = (f32[16,16,128]{2,1,0:T(8,128)S(1)}, f32[16,16,128]{2,1,0:T(8,128)}, u32[]{:S(2)}) copy-start(f32[16,16,128]{2,1,0:T(8,128)} %param.8) | copy-start | bytes 393220
  1.7 17.8 %copy-start.4 = (f32[16,16,128]{2,1,0:T(8,128)S(1)}, f32[16,16,128]{2,1,0:T(8,128)}, u32[]{:S(2)}) copy-start(f32[16,16,128]{2,1,0:T(8,128)} %param.7) | copy-start | bytes 393220
  1.7 17.8 %copy-start.5 = (f32[16,16,128]{2,1,0:T(8,128)S(1)}, f32[16,16,128]{2,1,0:T(8,128)}, u32[]{:S(2)}) copy-start(f32[16,16,128]{2,1,0:T(8,128)} %param.6) | copy-start | bytes 393220
  1.9 13.4 %collective-permute-start = (f32[3,16,16,4]{3,2,1,0:T(8,128)S(1)}, f32[3,16,16,4]{3,2,1,0:T(8,128)S(1)}, u32[]{:S(2)}, u32[]{:S(2)}) collective-permute-start(f32[3,16,16,4]{3,2,1,0:T(8,128)S(1)} %get-tuple-element.11), channel_id=1, source_target_pairs={{0,8},{8,16},{16,24},{1,9},{9,17},{17,25},{2,10},{10,18},{18,26},{... | collective-permute-start | bytes 36872 | tf_op jit(solution)/shard_map/ppermute | solution.py:32
  7.0 12.5 %collective-permute-start.1 = (f32[3,16,16,4]{3,2,1,0:T(8,128)S(1)}, f32[3,16,16,4]{3,2,1,0:T(8,128)S(1)}, u32[]{:S(2)}, u32[]{:S(2)}) collective-permute-start(f32[3,16,16,4]{3,2,1,0:T(8,128)S(1)} %get-tuple-element.12), channel_id=1, source_target_pairs={{8,0},{16,8},{24,16},{9,1},{17,9},{25,17},{10,2},{18,10},{26,18},{... | collective-permute-start | bytes 36872 | tf_op jit(solution)/shard_map/ppermute | solution.py:33
  20.4 4.9 %collective-permute-start.2 = (f32[3,16,544]{2,1,0:T(8,128)S(1)}, f32[3,16,544]{2,1,0:T(8,128)S(1)}, u32[]{:S(2)}, u32[]{:S(2)}) collective-permute-start(f32[3,16,544]{2,1,0:T(8,128)S(1)} %slice_select_fusion), channel_id=1, source_target_pairs={{0,1},{1,0},{2,3},{3,2},{4,5},{5,4},{6,7},{7,6},{8,9},{9,8},{10,11... | collective-permute-start | bytes 313352 | tf_op jit(solution)/shard_map/ppermute | solution.py:28
  25.7 4.7 %collective-permute-start.3 = (f32[3,4,3264]{2,1,0:T(4,128)S(1)}, f32[3,4,3264]{2,1,0:T(4,128)S(1)}, u32[]{:S(2)}, u32[]{:S(2)}) collective-permute-start(f32[3,4,3264]{2,1,0:T(4,128)S(1)} %get-tuple-element.9), channel_id=1, source_target_pairs={{0,2},{2,4},{4,6},{1,3},{3,5},{5,7},{8,10},{10,12},{12,14},{9,11},... | collective-permute-start | bytes 470024 | tf_op jit(solution)/shard_map/ppermute | solution.py:32
  27.0 5.0 %collective-permute-start.4 = (f32[3,4,3264]{2,1,0:T(4,128)S(1)}, f32[3,4,3264]{2,1,0:T(4,128)S(1)}, u32[]{:S(2)}, u32[]{:S(2)}) collective-permute-start(f32[3,4,3264]{2,1,0:T(4,128)S(1)} %get-tuple-element.10), channel_id=1, source_target_pairs={{2,0},{4,2},{6,4},{3,1},{5,3},{7,5},{10,8},{12,10},{14,12},{11,9},... | collective-permute-start | bytes 470024 | tf_op jit(solution)/shard_map/ppermute | solution.py:33
  30.3 6.1 %copy-start.8 = (s32[512]{0:T(512)}, s32[512]{0:T(512)S(1)}, u32[]{:S(2)}) copy-start(s32[512]{0:T(512)S(1)} %eq.44) | copy-start | bytes 6148
  33.2 0.7 copy-start.1
  34.0 11.0 %copy-start.7 = (s32[8,4]{0,1:T(4,128)S(1)}, s32[8,4]{0,1:T(4,128)}, u32[]{:S(2)}) copy-start(s32[8,4]{0,1:T(4,128)} %param.11) | copy-start | bytes 388
  37.5 15.0 %all-to-all-start = ((f32[32,1,512]{2,1,0:T(1,128)}), f32[32,1,512]{2,1,0:T(1,128)}, u32[]{:S(2)}, u32[]{:S(2)}) async-start(f32[32,1,512]{2,1,0:T(1,128)} %broadcast_in_dim.55), calls=%async_computation | async-start | bytes 131072 | tf_op jit(solution)/shard_map/all_to_all | solution.py:114
  56.1 0.6 copy-start.6
  71.6 10.9 %all-to-all-start.2 = ((f32[32,1,512]{2,1,0:T(1,128)}), f32[32,1,512]{2,1,0:T(1,128)}, u32[]{:S(2)}, u32[]{:S(2)}) async-start(f32[32,1,512]{2,1,0:T(1,128)} %broadcast_in_dim.57), calls=%async_computation.2 | async-start | bytes 131072 | tf_op jit(solution)/shard_map/all_to_all | solution.py:114
  86.0 13.1 %copy-start.9 = (f32[512]{0:T(512)}, f32[512]{0:T(512)S(1)}, u32[]{:S(2)}) copy-start(f32[512]{0:T(512)S(1)} %divide_add_fusion) | copy-start | bytes 6148
  86.0 13.1 %copy-start.10 = (s32[204]{0:T(256)S(1)}, s32[204]{0:T(256)}, u32[]{:S(2)}) copy-start(s32[204]{0:T(256)} %get-tuple-element.29) | copy-start | bytes 2452
  86.0 13.1 %copy-start.11 = (s32[204]{0:T(256)S(1)}, s32[204]{0:T(256)}, u32[]{:S(2)}) copy-start(s32[204]{0:T(256)} %get-tuple-element.30) | copy-start | bytes 2452
  86.0 13.1 %copy-start.12 = (pred[204]{0:T(512)(128)(4,1)S(1)}, pred[204]{0:T(512)(128)(4,1)}, u32[]{:S(2)}) copy-start(pred[204]{0:T(512)(128)(4,1)} %get-tuple-element.31) | copy-start | bytes 616
  86.0 13.1 %copy-start.13 = (pred[204]{0:T(512)(128)(4,1)S(1)}, pred[204]{0:T(512)(128)(4,1)}, u32[]{:S(2)}) copy-start(pred[204]{0:T(512)(128)(4,1)} %get-tuple-element.32) | copy-start | bytes 616
  88.0 10.2 %all-to-all-start.3 = ((f32[32,1,512]{2,1,0:T(1,128)}), f32[32,1,512]{2,1,0:T(1,128)S(1)}, u32[]{:S(2)}, u32[]{:S(2)}) async-start(f32[32,1,512]{2,1,0:T(1,128)} %broadcast_in_dim.58), calls=%async_computation.3 | async-start | bytes 131072 | tf_op jit(solution)/shard_map/all_to_all | solution.py:114
  99.1 2.3 %copy-start.2 = (f32[24,3264]{1,0:T(8,128)S(1)}, f32[24,3264]{1,0:T(8,128)}, u32[]{:S(2)}) copy-start(f32[24,3264]{1,0:T(8,128)} %copy-done.1) | copy-start | bytes 940036

commit v8 on v7

--- a/solution.py
+++ b/solution.py
@@ -11,6 +11,22 @@
 WEIGHT = 2.0 / 3.0
 ALL_AXES = ("grp", "gx", "gy")
 PAIRS = ((0, 1), (0, -1), (1, 1), (1, -1), (2, 1), (2, -1))
+
+
+def padded_size(shape):
+    size = -(-shape[-1] // 128) * 128
+    if len(shape) > 1:
+        size *= -(-shape[-2] // 8) * 8
+    for extent in shape[:-2]:
+        size *= extent
+    return size
+
+
+def permute(slab, axis, pairs):
+    count = slab.size
+    if count % 128 == 0 and padded_size(slab.shape) > count + count // 4:
+        return lax.ppermute(slab.reshape(-1, 128), axis, pairs).reshape(slab.shape)
+    return lax.ppermute(slab, axis, pairs)
 
 
 def exchange(cells, sides, width):
@@ -25,12 +41,12 @@
         elif count == 2:
             index = lax.axis_index(axis)
             sent = jnp.where(index == 0, tail, head)
-            got = lax.ppermute(sent, axis, [(0, 1), (1, 0)])
+            got = permute(sent, axis, [(0, 1), (1, 0)])
             before = jnp.where(index == 1, got, 0.0)
             after = jnp.where(index == 0, got, 0.0)
         else:
-            before = lax.ppermute(tail, axis, [(i, i + 1) for i in range(count - 1)])
-            after = lax.ppermute(head, axis, [(i + 1, i) for i in range(count - 1)])
+            before = permute(tail, axis, [(i, i + 1) for i in range(count - 1)])
+            after = permute(head, axis, [(i + 1, i) for i in range(count - 1)])
         cells = jnp.concatenate([before, cells, after], axis=dim)
     return cells
 

time: 105 us -> 99.3 us (0.946)
  waiting for transfers between devices: 36.6 us -> 29.1 us
  local copies, waits for them, and re-layouts: 11.1 us -> 12.9 us
    ppermute x5, waiting for transfers between devices: 15.9 us -> 8.48 us  [the longest x4 5.09 us: permute(): return lax.ppermute(slab.reshape(-1, 128), axis, pairs).reshape(slab.shape)]
    reshape x0 -> x8, local copies, waits for them, and re-layouts: none -> 1.84 us  [permute(): return lax.ppermute(slab.reshape(-1, 128), axis, pairs).reshape(slab.shape)]
  transfers between devices with their start and end apart: 8 -> 8, of which waited for: 7 -> 6; matrix products, arithmetic and copies ran while one was open for 4% -> 5% of each run, Pallas kernels for 0% -> 0%
where the time goes in v8:
time: 99.3 us; the launch traced here: 98.5 us
  waiting for transfers between devices  29.1 us (29%)
  starting transfers between devices  23.8 us (24%)
  local copies, waits for them, and re-layouts  12.9 us (13%)
  matrix products  11.3 us (11%)
  other arithmetic  10.3 us (10%)
  blocking collectives  9.96 us (10%)
  between operations  1.13 us (1%)
    all_to_all x3, waiting for transfers between devices, everyone(): return lax.all_to_all(copies, ALL_AXES, 0, 0, tiled=True).reshape(-1)  20.7 us
    all_to_all x3, starting transfers between devices, everyone(): return lax.all_to_all(copies, ALL_AXES, 0, 0, tiled=True).reshape(-1)  13.5 us
    all_to_all x1, blocking collectives, everyone(): return lax.all_to_all(copies, ALL_AXES, 0, 0, tiled=True).reshape(-1)  9.96 us
    dot_general x9, matrix products, dot(): return jnp.dot(left, right, precision=lax.Precision.HIGHEST)  9.74 us
    ppermute x4, starting transfers between devices, permute(): return lax.ppermute(slab.reshape(-1, 128), axis, pairs).reshape(slab.shape)  8.8 us
    ppermute x4, waiting for transfers between devices, permute(): return lax.ppermute(slab.reshape(-1, 128), axis, pairs).reshape(slab.shape)  5.09 us
    ppermute x1, waiting for transfers between devices, permute(): return lax.ppermute(slab, axis, pairs)  3.38 us
    all_to_all x4, other arithmetic, everyone(): return lax.all_to_all(copies, ALL_AXES, 0, 0, tiled=True).reshape(-1)  3.15 us
  transfers between devices with their start and end apart: 8, of which 6 were waited for; matrix products, arithmetic and copies ran while one was open for 5% of the time, Pallas kernels for 0%

profile of v8, /device:TPU:0, one launch (start us, length us, event | category | flops | bytes accessed | tf_op | source)
XLA Modules:
  0.0 98.5 jit_solution(13067785412748034394)
XLA Ops:
  0.6 1.1 %pad_maximum_fusion.2 = f32[3,16,16,128]{3,2,1,0:T(8,128)S(1)} fusion(f32[1,16,16,128]{3,2,1,0:T(8,128)} %bitcast.80, f32[1,16,16,128]{3,2,1,0:T(8,128)} %bitcast.82, f32[1,16,16,128]{3,2,1,0:T(8,128)} %bitcast.84), kind=kLoop, calls=%fused_computation.102 | loop fusion | flops 196608 | bytes 786432 | tf_op jit(solution)/shard_map/stack | solution.py:136
  2.1 4.9 %collective-permute-start = (f32[24,128]{1,0:T(8,128)S(1)}, f32[24,128]{1,0:T(8,128)S(1)}, u32[]{:S(2)}, u32[]{:S(2)}) collective-permute-start(f32[24,128]{1,0:T(8,128)S(1)} %reshape.109), channel_id=1, source_target_pairs={{0,8},{8,16},{16,24},{1,9},{9,17},{17,25},{2,10},{10,18},{18,26},{... | collective-permute-start | bytes 36872 | tf_op jit(solution)/shard_map/ppermute | solution.py:28
  7.3 1.3 %collective-permute-start.1 = (f32[24,128]{1,0:T(8,128)S(1)}, f32[24,128]{1,0:T(8,128)S(1)}, u32[]{:S(2)}, u32[]{:S(2)}) collective-permute-start(f32[24,128]{1,0:T(8,128)S(1)} %reshape.111), channel_id=1, source_target_pairs={{8,0},{16,8},{24,16},{9,1},{17,9},{25,17},{10,2},{18,10},{26,18},{... | collective-permute-start | bytes 36872 | tf_op jit(solution)/shard_map/ppermute | solution.py:28
  9.3 3.6 %collective-permute-done.1 = f32[24,128]{1,0:T(8,128)S(1)} collective-permute-done((f32[24,128]{1,0:T(8,128)S(1)}, f32[24,128]{1,0:T(8,128)S(1)}, u32[]{:S(2)}, u32[]{:S(2)}) %collective-permute-start.1) | collective-permute-done | bytes 12320 | tf_op jit(solution)/shard_map/ppermute | solution.py:28
  14.2 1.6 %collective-permute-start.2 = (f32[3,16,544]{2,1,0:T(8,128)S(1)}, f32[3,16,544]{2,1,0:T(8,128)S(1)}, u32[]{:S(2)}, u32[]{:S(2)}) collective-permute-start(f32[3,16,544]{2,1,0:T(8,128)S(1)} %slice_select_fusion), channel_id=1, source_target_pairs={{0,1},{1,0},{2,3},{3,2},{4,5},{5,4},{6,7},{7,6},{8,9},{9,8},{10,11... | collective-permute-start | bytes 313352 | tf_op jit(solution)/shard_map/ppermute | solution.py:29
  15.7 3.4 %collective-permute-done.2 = f32[3,16,544]{2,1,0:T(8,128)S(1)} collective-permute-done((f32[3,16,544]{2,1,0:T(8,128)S(1)}, f32[3,16,544]{2,1,0:T(8,128)S(1)}, u32[]{:S(2)}, u32[]{:S(2)}) %collective-permute-start.2) | collective-permute-done | bytes 104480 | tf_op jit(solution)/shard_map/ppermute | solution.py:29
  19.6 1.3 %collective-permute-start.3 = (f32[306,128]{1,0:T(8,128)S(1)}, f32[306,128]{1,0:T(8,128)S(1)}, u32[]{:S(2)}, u32[]{:S(2)}) collective-permute-start(f32[306,128]{1,0:T(8,128)S(1)} %reshape.114), channel_id=1, source_target_pairs={{0,2},{2,4},{4,6},{1,3},{3,5},{5,7},{8,10},{10,12},{12,14},{9,11},... | collective-permute-start | bytes 470024 | tf_op jit(solution)/shard_map/ppermute | solution.py:28
  21.1 1.3 %collective-permute-start.4 = (f32[306,128]{1,0:T(8,128)S(1)}, f32[306,128]{1,0:T(8,128)S(1)}, u32[]{:S(2)}, u32[]{:S(2)}) collective-permute-start(f32[306,128]{1,0:T(8,128)S(1)} %reshape.116), channel_id=1, source_target_pairs={{2,0},{4,2},{6,4},{3,1},{5,3},{7,5},{10,8},{12,10},{14,12},{11,9},... | collective-permute-start | bytes 470024 | tf_op jit(solution)/shard_map/ppermute | solution.py:28
  22.4 1.9 %slice.183 = s32[4,4,32]{2,1,0:T(4,128)S(1)} slice(s32[16,16,128]{2,1,0:T(8,128)} %param.9), slice={[0:16:4], [0:16:4], [0:128:4]} | slice | bytes 4096 | tf_op jit(solution)/shard_map/slice | solution.py:167
  24.7 1.5 %collective-permute-done.4 = f32[306,128]{1,0:T(8,128)S(1)} collective-permute-done((f32[306,128]{1,0:T(8,128)S(1)}, f32[306,128]{1,0:T(8,128)S(1)}, u32[]{:S(2)}, u32[]{:S(2)}) %collective-permute-start.4) | collective-permute-done | bytes 156704 | tf_op jit(solution)/shard_map/ppermute | solution.py:28
  28.2 2.2 %fusion.12 = f32[24,128]{1,0:T(8,128)S(1)} fusion(s32[128]{0:T(128)S(1)} %get-tuple-element.24, s32[128]{0:T(128)S(1)} %get-tuple-element.25, s32[3264]{0:T(1024)S(1)} %get-tuple-element.16, s32[3264]{0:T(1024)S(1)} %get-tuple-element.17, s32[128]{0:T(128)S(1)} %get-tuple-element.23, s32[128]{0:T(128)S(1)} %get-tuple-element.26, ...), kind=kOutput, calls=%fused_computation.23 | convolution fusion | flops 131056128 | bytes 3283969 | tf_op jit(solution)/shard_map/dot_general | solution.py:111
  31.8 7.4 %all-to-all-start = ((f32[32,1,512]{2,1,0:T(1,128)}), f32[32,1,512]{2,1,0:T(1,128)}, u32[]{:S(2)}, u32[]{:S(2)}) async-start(f32[32,1,512]{2,1,0:T(1,128)} %broadcast_in_dim.55), calls=%async_computation | async-start | bytes 131072 | tf_op jit(solution)/shard_map/all_to_all | solution.py:130
  40.0 6.8 %all-to-all-done = f32[32,1,512]{2,1,0:T(1,128)} async-done(((f32[32,1,512]{2,1,0:T(1,128)}), f32[32,1,512]{2,1,0:T(1,128)}, u32[]{:S(2)}, u32[]{:S(2)}) %all-to-all-start) | async-done | bytes 65568 | tf_op jit(solution)/shard_map/all_to_all | solution.py:130
  46.9 1.0 %reduce = f32[32,512]{1,0:T(8,128)S(1)} reduce(f32[32,1,512]{2,1,0:T(1,128)} %all-to-all-done, f32[]{:T(128)} %constant.146), dimensions={1}, to_apply=%all_to_all.16.reduce_sub_computation | reduce | bytes 131076 | tf_op jit(solution)/shard_map/all_to_all | solution.py:130
  47.8 0.7 reshape_reshape.12
  48.6 1.1 %fusion.202 = f32[32,64]{1,0:T(8,128)S(1)} fusion(f32[256,64]{1,0:T(8,128)} %reshape_reshape.12, s32[32]{0:T(128)} %eq.48), kind=kOutput, calls=%fused_computation.273 | convolution fusion | flops 6299648 | bytes 73856 | tf_op jit(solution)/shard_map/dot_general | solution.py:111
  51.0 10.0 %all_to_all.24 = f32[32,1,512]{2,1,0:T(1,128)} all-to-all(f32[32,1,512]{2,1,0:T(1,128)S(1)} %broadcast_in_dim.56), channel_id=1, replica_groups=mesh['grp'=4,'gx'=4,'gy'=2] {'grp','gx','gy'}, dimensions={0} | all-to-all | bytes 131072 | tf_op jit(solution)/shard_map/all_to_all | solution.py:130
  61.0 1.0 %reduce.1 = f32[32,512]{1,0:T(8,128)S(1)} reduce(f32[32,1,512]{2,1,0:T(1,128)} %all_to_all.24, f32[]{:T(128)} %constant.146), dimensions={1}, to_apply=%all_to_all.17.reduce_sub_computation | reduce | bytes 131076 | tf_op jit(solution)/shard_map/all_to_all | solution.py:130
  62.0 0.7 reshape_reshape.13
  62.7 1.1 %fusion.201 = f32[32,64]{1,0:T(8,128)S(1)} fusion(f32[256,64]{1,0:T(8,128)} %reshape_reshape.13, s32[32]{0:T(128)} %eq.48), kind=kOutput, calls=%fused_computation.272 | convolution fusion | flops 6299648 | bytes 73856 | tf_op jit(solution)/shard_map/dot_general | solution.py:111
  64.5 0.7 divide_add_fusion.1
  65.9 3.3 %all-to-all-start.2 = ((f32[32,1,512]{2,1,0:T(1,128)}), f32[32,1,512]{2,1,0:T(1,128)}, u32[]{:S(2)}, u32[]{:S(2)}) async-start(f32[32,1,512]{2,1,0:T(1,128)} %broadcast_in_dim.57), calls=%async_computation.2 | async-start | bytes 131072 | tf_op jit(solution)/shard_map/all_to_all | solution.py:130
  70.3 6.4 %all-to-all-done.2 = f32[32,1,512]{2,1,0:T(1,128)} async-done(((f32[32,1,512]{2,1,0:T(1,128)}), f32[32,1,512]{2,1,0:T(1,128)}, u32[]{:S(2)}, u32[]{:S(2)}) %all-to-all-start.2) | async-done | bytes 65568 | tf_op jit(solution)/shard_map/all_to_all | solution.py:130
  76.7 1.0 %reduce.2 = f32[32,512]{1,0:T(8,128)S(1)} reduce(f32[32,1,512]{2,1,0:T(1,128)} %all-to-all-done.2, f32[]{:T(128)} %constant.146), dimensions={1}, to_apply=%all_to_all.18.reduce_sub_computation | reduce | bytes 131076 | tf_op jit(solution)/shard_map/all_to_all | solution.py:130
  77.7 0.7 reshape_reshape.14
  78.5 1.1 %fusion.200 = f32[32,64]{1,0:T(8,128)S(1)} fusion(f32[256,64]{1,0:T(8,128)} %reshape_reshape.14, s32[32]{0:T(128)} %eq.48), kind=kOutput, calls=%fused_computation.271 | convolution fusion | flops 6299648 | bytes 73856 | tf_op jit(solution)/shard_map/dot_general | solution.py:111
  80.3 1.3 %fusion.28 = f32[1,512]{1,0:T(1,128)S(1)} fusion(f32[512,1]{0,1:T(1,128)S(1)} %bitcast.93, s32[512]{0:T(512)} %copy-done.8), kind=kOutput, calls=%fused_computation.39 | convolution fusion | flops 3407872 | bytes 6144 | tf_op jit(solution)/shard_map/dot_general | solution.py:111
  81.6 0.7 broadcast_in_dim.58
  82.3 2.8 %all-to-all-start.3 = ((f32[32,1,512]{2,1,0:T(1,128)}), f32[32,1,512]{2,1,0:T(1,128)S(1)}, u32[]{:S(2)}, u32[]{:S(2)}) async-start(f32[32,1,512]{2,1,0:T(1,128)} %broadcast_in_dim.58), calls=%async_computation.3 | async-start | bytes 131072 | tf_op jit(solution)/shard_map/all_to_all | solution.py:130
  85.1 7.4 %all-to-all-done.3 = f32[32,1,512]{2,1,0:T(1,128)S(1)} async-done(((f32[32,1,512]{2,1,0:T(1,128)}), f32[32,1,512]{2,1,0:T(1,128)S(1)}, u32[]{:S(2)}, u32[]{:S(2)}) %all-to-all-start.3) | async-done | bytes 65568 | tf_op jit(solution)/shard_map/all_to_all | solution.py:130
  93.4 1.8 %fusion.4 = f32[6,3264]{1,0:T(8,128)S(1)} fusion(f32[6,204]{1,0:T(8,128)S(1)} %reshape.127, s32[204]{0:T(256)S(1)} %copy-done.11, s32[204]{0:T(256)S(1)} %get-tuple-element.33, s32[3264]{0:T(1024)S(1)} %get-tuple-element.16, s32[3264]{0:T(1024)S(1)} %get-tuple-element.17, s32[204]{0:T(256)S(1)} %copy-done.10, s32[204]{0:T(256)S(1)} %get-tuple-element.34, ...), kind=kOutput, calls=%fused_computation.10 | convolution fusion | flops 58595328 | bytes 145657 | tf_op jit(solution)/shard_map/dot_general | solution.py:111
  97.8 0.8 slice.225
  (97 shorter events, 15.6 us)
Async XLA Ops:
  1.7 7.0 %copy-start = (f32[8,64,256]{2,1,0:T(8,128)S(1)}, f32[8,64,256]{2,1,0:T(8,128)}, u32[]{:S(2)}) copy-start(f32[8,64,256]{2,1,0:T(8,128)} %param.10) | copy-start | bytes 1572868
  1.9 11.4 %copy-start.3 = (f32[16,16,128]{2,1,0:T(8,128)S(1)}, f32[16,16,128]{2,1,0:T(8,128)}, u32[]{:S(2)}) copy-start(f32[16,16,128]{2,1,0:T(8,128)} %param.8) | copy-start | bytes 393220
  1.9 11.4 %copy-start.4 = (f32[16,16,128]{2,1,0:T(8,128)S(1)}, f32[16,16,128]{2,1,0:T(8,128)}, u32[]{:S(2)}) copy-start(f32[16,16,128]{2,1,0:T(8,128)} %param.7) | copy-start | bytes 393220
  1.9 11.4 %copy-start.5 = (f32[16,16,128]{2,1,0:T(8,128)S(1)}, f32[16,16,128]{2,1,0:T(8,128)}, u32[]{:S(2)}) copy-start(f32[16,16,128]{2,1,0:T(8,128)} %param.6) | copy-start | bytes 393220
  2.1 6.7 %collective-permute-start = (f32[24,128]{1,0:T(8,128)S(1)}, f32[24,128]{1,0:T(8,128)S(1)}, u32[]{:S(2)}, u32[]{:S(2)}) collective-permute-start(f32[24,128]{1,0:T(8,128)S(1)} %reshape.109), channel_id=1, source_target_pairs={{0,8},{8,16},{16,24},{1,9},{9,17},{17,25},{2,10},{10,18},{18,26},{... | collective-permute-start | bytes 36872 | tf_op jit(solution)/shard_map/ppermute | solution.py:28
  7.3 5.6 %collective-permute-start.1 = (f32[24,128]{1,0:T(8,128)S(1)}, f32[24,128]{1,0:T(8,128)S(1)}, u32[]{:S(2)}, u32[]{:S(2)}) collective-permute-start(f32[24,128]{1,0:T(8,128)S(1)} %reshape.111), channel_id=1, source_target_pairs={{8,0},{16,8},{24,16},{9,1},{17,9},{25,17},{10,2},{18,10},{26,18},{... | collective-permute-start | bytes 36872 | tf_op jit(solution)/shard_map/ppermute | solution.py:28
  14.2 4.9 %collective-permute-start.2 = (f32[3,16,544]{2,1,0:T(8,128)S(1)}, f32[3,16,544]{2,1,0:T(8,128)S(1)}, u32[]{:S(2)}, u32[]{:S(2)}) collective-permute-start(f32[3,16,544]{2,1,0:T(8,128)S(1)} %slice_select_fusion), channel_id=1, source_target_pairs={{0,1},{1,0},{2,3},{3,2},{4,5},{5,4},{6,7},{7,6},{8,9},{9,8},{10,11... | collective-permute-start | bytes 313352 | tf_op jit(solution)/shard_map/ppermute | solution.py:29
  19.6 4.9 %collective-permute-start.3 = (f32[306,128]{1,0:T(8,128)S(1)}, f32[306,128]{1,0:T(8,128)S(1)}, u32[]{:S(2)}, u32[]{:S(2)}) collective-permute-start(f32[306,128]{1,0:T(8,128)S(1)} %reshape.114), channel_id=1, source_target_pairs={{0,2},{2,4},{4,6},{1,3},{3,5},{5,7},{8,10},{10,12},{12,14},{9,11},... | collective-permute-start | bytes 470024 | tf_op jit(solution)/shard_map/ppermute | solution.py:28
  21.1 5.0 %collective-permute-start.4 = (f32[306,128]{1,0:T(8,128)S(1)}, f32[306,128]{1,0:T(8,128)S(1)}, u32[]{:S(2)}, u32[]{:S(2)}) collective-permute-start(f32[306,128]{1,0:T(8,128)S(1)} %reshape.116), channel_id=1, source_target_pairs={{2,0},{4,2},{6,4},{3,1},{5,3},{7,5},{10,8},{12,10},{14,12},{11,9},... | collective-permute-start | bytes 470024 | tf_op jit(solution)/shard_map/ppermute | solution.py:28
  24.4 6.2 %copy-start.8 = (s32[512]{0:T(512)}, s32[512]{0:T(512)S(1)}, u32[]{:S(2)}) copy-start(s32[512]{0:T(512)S(1)} %eq.44) | copy-start | bytes 6148
  27.5 0.7 copy-start.1
  28.2 11.0 %copy-start.7 = (s32[8,4]{0,1:T(4,128)S(1)}, s32[8,4]{0,1:T(4,128)}, u32[]{:S(2)}) copy-start(s32[8,4]{0,1:T(4,128)} %param.11) | copy-start | bytes 388
  31.8 15.0 %all-to-all-start = ((f32[32,1,512]{2,1,0:T(1,128)}), f32[32,1,512]{2,1,0:T(1,128)}, u32[]{:S(2)}, u32[]{:S(2)}) async-start(f32[32,1,512]{2,1,0:T(1,128)} %broadcast_in_dim.55), calls=%async_computation | async-start | bytes 131072 | tf_op jit(solution)/shard_map/all_to_all | solution.py:130
  50.4 0.6 copy-start.6
  65.9 10.9 %all-to-all-start.2 = ((f32[32,1,512]{2,1,0:T(1,128)}), f32[32,1,512]{2,1,0:T(1,128)}, u32[]{:S(2)}, u32[]{:S(2)}) async-start(f32[32,1,512]{2,1,0:T(1,128)} %broadcast_in_dim.57), calls=%async_computation.2 | async-start | bytes 131072 | tf_op jit(solution)/shard_map/all_to_all | solution.py:130
  80.3 13.1 %copy-start.9 = (f32[512]{0:T(512)}, f32[512]{0:T(512)S(1)}, u32[]{:S(2)}) copy-start(f32[512]{0:T(512)S(1)} %divide_add_fusion) | copy-start | bytes 6148
  80.3 13.1 %copy-start.10 = (s32[204]{0:T(256)S(1)}, s32[204]{0:T(256)}, u32[]{:S(2)}) copy-start(s32[204]{0:T(256)} %get-tuple-element.29) | copy-start | bytes 2452
  80.3 13.1 %copy-start.11 = (s32[204]{0:T(256)S(1)}, s32[204]{0:T(256)}, u32[]{:S(2)}) copy-start(s32[204]{0:T(256)} %get-tuple-element.30) | copy-start | bytes 2452
  80.3 13.1 %copy-start.12 = (pred[204]{0:T(512)(128)(4,1)S(1)}, pred[204]{0:T(512)(128)(4,1)}, u32[]{:S(2)}) copy-start(pred[204]{0:T(512)(128)(4,1)} %get-tuple-element.31) | copy-start | bytes 616
  80.3 13.1 %copy-start.13 = (pred[204]{0:T(512)(128)(4,1)S(1)}, pred[204]{0:T(512)(128)(4,1)}, u32[]{:S(2)}) copy-start(pred[204]{0:T(512)(128)(4,1)} %get-tuple-element.32) | copy-start | bytes 616
  82.3 10.2 %all-to-all-start.3 = ((f32[32,1,512]{2,1,0:T(1,128)}), f32[32,1,512]{2,1,0:T(1,128)S(1)}, u32[]{:S(2)}, u32[]{:S(2)}) async-start(f32[32,1,512]{2,1,0:T(1,128)} %broadcast_in_dim.58), calls=%async_computation.3 | async-start | bytes 131072 | tf_op jit(solution)/shard_map/all_to_all | solution.py:130
  93.4 2.3 %copy-start.2 = (f32[24,3264]{1,0:T(8,128)S(1)}, f32[24,3264]{1,0:T(8,128)}, u32[]{:S(2)}) copy-start(f32[24,3264]{1,0:T(8,128)} %copy-done.1) | copy-start | bytes 940036

commit v9 on v8

--- a/solution.py
+++ b/solution.py
@@ -163,11 +163,16 @@
     live = lax.axis_index("grp") >= 0
     pick_x = box_matrix(bx, rows, 1, HALO, live)
     pick_yz = box_matrix(by * bz, span_y * span_z, span_z, HALO, live, bz).T
-    box_totals = dot(pick_x, dot(smoothed, pick_yz)).reshape(-1)
     box_labels = aggregate_ids[::BOX, ::BOX, ::BOX].reshape(-1)
     placed = (
         box_labels[:, None] == lax.broadcasted_iota(jnp.int32, (box_labels.shape[0],) * 2, 1)
     ).astype(source.dtype)
+    spread_x = box_matrix(bx + 2, rows, 1, 0, live).T
+    spread_yz = box_matrix((by + 2) * (bz + 2), span_y * span_z, span_z, 0, live, bz + 2)
+    pick_x, pick_yz, placed, spread_x, spread_yz = lax.optimization_barrier(
+        (pick_x, pick_yz, placed, spread_x, spread_yz)
+    )
+    box_totals = dot(pick_x, dot(smoothed, pick_yz)).reshape(-1)
     coarse_rhs = dot(box_totals[None, :], placed)[0]
     eye = lax.broadcasted_iota(jnp.int32, (64, 64), 0) == lax.broadcasted_iota(jnp.int32, (64, 64), 1)
     coarse_diag = jnp.sum(jnp.where(eye[None], coarse_values[:, :, :64], 0.0), axis=2).reshape(-1)
@@ -179,6 +184,7 @@
     pick = (
         coarse_columns.reshape(-1, 1) == lax.broadcasted_iota(jnp.int32, (coarse_columns.size, tables), 1)
     ).astype(source.dtype)
+    pick = lax.optimization_barrier(pick)
     coarse_error = coarse_rhs / coarse_diag
     for sweep_number in range(CITER - 1):
         pooled = everyone(coarse_error)
@@ -199,8 +205,6 @@
         (bx + 2, by + 2, bz + 2),
     )
     window = window.reshape(bx + 2, (by + 2) * (bz + 2))
-    spread_x = box_matrix(bx + 2, rows, 1, 0, live).T
-    spread_yz = box_matrix((by + 2) * (bz + 2), span_y * span_z, span_z, 0, live, bz + 2)
     lifted = dot(spread_x, dot(window, spread_yz))
     solution = jnp.where(mask, solution + (lifted - WEIGHT * op(lifted) / diagonal), 0.0)
     for sweep_number in range(NU):

time: 99.3 us -> 116 us (1.17)
  other arithmetic: 10.3 us -> 21.3 us
  blocking collectives: 9.96 us -> 20 us
  waiting for transfers between devices: 29.1 us -> 21.6 us
  local copies, waits for them, and re-layouts: 12.9 us -> 15.4 us
  matrix products: 11.3 us -> 13 us
  starting transfers between devices: 23.8 us -> 22.4 us
    all_to_all x1 -> x2, blocking collectives: 9.96 us -> 20 us  [everyone(): return lax.all_to_all(copies, ALL_AXES, 0, 0, tiled=True).reshape(-1)]
    convert_element_type x0 -> x6, other arithmetic: none -> 8.9 us  [the longest x4 7.66 us: box_matrix(): return (hit & live).astype(jnp.float32)]
    all_to_all x3 -> x2, waiting for transfers between devices: 20.7 us -> 15.1 us  [everyone(): return lax.all_to_all(copies, ALL_AXES, 0, 0, tiled=True).reshape(-1)]
    another operation x3, local copies, waits for them, and re-layouts: 2.22 us -> 4.73 us  [local(): blocks = dot(pick, pooled.reshape(tables, 64))]
    ppermute x4, waiting for transfers between devices: 5.09 us -> 3.14 us  [permute(): return lax.ppermute(slab.reshape(-1, 128), axis, pairs).reshape(slab.shape)]
    all_to_all x4, other arithmetic: 3.15 us -> 5 us  [everyone(): return lax.all_to_all(copies, ALL_AXES, 0, 0, tiled=True).reshape(-1)]
    dot_general x9, matrix products: 9.74 us -> 11.5 us  [dot(): return jnp.dot(left, right, precision=lax.Precision.HIGHEST)]
    all_to_all x3 -> x2, starting transfers between devices: 13.5 us -> 12.1 us  [everyone(): return lax.all_to_all(copies, ALL_AXES, 0, 0, tiled=True).reshape(-1)]
  transfers between devices with their start and end apart: 8 -> 7, of which waited for: 6 -> 4; matrix products, arithmetic and copies ran while one was open for 5% -> 11% of each run, Pallas kernels for 0% -> 0%
where the time goes in v9:
time: 116 us; the launch traced here: 115 us
  starting transfers between devices  22.4 us (19%)
  waiting for transfers between devices  21.6 us (19%)
  other arithmetic  21.3 us (18%)
  blocking collectives  20 us (17%)
  local copies, waits for them, and re-layouts  15.4 us (13%)
  matrix products  13 us (11%)
    all_to_all x2, blocking collectives, everyone(): return lax.all_to_all(copies, ALL_AXES, 0, 0, tiled=True).reshape(-1)  20 us
    all_to_all x2, waiting for transfers between devices, everyone(): return lax.all_to_all(copies, ALL_AXES, 0, 0, tiled=True).reshape(-1)  15.1 us
    all_to_all x2, starting transfers between devices, everyone(): return lax.all_to_all(copies, ALL_AXES, 0, 0, tiled=True).reshape(-1)  12.1 us
    dot_general x9, matrix products, dot(): return jnp.dot(left, right, precision=lax.Precision.HIGHEST)  11.5 us
    ppermute x4, starting transfers between devices, permute(): return lax.ppermute(slab.reshape(-1, 128), axis, pairs).reshape(slab.shape)  8.81 us
    convert_element_type x4, other arithmetic, box_matrix(): return (hit & live).astype(jnp.float32)  7.66 us
    all_to_all x4, other arithmetic, everyone(): return lax.all_to_all(copies, ALL_AXES, 0, 0, tiled=True).reshape(-1)  5 us
    another operation x3, local copies, waits for them, and re-layouts, local(): blocks = dot(pick, pooled.reshape(tables, 64))  4.73 us
  transfers between devices with their start and end apart: 7, of which 4 were waited for; matrix products, arithmetic and copies ran while one was open for 11% of the time, Pallas kernels for 0%

profile of v9, /device:TPU:0, one launch (start us, length us, event | category | flops | bytes accessed | tf_op | source)
XLA Modules:
  0.0 114.9 jit_solution(7701914341528479641)
XLA Ops:
  0.6 1.1 pad_maximum_fusion.2
  2.1 4.9 %collective-permute-start = (f32[24,128]{1,0:T(8,128)S(1)}, f32[24,128]{1,0:T(8,128)S(1)}, u32[]{:S(2)}, u32[]{:S(2)}) collective-permute-start(f32[24,128]{1,0:T(8,128)S(1)} %reshape.109), channel_id=1, source_target_pairs={{0,8},{8,16},{16,24},{1,9},{9,17},{17,25},{2,10},{10,18},{18,26},{... | collective-permute-start | bytes 36872 | tf_op jit(solution)/shard_map/ppermute | solution.py:28
  7.2 1.3 %collective-permute-start.1 = (f32[24,128]{1,0:T(8,128)S(1)}, f32[24,128]{1,0:T(8,128)S(1)}, u32[]{:S(2)}, u32[]{:S(2)}) collective-permute-start(f32[24,128]{1,0:T(8,128)S(1)} %reshape.111), channel_id=1, source_target_pairs={{8,0},{16,8},{24,16},{9,1},{17,9},{25,17},{10,2},{18,10},{26,18},{... | collective-permute-start | bytes 36872 | tf_op jit(solution)/shard_map/ppermute | solution.py:28
  8.7 1.9 %slice.183 = s32[4,4,32]{2,1,0:T(4,128)S(1)} slice(s32[16,16,128]{2,1,0:T(8,128)} %param.9), slice={[0:16:4], [0:16:4], [0:128:4]} | slice | bytes 4096 | tf_op jit(solution)/shard_map/slice | solution.py:166
  10.7 1.2 %fusion.12 = f32[512,512]{1,0:T(8,128)} fusion(s32[512]{0:T(512)S(1)} %eq.44), kind=kLoop, calls=%fused_computation.25 | loop fusion | flops 524288 | bytes 1050624 | tf_op jit(solution)/shard_map/convert_element_type | solution.py:169
  11.9 2.5 %fusion.4 = f32[204,3264]{1,0:T(8,128)} fusion(s32[204]{0:T(256)S(1)} %get-tuple-element.42, s32[204]{0:T(256)S(1)} %get-tuple-element.45, s32[3264]{0:T(1024)S(1)} %get-tuple-element.26, s32[3264]{0:T(1024)S(1)} %get-tuple-element.27, s32[204]{0:T(256)S(1)} %get-tuple-element.41, s32[204]{0:T(256)S(1)} %get-tuple-element.46, ...), kind=kLoop, calls=%fused_computation.10 | loop fusion | flops 11319552 | bytes 2725849 | tf_op jit(solution)/shard_map/convert_element_type | solution.py:124
  14.3 5.1 %fusion.11 = f32[3264,128]{1,0:T(8,128)} fusion(s32[128]{0:T(128)S(1)} %get-tuple-element.36, s32[128]{0:T(128)S(1)} %get-tuple-element.37, s32[3264]{0:T(1024)S(1)} %get-tuple-element.26, s32[3264]{0:T(1024)S(1)} %get-tuple-element.27, s32[128]{0:T(128)S(1)} %get-tuple-element.35, s32[128]{0:T(128)S(1)} %get-tuple-element.38, ...), kind=kLoop, calls=%fused_computation.23 | loop fusion | flops 7938048 | bytes 1732225 | tf_op jit(solution)/shard_map/convert_element_type | solution.py:124
  21.3 1.6 %collective-permute-start.2 = (f32[3,16,544]{2,1,0:T(8,128)S(1)}, f32[3,16,544]{2,1,0:T(8,128)S(1)}, u32[]{:S(2)}, u32[]{:S(2)}) collective-permute-start(f32[3,16,544]{2,1,0:T(8,128)S(1)} %slice_select_fusion), channel_id=1, source_target_pairs={{0,1},{1,0},{2,3},{3,2},{4,5},{5,4},{6,7},{7,6},{8,9},{9,8},{10,11... | collective-permute-start | bytes 313352 | tf_op jit(solution)/shard_map/ppermute | solution.py:29
  22.8 3.4 %collective-permute-done.2 = f32[3,16,544]{2,1,0:T(8,128)S(1)} collective-permute-done((f32[3,16,544]{2,1,0:T(8,128)S(1)}, f32[3,16,544]{2,1,0:T(8,128)S(1)}, u32[]{:S(2)}, u32[]{:S(2)}) %collective-permute-start.2) | collective-permute-done | bytes 104480 | tf_op jit(solution)/shard_map/ppermute | solution.py:29
  26.7 1.3 %collective-permute-start.3 = (f32[306,128]{1,0:T(8,128)S(1)}, f32[306,128]{1,0:T(8,128)S(1)}, u32[]{:S(2)}, u32[]{:S(2)}) collective-permute-start(f32[306,128]{1,0:T(8,128)S(1)} %reshape.114), channel_id=1, source_target_pairs={{0,2},{2,4},{4,6},{1,3},{3,5},{5,7},{8,10},{10,12},{12,14},{9,11},... | collective-permute-start | bytes 470024 | tf_op jit(solution)/shard_map/ppermute | solution.py:28
  28.2 1.3 %collective-permute-start.4 = (f32[306,128]{1,0:T(8,128)S(1)}, f32[306,128]{1,0:T(8,128)S(1)}, u32[]{:S(2)}, u32[]{:S(2)}) collective-permute-start(f32[306,128]{1,0:T(8,128)S(1)} %reshape.116), channel_id=1, source_target_pairs={{2,0},{4,2},{6,4},{3,1},{5,3},{7,5},{10,8},{12,10},{14,12},{11,9},... | collective-permute-start | bytes 470024 | tf_op jit(solution)/shard_map/ppermute | solution.py:28
  30.1 3.1 %collective-permute-done.4 = f32[306,128]{1,0:T(8,128)S(1)} collective-permute-done((f32[306,128]{1,0:T(8,128)S(1)}, f32[306,128]{1,0:T(8,128)S(1)}, u32[]{:S(2)}, u32[]{:S(2)}) %collective-permute-start.4) | collective-permute-done | bytes 156704 | tf_op jit(solution)/shard_map/ppermute | solution.py:28
  36.2 1.6 %fusion.76 = f32[24,128]{1,0:T(8,128)S(1)} fusion(f32[3264,128]{1,0:T(8,128)S(1)} %copy-done.1, f32[24,3264]{1,0:T(8,128)S(1)} %get-tuple-element.13, f32[24,3264]{1,0:T(8,128)S(1)} %divide_select_fusion, f32[24,3264]{1,0:T(8,128)S(1)} %get-tuple-element.14, f32[24,3264]{1,0:T(8,128)S(1)} %get-tuple-element.15, f32[24,3264]{1,0:T(8,128)S(1)} %get-tuple-element.16, ...), kind=kOutput, calls=%fused_computation.134 | convolution fusion | flops 123535872 | bytes 4878336 | tf_op jit(solution)/shard_map/dot_general | solution.py:111
  39.3 9.5 %all-to-all-start = ((f32[32,1,512]{2,1,0:T(1,128)}), f32[32,1,512]{2,1,0:T(1,128)}, u32[]{:S(2)}, u32[]{:S(2)}) async-start(f32[32,1,512]{2,1,0:T(1,128)} %broadcast_in_dim.55), calls=%async_computation | async-start | bytes 131072 | tf_op jit(solution)/shard_map/all_to_all | solution.py:130
  48.8 7.5 %all-to-all-done = f32[32,1,512]{2,1,0:T(1,128)} async-done(((f32[32,1,512]{2,1,0:T(1,128)}), f32[32,1,512]{2,1,0:T(1,128)}, u32[]{:S(2)}, u32[]{:S(2)}) %all-to-all-start) | async-done | bytes 65568 | tf_op jit(solution)/shard_map/all_to_all | solution.py:130
  56.4 1.6 %reduce = f32[32,512]{1,0:T(8,128)} reduce(f32[32,1,512]{2,1,0:T(1,128)} %all-to-all-done, f32[]{:T(128)} %constant.146), dimensions={1}, to_apply=%all_to_all.16.reduce_sub_computation | reduce | bytes 131076 | tf_op jit(solution)/shard_map/all_to_all | solution.py:130
  58.0 1.6 %reshape_reshape.12 = f32[256,64]{1,0:T(8,128)} reshape(f32[32,512]{1,0:T(8,128)} %reduce) | data formatting | bytes 131072 | tf_op jit(solution)/shard_map/reshape;reshape | solution.py:191
  59.6 1.1 fusion.198
  62.1 10.0 %all_to_all.24 = f32[32,1,512]{2,1,0:T(1,128)} all-to-all(f32[32,1,512]{2,1,0:T(1,128)S(1)} %broadcast_in_dim.56), channel_id=1, replica_groups=mesh['grp'=4,'gx'=4,'gy'=2] {'grp','gx','gy'}, dimensions={0} | all-to-all | bytes 131072 | tf_op jit(solution)/shard_map/all_to_all | solution.py:130
  72.1 1.6 %reduce.1 = f32[32,512]{1,0:T(8,128)} reduce(f32[32,1,512]{2,1,0:T(1,128)} %all_to_all.24, f32[]{:T(128)} %constant.146), dimensions={1}, to_apply=%all_to_all.17.reduce_sub_computation | reduce | bytes 131076 | tf_op jit(solution)/shard_map/all_to_all | solution.py:130
  73.7 1.6 %reshape_reshape.13 = f32[256,64]{1,0:T(8,128)} reshape(f32[32,512]{1,0:T(8,128)} %reduce.1) | data formatting | bytes 131072 | tf_op jit(solution)/shard_map/reshape;reshape | solution.py:191
  75.3 1.1 fusion.200
  77.8 10.0 %all_to_all.25 = f32[32,1,512]{2,1,0:T(1,128)} all-to-all(f32[32,1,512]{2,1,0:T(1,128)S(1)} %broadcast_in_dim.57), channel_id=1, replica_groups=mesh['grp'=4,'gx'=4,'gy'=2] {'grp','gx','gy'}, dimensions={0} | all-to-all | bytes 131072 | tf_op jit(solution)/shard_map/all_to_all | solution.py:130
  87.8 1.6 %reduce.2 = f32[32,512]{1,0:T(8,128)} reduce(f32[32,1,512]{2,1,0:T(1,128)} %all_to_all.25, f32[]{:T(128)} %constant.146), dimensions={1}, to_apply=%all_to_all.18.reduce_sub_computation | reduce | bytes 131076 | tf_op jit(solution)/shard_map/all_to_all | solution.py:130
  89.4 1.6 %reshape_reshape.14 = f32[256,64]{1,0:T(8,128)} reshape(f32[32,512]{1,0:T(8,128)} %reduce.2) | data formatting | bytes 131072 | tf_op jit(solution)/shard_map/reshape;reshape | solution.py:191
  91.0 1.1 fusion.202
  92.8 2.2 %fusion.204 = f32[1,512]{1,0:T(1,128)S(1)} fusion(f32[512,512]{1,0:T(8,128)} %fusion.12, f32[512,1]{0,1:T(1,128)S(1)} %bitcast.102), kind=kOutput, calls=%fused_computation.295 | convolution fusion | flops 3145728 | bytes 1052672 | tf_op jit(solution)/shard_map/dot_general | solution.py:111
  95.7 2.6 %all-to-all-start.3 = ((f32[32,1,512]{2,1,0:T(1,128)}), f32[32,1,512]{2,1,0:T(1,128)S(1)}, u32[]{:S(2)}, u32[]{:S(2)}) async-start(f32[32,1,512]{2,1,0:T(1,128)} %broadcast_in_dim.58), calls=%async_computation.3 | async-start | bytes 131072 | tf_op jit(solution)/shard_map/all_to_all | solution.py:130
  98.2 7.6 %all-to-all-done.3 = f32[32,1,512]{2,1,0:T(1,128)S(1)} async-done(((f32[32,1,512]{2,1,0:T(1,128)}), f32[32,1,512]{2,1,0:T(1,128)S(1)}, u32[]{:S(2)}, u32[]{:S(2)}) %all-to-all-start.3) | async-done | bytes 65568 | tf_op jit(solution)/shard_map/all_to_all | solution.py:130
  106.7 3.2 %fusion.205 = f32[6,3264]{1,0:T(8,128)S(1)} fusion(f32[6,204]{1,0:T(8,128)S(1)} %reshape.127, f32[204,3264]{1,0:T(8,128)} %fusion.4), kind=kOutput, calls=%fused_computation.296 | convolution fusion | flops 47941632 | bytes 2746656 | tf_op jit(solution)/shard_map/dot_general | solution.py:111
  111.5 1.3 %fusion.168 = f32[24,3264]{1,0:T(8,128)} fusion(f32[24,3264]{1,0:T(8,128)S(1)} %fusion.169, f32[24,3264]{1,0:T(8,128)S(1)} %get-tuple-element.18, f32[24,3264]{1,0:T(8,128)S(1)} %get-tuple-element.17, f32[24,3264]{1,0:T(8,128)S(1)} %get-tuple-element.16, f32[24,3264]{1,0:T(8,128)S(1)} %get-tuple-element.15, f32[24,3264]{1,0:T(8,128)S(1)} %get-tuple-element.14, ...), kind=kLoop, calls=%fused_computation.230 | loop fusion | flops 3290112 | bytes 3192224 | tf_op jit(solution)/shard_map/jit(_where)/select_n | solution.py:211
  112.8 1.4 %reshape.128 = f32[24,24,136]{2,1,0:T(8,128)S(1)} reshape(f32[24,3264]{1,0:T(8,128)} %fusion.168) | data formatting | bytes 626688 | tf_op jit(solution)/shard_map/reshape | solution.py:95
  (98 shorter events, 15.5 us)
Async XLA Ops:
  2.1 17.4 %collective-permute-start = (f32[24,128]{1,0:T(8,128)S(1)}, f32[24,128]{1,0:T(8,128)S(1)}, u32[]{:S(2)}, u32[]{:S(2)}) collective-permute-start(f32[24,128]{1,0:T(8,128)S(1)} %reshape.109), channel_id=1, source_target_pairs={{0,8},{8,16},{16,24},{1,9},{9,17},{17,25},{2,10},{10,18},{18,26},{... | collective-permute-start | bytes 36872 | tf_op jit(solution)/shard_map/ppermute | solution.py:28
  7.2 12.7 %collective-permute-start.1 = (f32[24,128]{1,0:T(8,128)S(1)}, f32[24,128]{1,0:T(8,128)S(1)}, u32[]{:S(2)}, u32[]{:S(2)}) collective-permute-start(f32[24,128]{1,0:T(8,128)S(1)} %reshape.111), channel_id=1, source_target_pairs={{8,0},{16,8},{24,16},{9,1},{17,9},{25,17},{10,2},{18,10},{26,18},{... | collective-permute-start | bytes 36872 | tf_op jit(solution)/shard_map/ppermute | solution.py:28
  14.3 6.0 %copy-start.5 = (f32[16,16,128]{2,1,0:T(8,128)S(1)}, f32[16,16,128]{2,1,0:T(8,128)}, u32[]{:S(2)}) copy-start(f32[16,16,128]{2,1,0:T(8,128)} %param.8) | copy-start | bytes 393220
  14.3 6.0 %copy-start.6 = (f32[16,16,128]{2,1,0:T(8,128)S(1)}, f32[16,16,128]{2,1,0:T(8,128)}, u32[]{:S(2)}) copy-start(f32[16,16,128]{2,1,0:T(8,128)} %param.7) | copy-start | bytes 393220
  14.3 6.0 %copy-start.7 = (f32[16,16,128]{2,1,0:T(8,128)S(1)}, f32[16,16,128]{2,1,0:T(8,128)}, u32[]{:S(2)}) copy-start(f32[16,16,128]{2,1,0:T(8,128)} %param.6) | copy-start | bytes 393220
  21.1 8.4 %copy-start.2 = (f32[8,64,256]{2,1,0:T(8,128)S(1)}, f32[8,64,256]{2,1,0:T(8,128)}, u32[]{:S(2)}) copy-start(f32[8,64,256]{2,1,0:T(8,128)} %param.10) | copy-start | bytes 1572868
  21.3 8.5 %copy-start.11 = (s32[8,4]{0,1:T(4,128)S(1)}, s32[8,4]{0,1:T(4,128)}, u32[]{:S(2)}) copy-start(s32[8,4]{0,1:T(4,128)} %param.11) | copy-start | bytes 388
  21.3 4.9 %collective-permute-start.2 = (f32[3,16,544]{2,1,0:T(8,128)S(1)}, f32[3,16,544]{2,1,0:T(8,128)S(1)}, u32[]{:S(2)}, u32[]{:S(2)}) collective-permute-start(f32[3,16,544]{2,1,0:T(8,128)S(1)} %slice_select_fusion), channel_id=1, source_target_pairs={{0,1},{1,0},{2,3},{3,2},{4,5},{5,4},{6,7},{7,6},{8,9},{9,8},{10,11... | collective-permute-start | bytes 313352 | tf_op jit(solution)/shard_map/ppermute | solution.py:29
  26.7 3.2 %collective-permute-start.3 = (f32[306,128]{1,0:T(8,128)S(1)}, f32[306,128]{1,0:T(8,128)S(1)}, u32[]{:S(2)}, u32[]{:S(2)}) collective-permute-start(f32[306,128]{1,0:T(8,128)S(1)} %reshape.114), channel_id=1, source_target_pairs={{0,2},{2,4},{4,6},{1,3},{3,5},{5,7},{8,10},{10,12},{12,14},{9,11},... | collective-permute-start | bytes 470024 | tf_op jit(solution)/shard_map/ppermute | solution.py:28
  28.2 5.0 %collective-permute-start.4 = (f32[306,128]{1,0:T(8,128)S(1)}, f32[306,128]{1,0:T(8,128)S(1)}, u32[]{:S(2)}, u32[]{:S(2)}) collective-permute-start(f32[306,128]{1,0:T(8,128)S(1)} %reshape.116), channel_id=1, source_target_pairs={{2,0},{4,2},{6,4},{3,1},{5,3},{7,5},{10,8},{12,10},{14,12},{11,9},... | collective-permute-start | bytes 470024 | tf_op jit(solution)/shard_map/ppermute | solution.py:28
  34.6 3.2 %copy-start.3 = (f32[24,3264]{1,0:T(8,128)}, f32[24,3264]{1,0:T(8,128)S(1)}, u32[]{:S(2)}) copy-start(f32[24,3264]{1,0:T(8,128)S(1)} %fusion.171) | copy-start | bytes 940036
  34.6 1.6 %copy-start.1 = (f32[3264,128]{1,0:T(8,128)S(1)}, f32[3264,128]{1,0:T(8,128)}, u32[]{:S(2)}) copy-start(f32[3264,128]{1,0:T(8,128)} %fusion.11) | copy-start | bytes 5013508
  36.2 1.8 %copy-start = (f32[512,512]{1,0:T(8,128)S(1)}, f32[512,512]{1,0:T(8,128)}, u32[]{:S(2)}) copy-start(f32[512,512]{1,0:T(8,128)} %fusion.12) | copy-start | bytes 3145732
  38.6 21.0 %copy-start.8 = (f32[512]{0:T(512)}, f32[512]{0:T(512)S(1)}, u32[]{:S(2)}) copy-start(f32[512]{0:T(512)S(1)} %div.70) | copy-start | bytes 6148
  39.3 17.1 %all-to-all-start = ((f32[32,1,512]{2,1,0:T(1,128)}), f32[32,1,512]{2,1,0:T(1,128)}, u32[]{:S(2)}, u32[]{:S(2)}) async-start(f32[32,1,512]{2,1,0:T(1,128)} %broadcast_in_dim.55), calls=%async_computation | async-start | bytes 131072 | tf_op jit(solution)/shard_map/all_to_all | solution.py:130
  62.0 13.2 %copy-start.9 = (f32[512]{0:T(512)}, f32[512]{0:T(512)S(1)}, u32[]{:S(2)}) copy-start(f32[512]{0:T(512)S(1)} %divide_add_fusion.2) | copy-start | bytes 6148
  92.8 17.2 %copy-start.10 = (f32[512]{0:T(512)}, f32[512]{0:T(512)S(1)}, u32[]{:S(2)}) copy-start(f32[512]{0:T(512)S(1)} %divide_add_fusion) | copy-start | bytes 6148
  95.7 10.2 %all-to-all-start.3 = ((f32[32,1,512]{2,1,0:T(1,128)}), f32[32,1,512]{2,1,0:T(1,128)S(1)}, u32[]{:S(2)}, u32[]{:S(2)}) async-start(f32[32,1,512]{2,1,0:T(1,128)} %broadcast_in_dim.58), calls=%async_computation.3 | async-start | bytes 131072 | tf_op jit(solution)/shard_map/all_to_all | solution.py:130
  106.6 3.7 %copy-start.4 = (f32[24,3264]{1,0:T(8,128)S(1)}, f32[24,3264]{1,0:T(8,128)}, u32[]{:S(2)}) copy-start(f32[24,3264]{1,0:T(8,128)} %copy-done.3) | copy-start | bytes 940036

commit v10 on v8

--- a/solution.py
+++ b/solution.py
@@ -44,6 +44,15 @@
             got = permute(sent, axis, [(0, 1), (1, 0)])
             before = jnp.where(index == 1, got, 0.0)
             after = jnp.where(index == 0, got, 0.0)
+        elif count % 2 == 0:
+            index = lax.axis_index(axis)
+            even = index % 2 == 0
+            first = [(i + d, i + 1 - d) for i in range(0, count, 2) for d in (0, 1)]
+            second = [(i + d, i + 1 - d) for i in range(1, count - 1, 2) for d in (0, 1)]
+            got_first = permute(jnp.where(even, tail, head), axis, first)
+            got_second = permute(jnp.where(even, head, tail), axis, second)
+            before = jnp.where(even, got_second, got_first)
+            after = jnp.where(even, got_first, got_second)
         else:
             before = permute(tail, axis, [(i, i + 1) for i in range(count - 1)])
             after = permute(head, axis, [(i + 1, i) for i in range(count - 1)])

time: 99.3 us -> 94.7 us (0.954)
  waiting for transfers between devices: 29.1 us -> 25.4 us
    ppermute x4, waiting for transfers between devices: 5.09 us -> 1.41 us  [permute(): return lax.ppermute(slab.reshape(-1, 128), axis, pairs).reshape(slab.shape)]
    all_to_all x3, starting transfers between devices: 13.5 us -> 11.2 us  [everyone(): return lax.all_to_all(copies, ALL_AXES, 0, 0, tiled=True).reshape(-1)]
    ppermute x4, starting transfers between devices: 8.8 us -> 10.2 us  [permute(): return lax.ppermute(slab.reshape(-1, 128), axis, pairs).reshape(slab.shape)]
    select_n x0 -> x4, local copies, waits for them, and re-layouts: none -> 1.1 us  [the longest x2 0.55 us: exchange(): after = jnp.where(even, got_first, got_second)]
    reshape x8 -> x4, local copies, waits for them, and re-layouts: 1.84 us -> 0.74 us  [permute(): return lax.ppermute(slab.reshape(-1, 128), axis, pairs).reshape(slab.shape)]
  transfers between devices with their start and end apart: 8 -> 8, of which waited for: 6 -> 5; matrix products, arithmetic and copies ran while one was open for 5% -> 5% of each run, Pallas kernels for 0% -> 0%
where the time goes in v10:
time: 94.7 us; the launch traced here: 94 us
  waiting for transfers between devices  25.4 us (27%)
  starting transfers between devices  22.9 us (24%)
  local copies, waits for them, and re-layouts  12.7 us (13%)
  matrix products  11.3 us (12%)
  other arithmetic  10.5 us (11%)
  blocking collectives  9.97 us (11%)
  between operations  1.13 us (1%)
    all_to_all x3, waiting for transfers between devices, everyone(): return lax.all_to_all(copies, ALL_AXES, 0, 0, tiled=True).reshape(-1)  20.6 us
    all_to_all x3, starting transfers between devices, everyone(): return lax.all_to_all(copies, ALL_AXES, 0, 0, tiled=True).reshape(-1)  11.2 us
    ppermute x4, starting transfers between devices, permute(): return lax.ppermute(slab.reshape(-1, 128), axis, pairs).reshape(slab.shape)  10.2 us
    all_to_all x1, blocking collectives, everyone(): return lax.all_to_all(copies, ALL_AXES, 0, 0, tiled=True).reshape(-1)  9.97 us
    dot_general x9, matrix products, dot(): return jnp.dot(left, right, precision=lax.Precision.HIGHEST)  9.75 us
    ppermute x1, waiting for transfers between devices, permute(): return lax.ppermute(slab, axis, pairs)  3.38 us
    all_to_all x4, other arithmetic, everyone(): return lax.all_to_all(copies, ALL_AXES, 0, 0, tiled=True).reshape(-1)  3.15 us
    another operation x3, local copies, waits for them, and re-layouts, local(): blocks = dot(pick, pooled.reshape(tables, 64))  2.22 us
  transfers between devices with their start and end apart: 8, of which 5 were waited for; matrix products, arithmetic and copies ran while one was open for 5% of the time, Pallas kernels for 0%

profile of v10, /device:TPU:0, one launch (start us, length us, event | category | flops | bytes accessed | tf_op | source)
XLA Modules:
  0.0 94.0 jit_solution(2148526724586419565)
XLA Ops:
  0.6 1.1 %pad_maximum_fusion.2 = f32[3,16,16,128]{3,2,1,0:T(8,128)S(1)} fusion(f32[1,16,16,128]{3,2,1,0:T(8,128)} %bitcast.80, f32[1,16,16,128]{3,2,1,0:T(8,128)} %bitcast.82, f32[1,16,16,128]{3,2,1,0:T(8,128)} %bitcast.84), kind=kLoop, calls=%fused_computation.102 | loop fusion | flops 196608 | bytes 786432 | tf_op jit(solution)/shard_map/stack | solution.py:145
  3.0 5.9 %collective-permute-start.1 = (f32[24,128]{1,0:T(8,128)S(1)}, f32[24,128]{1,0:T(8,128)S(1)}, u32[]{:S(2)}, u32[]{:S(2)}) collective-permute-start(f32[24,128]{1,0:T(8,128)S(1)} %reshape.110), channel_id=1, source_target_pairs={{0,8},{8,0},{16,24},{24,16},{1,9},{9,1},{17,25},{25,17},{2,10},{10... | collective-permute-start | bytes 36872 | tf_op jit(solution)/shard_map/ppermute | solution.py:28
  9.2 1.4 %collective-permute-done.1 = f32[24,128]{1,0:T(8,128)S(1)} collective-permute-done((f32[24,128]{1,0:T(8,128)S(1)}, f32[24,128]{1,0:T(8,128)S(1)}, u32[]{:S(2)}, u32[]{:S(2)}) %collective-permute-start.1) | collective-permute-done | bytes 12320 | tf_op jit(solution)/shard_map/ppermute | solution.py:28
  12.3 1.6 %collective-permute-start.2 = (f32[3,16,544]{2,1,0:T(8,128)S(1)}, f32[3,16,544]{2,1,0:T(8,128)S(1)}, u32[]{:S(2)}, u32[]{:S(2)}) collective-permute-start(f32[3,16,544]{2,1,0:T(8,128)S(1)} %slice_select_fusion.4), channel_id=1, source_target_pairs={{0,1},{1,0},{2,3},{3,2},{4,5},{5,4},{6,7},{7,6},{8,9},{9,8},{10,11... | collective-permute-start | bytes 313352 | tf_op jit(solution)/shard_map/ppermute | solution.py:29
  13.9 3.4 %collective-permute-done.2 = f32[3,16,544]{2,1,0:T(8,128)S(1)} collective-permute-done((f32[3,16,544]{2,1,0:T(8,128)S(1)}, f32[3,16,544]{2,1,0:T(8,128)S(1)}, u32[]{:S(2)}, u32[]{:S(2)}) %collective-permute-start.2) | collective-permute-done | bytes 104480 | tf_op jit(solution)/shard_map/ppermute | solution.py:29
  17.8 0.7 collective-permute-start.3
  18.6 2.9 %collective-permute-start.4 = (f32[306,128]{1,0:T(8,128)S(1)}, f32[306,128]{1,0:T(8,128)S(1)}, u32[]{:S(2)}, u32[]{:S(2)}) collective-permute-start(f32[306,128]{1,0:T(8,128)S(1)} %reshape.113), channel_id=1, source_target_pairs={{0,2},{2,0},{4,6},{6,4},{1,3},{3,1},{5,7},{7,5},{8,10},{10,8},{12,... | collective-permute-start | bytes 470024 | tf_op jit(solution)/shard_map/ppermute | solution.py:28
  21.6 1.9 %slice.183 = s32[4,4,32]{2,1,0:T(4,128)S(1)} slice(s32[16,16,128]{2,1,0:T(8,128)} %param.9), slice={[0:16:4], [0:16:4], [0:128:4]} | slice | bytes 4096 | tf_op jit(solution)/shard_map/slice | solution.py:176
  26.0 2.2 %fusion.12 = f32[24,128]{1,0:T(8,128)S(1)} fusion(s32[128]{0:T(128)S(1)} %get-tuple-element.28, s32[128]{0:T(128)S(1)} %get-tuple-element.29, s32[3264]{0:T(1024)S(1)} %get-tuple-element.20, s32[3264]{0:T(1024)S(1)} %get-tuple-element.21, s32[128]{0:T(128)S(1)} %get-tuple-element.27, s32[128]{0:T(128)S(1)} %get-tuple-element.30, ...), kind=kOutput, calls=%fused_computation.23 | convolution fusion | flops 131056128 | bytes 3283969 | tf_op jit(solution)/shard_map/dot_general | solution.py:120
  28.9 0.7 broadcast_in_dim.55
  29.5 5.1 %all-to-all-start = ((f32[32,1,512]{2,1,0:T(1,128)}), f32[32,1,512]{2,1,0:T(1,128)}, u32[]{:S(2)}, u32[]{:S(2)}) async-start(f32[32,1,512]{2,1,0:T(1,128)} %broadcast_in_dim.55), calls=%async_computation | async-start | bytes 131072 | tf_op jit(solution)/shard_map/all_to_all | solution.py:139
  35.4 6.8 %all-to-all-done = f32[32,1,512]{2,1,0:T(1,128)} async-done(((f32[32,1,512]{2,1,0:T(1,128)}), f32[32,1,512]{2,1,0:T(1,128)}, u32[]{:S(2)}, u32[]{:S(2)}) %all-to-all-start) | async-done | bytes 65568 | tf_op jit(solution)/shard_map/all_to_all | solution.py:139
  42.3 1.0 %reduce = f32[32,512]{1,0:T(8,128)S(1)} reduce(f32[32,1,512]{2,1,0:T(1,128)} %all-to-all-done, f32[]{:T(128)} %constant.161), dimensions={1}, to_apply=%all_to_all.16.reduce_sub_computation | reduce | bytes 131076 | tf_op jit(solution)/shard_map/all_to_all | solution.py:139
  43.3 0.7 reshape_reshape.12
  44.0 1.1 %fusion.202 = f32[32,64]{1,0:T(8,128)S(1)} fusion(f32[256,64]{1,0:T(8,128)} %reshape_reshape.12, s32[32]{0:T(128)} %eq.59), kind=kOutput, calls=%fused_computation.279 | convolution fusion | flops 6299648 | bytes 73856 | tf_op jit(solution)/shard_map/dot_general | solution.py:120
  46.4 10.0 %all_to_all.24 = f32[32,1,512]{2,1,0:T(1,128)} all-to-all(f32[32,1,512]{2,1,0:T(1,128)S(1)} %broadcast_in_dim.56), channel_id=1, replica_groups=mesh['grp'=4,'gx'=4,'gy'=2] {'grp','gx','gy'}, dimensions={0} | all-to-all | bytes 131072 | tf_op jit(solution)/shard_map/all_to_all | solution.py:139
  56.4 1.0 %reduce.1 = f32[32,512]{1,0:T(8,128)S(1)} reduce(f32[32,1,512]{2,1,0:T(1,128)} %all_to_all.24, f32[]{:T(128)} %constant.161), dimensions={1}, to_apply=%all_to_all.17.reduce_sub_computation | reduce | bytes 131076 | tf_op jit(solution)/shard_map/all_to_all | solution.py:139
  57.4 0.7 reshape_reshape.13
  58.1 1.1 %fusion.201 = f32[32,64]{1,0:T(8,128)S(1)} fusion(f32[256,64]{1,0:T(8,128)} %reshape_reshape.13, s32[32]{0:T(128)} %eq.59), kind=kOutput, calls=%fused_computation.278 | convolution fusion | flops 6299648 | bytes 73856 | tf_op jit(solution)/shard_map/dot_general | solution.py:120
  59.9 0.7 divide_add_fusion.1
  60.6 0.7 broadcast_in_dim.57
  61.3 3.3 %all-to-all-start.2 = ((f32[32,1,512]{2,1,0:T(1,128)}), f32[32,1,512]{2,1,0:T(1,128)}, u32[]{:S(2)}, u32[]{:S(2)}) async-start(f32[32,1,512]{2,1,0:T(1,128)} %broadcast_in_dim.57), calls=%async_computation.2 | async-start | bytes 131072 | tf_op jit(solution)/shard_map/all_to_all | solution.py:139
  65.8 6.4 %all-to-all-done.2 = f32[32,1,512]{2,1,0:T(1,128)} async-done(((f32[32,1,512]{2,1,0:T(1,128)}), f32[32,1,512]{2,1,0:T(1,128)}, u32[]{:S(2)}, u32[]{:S(2)}) %all-to-all-start.2) | async-done | bytes 65568 | tf_op jit(solution)/shard_map/all_to_all | solution.py:139
  72.2 1.0 %reduce.2 = f32[32,512]{1,0:T(8,128)S(1)} reduce(f32[32,1,512]{2,1,0:T(1,128)} %all-to-all-done.2, f32[]{:T(128)} %constant.161), dimensions={1}, to_apply=%all_to_all.18.reduce_sub_computation | reduce | bytes 131076 | tf_op jit(solution)/shard_map/all_to_all | solution.py:139
  73.2 0.7 reshape_reshape.14
  73.9 1.1 %fusion.200 = f32[32,64]{1,0:T(8,128)S(1)} fusion(f32[256,64]{1,0:T(8,128)} %reshape_reshape.14, s32[32]{0:T(128)} %eq.59), kind=kOutput, calls=%fused_computation.277 | convolution fusion | flops 6299648 | bytes 73856 | tf_op jit(solution)/shard_map/dot_general | solution.py:120
  75.8 1.3 %fusion.28 = f32[1,512]{1,0:T(1,128)S(1)} fusion(f32[512,1]{0,1:T(1,128)S(1)} %bitcast.93, s32[512]{0:T(512)} %copy-done.8), kind=kOutput, calls=%fused_computation.39 | convolution fusion | flops 3407872 | bytes 6144 | tf_op jit(solution)/shard_map/dot_general | solution.py:120
  77.1 0.7 broadcast_in_dim.58
  77.8 2.8 %all-to-all-start.3 = ((f32[32,1,512]{2,1,0:T(1,128)}), f32[32,1,512]{2,1,0:T(1,128)S(1)}, u32[]{:S(2)}, u32[]{:S(2)}) async-start(f32[32,1,512]{2,1,0:T(1,128)} %broadcast_in_dim.58), calls=%async_computation.3 | async-start | bytes 131072 | tf_op jit(solution)/shard_map/all_to_all | solution.py:139
  80.5 7.4 %all-to-all-done.3 = f32[32,1,512]{2,1,0:T(1,128)S(1)} async-done(((f32[32,1,512]{2,1,0:T(1,128)}), f32[32,1,512]{2,1,0:T(1,128)S(1)}, u32[]{:S(2)}, u32[]{:S(2)}) %all-to-all-start.3) | async-done | bytes 65568 | tf_op jit(solution)/shard_map/all_to_all | solution.py:139
  88.9 1.8 %fusion.4 = f32[6,3264]{1,0:T(8,128)S(1)} fusion(f32[6,204]{1,0:T(8,128)S(1)} %reshape.123, s32[204]{0:T(256)S(1)} %copy-done.11, s32[204]{0:T(256)S(1)} %get-tuple-element.37, s32[3264]{0:T(1024)S(1)} %get-tuple-element.20, s32[3264]{0:T(1024)S(1)} %get-tuple-element.21, s32[204]{0:T(256)S(1)} %copy-done.10, s32[204]{0:T(256)S(1)} %get-tuple-element.38, ...), kind=kOutput, calls=%fused_computation.10 | convolution fusion | flops 58595328 | bytes 145657 | tf_op jit(solution)/shard_map/dot_general | solution.py:120
  93.2 0.8 slice.225
  (99 shorter events, 15.0 us)
Async XLA Ops:
  1.7 7.3 %copy-start = (f32[8,64,256]{2,1,0:T(8,128)S(1)}, f32[8,64,256]{2,1,0:T(8,128)}, u32[]{:S(2)}) copy-start(f32[8,64,256]{2,1,0:T(8,128)} %param.10) | copy-start | bytes 1572868
  1.9 9.5 %copy-start.3 = (f32[16,16,128]{2,1,0:T(8,128)S(1)}, f32[16,16,128]{2,1,0:T(8,128)}, u32[]{:S(2)}) copy-start(f32[16,16,128]{2,1,0:T(8,128)} %param.8) | copy-start | bytes 393220
  1.9 9.5 %copy-start.4 = (f32[16,16,128]{2,1,0:T(8,128)S(1)}, f32[16,16,128]{2,1,0:T(8,128)}, u32[]{:S(2)}) copy-start(f32[16,16,128]{2,1,0:T(8,128)} %param.7) | copy-start | bytes 393220
  1.9 9.5 %copy-start.5 = (f32[16,16,128]{2,1,0:T(8,128)S(1)}, f32[16,16,128]{2,1,0:T(8,128)}, u32[]{:S(2)}) copy-start(f32[16,16,128]{2,1,0:T(8,128)} %param.6) | copy-start | bytes 393220
  2.1 7.1 %collective-permute-start = (f32[24,128]{1,0:T(8,128)S(1)}, f32[24,128]{1,0:T(8,128)S(1)}, u32[]{:S(2)}, u32[]{:S(2)}) collective-permute-start(f32[24,128]{1,0:T(8,128)S(1)} %reshape.109), channel_id=1, source_target_pairs={{8,16},{16,8},{9,17},{17,9},{10,18},{18,10},{11,19},{19,11},{12,20... | collective-permute-start | bytes 36872 | tf_op jit(solution)/shard_map/ppermute | solution.py:28
  3.0 7.6 %collective-permute-start.1 = (f32[24,128]{1,0:T(8,128)S(1)}, f32[24,128]{1,0:T(8,128)S(1)}, u32[]{:S(2)}, u32[]{:S(2)}) collective-permute-start(f32[24,128]{1,0:T(8,128)S(1)} %reshape.110), channel_id=1, source_target_pairs={{0,8},{8,0},{16,24},{24,16},{1,9},{9,1},{17,25},{25,17},{2,10},{10... | collective-permute-start | bytes 36872 | tf_op jit(solution)/shard_map/ppermute | solution.py:28
  12.3 4.9 %collective-permute-start.2 = (f32[3,16,544]{2,1,0:T(8,128)S(1)}, f32[3,16,544]{2,1,0:T(8,128)S(1)}, u32[]{:S(2)}, u32[]{:S(2)}) collective-permute-start(f32[3,16,544]{2,1,0:T(8,128)S(1)} %slice_select_fusion.4), channel_id=1, source_target_pairs={{0,1},{1,0},{2,3},{3,2},{4,5},{5,4},{6,7},{7,6},{8,9},{9,8},{10,11... | collective-permute-start | bytes 313352 | tf_op jit(solution)/shard_map/ppermute | solution.py:29
  17.8 5.8 %collective-permute-start.3 = (f32[306,128]{1,0:T(8,128)S(1)}, f32[306,128]{1,0:T(8,128)S(1)}, u32[]{:S(2)}, u32[]{:S(2)}) collective-permute-start(f32[306,128]{1,0:T(8,128)S(1)} %reshape.112), channel_id=1, source_target_pairs={{2,4},{4,2},{3,5},{5,3},{10,12},{12,10},{11,13},{13,11},{18,20},{2... | collective-permute-start | bytes 470024 | tf_op jit(solution)/shard_map/ppermute | solution.py:28
  18.6 5.0 %collective-permute-start.4 = (f32[306,128]{1,0:T(8,128)S(1)}, f32[306,128]{1,0:T(8,128)S(1)}, u32[]{:S(2)}, u32[]{:S(2)}) collective-permute-start(f32[306,128]{1,0:T(8,128)S(1)} %reshape.113), channel_id=1, source_target_pairs={{0,2},{2,0},{4,6},{6,4},{1,3},{3,1},{5,7},{7,5},{8,10},{10,8},{12,... | collective-permute-start | bytes 470024 | tf_op jit(solution)/shard_map/ppermute | solution.py:28
  23.5 4.8 %copy-start.8 = (s32[512]{0:T(512)}, s32[512]{0:T(512)S(1)}, u32[]{:S(2)}) copy-start(s32[512]{0:T(512)S(1)} %eq.55) | copy-start | bytes 6148
  25.2 0.7 copy-start.1
  26.0 8.7 %copy-start.7 = (s32[8,4]{0,1:T(4,128)S(1)}, s32[8,4]{0,1:T(4,128)}, u32[]{:S(2)}) copy-start(s32[8,4]{0,1:T(4,128)} %param.11) | copy-start | bytes 388
  29.5 12.7 %all-to-all-start = ((f32[32,1,512]{2,1,0:T(1,128)}), f32[32,1,512]{2,1,0:T(1,128)}, u32[]{:S(2)}, u32[]{:S(2)}) async-start(f32[32,1,512]{2,1,0:T(1,128)} %broadcast_in_dim.55), calls=%async_computation | async-start | bytes 131072 | tf_op jit(solution)/shard_map/all_to_all | solution.py:139
  45.8 0.6 copy-start.6
  61.3 10.9 %all-to-all-start.2 = ((f32[32,1,512]{2,1,0:T(1,128)}), f32[32,1,512]{2,1,0:T(1,128)}, u32[]{:S(2)}, u32[]{:S(2)}) async-start(f32[32,1,512]{2,1,0:T(1,128)} %broadcast_in_dim.57), calls=%async_computation.2 | async-start | bytes 131072 | tf_op jit(solution)/shard_map/all_to_all | solution.py:139
  75.7 13.1 %copy-start.9 = (f32[512]{0:T(512)}, f32[512]{0:T(512)S(1)}, u32[]{:S(2)}) copy-start(f32[512]{0:T(512)S(1)} %divide_add_fusion) | copy-start | bytes 6148
  75.7 13.1 %copy-start.10 = (s32[204]{0:T(256)S(1)}, s32[204]{0:T(256)}, u32[]{:S(2)}) copy-start(s32[204]{0:T(256)} %get-tuple-element.33) | copy-start | bytes 2452
  75.8 13.1 %copy-start.11 = (s32[204]{0:T(256)S(1)}, s32[204]{0:T(256)}, u32[]{:S(2)}) copy-start(s32[204]{0:T(256)} %get-tuple-element.34) | copy-start | bytes 2452
  75.8 13.1 %copy-start.12 = (pred[204]{0:T(512)(128)(4,1)S(1)}, pred[204]{0:T(512)(128)(4,1)}, u32[]{:S(2)}) copy-start(pred[204]{0:T(512)(128)(4,1)} %get-tuple-element.35) | copy-start | bytes 616
  75.8 13.1 %copy-start.13 = (pred[204]{0:T(512)(128)(4,1)S(1)}, pred[204]{0:T(512)(128)(4,1)}, u32[]{:S(2)}) copy-start(pred[204]{0:T(512)(128)(4,1)} %get-tuple-element.36) | copy-start | bytes 616
  77.8 10.2 %all-to-all-start.3 = ((f32[32,1,512]{2,1,0:T(1,128)}), f32[32,1,512]{2,1,0:T(1,128)S(1)}, u32[]{:S(2)}, u32[]{:S(2)}) async-start(f32[32,1,512]{2,1,0:T(1,128)} %broadcast_in_dim.58), calls=%async_computation.3 | async-start | bytes 131072 | tf_op jit(solution)/shard_map/all_to_all | solution.py:139
  88.9 2.3 %copy-start.2 = (f32[24,3264]{1,0:T(8,128)S(1)}, f32[24,3264]{1,0:T(8,128)}, u32[]{:S(2)}) copy-start(f32[24,3264]{1,0:T(8,128)} %copy-done.1) | copy-start | bytes 940036

commit v11 on v10

--- a/solution.py
+++ b/solution.py
@@ -171,9 +171,15 @@
     bx, by, bz = size_x // BOX, size_y // BOX, size_z // BOX
     live = lax.axis_index("grp") >= 0
     pick_x = box_matrix(bx, rows, 1, HALO, live)
-    pick_yz = box_matrix(by * bz, span_y * span_z, span_z, HALO, live, bz).T
-    box_totals = dot(pick_x, dot(smoothed, pick_yz)).reshape(-1)
-    box_labels = aggregate_ids[::BOX, ::BOX, ::BOX].reshape(-1)
+    pick_y = box_matrix(by, span_y, 1, HALO, live)
+    pick_z = box_matrix(bz, span_z, 1, HALO, live)
+    rows_summed = dot(pick_x, smoothed).reshape(bx, span_y, span_z)
+    box_totals = jnp.einsum(
+        "ayz,by,cz->abc", rows_summed, pick_y, pick_z, precision=lax.Precision.HIGHEST
+    ).reshape(-1)
+    corner_ids = aggregate_ids[::BOX, ::BOX].reshape(bx * by, size_z).astype(source.dtype)
+    first_z = lax.broadcasted_iota(jnp.int32, (size_z, bz), 0) == BOX * lax.broadcasted_iota(jnp.int32, (size_z, bz), 1)
+    box_labels = dot(corner_ids, first_z.astype(source.dtype)).astype(jnp.int32).reshape(-1)
     placed = (
         box_labels[:, None] == lax.broadcasted_iota(jnp.int32, (box_labels.shape[0],) * 2, 1)
     ).astype(source.dtype)

time: 94.7 us -> 96.2 us (1.016)
  other arithmetic: 10.5 us -> 11.6 us
  waiting for transfers between devices: 25.4 us -> 24.4 us
    dot_general x0 -> x2, matrix products: none -> 1.83 us  [local(): jnp.einsum('ayz,by,cz->abc', rows_summed, pick_y, pick_z, precision=lax.P...]
    dot_general x9, matrix products: 9.75 us -> 8.42 us  [dot(): return jnp.dot(left, right, precision=lax.Precision.HIGHEST)]
  transfers between devices with their start and end apart: 8 -> 8, of which waited for: 5 -> 5; matrix products, arithmetic and copies ran while one was open for 5% -> 6% of each run, Pallas kernels for 0% -> 0%
where the time goes in v11:
time: 96.2 us; the launch traced here: 95.4 us
  waiting for transfers between devices  24.4 us (25%)
  starting transfers between devices  23.3 us (24%)
  local copies, waits for them, and re-layouts  13.1 us (14%)
  matrix products  11.8 us (12%)
  other arithmetic  11.6 us (12%)
  blocking collectives  9.97 us (10%)
  between operations  1.14 us (1%)
    all_to_all x3, waiting for transfers between devices, everyone(): return lax.all_to_all(copies, ALL_AXES, 0, 0, tiled=True).reshape(-1)  20.7 us
    all_to_all x3, starting transfers between devices, everyone(): return lax.all_to_all(copies, ALL_AXES, 0, 0, tiled=True).reshape(-1)  11.6 us
    ppermute x4, starting transfers between devices, permute(): return lax.ppermute(slab.reshape(-1, 128), axis, pairs).reshape(slab.shape)  10.2 us
    all_to_all x1, blocking collectives, everyone(): return lax.all_to_all(copies, ALL_AXES, 0, 0, tiled=True).reshape(-1)  9.97 us
    dot_general x9, matrix products, dot(): return jnp.dot(left, right, precision=lax.Precision.HIGHEST)  8.42 us
    all_to_all x4, other arithmetic, everyone(): return lax.all_to_all(copies, ALL_AXES, 0, 0, tiled=True).reshape(-1)  3.15 us
    ppermute x1, waiting for transfers between devices, permute(): return lax.ppermute(slab, axis, pairs)  2.82 us
    another operation x3, local copies, waits for them, and re-layouts, local(): blocks = dot(pick, pooled.reshape(tables, 64))  2.22 us
  transfers between devices with their start and end apart: 8, of which 5 were waited for; matrix products, arithmetic and copies ran while one was open for 6% of the time, Pallas kernels for 0%

profile of v11, /device:TPU:0, one launch (start us, length us, event | category | flops | bytes accessed | tf_op | source)
XLA Modules:
  0.0 95.4 jit_solution(8962522683373212996)
XLA Ops:
  0.6 1.1 %pad_maximum_fusion.2 = f32[3,16,16,128]{3,2,1,0:T(8,128)S(1)} fusion(f32[1,16,16,128]{3,2,1,0:T(8,128)} %bitcast.90, f32[1,16,16,128]{3,2,1,0:T(8,128)} %bitcast.92, f32[1,16,16,128]{3,2,1,0:T(8,128)} %bitcast.94), kind=kLoop, calls=%fused_computation.77 | loop fusion | flops 196608 | bytes 786432 | tf_op jit(solution)/shard_map/stack | solution.py:145
  3.0 5.9 %collective-permute-start.1 = (f32[24,128]{1,0:T(8,128)S(1)}, f32[24,128]{1,0:T(8,128)S(1)}, u32[]{:S(2)}, u32[]{:S(2)}) collective-permute-start(f32[24,128]{1,0:T(8,128)S(1)} %reshape.115), channel_id=1, source_target_pairs={{0,8},{8,0},{16,24},{24,16},{1,9},{9,1},{17,25},{25,17},{2,10},{10... | collective-permute-start | bytes 36872 | tf_op jit(solution)/shard_map/ppermute | solution.py:28
  9.5 1.6 %slice.183 = s32[4,4,128]{2,1,0:T(4,128)S(1)} slice(s32[16,16,128]{2,1,0:T(8,128)} %param.9), slice={[0:16:4], [0:16:4], [0:128:1]} | slice | bytes 16384 | tf_op jit(solution)/shard_map/slice | solution.py:180
  13.2 1.6 %collective-permute-start.2 = (f32[3,16,544]{2,1,0:T(8,128)S(1)}, f32[3,16,544]{2,1,0:T(8,128)S(1)}, u32[]{:S(2)}, u32[]{:S(2)}) collective-permute-start(f32[3,16,544]{2,1,0:T(8,128)S(1)} %slice_select_fusion.4), channel_id=1, source_target_pairs={{0,1},{1,0},{2,3},{3,2},{4,5},{5,4},{6,7},{7,6},{8,9},{9,8},{10,11... | collective-permute-start | bytes 313352 | tf_op jit(solution)/shard_map/ppermute | solution.py:29
  15.3 2.8 %collective-permute-done.2 = f32[3,16,544]{2,1,0:T(8,128)S(1)} collective-permute-done((f32[3,16,544]{2,1,0:T(8,128)S(1)}, f32[3,16,544]{2,1,0:T(8,128)S(1)}, u32[]{:S(2)}, u32[]{:S(2)}) %collective-permute-start.2) | collective-permute-done | bytes 104480 | tf_op jit(solution)/shard_map/ppermute | solution.py:29
  19.5 2.9 %collective-permute-start.4 = (f32[306,128]{1,0:T(8,128)S(1)}, f32[306,128]{1,0:T(8,128)S(1)}, u32[]{:S(2)}, u32[]{:S(2)}) collective-permute-start(f32[306,128]{1,0:T(8,128)S(1)} %reshape.118), channel_id=1, source_target_pairs={{0,2},{2,0},{4,6},{6,4},{1,3},{3,1},{5,7},{7,5},{8,10},{10,8},{12,... | collective-permute-start | bytes 470024 | tf_op jit(solution)/shard_map/ppermute | solution.py:28
  22.6 0.8 collective-permute-done.4
  25.8 0.9 fusion.172
  26.7 0.8 reshape.119
  27.5 1.0 %fusion.208 = f32[4,4,136]{2,0,1:T(4,128)S(1)} fusion(f32[4,24,136]{2,1,0:T(8,128)} %reshape.119, pred[4,24]{1,0:T(4,128)(4,1)S(1)} %and_and_fusion), kind=kOutput, calls=%fused_computation.297 | convolution fusion | flops 626688 | bytes 61024 | tf_op jit(solution)/shard_map/ayz,by,cz->abc/dot_general | solution.py:177
  28.5 0.8 convolution_bitcast_fusion
  30.6 5.5 %all-to-all-start = ((f32[32,1,512]{2,1,0:T(1,128)}), f32[32,1,512]{2,1,0:T(1,128)}, u32[]{:S(2)}, u32[]{:S(2)}) async-start(f32[32,1,512]{2,1,0:T(1,128)} %broadcast_in_dim.55), calls=%async_computation | async-start | bytes 131072 | tf_op jit(solution)/shard_map/all_to_all | solution.py:139
  36.8 6.9 %all-to-all-done = f32[32,1,512]{2,1,0:T(1,128)} async-done(((f32[32,1,512]{2,1,0:T(1,128)}), f32[32,1,512]{2,1,0:T(1,128)}, u32[]{:S(2)}, u32[]{:S(2)}) %all-to-all-start) | async-done | bytes 65568 | tf_op jit(solution)/shard_map/all_to_all | solution.py:139
  43.7 1.0 %reduce = f32[32,512]{1,0:T(8,128)S(1)} reduce(f32[32,1,512]{2,1,0:T(1,128)} %all-to-all-done, f32[]{:T(128)} %constant.127), dimensions={1}, to_apply=%all_to_all.16.reduce_sub_computation | reduce | bytes 131076 | tf_op jit(solution)/shard_map/all_to_all | solution.py:139
  44.7 0.7 reshape_reshape.12
  45.5 1.1 %fusion.181 = f32[32,64]{1,0:T(8,128)S(1)} fusion(f32[256,64]{1,0:T(8,128)} %reshape_reshape.12, s32[32]{0:T(128)} %eq.60), kind=kOutput, calls=%fused_computation.256 | convolution fusion | flops 6299648 | bytes 73856 | tf_op jit(solution)/shard_map/dot_general | solution.py:120
  47.9 10.0 %all_to_all.24 = f32[32,1,512]{2,1,0:T(1,128)} all-to-all(f32[32,1,512]{2,1,0:T(1,128)S(1)} %broadcast_in_dim.56), channel_id=1, replica_groups=mesh['grp'=4,'gx'=4,'gy'=2] {'grp','gx','gy'}, dimensions={0} | all-to-all | bytes 131072 | tf_op jit(solution)/shard_map/all_to_all | solution.py:139
  57.8 1.0 %reduce.1 = f32[32,512]{1,0:T(8,128)S(1)} reduce(f32[32,1,512]{2,1,0:T(1,128)} %all_to_all.24, f32[]{:T(128)} %constant.127), dimensions={1}, to_apply=%all_to_all.17.reduce_sub_computation | reduce | bytes 131076 | tf_op jit(solution)/shard_map/all_to_all | solution.py:139
  58.8 0.7 reshape_reshape.13
  59.6 1.1 %fusion.180 = f32[32,64]{1,0:T(8,128)S(1)} fusion(f32[256,64]{1,0:T(8,128)} %reshape_reshape.13, s32[32]{0:T(128)} %eq.60), kind=kOutput, calls=%fused_computation.255 | convolution fusion | flops 6299648 | bytes 73856 | tf_op jit(solution)/shard_map/dot_general | solution.py:120
  61.4 0.7 divide_add_fusion.1
  62.7 3.3 %all-to-all-start.2 = ((f32[32,1,512]{2,1,0:T(1,128)}), f32[32,1,512]{2,1,0:T(1,128)}, u32[]{:S(2)}, u32[]{:S(2)}) async-start(f32[32,1,512]{2,1,0:T(1,128)} %broadcast_in_dim.57), calls=%async_computation.2 | async-start | bytes 131072 | tf_op jit(solution)/shard_map/all_to_all | solution.py:139
  67.2 6.4 %all-to-all-done.2 = f32[32,1,512]{2,1,0:T(1,128)} async-done(((f32[32,1,512]{2,1,0:T(1,128)}), f32[32,1,512]{2,1,0:T(1,128)}, u32[]{:S(2)}, u32[]{:S(2)}) %all-to-all-start.2) | async-done | bytes 65568 | tf_op jit(solution)/shard_map/all_to_all | solution.py:139
  73.6 1.0 %reduce.2 = f32[32,512]{1,0:T(8,128)S(1)} reduce(f32[32,1,512]{2,1,0:T(1,128)} %all-to-all-done.2, f32[]{:T(128)} %constant.127), dimensions={1}, to_apply=%all_to_all.18.reduce_sub_computation | reduce | bytes 131076 | tf_op jit(solution)/shard_map/all_to_all | solution.py:139
  74.6 0.7 reshape_reshape.14
  75.4 1.1 %fusion.179 = f32[32,64]{1,0:T(8,128)S(1)} fusion(f32[256,64]{1,0:T(8,128)} %reshape_reshape.14, s32[32]{0:T(128)} %eq.60), kind=kOutput, calls=%fused_computation.254 | convolution fusion | flops 6299648 | bytes 73856 | tf_op jit(solution)/shard_map/dot_general | solution.py:120
  77.2 1.3 %fusion.21 = f32[1,512]{1,0:T(1,128)S(1)} fusion(f32[512,1]{0,1:T(1,128)S(1)} %bitcast.104, s32[512]{0:T(512)} %copy-done.8), kind=kOutput, calls=%fused_computation.29 | convolution fusion | flops 3407872 | bytes 6144 | tf_op jit(solution)/shard_map/dot_general | solution.py:120
  78.5 0.7 broadcast_in_dim.58
  79.2 2.8 %all-to-all-start.3 = ((f32[32,1,512]{2,1,0:T(1,128)}), f32[32,1,512]{2,1,0:T(1,128)S(1)}, u32[]{:S(2)}, u32[]{:S(2)}) async-start(f32[32,1,512]{2,1,0:T(1,128)} %broadcast_in_dim.58), calls=%async_computation.3 | async-start | bytes 131072 | tf_op jit(solution)/shard_map/all_to_all | solution.py:139
  82.0 7.4 %all-to-all-done.3 = f32[32,1,512]{2,1,0:T(1,128)S(1)} async-done(((f32[32,1,512]{2,1,0:T(1,128)}), f32[32,1,512]{2,1,0:T(1,128)S(1)}, u32[]{:S(2)}, u32[]{:S(2)}) %all-to-all-start.3) | async-done | bytes 65568 | tf_op jit(solution)/shard_map/all_to_all | solution.py:139
  90.3 1.8 %fusion.4 = f32[6,3264]{1,0:T(8,128)S(1)} fusion(f32[6,204]{1,0:T(8,128)S(1)} %reshape.129, s32[204]{0:T(256)S(1)} %copy-done.11, s32[204]{0:T(256)S(1)} %get-tuple-element.33, s32[3264]{0:T(1024)S(1)} %get-tuple-element.20, s32[3264]{0:T(1024)S(1)} %get-tuple-element.21, s32[204]{0:T(256)S(1)} %copy-done.10, s32[204]{0:T(256)S(1)} %get-tuple-element.34, ...), kind=kOutput, calls=%fused_computation.10 | convolution fusion | flops 58595328 | bytes 145657 | tf_op jit(solution)/shard_map/dot_general | solution.py:120
  94.7 0.8 slice.225
  (107 shorter events, 18.0 us)
Async XLA Ops:
  1.7 9.5 %copy-start = (f32[8,64,256]{2,1,0:T(8,128)S(1)}, f32[8,64,256]{2,1,0:T(8,128)}, u32[]{:S(2)}) copy-start(f32[8,64,256]{2,1,0:T(8,128)} %param.10) | copy-start | bytes 1572868
  1.9 10.4 %copy-start.3 = (f32[16,16,128]{2,1,0:T(8,128)S(1)}, f32[16,16,128]{2,1,0:T(8,128)}, u32[]{:S(2)}) copy-start(f32[16,16,128]{2,1,0:T(8,128)} %param.8) | copy-start | bytes 393220
  1.9 10.4 %copy-start.4 = (f32[16,16,128]{2,1,0:T(8,128)S(1)}, f32[16,16,128]{2,1,0:T(8,128)}, u32[]{:S(2)}) copy-start(f32[16,16,128]{2,1,0:T(8,128)} %param.7) | copy-start | bytes 393220
  1.9 10.4 %copy-start.5 = (f32[16,16,128]{2,1,0:T(8,128)S(1)}, f32[16,16,128]{2,1,0:T(8,128)}, u32[]{:S(2)}) copy-start(f32[16,16,128]{2,1,0:T(8,128)} %param.6) | copy-start | bytes 393220
  2.1 9.3 %collective-permute-start = (f32[24,128]{1,0:T(8,128)S(1)}, f32[24,128]{1,0:T(8,128)S(1)}, u32[]{:S(2)}, u32[]{:S(2)}) collective-permute-start(f32[24,128]{1,0:T(8,128)S(1)} %reshape.114), channel_id=1, source_target_pairs={{8,16},{16,8},{9,17},{17,9},{10,18},{18,10},{11,19},{19,11},{12,20... | collective-permute-start | bytes 36872 | tf_op jit(solution)/shard_map/ppermute | solution.py:28
  3.0 8.5 %collective-permute-start.1 = (f32[24,128]{1,0:T(8,128)S(1)}, f32[24,128]{1,0:T(8,128)S(1)}, u32[]{:S(2)}, u32[]{:S(2)}) collective-permute-start(f32[24,128]{1,0:T(8,128)S(1)} %reshape.115), channel_id=1, source_target_pairs={{0,8},{8,0},{16,24},{24,16},{1,9},{9,1},{17,25},{25,17},{2,10},{10... | collective-permute-start | bytes 36872 | tf_op jit(solution)/shard_map/ppermute | solution.py:28
  13.2 4.9 %collective-permute-start.2 = (f32[3,16,544]{2,1,0:T(8,128)S(1)}, f32[3,16,544]{2,1,0:T(8,128)S(1)}, u32[]{:S(2)}, u32[]{:S(2)}) collective-permute-start(f32[3,16,544]{2,1,0:T(8,128)S(1)} %slice_select_fusion.4), channel_id=1, source_target_pairs={{0,1},{1,0},{2,3},{3,2},{4,5},{5,4},{6,7},{7,6},{8,9},{9,8},{10,11... | collective-permute-start | bytes 313352 | tf_op jit(solution)/shard_map/ppermute | solution.py:29
  18.7 4.0 %collective-permute-start.3 = (f32[306,128]{1,0:T(8,128)S(1)}, f32[306,128]{1,0:T(8,128)S(1)}, u32[]{:S(2)}, u32[]{:S(2)}) collective-permute-start(f32[306,128]{1,0:T(8,128)S(1)} %reshape.117), channel_id=1, source_target_pairs={{2,4},{4,2},{3,5},{5,3},{10,12},{12,10},{11,13},{13,11},{18,20},{2... | collective-permute-start | bytes 470024 | tf_op jit(solution)/shard_map/ppermute | solution.py:28
  19.5 4.0 %collective-permute-start.4 = (f32[306,128]{1,0:T(8,128)S(1)}, f32[306,128]{1,0:T(8,128)S(1)}, u32[]{:S(2)}, u32[]{:S(2)}) collective-permute-start(f32[306,128]{1,0:T(8,128)S(1)} %reshape.118), channel_id=1, source_target_pairs={{0,2},{2,0},{4,6},{6,4},{1,3},{3,1},{5,7},{7,5},{8,10},{10,8},{12,... | collective-permute-start | bytes 470024 | tf_op jit(solution)/shard_map/ppermute | solution.py:28
  22.5 6.9 %copy-start.8 = (s32[512]{0:T(512)}, s32[512]{0:T(512)S(1)}, u32[]{:S(2)}) copy-start(s32[512]{0:T(512)S(1)} %eq.56) | copy-start | bytes 6148
  25.0 0.7 copy-start.1
  25.8 2.8 %copy-start.12 = (s32[136]{0:T(256)S(1)}, s32[136]{0:T(256)}, u32[]{:S(2)}) copy-start(s32[136]{0:T(256)} %iota_add_fusion) | copy-start | bytes 1636
  25.8 10.4 %copy-start.7 = (s32[8,4]{0,1:T(4,128)S(1)}, s32[8,4]{0,1:T(4,128)}, u32[]{:S(2)}) copy-start(s32[8,4]{0,1:T(4,128)} %param.11) | copy-start | bytes 388
  30.6 13.1 %all-to-all-start = ((f32[32,1,512]{2,1,0:T(1,128)}), f32[32,1,512]{2,1,0:T(1,128)}, u32[]{:S(2)}, u32[]{:S(2)}) async-start(f32[32,1,512]{2,1,0:T(1,128)} %broadcast_in_dim.55), calls=%async_computation | async-start | bytes 131072 | tf_op jit(solution)/shard_map/all_to_all | solution.py:139
  47.3 0.6 copy-start.6
  62.7 10.9 %all-to-all-start.2 = ((f32[32,1,512]{2,1,0:T(1,128)}), f32[32,1,512]{2,1,0:T(1,128)}, u32[]{:S(2)}, u32[]{:S(2)}) async-start(f32[32,1,512]{2,1,0:T(1,128)} %broadcast_in_dim.57), calls=%async_computation.2 | async-start | bytes 131072 | tf_op jit(solution)/shard_map/all_to_all | solution.py:139
  77.2 13.1 %copy-start.9 = (f32[512]{0:T(512)}, f32[512]{0:T(512)S(1)}, u32[]{:S(2)}) copy-start(f32[512]{0:T(512)S(1)} %divide_add_fusion) | copy-start | bytes 6148
  77.2 13.1 %copy-start.10 = (s32[204]{0:T(256)S(1)}, s32[204]{0:T(256)}, u32[]{:S(2)}) copy-start(s32[204]{0:T(256)} %get-tuple-element.29) | copy-start | bytes 2452
  77.2 13.1 %copy-start.11 = (s32[204]{0:T(256)S(1)}, s32[204]{0:T(256)}, u32[]{:S(2)}) copy-start(s32[204]{0:T(256)} %get-tuple-element.30) | copy-start | bytes 2452
  77.2 13.1 %copy-start.13 = (pred[204]{0:T(512)(128)(4,1)S(1)}, pred[204]{0:T(512)(128)(4,1)}, u32[]{:S(2)}) copy-start(pred[204]{0:T(512)(128)(4,1)} %get-tuple-element.31) | copy-start | bytes 616
  77.2 13.1 %copy-start.14 = (pred[204]{0:T(512)(128)(4,1)S(1)}, pred[204]{0:T(512)(128)(4,1)}, u32[]{:S(2)}) copy-start(pred[204]{0:T(512)(128)(4,1)} %get-tuple-element.32) | copy-start | bytes 616
  79.2 10.2 %all-to-all-start.3 = ((f32[32,1,512]{2,1,0:T(1,128)}), f32[32,1,512]{2,1,0:T(1,128)S(1)}, u32[]{:S(2)}, u32[]{:S(2)}) async-start(f32[32,1,512]{2,1,0:T(1,128)} %broadcast_in_dim.58), calls=%async_computation.3 | async-start | bytes 131072 | tf_op jit(solution)/shard_map/all_to_all | solution.py:139
  90.3 2.3 %copy-start.2 = (f32[24,3264]{1,0:T(8,128)S(1)}, f32[24,3264]{1,0:T(8,128)}, u32[]{:S(2)}) copy-start(f32[24,3264]{1,0:T(8,128)} %copy-done.1) | copy-start | bytes 940036

commit v12 on v10

--- a/solution.py
+++ b/solution.py
@@ -173,7 +173,9 @@
     pick_x = box_matrix(bx, rows, 1, HALO, live)
     pick_yz = box_matrix(by * bz, span_y * span_z, span_z, HALO, live, bz).T
     box_totals = dot(pick_x, dot(smoothed, pick_yz)).reshape(-1)
-    box_labels = aggregate_ids[::BOX, ::BOX, ::BOX].reshape(-1)
+    corner_ids = aggregate_ids[::BOX, ::BOX].reshape(bx * by, size_z).astype(source.dtype)
+    first_z = lax.broadcasted_iota(jnp.int32, (size_z, bz), 0) == BOX * lax.broadcasted_iota(jnp.int32, (size_z, bz), 1)
+    box_labels = dot(corner_ids, first_z.astype(source.dtype)).astype(jnp.int32).reshape(-1)
     placed = (
         box_labels[:, None] == lax.broadcasted_iota(jnp.int32, (box_labels.shape[0],) * 2, 1)
     ).astype(source.dtype)

time: 94.7 us -> 95.4 us (level)
  other arithmetic: 10.5 us -> 11.6 us
    dot_general x9 -> x10, matrix products: 9.75 us -> 9.88 us  [dot(): return jnp.dot(left, right, precision=lax.Precision.HIGHEST)]
  transfers between devices with their start and end apart: 8 -> 8, of which waited for: 5 -> 5; matrix products, arithmetic and copies ran while one was open for 5% -> 6% of each run, Pallas kernels for 0% -> 0%
where the time goes in v12:
time: 95.4 us; the launch traced here: 94.7 us
  waiting for transfers between devices  24.9 us (26%)
  starting transfers between devices  23.3 us (24%)
  local copies, waits for them, and re-layouts  12.4 us (13%)
  other arithmetic  11.6 us (12%)
  matrix products  11.5 us (12%)
  blocking collectives  9.96 us (10%)
  between operations  1.1 us (1%)
    all_to_all x3, waiting for transfers between devices, everyone(): return lax.all_to_all(copies, ALL_AXES, 0, 0, tiled=True).reshape(-1)  20.6 us
    all_to_all x3, starting transfers between devices, everyone(): return lax.all_to_all(copies, ALL_AXES, 0, 0, tiled=True).reshape(-1)  11.5 us
    ppermute x4, starting transfers between devices, permute(): return lax.ppermute(slab.reshape(-1, 128), axis, pairs).reshape(slab.shape)  10.2 us
    all_to_all x1, blocking collectives, everyone(): return lax.all_to_all(copies, ALL_AXES, 0, 0, tiled=True).reshape(-1)  9.96 us
    dot_general x10, matrix products, dot(): return jnp.dot(left, right, precision=lax.Precision.HIGHEST)  9.88 us
    ppermute x1, waiting for transfers between devices, permute(): return lax.ppermute(slab, axis, pairs)  3.38 us
    all_to_all x4, other arithmetic, everyone(): return lax.all_to_all(copies, ALL_AXES, 0, 0, tiled=True).reshape(-1)  3.15 us
    another operation x3, local copies, waits for them, and re-layouts, local(): blocks = dot(pick, pooled.reshape(tables, 64))  2.22 us
  transfers between devices with their start and end apart: 8, of which 5 were waited for; matrix products, arithmetic and copies ran while one was open for 6% of the time, Pallas kernels for 0%

profile of v12, /device:TPU:0, one launch (start us, length us, event | category | flops | bytes accessed | tf_op | source)
XLA Modules:
  0.0 94.7 jit_solution(17787601820314196453)
XLA Ops:
  0.6 1.1 %pad_maximum_fusion.2 = f32[3,16,16,128]{3,2,1,0:T(8,128)S(1)} fusion(f32[1,16,16,128]{3,2,1,0:T(8,128)} %bitcast.84, f32[1,16,16,128]{3,2,1,0:T(8,128)} %bitcast.86, f32[1,16,16,128]{3,2,1,0:T(8,128)} %bitcast.88), kind=kLoop, calls=%fused_computation.104 | loop fusion | flops 196608 | bytes 786432 | tf_op jit(solution)/shard_map/stack | solution.py:145
  3.0 5.9 %collective-permute-start.1 = (f32[24,128]{1,0:T(8,128)S(1)}, f32[24,128]{1,0:T(8,128)S(1)}, u32[]{:S(2)}, u32[]{:S(2)}) collective-permute-start(f32[24,128]{1,0:T(8,128)S(1)} %reshape.112), channel_id=1, source_target_pairs={{0,8},{8,0},{16,24},{24,16},{1,9},{9,1},{17,25},{25,17},{2,10},{10... | collective-permute-start | bytes 36872 | tf_op jit(solution)/shard_map/ppermute | solution.py:28
  9.5 1.6 %slice.183 = s32[4,4,128]{2,1,0:T(4,128)S(1)} slice(s32[16,16,128]{2,1,0:T(8,128)} %param.9), slice={[0:16:4], [0:16:4], [0:128:1]} | slice | bytes 16384 | tf_op jit(solution)/shard_map/slice | solution.py:176
  13.7 1.6 %collective-permute-start.2 = (f32[3,16,544]{2,1,0:T(8,128)S(1)}, f32[3,16,544]{2,1,0:T(8,128)S(1)}, u32[]{:S(2)}, u32[]{:S(2)}) collective-permute-start(f32[3,16,544]{2,1,0:T(8,128)S(1)} %slice_select_fusion.4), channel_id=1, source_target_pairs={{0,1},{1,0},{2,3},{3,2},{4,5},{5,4},{6,7},{7,6},{8,9},{9,8},{10,11... | collective-permute-start | bytes 313352 | tf_op jit(solution)/shard_map/ppermute | solution.py:29
  15.3 3.4 %collective-permute-done.2 = f32[3,16,544]{2,1,0:T(8,128)S(1)} collective-permute-done((f32[3,16,544]{2,1,0:T(8,128)S(1)}, f32[3,16,544]{2,1,0:T(8,128)S(1)}, u32[]{:S(2)}, u32[]{:S(2)}) %collective-permute-start.2) | collective-permute-done | bytes 104480 | tf_op jit(solution)/shard_map/ppermute | solution.py:29
  19.2 0.7 collective-permute-start.3
  20.0 2.9 %collective-permute-start.4 = (f32[306,128]{1,0:T(8,128)S(1)}, f32[306,128]{1,0:T(8,128)S(1)}, u32[]{:S(2)}, u32[]{:S(2)}) collective-permute-start(f32[306,128]{1,0:T(8,128)S(1)} %reshape.115), channel_id=1, source_target_pairs={{0,2},{2,0},{4,6},{6,4},{1,3},{3,1},{5,7},{7,5},{8,10},{10,8},{12,... | collective-permute-start | bytes 470024 | tf_op jit(solution)/shard_map/ppermute | solution.py:28
  23.2 0.8 collective-permute-done.4
  26.3 2.2 %fusion.12 = f32[24,128]{1,0:T(8,128)S(1)} fusion(s32[128]{0:T(128)S(1)} %get-tuple-element.28, s32[128]{0:T(128)S(1)} %copy-done.12, s32[3264]{0:T(1024)S(1)} %get-tuple-element.20, s32[3264]{0:T(1024)S(1)} %get-tuple-element.21, s32[128]{0:T(128)S(1)} %get-tuple-element.27, s32[128]{0:T(128)S(1)} %copy-done.13, s32[3264]{0:T(1024)S(1)} %get-tuple-element.19, ...), kind=kOutput, calls=%fused_computation.23 | convolution fusion | flops 131056128 | bytes 3283969 | tf_op jit(solution)/shard_map/dot_general | solution.py:120
  29.2 0.7 broadcast_in_dim.55
  29.9 5.5 %all-to-all-start = ((f32[32,1,512]{2,1,0:T(1,128)}), f32[32,1,512]{2,1,0:T(1,128)}, u32[]{:S(2)}, u32[]{:S(2)}) async-start(f32[32,1,512]{2,1,0:T(1,128)} %broadcast_in_dim.55), calls=%async_computation | async-start | bytes 131072 | tf_op jit(solution)/shard_map/all_to_all | solution.py:139
  36.2 6.8 %all-to-all-done = f32[32,1,512]{2,1,0:T(1,128)} async-done(((f32[32,1,512]{2,1,0:T(1,128)}), f32[32,1,512]{2,1,0:T(1,128)}, u32[]{:S(2)}, u32[]{:S(2)}) %all-to-all-start) | async-done | bytes 65568 | tf_op jit(solution)/shard_map/all_to_all | solution.py:139
  43.0 1.0 %reduce = f32[32,512]{1,0:T(8,128)S(1)} reduce(f32[32,1,512]{2,1,0:T(1,128)} %all-to-all-done, f32[]{:T(128)} %constant.162), dimensions={1}, to_apply=%all_to_all.16.reduce_sub_computation | reduce | bytes 131076 | tf_op jit(solution)/shard_map/all_to_all | solution.py:139
  44.0 0.7 reshape_reshape.12
  44.8 1.1 %fusion.203 = f32[32,64]{1,0:T(8,128)S(1)} fusion(f32[256,64]{1,0:T(8,128)} %reshape_reshape.12, s32[32]{0:T(128)} %eq.63), kind=kOutput, calls=%fused_computation.282 | convolution fusion | flops 6299648 | bytes 73856 | tf_op jit(solution)/shard_map/dot_general | solution.py:120
  47.2 10.0 %all_to_all.24 = f32[32,1,512]{2,1,0:T(1,128)} all-to-all(f32[32,1,512]{2,1,0:T(1,128)S(1)} %broadcast_in_dim.56), channel_id=1, replica_groups=mesh['grp'=4,'gx'=4,'gy'=2] {'grp','gx','gy'}, dimensions={0} | all-to-all | bytes 131072 | tf_op jit(solution)/shard_map/all_to_all | solution.py:139
  57.1 1.0 %reduce.1 = f32[32,512]{1,0:T(8,128)S(1)} reduce(f32[32,1,512]{2,1,0:T(1,128)} %all_to_all.24, f32[]{:T(128)} %constant.162), dimensions={1}, to_apply=%all_to_all.17.reduce_sub_computation | reduce | bytes 131076 | tf_op jit(solution)/shard_map/all_to_all | solution.py:139
  58.1 0.7 reshape_reshape.13
  58.9 1.1 %fusion.202 = f32[32,64]{1,0:T(8,128)S(1)} fusion(f32[256,64]{1,0:T(8,128)} %reshape_reshape.13, s32[32]{0:T(128)} %eq.63), kind=kOutput, calls=%fused_computation.281 | convolution fusion | flops 6299648 | bytes 73856 | tf_op jit(solution)/shard_map/dot_general | solution.py:120
  60.7 0.7 divide_add_fusion.1
  61.4 0.7 broadcast_in_dim.57
  62.0 3.3 %all-to-all-start.2 = ((f32[32,1,512]{2,1,0:T(1,128)}), f32[32,1,512]{2,1,0:T(1,128)}, u32[]{:S(2)}, u32[]{:S(2)}) async-start(f32[32,1,512]{2,1,0:T(1,128)} %broadcast_in_dim.57), calls=%async_computation.2 | async-start | bytes 131072 | tf_op jit(solution)/shard_map/all_to_all | solution.py:139
  66.5 6.4 %all-to-all-done.2 = f32[32,1,512]{2,1,0:T(1,128)} async-done(((f32[32,1,512]{2,1,0:T(1,128)}), f32[32,1,512]{2,1,0:T(1,128)}, u32[]{:S(2)}, u32[]{:S(2)}) %all-to-all-start.2) | async-done | bytes 65568 | tf_op jit(solution)/shard_map/all_to_all | solution.py:139
  72.9 1.0 %reduce.2 = f32[32,512]{1,0:T(8,128)S(1)} reduce(f32[32,1,512]{2,1,0:T(1,128)} %all-to-all-done.2, f32[]{:T(128)} %constant.162), dimensions={1}, to_apply=%all_to_all.18.reduce_sub_computation | reduce | bytes 131076 | tf_op jit(solution)/shard_map/all_to_all | solution.py:139
  73.9 0.7 reshape_reshape.14
  74.6 1.1 %fusion.201 = f32[32,64]{1,0:T(8,128)S(1)} fusion(f32[256,64]{1,0:T(8,128)} %reshape_reshape.14, s32[32]{0:T(128)} %eq.63), kind=kOutput, calls=%fused_computation.280 | convolution fusion | flops 6299648 | bytes 73856 | tf_op jit(solution)/shard_map/dot_general | solution.py:120
  76.5 1.3 %fusion.29 = f32[1,512]{1,0:T(1,128)S(1)} fusion(f32[512,1]{0,1:T(1,128)S(1)} %bitcast.98, s32[512]{0:T(512)} %copy-done.8), kind=kOutput, calls=%fused_computation.41 | convolution fusion | flops 3407872 | bytes 6144 | tf_op jit(solution)/shard_map/dot_general | solution.py:120
  77.8 0.7 broadcast_in_dim.58
  78.5 2.8 %all-to-all-start.3 = ((f32[32,1,512]{2,1,0:T(1,128)}), f32[32,1,512]{2,1,0:T(1,128)S(1)}, u32[]{:S(2)}, u32[]{:S(2)}) async-start(f32[32,1,512]{2,1,0:T(1,128)} %broadcast_in_dim.58), calls=%async_computation.3 | async-start | bytes 131072 | tf_op jit(solution)/shard_map/all_to_all | solution.py:139
  81.3 7.4 %all-to-all-done.3 = f32[32,1,512]{2,1,0:T(1,128)S(1)} async-done(((f32[32,1,512]{2,1,0:T(1,128)}), f32[32,1,512]{2,1,0:T(1,128)S(1)}, u32[]{:S(2)}, u32[]{:S(2)}) %all-to-all-start.3) | async-done | bytes 65568 | tf_op jit(solution)/shard_map/all_to_all | solution.py:139
  89.6 1.8 %fusion.4 = f32[6,3264]{1,0:T(8,128)S(1)} fusion(f32[6,204]{1,0:T(8,128)S(1)} %reshape.125, s32[204]{0:T(256)S(1)} %copy-done.11, s32[204]{0:T(256)S(1)} %get-tuple-element.37, s32[3264]{0:T(1024)S(1)} %get-tuple-element.20, s32[3264]{0:T(1024)S(1)} %get-tuple-element.21, s32[204]{0:T(256)S(1)} %copy-done.10, s32[204]{0:T(256)S(1)} %get-tuple-element.38, ...), kind=kOutput, calls=%fused_computation.10 | convolution fusion | flops 58595328 | bytes 145657 | tf_op jit(solution)/shard_map/dot_general | solution.py:120
  94.0 0.8 slice.225
  (108 shorter events, 16.2 us)
Async XLA Ops:
  1.7 9.5 %copy-start = (f32[8,64,256]{2,1,0:T(8,128)S(1)}, f32[8,64,256]{2,1,0:T(8,128)}, u32[]{:S(2)}) copy-start(f32[8,64,256]{2,1,0:T(8,128)} %param.10) | copy-start | bytes 1572868
  1.9 10.9 %copy-start.3 = (f32[16,16,128]{2,1,0:T(8,128)S(1)}, f32[16,16,128]{2,1,0:T(8,128)}, u32[]{:S(2)}) copy-start(f32[16,16,128]{2,1,0:T(8,128)} %param.8) | copy-start | bytes 393220
  1.9 10.9 %copy-start.4 = (f32[16,16,128]{2,1,0:T(8,128)S(1)}, f32[16,16,128]{2,1,0:T(8,128)}, u32[]{:S(2)}) copy-start(f32[16,16,128]{2,1,0:T(8,128)} %param.7) | copy-start | bytes 393220
  1.9 10.9 %copy-start.5 = (f32[16,16,128]{2,1,0:T(8,128)S(1)}, f32[16,16,128]{2,1,0:T(8,128)}, u32[]{:S(2)}) copy-start(f32[16,16,128]{2,1,0:T(8,128)} %param.6) | copy-start | bytes 393220
  2.1 9.9 %collective-permute-start = (f32[24,128]{1,0:T(8,128)S(1)}, f32[24,128]{1,0:T(8,128)S(1)}, u32[]{:S(2)}, u32[]{:S(2)}) collective-permute-start(f32[24,128]{1,0:T(8,128)S(1)} %reshape.111), channel_id=1, source_target_pairs={{8,16},{16,8},{9,17},{17,9},{10,18},{18,10},{11,19},{19,11},{12,20... | collective-permute-start | bytes 36872 | tf_op jit(solution)/shard_map/ppermute | solution.py:28
  3.0 9.0 %collective-permute-start.1 = (f32[24,128]{1,0:T(8,128)S(1)}, f32[24,128]{1,0:T(8,128)S(1)}, u32[]{:S(2)}, u32[]{:S(2)}) collective-permute-start(f32[24,128]{1,0:T(8,128)S(1)} %reshape.112), channel_id=1, source_target_pairs={{0,8},{8,0},{16,24},{24,16},{1,9},{9,1},{17,25},{25,17},{2,10},{10... | collective-permute-start | bytes 36872 | tf_op jit(solution)/shard_map/ppermute | solution.py:28
  13.7 4.9 %collective-permute-start.2 = (f32[3,16,544]{2,1,0:T(8,128)S(1)}, f32[3,16,544]{2,1,0:T(8,128)S(1)}, u32[]{:S(2)}, u32[]{:S(2)}) collective-permute-start(f32[3,16,544]{2,1,0:T(8,128)S(1)} %slice_select_fusion.4), channel_id=1, source_target_pairs={{0,1},{1,0},{2,3},{3,2},{4,5},{5,4},{6,7},{7,6},{8,9},{9,8},{10,11... | collective-permute-start | bytes 313352 | tf_op jit(solution)/shard_map/ppermute | solution.py:29
  19.2 4.0 %collective-permute-start.3 = (f32[306,128]{1,0:T(8,128)S(1)}, f32[306,128]{1,0:T(8,128)S(1)}, u32[]{:S(2)}, u32[]{:S(2)}) collective-permute-start(f32[306,128]{1,0:T(8,128)S(1)} %reshape.114), channel_id=1, source_target_pairs={{2,4},{4,2},{3,5},{5,3},{10,12},{12,10},{11,13},{13,11},{18,20},{2... | collective-permute-start | bytes 470024 | tf_op jit(solution)/shard_map/ppermute | solution.py:28
  20.0 4.0 %collective-permute-start.4 = (f32[306,128]{1,0:T(8,128)S(1)}, f32[306,128]{1,0:T(8,128)S(1)}, u32[]{:S(2)}, u32[]{:S(2)}) collective-permute-start(f32[306,128]{1,0:T(8,128)S(1)} %reshape.115), channel_id=1, source_target_pairs={{0,2},{2,0},{4,6},{6,4},{1,3},{3,1},{5,7},{7,5},{8,10},{10,8},{12,... | collective-permute-start | bytes 470024 | tf_op jit(solution)/shard_map/ppermute | solution.py:28
  23.1 5.7 %copy-start.8 = (s32[512]{0:T(512)}, s32[512]{0:T(512)S(1)}, u32[]{:S(2)}) copy-start(s32[512]{0:T(512)S(1)} %eq.59) | copy-start | bytes 6148
  25.6 0.7 copy-start.1
  25.6 0.7 copy-start.12
  25.6 0.7 copy-start.13
  26.3 2.2 %copy-start.14 = (s32[4]{0:T(128)S(1)}, s32[4]{0:T(128)}, u32[]{:S(2)}) copy-start(s32[4]{0:T(128)} %get-tuple-element.32) | copy-start | bytes 52
  26.3 9.1 %copy-start.7 = (s32[8,4]{0,1:T(4,128)S(1)}, s32[8,4]{0,1:T(4,128)}, u32[]{:S(2)}) copy-start(s32[8,4]{0,1:T(4,128)} %param.11) | copy-start | bytes 388
  29.9 13.1 %all-to-all-start = ((f32[32,1,512]{2,1,0:T(1,128)}), f32[32,1,512]{2,1,0:T(1,128)}, u32[]{:S(2)}, u32[]{:S(2)}) async-start(f32[32,1,512]{2,1,0:T(1,128)} %broadcast_in_dim.55), calls=%async_computation | async-start | bytes 131072 | tf_op jit(solution)/shard_map/all_to_all | solution.py:139
  46.6 0.6 copy-start.6
  62.0 10.9 %all-to-all-start.2 = ((f32[32,1,512]{2,1,0:T(1,128)}), f32[32,1,512]{2,1,0:T(1,128)}, u32[]{:S(2)}, u32[]{:S(2)}) async-start(f32[32,1,512]{2,1,0:T(1,128)} %broadcast_in_dim.57), calls=%async_computation.2 | async-start | bytes 131072 | tf_op jit(solution)/shard_map/all_to_all | solution.py:139
  76.5 13.1 %copy-start.9 = (f32[512]{0:T(512)}, f32[512]{0:T(512)S(1)}, u32[]{:S(2)}) copy-start(f32[512]{0:T(512)S(1)} %divide_add_fusion) | copy-start | bytes 6148
  76.5 13.1 %copy-start.10 = (s32[204]{0:T(256)S(1)}, s32[204]{0:T(256)}, u32[]{:S(2)}) copy-start(s32[204]{0:T(256)} %get-tuple-element.33) | copy-start | bytes 2452
  76.5 13.1 %copy-start.11 = (s32[204]{0:T(256)S(1)}, s32[204]{0:T(256)}, u32[]{:S(2)}) copy-start(s32[204]{0:T(256)} %get-tuple-element.34) | copy-start | bytes 2452
  76.5 13.1 %copy-start.15 = (pred[204]{0:T(512)(128)(4,1)S(1)}, pred[204]{0:T(512)(128)(4,1)}, u32[]{:S(2)}) copy-start(pred[204]{0:T(512)(128)(4,1)} %get-tuple-element.35) | copy-start | bytes 616
  76.5 13.1 %copy-start.16 = (pred[204]{0:T(512)(128)(4,1)S(1)}, pred[204]{0:T(512)(128)(4,1)}, u32[]{:S(2)}) copy-start(pred[204]{0:T(512)(128)(4,1)} %get-tuple-element.36) | copy-start | bytes 616
  78.5 10.2 %all-to-all-start.3 = ((f32[32,1,512]{2,1,0:T(1,128)}), f32[32,1,512]{2,1,0:T(1,128)S(1)}, u32[]{:S(2)}, u32[]{:S(2)}) async-start(f32[32,1,512]{2,1,0:T(1,128)} %broadcast_in_dim.58), calls=%async_computation.3 | async-start | bytes 131072 | tf_op jit(solution)/shard_map/all_to_all | solution.py:139
  89.6 2.3 %copy-start.2 = (f32[24,3264]{1,0:T(8,128)S(1)}, f32[24,3264]{1,0:T(8,128)}, u32[]{:S(2)}) copy-start(f32[24,3264]{1,0:T(8,128)} %copy-done.1) | copy-start | bytes 940036

commit v13 on v12

--- a/solution.py
+++ b/solution.py
@@ -120,6 +120,24 @@
     return jnp.dot(left, right, precision=lax.Precision.HIGHEST)
 
 
+def split_parts(values):
+    high = lax.reduce_precision(values, exponent_bits=8, mantissa_bits=7)
+    rest = values - high
+    middle = lax.reduce_precision(rest, exponent_bits=8, mantissa_bits=7)
+    low = rest - middle
+    return tuple(part.astype(jnp.bfloat16) for part in (high, middle, low))
+
+
+def select_dot(left, right, ones_left):
+    if ones_left:
+        ones = left.astype(jnp.bfloat16)
+        parts = [jnp.dot(ones, part, preferred_element_type=jnp.float32) for part in split_parts(right)]
+    else:
+        ones = right.astype(jnp.bfloat16)
+        parts = [jnp.dot(part, ones, preferred_element_type=jnp.float32) for part in split_parts(left)]
+    return (parts[0] + parts[1]) + parts[2]
+
+
 def box_matrix(boxes, cells, stride, offset, live, inner=None):
     box = lax.broadcasted_iota(jnp.int32, (boxes, cells), 0)
     cell = lax.broadcasted_iota(jnp.int32, (boxes, cells), 1)
@@ -172,14 +190,14 @@
     live = lax.axis_index("grp") >= 0
     pick_x = box_matrix(bx, rows, 1, HALO, live)
     pick_yz = box_matrix(by * bz, span_y * span_z, span_z, HALO, live, bz).T
-    box_totals = dot(pick_x, dot(smoothed, pick_yz)).reshape(-1)
+    box_totals = select_dot(pick_x, select_dot(smoothed, pick_yz, False), True).reshape(-1)
     corner_ids = aggregate_ids[::BOX, ::BOX].reshape(bx * by, size_z).astype(source.dtype)
     first_z = lax.broadcasted_iota(jnp.int32, (size_z, bz), 0) == BOX * lax.broadcasted_iota(jnp.int32, (size_z, bz), 1)
     box_labels = dot(corner_ids, first_z.astype(source.dtype)).astype(jnp.int32).reshape(-1)
     placed = (
         box_labels[:, None] == lax.broadcasted_iota(jnp.int32, (box_labels.shape[0],) * 2, 1)
     ).astype(source.dtype)
-    coarse_rhs = dot(box_totals[None, :], placed)[0]
+    coarse_rhs = select_dot(box_totals[None, :], placed, False)[0]
     eye = lax.broadcasted_iota(jnp.int32, (64, 64), 0) == lax.broadcasted_iota(jnp.int32, (64, 64), 1)
     coarse_diag = jnp.sum(jnp.where(eye[None], coarse_values[:, :, :64], 0.0), axis=2).reshape(-1)
     block_rows = coarse_values.shape[0]
@@ -193,14 +211,14 @@
     coarse_error = coarse_rhs / coarse_diag
     for sweep_number in range(CITER - 1):
         pooled = everyone(coarse_error)
-        blocks = dot(pick, pooled.reshape(tables, 64))
+        blocks = select_dot(pick, pooled.reshape(tables, 64), True)
         blocks = blocks.reshape(block_rows, -1)
         applied = jnp.einsum(
             "bim,bm->bi", coarse_values, blocks, precision=lax.Precision.HIGHEST
         ).reshape(-1)
         coarse_error = coarse_error + (coarse_rhs - applied) / coarse_diag
 
-    small = dot(placed, coarse_error[:, None]).reshape(-1)
+    small = select_dot(placed, coarse_error[:, None], True).reshape(-1)
     every = everyone(small).reshape(groups, grid_x, grid_y, bx, by, bz)
     boxes = every.transpose(1, 3, 2, 4, 0, 5).reshape(grid_x * bx, grid_y * by, groups * bz)
     boxes = jnp.pad(boxes, 1)
@@ -212,7 +230,7 @@
     window = window.reshape(bx + 2, (by + 2) * (bz + 2))
     spread_x = box_matrix(bx + 2, rows, 1, 0, live).T
     spread_yz = box_matrix((by + 2) * (bz + 2), span_y * span_z, span_z, 0, live, bz + 2)
-    lifted = dot(spread_x, dot(window, spread_yz))
+    lifted = select_dot(spread_x, select_dot(window, spread_yz, False), True)
     solution = jnp.where(mask, solution + (lifted - WEIGHT * op(lifted) / diagonal), 0.0)
     for sweep_number in range(NU):
         solution = jnp.where(mask, solution + WEIGHT * (src - op(solution)) / diagonal, 0.0)

time: 95.4 us -> 116 us (1.22)
  matrix products: 11.5 us -> 27.6 us
  local copies, waits for them, and re-layouts: 12.4 us -> 15.7 us
  other arithmetic: 11.6 us -> 14.3 us
    dot_general x0 -> x27, matrix products: none -> 25.9 us  [the longest x9 13.9 us: select_dot(): jnp.dot(part, ones, preferred_element_type=jnp.float32)]
    dot_general x10 -> x1, matrix products: 9.88 us -> 0.13 us  [dot(): return jnp.dot(left, right, precision=lax.Precision.HIGHEST)]
    reshape x3, local copies, waits for them, and re-layouts: 0.24 us -> 2.39 us  [local(): blocks = blocks.reshape(block_rows, -1)]
  transfers between devices with their start and end apart: 8 -> 8, of which waited for: 5 -> 5; matrix products, arithmetic and copies ran while one was open for 6% -> 5% of each run, Pallas kernels for 0% -> 0%
where the time goes in v13:
time: 116 us; the launch traced here: 115 us
  matrix products  27.6 us (24%)
  waiting for transfers between devices  24.3 us (21%)
  starting transfers between devices  22.5 us (19%)
  local copies, waits for them, and re-layouts  15.7 us (14%)
  other arithmetic  14.3 us (12%)
  blocking collectives  9.3 us (8%)
  between operations  1.17 us (1%)
    all_to_all x3, waiting for transfers between devices, everyone(): return lax.all_to_all(copies, ALL_AXES, 0, 0, tiled=True).reshape(-1)  20.1 us
    dot_general x9, matrix products, select_dot(): jnp.dot(part, ones, preferred_element_type=jnp.float32)  13.9 us
    dot_general x18, matrix products, select_dot(): jnp.dot(ones, part, preferred_element_type=jnp.float32)  12 us
    all_to_all x3, starting transfers between devices, everyone(): return lax.all_to_all(copies, ALL_AXES, 0, 0, tiled=True).reshape(-1)  10.6 us
    ppermute x4, starting transfers between devices, permute(): return lax.ppermute(slab.reshape(-1, 128), axis, pairs).reshape(slab.shape)  10.4 us
    all_to_all x1, blocking collectives, everyone(): return lax.all_to_all(copies, ALL_AXES, 0, 0, tiled=True).reshape(-1)  9.3 us
    ppermute x1, waiting for transfers between devices, permute(): return lax.ppermute(slab, axis, pairs)  3.38 us
    another operation x3, local copies, waits for them, and re-layouts, local(): blocks = select_dot(pick, pooled.reshape(tables, 64), True)  2.77 us
  transfers between devices with their start and end apart: 8, of which 5 were waited for; matrix products, arithmetic and copies ran while one was open for 5% of the time, Pallas kernels for 0%

profile of v13, /device:TPU:0, one launch (start us, length us, event | category | flops | bytes accessed | tf_op | source)
XLA Modules:
  0.0 114.8 jit_solution(10178870662731219092)
XLA Ops:
  0.6 1.1 pad_maximum_fusion.2
  3.0 5.9 %collective-permute-start.1 = (f32[24,128]{1,0:T(8,128)S(1)}, f32[24,128]{1,0:T(8,128)S(1)}, u32[]{:S(2)}, u32[]{:S(2)}) collective-permute-start(f32[24,128]{1,0:T(8,128)S(1)} %reshape.200), channel_id=1, source_target_pairs={{0,8},{8,0},{16,24},{24,16},{1,9},{9,1},{17,25},{25,17},{2,10},{10... | collective-permute-start | bytes 36872 | tf_op jit(solution)/shard_map/ppermute | solution.py:28
  9.5 1.6 %slice.183 = s32[4,4,128]{2,1,0:T(4,128)S(1)} slice(s32[16,16,128]{2,1,0:T(8,128)} %param.9), slice={[0:16:4], [0:16:4], [0:128:1]} | slice | bytes 16384 | tf_op jit(solution)/shard_map/slice | solution.py:194
  13.7 1.6 %collective-permute-start.2 = (f32[3,16,544]{2,1,0:T(8,128)S(1)}, f32[3,16,544]{2,1,0:T(8,128)S(1)}, u32[]{:S(2)}, u32[]{:S(2)}) collective-permute-start(f32[3,16,544]{2,1,0:T(8,128)S(1)} %slice_select_fusion.4), channel_id=1, source_target_pairs={{0,1},{1,0},{2,3},{3,2},{4,5},{5,4},{6,7},{7,6},{8,9},{9,8},{10,11... | collective-permute-start | bytes 313352 | tf_op jit(solution)/shard_map/ppermute | solution.py:29
  15.3 3.4 %collective-permute-done.2 = f32[3,16,544]{2,1,0:T(8,128)S(1)} collective-permute-done((f32[3,16,544]{2,1,0:T(8,128)S(1)}, f32[3,16,544]{2,1,0:T(8,128)S(1)}, u32[]{:S(2)}, u32[]{:S(2)}) %collective-permute-start.2) | collective-permute-done | bytes 104480 | tf_op jit(solution)/shard_map/ppermute | solution.py:29
  19.2 0.9 collective-permute-start.3
  20.2 2.9 %collective-permute-start.4 = (f32[306,128]{1,0:T(8,128)S(1)}, f32[306,128]{1,0:T(8,128)S(1)}, u32[]{:S(2)}, u32[]{:S(2)}) collective-permute-start(f32[306,128]{1,0:T(8,128)S(1)} %reshape.203), channel_id=1, source_target_pairs={{0,2},{2,0},{4,6},{6,4},{1,3},{3,1},{5,7},{7,5},{8,10},{10,8},{12,... | collective-permute-start | bytes 470024 | tf_op jit(solution)/shard_map/ppermute | solution.py:28
  27.2 2.8 %fusion.177 = f32[24,128]{1,0:T(8,128)S(1)} fusion(f32[24,3264]{1,0:T(8,128)S(1)} %fusion.87, s32[128]{0:T(128)S(1)} %get-tuple-element.37, s32[128]{0:T(128)S(1)} %get-tuple-element.38, s32[3264]{0:T(1024)S(1)} %get-tuple-element.29, s32[3264]{0:T(1024)S(1)} %get-tuple-element.30, s32[128]{0:T(128)S(1)} %get-tuple-element.36, s32[128]{0:T(128)S(1)} %copy-done.26, ...), kind=kOutput, calls=%fused_computation.282 | convolution fusion | flops 28566528 | bytes 386689 | tf_op jit(solution)/shard_map/dot_general | solution.py:137
  30.0 2.8 %convolution_add_fusion.11 = f32[24,128]{1,0:T(8,128)S(1)} fusion(f32[24,128]{1,0:T(8,128)S(1)} %fusion.177, f32[24,3264]{1,0:T(8,128)S(1)} %fusion.87, s32[128]{0:T(128)S(1)} %get-tuple-element.37, s32[128]{0:T(128)S(1)} %get-tuple-element.38, s32[3264]{0:T(1024)S(1)} %get-tuple-element.29, s32[3264]{0:T(1024)S(1)} %get-tuple-element.30, ...), kind=kOutput, calls=%fused_computation.35 | convolution fusion | flops 28726272 | bytes 398977 | tf_op jit(solution)/shard_map/dot_general | solution.py:137
  32.9 2.8 %convolution_add_fusion.10 = f32[24,128]{1,0:T(8,128)S(1)} fusion(f32[24,128]{1,0:T(8,128)S(1)} %convolution_add_fusion.11, f32[24,3264]{1,0:T(8,128)S(1)} %fusion.87, s32[128]{0:T(128)S(1)} %get-tuple-element.37, s32[128]{0:T(128)S(1)} %get-tuple-element.38, s32[3264]{0:T(1024)S(1)} %get-tuple-element.29, s32[3264]{0:T(1024)S(1)} %get-tuple-element.30, ...), kind=kOutput, calls=%fused_computation.34 | convolution fusion | flops 28804608 | bytes 398977 | tf_op jit(solution)/shard_map/dot_general | solution.py:137
  38.3 5.4 %all-to-all-start = ((f32[32,1,512]{2,1,0:T(1,128)}), f32[32,1,512]{2,1,0:T(1,128)S(1)}, u32[]{:S(2)}, u32[]{:S(2)}) async-start(f32[32,1,512]{2,1,0:T(1,128)} %broadcast_in_dim.55), calls=%async_computation | async-start | bytes 131072 | tf_op jit(solution)/shard_map/all_to_all | solution.py:157
  44.4 6.7 %all-to-all-done = f32[32,1,512]{2,1,0:T(1,128)S(1)} async-done(((f32[32,1,512]{2,1,0:T(1,128)}), f32[32,1,512]{2,1,0:T(1,128)S(1)}, u32[]{:S(2)}, u32[]{:S(2)}) %all-to-all-start) | async-done | bytes 65568 | tf_op jit(solution)/shard_map/all_to_all | solution.py:157
  51.9 0.9 reshape_reshape.12
  52.8 0.8 fusion.185
  53.6 0.8 convolution_add_fusion.9
  54.5 1.4 %convolution_add_fusion.8 = f32[32,64]{1,0:T(8,128)} fusion(f32[32,64]{1,0:T(8,128)S(1)} %convolution_add_fusion.9, f32[256,64]{1,0:T(8,128)S(1)} %reshape_reshape.12, s32[32]{0:T(128)} %eq.63), kind=kOutput, calls=%fused_computation.32 | convolution fusion | flops 1157120 | bytes 82048 | tf_op jit(solution)/shard_map/dot_general | solution.py:134
  58.6 9.3 %all_to_all.24 = f32[32,1,512]{2,1,0:T(1,128)S(1)} all-to-all(f32[32,1,512]{2,1,0:T(1,128)S(1)} %broadcast_in_dim.56), channel_id=1, replica_groups=mesh['grp'=4,'gx'=4,'gy'=2] {'grp','gx','gy'}, dimensions={0} | all-to-all | bytes 131072 | tf_op jit(solution)/shard_map/all_to_all | solution.py:157
  68.7 0.9 reshape_reshape.13
  69.6 0.8 fusion.186
  70.4 0.8 convolution_add_fusion.7
  71.3 1.4 %convolution_add_fusion.6 = f32[32,64]{1,0:T(8,128)} fusion(f32[32,64]{1,0:T(8,128)S(1)} %convolution_add_fusion.7, f32[256,64]{1,0:T(8,128)S(1)} %reshape_reshape.13, s32[32]{0:T(128)} %eq.63), kind=kOutput, calls=%fused_computation.30 | convolution fusion | flops 1157120 | bytes 82048 | tf_op jit(solution)/shard_map/dot_general | solution.py:134
  75.5 2.6 %all-to-all-start.2 = ((f32[32,1,512]{2,1,0:T(1,128)}), f32[32,1,512]{2,1,0:T(1,128)S(1)}, u32[]{:S(2)}, u32[]{:S(2)}) async-start(f32[32,1,512]{2,1,0:T(1,128)} %broadcast_in_dim.57), calls=%async_computation.2 | async-start | bytes 131072 | tf_op jit(solution)/shard_map/all_to_all | solution.py:157
  79.3 6.4 %all-to-all-done.2 = f32[32,1,512]{2,1,0:T(1,128)S(1)} async-done(((f32[32,1,512]{2,1,0:T(1,128)}), f32[32,1,512]{2,1,0:T(1,128)S(1)}, u32[]{:S(2)}, u32[]{:S(2)}) %all-to-all-start.2) | async-done | bytes 65568 | tf_op jit(solution)/shard_map/all_to_all | solution.py:157
  86.4 0.9 reshape_reshape.14
  88.2 0.8 convolution_add_fusion.5
  89.0 1.4 %convolution_add_fusion.4 = f32[32,64]{1,0:T(8,128)} fusion(f32[32,64]{1,0:T(8,128)S(1)} %convolution_add_fusion.5, f32[256,64]{1,0:T(8,128)S(1)} %reshape_reshape.14, s32[32]{0:T(128)} %eq.63), kind=kOutput, calls=%fused_computation.28 | convolution fusion | flops 1157120 | bytes 82048 | tf_op jit(solution)/shard_map/dot_general | solution.py:134
  92.6 1.0 fusion.13
  95.0 2.6 %all-to-all-start.3 = ((f32[32,1,512]{2,1,0:T(1,128)}), f32[32,1,512]{2,1,0:T(1,128)S(1)}, u32[]{:S(2)}, u32[]{:S(2)}) async-start(f32[32,1,512]{2,1,0:T(1,128)} %broadcast_in_dim.58), calls=%async_computation.3 | async-start | bytes 131072 | tf_op jit(solution)/shard_map/all_to_all | solution.py:157
  98.1 7.0 %all-to-all-done.3 = f32[32,1,512]{2,1,0:T(1,128)S(1)} async-done(((f32[32,1,512]{2,1,0:T(1,128)}), f32[32,1,512]{2,1,0:T(1,128)S(1)}, u32[]{:S(2)}, u32[]{:S(2)}) %all-to-all-start.3) | async-done | bytes 65568 | tf_op jit(solution)/shard_map/all_to_all | solution.py:157
  106.2 2.1 %fusion.222 = f32[6,3264]{1,0:T(8,128)S(1)} fusion(f32[6,204]{1,0:T(8,128)S(1)} %reshape.212, s32[204]{0:T(256)} %get-tuple-element.43, s32[204]{0:T(256)S(1)} %copy-done.24, s32[3264]{0:T(1024)S(1)} %copy-done.4, s32[3264]{0:T(1024)S(1)} %copy-done.6, s32[204]{0:T(256)S(1)} %copy-done.22, s32[204]{0:T(256)} %get-tuple-element.47, ...), kind=kOutput, calls=%fused_computation.353 | convolution fusion | flops 19978128 | bytes 145657 | tf_op jit(solution)/shard_map/dot_general | solution.py:137
  108.3 1.3 %convolution_add_fusion.3 = f32[6,3264]{1,0:T(8,128)S(1)} fusion(f32[6,3264]{1,0:T(8,128)S(1)} %fusion.222, f32[6,204]{1,0:T(8,128)S(1)} %reshape.212, s32[204]{0:T(256)S(1)} %copy-done.23, s32[204]{0:T(256)S(1)} %copy-done.24, s32[3264]{0:T(1024)S(1)} %copy-done.4, s32[3264]{0:T(1024)S(1)} %copy-done.6, s32[204]{0:T(256)S(1)} %copy-done.22, ...), kind=kOutput, calls=%fused_computation.3 | convolution fusion | flops 20000160 | bytes 223993 | tf_op jit(solution)/shard_map/dot_general | solution.py:137
  109.6 1.4 %convolution_add_fusion.2 = f32[6,3264]{1,0:T(8,128)S(1)} fusion(f32[6,3264]{1,0:T(8,128)S(1)} %convolution_add_fusion.3, f32[6,204]{1,0:T(8,128)S(1)} %reshape.212, s32[204]{0:T(256)S(1)} %copy-done.23, s32[204]{0:T(256)S(1)} %copy-done.24, s32[3264]{0:T(1024)S(1)} %copy-done.4, s32[3264]{0:T(1024)S(1)} %copy-done.6, s32[204]{0:T(256)S(1)} %copy-done.22, ...), kind=kOutput, calls=%fused_computation.2 | convolution fusion | flops 20001384 | bytes 223993 | tf_op jit(solution)/shard_map/dot_general | solution.py:137
  (163 shorter events, 31.1 us)
Async XLA Ops:
  1.7 9.5 %copy-start = (f32[8,64,256]{2,1,0:T(8,128)S(1)}, f32[8,64,256]{2,1,0:T(8,128)}, u32[]{:S(2)}) copy-start(f32[8,64,256]{2,1,0:T(8,128)} %param.10) | copy-start | bytes 1572868
  1.9 10.9 %copy-start.9 = (f32[16,16,128]{2,1,0:T(8,128)S(1)}, f32[16,16,128]{2,1,0:T(8,128)}, u32[]{:S(2)}) copy-start(f32[16,16,128]{2,1,0:T(8,128)} %param.8) | copy-start | bytes 393220
  1.9 10.9 %copy-start.10 = (f32[16,16,128]{2,1,0:T(8,128)S(1)}, f32[16,16,128]{2,1,0:T(8,128)}, u32[]{:S(2)}) copy-start(f32[16,16,128]{2,1,0:T(8,128)} %param.7) | copy-start | bytes 393220
  1.9 10.9 %copy-start.11 = (f32[16,16,128]{2,1,0:T(8,128)S(1)}, f32[16,16,128]{2,1,0:T(8,128)}, u32[]{:S(2)}) copy-start(f32[16,16,128]{2,1,0:T(8,128)} %param.6) | copy-start | bytes 393220
  2.1 9.8 %collective-permute-start = (f32[24,128]{1,0:T(8,128)S(1)}, f32[24,128]{1,0:T(8,128)S(1)}, u32[]{:S(2)}, u32[]{:S(2)}) collective-permute-start(f32[24,128]{1,0:T(8,128)S(1)} %reshape.199), channel_id=1, source_target_pairs={{8,16},{16,8},{9,17},{17,9},{10,18},{18,10},{11,19},{19,11},{12,20... | collective-permute-start | bytes 36872 | tf_op jit(solution)/shard_map/ppermute | solution.py:28
  3.0 8.9 %collective-permute-start.1 = (f32[24,128]{1,0:T(8,128)S(1)}, f32[24,128]{1,0:T(8,128)S(1)}, u32[]{:S(2)}, u32[]{:S(2)}) collective-permute-start(f32[24,128]{1,0:T(8,128)S(1)} %reshape.200), channel_id=1, source_target_pairs={{0,8},{8,0},{16,24},{24,16},{1,9},{9,1},{17,25},{25,17},{2,10},{10... | collective-permute-start | bytes 36872 | tf_op jit(solution)/shard_map/ppermute | solution.py:28
  8.9 23.9 %copy-start.3 = (s32[3264]{0:T(1024)}, s32[3264]{0:T(1024)S(1)}, u32[]{:S(2)}) copy-start(s32[3264]{0:T(1024)S(1)} %get-tuple-element.29) | copy-start | bytes 39172
  13.7 4.9 %collective-permute-start.2 = (f32[3,16,544]{2,1,0:T(8,128)S(1)}, f32[3,16,544]{2,1,0:T(8,128)S(1)}, u32[]{:S(2)}, u32[]{:S(2)}) collective-permute-start(f32[3,16,544]{2,1,0:T(8,128)S(1)} %slice_select_fusion.4), channel_id=1, source_target_pairs={{0,1},{1,0},{2,3},{3,2},{4,5},{5,4},{6,7},{7,6},{8,9},{9,8},{10,11... | collective-permute-start | bytes 313352 | tf_op jit(solution)/shard_map/ppermute | solution.py:29
  19.2 4.2 %collective-permute-start.3 = (f32[306,128]{1,0:T(8,128)S(1)}, f32[306,128]{1,0:T(8,128)S(1)}, u32[]{:S(2)}, u32[]{:S(2)}) collective-permute-start(f32[306,128]{1,0:T(8,128)S(1)} %reshape.202), channel_id=1, source_target_pairs={{2,4},{4,2},{3,5},{5,3},{10,12},{12,10},{11,13},{13,11},{18,20},{2... | collective-permute-start | bytes 470024 | tf_op jit(solution)/shard_map/ppermute | solution.py:28
  20.2 4.0 %collective-permute-start.4 = (f32[306,128]{1,0:T(8,128)S(1)}, f32[306,128]{1,0:T(8,128)S(1)}, u32[]{:S(2)}, u32[]{:S(2)}) collective-permute-start(f32[306,128]{1,0:T(8,128)S(1)} %reshape.203), channel_id=1, source_target_pairs={{0,2},{2,0},{4,6},{6,4},{1,3},{3,1},{5,7},{7,5},{8,10},{10,8},{12,... | collective-permute-start | bytes 470024 | tf_op jit(solution)/shard_map/ppermute | solution.py:28
  23.1 2.6 %copy-start.13 = (pred[24]{0:T(512)(128)(4,1)}, pred[24]{0:T(512)(128)(4,1)S(1)}, u32[]{:S(2)}) copy-start(pred[24]{0:T(512)(128)(4,1)S(1)} %compare_and_fusion.4) | copy-start | bytes 76
  23.2 13.6 %copy-start.20 = (s32[512]{0:T(512)}, s32[512]{0:T(512)S(1)}, u32[]{:S(2)}) copy-start(s32[512]{0:T(512)S(1)} %eq.59) | copy-start | bytes 6148
  23.3 13.7 %copy-start.12 = (f32[512]{0:T(512)}, f32[512]{0:T(512)S(1)}, u32[]{:S(2)}) copy-start(f32[512]{0:T(512)S(1)} %reshape.204) | copy-start | bytes 6148
  23.3 9.5 %copy-start.5 = (s32[3264]{0:T(1024)}, s32[3264]{0:T(1024)S(1)}, u32[]{:S(2)}) copy-start(s32[3264]{0:T(1024)S(1)} %get-tuple-element.30) | copy-start | bytes 39172
  23.3 9.5 %copy-start.7 = (s32[3264]{0:T(1024)}, s32[3264]{0:T(1024)S(1)}, u32[]{:S(2)}) copy-start(s32[3264]{0:T(1024)S(1)} %get-tuple-element.31) | copy-start | bytes 39172
  32.8 2.8 %copy-start.27 = (s32[4]{0:T(128)S(1)}, s32[4]{0:T(128)}, u32[]{:S(2)}) copy-start(s32[4]{0:T(128)} %get-tuple-element.40) | copy-start | bytes 52
  32.9 2.8 %copy-start.28 = (s32[4]{0:T(128)S(1)}, s32[4]{0:T(128)}, u32[]{:S(2)}) copy-start(s32[4]{0:T(128)} %get-tuple-element.41) | copy-start | bytes 52
  35.6 8.1 %copy-start.19 = (s32[8,4]{0,1:T(4,128)S(1)}, s32[8,4]{0,1:T(4,128)}, u32[]{:S(2)}) copy-start(s32[8,4]{0,1:T(4,128)} %param.11) | copy-start | bytes 388
  38.3 12.8 %all-to-all-start = ((f32[32,1,512]{2,1,0:T(1,128)}), f32[32,1,512]{2,1,0:T(1,128)S(1)}, u32[]{:S(2)}, u32[]{:S(2)}) async-start(f32[32,1,512]{2,1,0:T(1,128)} %broadcast_in_dim.55), calls=%async_computation | async-start | bytes 131072 | tf_op jit(solution)/shard_map/all_to_all | solution.py:157
  75.5 10.2 %all-to-all-start.2 = ((f32[32,1,512]{2,1,0:T(1,128)}), f32[32,1,512]{2,1,0:T(1,128)S(1)}, u32[]{:S(2)}, u32[]{:S(2)}) async-start(f32[32,1,512]{2,1,0:T(1,128)} %broadcast_in_dim.57), calls=%async_computation.2 | async-start | bytes 131072 | tf_op jit(solution)/shard_map/all_to_all | solution.py:157
  90.5 3.1 %copy-start.21 = (s32[512]{0:T(512)S(1)}, s32[512]{0:T(512)}, u32[]{:S(2)}) copy-start(s32[512]{0:T(512)} %copy-done.20) | copy-start | bytes 6148
  92.6 12.9 %copy-start.18 = (f32[512]{0:T(512)}, f32[512]{0:T(512)S(1)}, u32[]{:S(2)}) copy-start(f32[512]{0:T(512)S(1)} %get-tuple-element.3) | copy-start | bytes 6148
  93.9 12.1 %copy-start.4 = (s32[3264]{0:T(1024)S(1)}, s32[3264]{0:T(1024)}, u32[]{:S(2)}) copy-start(s32[3264]{0:T(1024)} %copy-done.3) | copy-start | bytes 39172
  93.9 12.1 %copy-start.6 = (s32[3264]{0:T(1024)S(1)}, s32[3264]{0:T(1024)}, u32[]{:S(2)}) copy-start(s32[3264]{0:T(1024)} %copy-done.5) | copy-start | bytes 39172
  93.9 12.1 %copy-start.8 = (s32[3264]{0:T(1024)S(1)}, s32[3264]{0:T(1024)}, u32[]{:S(2)}) copy-start(s32[3264]{0:T(1024)} %copy-done.7) | copy-start | bytes 39172
  94.3 11.8 %copy-start.22 = (s32[204]{0:T(256)S(1)}, s32[204]{0:T(256)}, u32[]{:S(2)}) copy-start(s32[204]{0:T(256)} %get-tuple-element.42) | copy-start | bytes 2452
  95.0 10.2 %all-to-all-start.3 = ((f32[32,1,512]{2,1,0:T(1,128)}), f32[32,1,512]{2,1,0:T(1,128)S(1)}, u32[]{:S(2)}, u32[]{:S(2)}) async-start(f32[32,1,512]{2,1,0:T(1,128)} %broadcast_in_dim.58), calls=%async_computation.3 | async-start | bytes 131072 | tf_op jit(solution)/shard_map/all_to_all | solution.py:157
  106.2 2.1 %copy-start.23 = (s32[204]{0:T(256)S(1)}, s32[204]{0:T(256)}, u32[]{:S(2)}) copy-start(s32[204]{0:T(256)} %get-tuple-element.43) | copy-start | bytes 2452
  106.2 2.1 %copy-start.25 = (s32[204]{0:T(256)S(1)}, s32[204]{0:T(256)}, u32[]{:S(2)}) copy-start(s32[204]{0:T(256)} %get-tuple-element.47) | copy-start | bytes 2452
  106.2 2.1 %copy-start.29 = (pred[204]{0:T(512)(128)(4,1)S(1)}, pred[204]{0:T(512)(128)(4,1)}, u32[]{:S(2)}) copy-start(pred[204]{0:T(512)(128)(4,1)} %get-tuple-element.44) | copy-start | bytes 616
  106.2 2.1 %copy-start.30 = (pred[204]{0:T(512)(128)(4,1)S(1)}, pred[204]{0:T(512)(128)(4,1)}, u32[]{:S(2)}) copy-start(pred[204]{0:T(512)(128)(4,1)} %get-tuple-element.45) | copy-start | bytes 616
  111.0 1.0 copy-start.14
  (7 other events, 5.1 us)

commit v14 on v10

--- a/solution.py
+++ b/solution.py
@@ -184,14 +184,19 @@
     grid_x = lax.axis_size("gx")
     grid_y = lax.axis_size("gy")
     groups = lax.axis_size("grp")
-    tables = groups * grid_x * grid_y * block_rows
+    devices = groups * grid_x * grid_y
+    column_list = coarse_columns.reshape(-1, 1)
     pick = (
-        coarse_columns.reshape(-1, 1) == lax.broadcasted_iota(jnp.int32, (coarse_columns.size, tables), 1)
+        column_list // block_rows == lax.broadcasted_iota(jnp.int32, (column_list.shape[0], devices), 1)
     ).astype(source.dtype)
+    within = column_list % block_rows
     coarse_error = coarse_rhs / coarse_diag
     for sweep_number in range(CITER - 1):
         pooled = everyone(coarse_error)
-        blocks = dot(pick, pooled.reshape(tables, 64))
+        rows_of = dot(pick, pooled.reshape(devices, -1))
+        blocks = rows_of[:, :64]
+        for part in range(1, block_rows):
+            blocks = jnp.where(within == part, rows_of[:, part * 64:(part + 1) * 64], blocks)
         blocks = blocks.reshape(block_rows, -1)
         applied = jnp.einsum(
             "bim,bm->bi", coarse_values, blocks, precision=lax.Precision.HIGHEST

time: 94.7 us -> 88.4 us (0.933)
  local copies, waits for them, and re-layouts: 12.7 us -> 9.35 us
  waiting for transfers between devices: 25.4 us -> 23.7 us
  other arithmetic: 10.5 us -> 11.7 us
    select_n x0 -> x4, other arithmetic: none -> 3.62 us  [the longest x3 2.45 us: local(): jnp.where(within == part, rows_of[:, part * 64:(part + 1) * 64], blocks)]
    all_to_all x4 -> x1, other arithmetic: 3.15 us -> 0.16 us  [everyone(): return lax.all_to_all(copies, ALL_AXES, 0, 0, tiled=True).reshape(-1)]
    another operation x3 -> x0, local copies, waits for them, and re-layouts: 2.22 us -> none  [local(): blocks = dot(pick, pooled.reshape(tables, 64))]
    ppermute x4, waiting for transfers between devices: 1.41 us -> 0.04 us  [permute(): return lax.ppermute(slab.reshape(-1, 128), axis, pairs).reshape(slab.shape)]
    eq x0 -> x2, other arithmetic: none -> 1.2 us  [local(): within == part]
  transfers between devices with their start and end apart: 8 -> 8, of which waited for: 5 -> 4; matrix products, arithmetic and copies ran while one was open for 5% -> 7% of each run, Pallas kernels for 0% -> 0%
where the time goes in v14:
time: 88.4 us; the launch traced here: 87.8 us
  waiting for transfers between devices  23.7 us (27%)
  starting transfers between devices  22.1 us (25%)
  other arithmetic  11.7 us (13%)
  matrix products  10.6 us (12%)
  local copies, waits for them, and re-layouts  9.35 us (11%)
  blocking collectives  9.3 us (11%)
  between operations  1.17 us (1%)
    all_to_all x3, waiting for transfers between devices, everyone(): return lax.all_to_all(copies, ALL_AXES, 0, 0, tiled=True).reshape(-1)  20.2 us
    all_to_all x3, starting transfers between devices, everyone(): return lax.all_to_all(copies, ALL_AXES, 0, 0, tiled=True).reshape(-1)  10.3 us
    ppermute x4, starting transfers between devices, permute(): return lax.ppermute(slab.reshape(-1, 128), axis, pairs).reshape(slab.shape)  10.2 us
    all_to_all x1, blocking collectives, everyone(): return lax.all_to_all(copies, ALL_AXES, 0, 0, tiled=True).reshape(-1)  9.3 us
    dot_general x9, matrix products, dot(): return jnp.dot(left, right, precision=lax.Precision.HIGHEST)  9.02 us
    ppermute x1, waiting for transfers between devices, permute(): return lax.ppermute(slab, axis, pairs)  3.38 us
    select_n x3, other arithmetic, local(): jnp.where(within == part, rows_of[:, part * 64:(part + 1) * 64], blocks)  2.45 us
    broadcast_in_dim x4, local copies, waits for them, and re-layouts, everyone(): copies = jnp.broadcast_to(vector[None], (count,) + vector.shape)  2.1 us
  transfers between devices with their start and end apart: 8, of which 4 were waited for; matrix products, arithmetic and copies ran while one was open for 7% of the time, Pallas kernels for 0%

profile of v14, /device:TPU:0, one launch (start us, length us, event | category | flops | bytes accessed | tf_op | source)
XLA Modules:
  0.0 87.8 jit_solution(18100147164984286097)
XLA Ops:
  0.6 1.1 %pad_maximum_fusion.2 = f32[3,16,16,128]{3,2,1,0:T(8,128)S(1)} fusion(f32[1,16,16,128]{3,2,1,0:T(8,128)} %bitcast.86, f32[1,16,16,128]{3,2,1,0:T(8,128)} %bitcast.88, f32[1,16,16,128]{3,2,1,0:T(8,128)} %bitcast.90), kind=kLoop, calls=%fused_computation.102 | loop fusion | flops 196608 | bytes 786432 | tf_op jit(solution)/shard_map/stack | solution.py:145
  2.2 0.7 collective-permute-start
  3.0 5.9 %collective-permute-start.1 = (f32[24,128]{1,0:T(8,128)S(1)}, f32[24,128]{1,0:T(8,128)S(1)}, u32[]{:S(2)}, u32[]{:S(2)}) collective-permute-start(f32[24,128]{1,0:T(8,128)S(1)} %reshape.251), channel_id=1, source_target_pairs={{0,8},{8,0},{16,24},{24,16},{1,9},{9,1},{17,25},{25,17},{2,10},{10... | collective-permute-start | bytes 36872 | tf_op jit(solution)/shard_map/ppermute | solution.py:28
  9.2 0.6 broadcast_compare_fusion.6
  9.8 0.6 broadcast_compare_fusion.3
  12.4 1.6 %collective-permute-start.2 = (f32[3,16,544]{2,1,0:T(8,128)S(1)}, f32[3,16,544]{2,1,0:T(8,128)S(1)}, u32[]{:S(2)}, u32[]{:S(2)}) collective-permute-start(f32[3,16,544]{2,1,0:T(8,128)S(1)} %slice_select_fusion.4), channel_id=1, source_target_pairs={{0,1},{1,0},{2,3},{3,2},{4,5},{5,4},{6,7},{7,6},{8,9},{9,8},{10,11... | collective-permute-start | bytes 313352 | tf_op jit(solution)/shard_map/ppermute | solution.py:29
  13.9 3.4 %collective-permute-done.2 = f32[3,16,544]{2,1,0:T(8,128)S(1)} collective-permute-done((f32[3,16,544]{2,1,0:T(8,128)S(1)}, f32[3,16,544]{2,1,0:T(8,128)S(1)}, u32[]{:S(2)}, u32[]{:S(2)}) %collective-permute-start.2) | collective-permute-done | bytes 104480 | tf_op jit(solution)/shard_map/ppermute | solution.py:29
  17.8 0.7 collective-permute-start.3
  18.7 2.9 %collective-permute-start.4 = (f32[306,128]{1,0:T(8,128)S(1)}, f32[306,128]{1,0:T(8,128)S(1)}, u32[]{:S(2)}, u32[]{:S(2)}) collective-permute-start(f32[306,128]{1,0:T(8,128)S(1)} %reshape.254), channel_id=1, source_target_pairs={{0,2},{2,0},{4,6},{6,4},{1,3},{3,1},{5,7},{7,5},{8,10},{10,8},{12,... | collective-permute-start | bytes 470024 | tf_op jit(solution)/shard_map/ppermute | solution.py:28
  21.6 1.9 %slice.255 = s32[4,4,32]{2,1,0:T(4,128)S(1)} slice(s32[16,16,128]{2,1,0:T(8,128)} %param.9), slice={[0:16:4], [0:16:4], [0:128:4]} | slice | bytes 4096 | tf_op jit(solution)/shard_map/slice | solution.py:176
  26.0 2.2 %fusion.12 = f32[24,128]{1,0:T(8,128)S(1)} fusion(s32[128]{0:T(128)S(1)} %get-tuple-element.36, s32[128]{0:T(128)S(1)} %get-tuple-element.37, s32[3264]{0:T(1024)S(1)} %get-tuple-element.28, s32[3264]{0:T(1024)S(1)} %get-tuple-element.29, s32[128]{0:T(128)S(1)} %get-tuple-element.35, s32[128]{0:T(128)S(1)} %get-tuple-element.38, ...), kind=kOutput, calls=%fused_computation.23 | convolution fusion | flops 131056128 | bytes 3283969 | tf_op jit(solution)/shard_map/dot_general | solution.py:120
  28.9 0.7 broadcast_in_dim.136
  29.6 5.0 %all-to-all-start = ((f32[32,1,512]{2,1,0:T(1,128)}), f32[32,1,512]{2,1,0:T(1,128)S(1)}, u32[]{:S(2)}, u32[]{:S(2)}) async-start(f32[32,1,512]{2,1,0:T(1,128)} %broadcast_in_dim.136), calls=%async_computation | async-start | bytes 131072 | tf_op jit(solution)/shard_map/all_to_all | solution.py:139
  34.6 1.2 %and_select_fusion = s32[32]{0:T(128)} fusion(s32[32]{0:T(128)} %copy-done.11), kind=kLoop, calls=%fused_computation.338 | loop fusion | flops 480 | bytes 256 | tf_op jit(solution)/shard_map/jit(floor_divide)/jit(_where)/select_n | solution.py:190
  35.7 6.4 %all-to-all-done = f32[32,1,512]{2,1,0:T(1,128)S(1)} async-done(((f32[32,1,512]{2,1,0:T(1,128)}), f32[32,1,512]{2,1,0:T(1,128)S(1)}, u32[]{:S(2)}, u32[]{:S(2)}) %all-to-all-start) | async-done | bytes 65568 | tf_op jit(solution)/shard_map/all_to_all | solution.py:139
  42.2 0.9 fusion.206
  43.1 0.8 fusion.232
  44.6 9.3 %all_to_all.33 = f32[32,1,512]{2,1,0:T(1,128)S(1)} all-to-all(f32[32,1,512]{2,1,0:T(1,128)S(1)} %broadcast_in_dim.143), channel_id=1, replica_groups=mesh['grp'=4,'gx'=4,'gy'=2] {'grp','gx','gy'}, dimensions={0} | all-to-all | bytes 131072 | tf_op jit(solution)/shard_map/all_to_all | solution.py:139
  53.9 0.9 fusion.203
  54.8 0.8 fusion.226
  56.3 0.7 broadcast_in_dim.144
  57.0 2.6 %all-to-all-start.2 = ((f32[32,1,512]{2,1,0:T(1,128)}), f32[32,1,512]{2,1,0:T(1,128)S(1)}, u32[]{:S(2)}, u32[]{:S(2)}) async-start(f32[32,1,512]{2,1,0:T(1,128)} %broadcast_in_dim.144), calls=%async_computation.2 | async-start | bytes 131072 | tf_op jit(solution)/shard_map/all_to_all | solution.py:139
  59.6 0.6 compare_and_fusion
  60.8 6.4 %all-to-all-done.2 = f32[32,1,512]{2,1,0:T(1,128)S(1)} async-done(((f32[32,1,512]{2,1,0:T(1,128)}), f32[32,1,512]{2,1,0:T(1,128)S(1)}, u32[]{:S(2)}, u32[]{:S(2)}) %all-to-all-start.2) | async-done | bytes 65568 | tf_op jit(solution)/shard_map/all_to_all | solution.py:139
  67.2 0.9 fusion.200
  68.1 0.8 fusion.220
  69.6 1.3 %fusion.28 = f32[1,512]{1,0:T(1,128)S(1)} fusion(f32[512,1]{0,1:T(1,128)S(1)} %bitcast.99, s32[512]{0:T(512)} %copy-done.7), kind=kOutput, calls=%fused_computation.39 | convolution fusion | flops 3407872 | bytes 6144 | tf_op jit(solution)/shard_map/dot_general | solution.py:120
  70.9 0.7 broadcast_in_dim.145
  71.6 2.8 %all-to-all-start.3 = ((f32[32,1,512]{2,1,0:T(1,128)}), f32[32,1,512]{2,1,0:T(1,128)S(1)}, u32[]{:S(2)}, u32[]{:S(2)}) async-start(f32[32,1,512]{2,1,0:T(1,128)} %broadcast_in_dim.145), calls=%async_computation.3 | async-start | bytes 131072 | tf_op jit(solution)/shard_map/all_to_all | solution.py:139
  74.4 7.4 %all-to-all-done.3 = f32[32,1,512]{2,1,0:T(1,128)S(1)} async-done(((f32[32,1,512]{2,1,0:T(1,128)}), f32[32,1,512]{2,1,0:T(1,128)S(1)}, u32[]{:S(2)}, u32[]{:S(2)}) %all-to-all-start.3) | async-done | bytes 65568 | tf_op jit(solution)/shard_map/all_to_all | solution.py:139
  82.7 1.8 %fusion.4 = f32[6,3264]{1,0:T(8,128)S(1)} fusion(f32[6,204]{1,0:T(8,128)S(1)} %reshape.265, s32[204]{0:T(256)S(1)} %copy-done.10, s32[204]{0:T(256)S(1)} %get-tuple-element.45, s32[3264]{0:T(1024)S(1)} %get-tuple-element.28, s32[3264]{0:T(1024)S(1)} %get-tuple-element.29, s32[204]{0:T(256)S(1)} %copy-done.9, s32[204]{0:T(256)S(1)} %get-tuple-element.46, ...), kind=kOutput, calls=%fused_computation.10 | convolution fusion | flops 58595328 | bytes 145657 | tf_op jit(solution)/shard_map/dot_general | solution.py:120
  87.1 0.8 slice.345
  (99 shorter events, 12.6 us)
Async XLA Ops:
  1.7 7.3 %copy-start.6 = (s32[8,4]{0,1:T(4,128)S(1)}, s32[8,4]{0,1:T(4,128)}, u32[]{:S(2)}) copy-start(s32[8,4]{0,1:T(4,128)} %param.11) | copy-start | bytes 388
  1.7 8.7 %copy-start = (f32[8,64,256]{2,1,0:T(8,128)S(1)}, f32[8,64,256]{2,1,0:T(8,128)}, u32[]{:S(2)}) copy-start(f32[8,64,256]{2,1,0:T(8,128)} %param.10) | copy-start | bytes 1572868
  1.9 9.5 %copy-start.3 = (f32[16,16,128]{2,1,0:T(8,128)S(1)}, f32[16,16,128]{2,1,0:T(8,128)}, u32[]{:S(2)}) copy-start(f32[16,16,128]{2,1,0:T(8,128)} %param.8) | copy-start | bytes 393220
  1.9 9.5 %copy-start.4 = (f32[16,16,128]{2,1,0:T(8,128)S(1)}, f32[16,16,128]{2,1,0:T(8,128)}, u32[]{:S(2)}) copy-start(f32[16,16,128]{2,1,0:T(8,128)} %param.7) | copy-start | bytes 393220
  1.9 9.5 %copy-start.5 = (f32[16,16,128]{2,1,0:T(8,128)S(1)}, f32[16,16,128]{2,1,0:T(8,128)}, u32[]{:S(2)}) copy-start(f32[16,16,128]{2,1,0:T(8,128)} %param.6) | copy-start | bytes 393220
  2.2 8.4 %collective-permute-start = (f32[24,128]{1,0:T(8,128)S(1)}, f32[24,128]{1,0:T(8,128)S(1)}, u32[]{:S(2)}, u32[]{:S(2)}) collective-permute-start(f32[24,128]{1,0:T(8,128)S(1)} %reshape.250), channel_id=1, source_target_pairs={{8,16},{16,8},{9,17},{17,9},{10,18},{18,10},{11,19},{19,11},{12,20... | collective-permute-start | bytes 36872 | tf_op jit(solution)/shard_map/ppermute | solution.py:28
  3.0 7.6 %collective-permute-start.1 = (f32[24,128]{1,0:T(8,128)S(1)}, f32[24,128]{1,0:T(8,128)S(1)}, u32[]{:S(2)}, u32[]{:S(2)}) collective-permute-start(f32[24,128]{1,0:T(8,128)S(1)} %reshape.251), channel_id=1, source_target_pairs={{0,8},{8,0},{16,24},{24,16},{1,9},{9,1},{17,25},{25,17},{2,10},{10... | collective-permute-start | bytes 36872 | tf_op jit(solution)/shard_map/ppermute | solution.py:28
  9.2 2.6 %copy-start.11 = (s32[32]{0:T(128)}, s32[32]{0:T(128)S(1)}, u32[]{:S(2)}) copy-start(s32[32]{0:T(128)S(1)} %reshape.257) | copy-start | bytes 388
  12.4 4.9 %collective-permute-start.2 = (f32[3,16,544]{2,1,0:T(8,128)S(1)}, f32[3,16,544]{2,1,0:T(8,128)S(1)}, u32[]{:S(2)}, u32[]{:S(2)}) collective-permute-start(f32[3,16,544]{2,1,0:T(8,128)S(1)} %slice_select_fusion.4), channel_id=1, source_target_pairs={{0,1},{1,0},{2,3},{3,2},{4,5},{5,4},{6,7},{7,6},{8,9},{9,8},{10,11... | collective-permute-start | bytes 313352 | tf_op jit(solution)/shard_map/ppermute | solution.py:29
  17.8 5.8 %collective-permute-start.3 = (f32[306,128]{1,0:T(8,128)S(1)}, f32[306,128]{1,0:T(8,128)S(1)}, u32[]{:S(2)}, u32[]{:S(2)}) collective-permute-start(f32[306,128]{1,0:T(8,128)S(1)} %reshape.253), channel_id=1, source_target_pairs={{2,4},{4,2},{3,5},{5,3},{10,12},{12,10},{11,13},{13,11},{18,20},{2... | collective-permute-start | bytes 470024 | tf_op jit(solution)/shard_map/ppermute | solution.py:28
  18.7 5.0 %collective-permute-start.4 = (f32[306,128]{1,0:T(8,128)S(1)}, f32[306,128]{1,0:T(8,128)S(1)}, u32[]{:S(2)}, u32[]{:S(2)}) collective-permute-start(f32[306,128]{1,0:T(8,128)S(1)} %reshape.254), channel_id=1, source_target_pairs={{0,2},{2,0},{4,6},{6,4},{1,3},{3,1},{5,7},{7,5},{8,10},{10,8},{12,... | collective-permute-start | bytes 470024 | tf_op jit(solution)/shard_map/ppermute | solution.py:28
  23.6 4.8 %copy-start.7 = (s32[512]{0:T(512)}, s32[512]{0:T(512)S(1)}, u32[]{:S(2)}) copy-start(s32[512]{0:T(512)S(1)} %eq.125) | copy-start | bytes 6148
  25.2 0.7 copy-start.1
  29.6 12.6 %all-to-all-start = ((f32[32,1,512]{2,1,0:T(1,128)}), f32[32,1,512]{2,1,0:T(1,128)S(1)}, u32[]{:S(2)}, u32[]{:S(2)}) async-start(f32[32,1,512]{2,1,0:T(1,128)} %broadcast_in_dim.136), calls=%async_computation | async-start | bytes 131072 | tf_op jit(solution)/shard_map/all_to_all | solution.py:139
  57.0 10.2 %all-to-all-start.2 = ((f32[32,1,512]{2,1,0:T(1,128)}), f32[32,1,512]{2,1,0:T(1,128)S(1)}, u32[]{:S(2)}, u32[]{:S(2)}) async-start(f32[32,1,512]{2,1,0:T(1,128)} %broadcast_in_dim.144), calls=%async_computation.2 | async-start | bytes 131072 | tf_op jit(solution)/shard_map/all_to_all | solution.py:139
  69.6 13.1 %copy-start.8 = (f32[512]{0:T(512)}, f32[512]{0:T(512)S(1)}, u32[]{:S(2)}) copy-start(f32[512]{0:T(512)S(1)} %divide_add_fusion) | copy-start | bytes 6148
  69.6 13.1 %copy-start.9 = (s32[204]{0:T(256)S(1)}, s32[204]{0:T(256)}, u32[]{:S(2)}) copy-start(s32[204]{0:T(256)} %get-tuple-element.41) | copy-start | bytes 2452
  69.6 13.1 %copy-start.10 = (s32[204]{0:T(256)S(1)}, s32[204]{0:T(256)}, u32[]{:S(2)}) copy-start(s32[204]{0:T(256)} %get-tuple-element.42) | copy-start | bytes 2452
  69.6 13.1 %copy-start.12 = (pred[204]{0:T(512)(128)(4,1)S(1)}, pred[204]{0:T(512)(128)(4,1)}, u32[]{:S(2)}) copy-start(pred[204]{0:T(512)(128)(4,1)} %get-tuple-element.43) | copy-start | bytes 616
  69.6 13.1 %copy-start.13 = (pred[204]{0:T(512)(128)(4,1)S(1)}, pred[204]{0:T(512)(128)(4,1)}, u32[]{:S(2)}) copy-start(pred[204]{0:T(512)(128)(4,1)} %get-tuple-element.44) | copy-start | bytes 616
  71.6 10.2 %all-to-all-start.3 = ((f32[32,1,512]{2,1,0:T(1,128)}), f32[32,1,512]{2,1,0:T(1,128)S(1)}, u32[]{:S(2)}, u32[]{:S(2)}) async-start(f32[32,1,512]{2,1,0:T(1,128)} %broadcast_in_dim.145), calls=%async_computation.3 | async-start | bytes 131072 | tf_op jit(solution)/shard_map/all_to_all | solution.py:139
  82.7 2.3 %copy-start.2 = (f32[24,3264]{1,0:T(8,128)S(1)}, f32[24,3264]{1,0:T(8,128)}, u32[]{:S(2)}) copy-start(f32[24,3264]{1,0:T(8,128)} %copy-done.1) | copy-start | bytes 940036

commit v15 on v14

--- a/solution.py
+++ b/solution.py
@@ -174,10 +174,8 @@
     pick_yz = box_matrix(by * bz, span_y * span_z, span_z, HALO, live, bz).T
     box_totals = dot(pick_x, dot(smoothed, pick_yz)).reshape(-1)
     box_labels = aggregate_ids[::BOX, ::BOX, ::BOX].reshape(-1)
-    placed = (
-        box_labels[:, None] == lax.broadcasted_iota(jnp.int32, (box_labels.shape[0],) * 2, 1)
-    ).astype(source.dtype)
-    coarse_rhs = dot(box_totals[None, :], placed)[0]
+    placed = box_labels[:, None] == lax.broadcasted_iota(jnp.int32, (box_labels.shape[0],) * 2, 1)
+    coarse_rhs = jnp.sum(jnp.where(placed, box_totals[:, None], 0.0), axis=0)
     eye = lax.broadcasted_iota(jnp.int32, (64, 64), 0) == lax.broadcasted_iota(jnp.int32, (64, 64), 1)
     coarse_diag = jnp.sum(jnp.where(eye[None], coarse_values[:, :, :64], 0.0), axis=2).reshape(-1)
     block_rows = coarse_values.shape[0]
@@ -203,7 +201,7 @@
         ).reshape(-1)
         coarse_error = coarse_error + (coarse_rhs - applied) / coarse_diag
 
-    small = dot(placed, coarse_error[:, None]).reshape(-1)
+    small = jnp.sum(jnp.where(placed, coarse_error[None, :], 0.0), axis=1)
     every = everyone(small).reshape(groups, grid_x, grid_y, bx, by, bz)
     boxes = every.transpose(1, 3, 2, 4, 0, 5).reshape(grid_x * bx, grid_y * by, groups * bz)
     boxes = jnp.pad(boxes, 1)

time: 88.4 us -> 88.2 us (level)
  matrix products: 10.6 us -> 8.63 us
  other arithmetic: 11.7 us -> 13.3 us
    dot_general x9 -> x7, matrix products: 9.02 us -> 7.08 us  [dot(): return jnp.dot(left, right, precision=lax.Precision.HIGHEST)]
    add x3, other arithmetic: 0.03 us -> 1.4 us  [local(): coarse_error = coarse_error + (coarse_rhs - applied) / coarse_diag]
  transfers between devices with their start and end apart: 8 -> 8, of which waited for: 4 -> 5; matrix products, arithmetic and copies ran while one was open for 7% -> 7% of each run, Pallas kernels for 0% -> 0%
where the time goes in v15:
time: 88.2 us; the launch traced here: 87.6 us
  waiting for transfers between devices  23.8 us (27%)
  starting transfers between devices  22.1 us (25%)
  other arithmetic  13.3 us (15%)
  local copies, waits for them, and re-layouts  9.31 us (11%)
  blocking collectives  9.3 us (11%)
  matrix products  8.63 us (10%)
  between operations  1.15 us (1%)
    all_to_all x3, waiting for transfers between devices, everyone(): return lax.all_to_all(copies, ALL_AXES, 0, 0, tiled=True).reshape(-1)  20.3 us
    all_to_all x3, starting transfers between devices, everyone(): return lax.all_to_all(copies, ALL_AXES, 0, 0, tiled=True).reshape(-1)  10.3 us
    ppermute x4, starting transfers between devices, permute(): return lax.ppermute(slab.reshape(-1, 128), axis, pairs).reshape(slab.shape)  10.2 us
    all_to_all x1, blocking collectives, everyone(): return lax.all_to_all(copies, ALL_AXES, 0, 0, tiled=True).reshape(-1)  9.3 us
    dot_general x7, matrix products, dot(): return jnp.dot(left, right, precision=lax.Precision.HIGHEST)  7.08 us
    ppermute x1, waiting for transfers between devices, permute(): return lax.ppermute(slab, axis, pairs)  3.38 us
    select_n x3, other arithmetic, local(): jnp.where(within == part, rows_of[:, part * 64:(part + 1) * 64], blocks)  2.36 us
    broadcast_in_dim x4, local copies, waits for them, and re-layouts, everyone(): copies = jnp.broadcast_to(vector[None], (count,) + vector.shape)  2.06 us
  transfers between devices with their start and end apart: 8, of which 5 were waited for; matrix products, arithmetic and copies ran while one was open for 7% of the time, Pallas kernels for 0%

profile of v15, /device:TPU:0, one launch (start us, length us, event | category | flops | bytes accessed | tf_op | source)
XLA Modules:
  0.0 87.6 jit_solution(4604182687208137760)
XLA Ops:
  0.6 1.1 %pad_maximum_fusion.2 = f32[3,16,16,128]{3,2,1,0:T(8,128)S(1)} fusion(f32[1,16,16,128]{3,2,1,0:T(8,128)} %bitcast.80, f32[1,16,16,128]{3,2,1,0:T(8,128)} %bitcast.82, f32[1,16,16,128]{3,2,1,0:T(8,128)} %bitcast.84), kind=kLoop, calls=%fused_computation.101 | loop fusion | flops 196608 | bytes 786432 | tf_op jit(solution)/shard_map/stack | solution.py:145
  2.2 0.7 collective-permute-start
  3.0 5.9 %collective-permute-start.1 = (f32[24,128]{1,0:T(8,128)S(1)}, f32[24,128]{1,0:T(8,128)S(1)}, u32[]{:S(2)}, u32[]{:S(2)}) collective-permute-start(f32[24,128]{1,0:T(8,128)S(1)} %reshape.309), channel_id=1, source_target_pairs={{0,8},{8,0},{16,24},{24,16},{1,9},{9,1},{17,25},{25,17},{2,10},{10... | collective-permute-start | bytes 36872 | tf_op jit(solution)/shard_map/ppermute | solution.py:28
  9.8 0.6 broadcast_compare_fusion.3
  12.4 1.6 %collective-permute-start.2 = (f32[3,16,544]{2,1,0:T(8,128)S(1)}, f32[3,16,544]{2,1,0:T(8,128)S(1)}, u32[]{:S(2)}, u32[]{:S(2)}) collective-permute-start(f32[3,16,544]{2,1,0:T(8,128)S(1)} %slice_select_fusion.4), channel_id=1, source_target_pairs={{0,1},{1,0},{2,3},{3,2},{4,5},{5,4},{6,7},{7,6},{8,9},{9,8},{10,11... | collective-permute-start | bytes 313352 | tf_op jit(solution)/shard_map/ppermute | solution.py:29
  13.9 3.4 %collective-permute-done.2 = f32[3,16,544]{2,1,0:T(8,128)S(1)} collective-permute-done((f32[3,16,544]{2,1,0:T(8,128)S(1)}, f32[3,16,544]{2,1,0:T(8,128)S(1)}, u32[]{:S(2)}, u32[]{:S(2)}) %collective-permute-start.2) | collective-permute-done | bytes 104480 | tf_op jit(solution)/shard_map/ppermute | solution.py:29
  17.8 0.7 collective-permute-start.3
  18.7 2.9 %collective-permute-start.4 = (f32[306,128]{1,0:T(8,128)S(1)}, f32[306,128]{1,0:T(8,128)S(1)}, u32[]{:S(2)}, u32[]{:S(2)}) collective-permute-start(f32[306,128]{1,0:T(8,128)S(1)} %reshape.312), channel_id=1, source_target_pairs={{0,2},{2,0},{4,6},{6,4},{1,3},{3,1},{5,7},{7,5},{8,10},{10,8},{12,... | collective-permute-start | bytes 470024 | tf_op jit(solution)/shard_map/ppermute | solution.py:28
  21.6 1.9 %slice.255 = s32[4,4,32]{2,1,0:T(4,128)S(1)} slice(s32[16,16,128]{2,1,0:T(8,128)} %param.9), slice={[0:16:4], [0:16:4], [0:128:4]} | slice | bytes 4096 | tf_op jit(solution)/shard_map/slice | solution.py:176
  26.0 2.2 %fusion.12 = f32[24,128]{1,0:T(8,128)S(1)} fusion(s32[128]{0:T(128)S(1)} %get-tuple-element.36, s32[128]{0:T(128)S(1)} %get-tuple-element.37, s32[3264]{0:T(1024)S(1)} %get-tuple-element.28, s32[3264]{0:T(1024)S(1)} %get-tuple-element.29, s32[128]{0:T(128)S(1)} %get-tuple-element.35, s32[128]{0:T(128)S(1)} %get-tuple-element.38, ...), kind=kOutput, calls=%fused_computation.23 | convolution fusion | flops 131056128 | bytes 3283969 | tf_op jit(solution)/shard_map/dot_general | solution.py:120
  28.6 0.7 broadcast_in_dim.164
  29.3 5.0 %all-to-all-start = ((f32[32,1,512]{2,1,0:T(1,128)}), f32[32,1,512]{2,1,0:T(1,128)S(1)}, u32[]{:S(2)}, u32[]{:S(2)}) async-start(f32[32,1,512]{2,1,0:T(1,128)} %broadcast_in_dim.164), calls=%async_computation | async-start | bytes 131072 | tf_op jit(solution)/shard_map/all_to_all | solution.py:139
  34.3 1.1 %and_select_fusion = s32[32]{0:T(128)} fusion(s32[32]{0:T(128)} %copy-done.12), kind=kLoop, calls=%fused_computation.337 | loop fusion | flops 480 | bytes 256 | tf_op jit(solution)/shard_map/jit(floor_divide)/jit(_where)/select_n | solution.py:188
  35.4 6.5 %all-to-all-done = f32[32,1,512]{2,1,0:T(1,128)S(1)} async-done(((f32[32,1,512]{2,1,0:T(1,128)}), f32[32,1,512]{2,1,0:T(1,128)S(1)}, u32[]{:S(2)}, u32[]{:S(2)}) %all-to-all-start) | async-done | bytes 65568 | tf_op jit(solution)/shard_map/all_to_all | solution.py:139
  41.9 0.8 fusion.202
  42.7 0.8 fusion.228
  44.2 0.7 divide_add_fusion.2
  45.0 9.3 %all_to_all.33 = f32[32,1,512]{2,1,0:T(1,128)S(1)} all-to-all(f32[32,1,512]{2,1,0:T(1,128)S(1)} %broadcast_in_dim.171), channel_id=1, replica_groups=mesh['grp'=4,'gx'=4,'gy'=2] {'grp','gx','gy'}, dimensions={0} | all-to-all | bytes 131072 | tf_op jit(solution)/shard_map/all_to_all | solution.py:139
  54.3 0.8 fusion.199
  55.1 0.8 fusion.222
  56.6 0.7 broadcast_in_dim.172
  57.3 2.6 %all-to-all-start.2 = ((f32[32,1,512]{2,1,0:T(1,128)}), f32[32,1,512]{2,1,0:T(1,128)S(1)}, u32[]{:S(2)}, u32[]{:S(2)}) async-start(f32[32,1,512]{2,1,0:T(1,128)} %broadcast_in_dim.172), calls=%async_computation.2 | async-start | bytes 131072 | tf_op jit(solution)/shard_map/all_to_all | solution.py:139
  59.8 0.6 compare_and_fusion
  61.0 6.4 %all-to-all-done.2 = f32[32,1,512]{2,1,0:T(1,128)S(1)} async-done(((f32[32,1,512]{2,1,0:T(1,128)}), f32[32,1,512]{2,1,0:T(1,128)S(1)}, u32[]{:S(2)}, u32[]{:S(2)}) %all-to-all-start.2) | async-done | bytes 65568 | tf_op jit(solution)/shard_map/all_to_all | solution.py:139
  67.4 0.8 fusion.196
  68.3 0.8 fusion.216
  69.8 0.7 divide_add_fusion
  70.7 0.7 broadcast_in_dim.174
  71.4 2.8 %all-to-all-start.3 = ((f32[32,1,512]{2,1,0:T(1,128)}), f32[32,1,512]{2,1,0:T(1,128)S(1)}, u32[]{:S(2)}, u32[]{:S(2)}) async-start(f32[32,1,512]{2,1,0:T(1,128)} %broadcast_in_dim.174), calls=%async_computation.3 | async-start | bytes 131072 | tf_op jit(solution)/shard_map/all_to_all | solution.py:139
  74.2 7.4 %all-to-all-done.3 = f32[32,1,512]{2,1,0:T(1,128)S(1)} async-done(((f32[32,1,512]{2,1,0:T(1,128)}), f32[32,1,512]{2,1,0:T(1,128)S(1)}, u32[]{:S(2)}, u32[]{:S(2)}) %all-to-all-start.3) | async-done | bytes 65568 | tf_op jit(solution)/shard_map/all_to_all | solution.py:139
  82.5 1.8 %fusion.4 = f32[6,3264]{1,0:T(8,128)S(1)} fusion(f32[6,204]{1,0:T(8,128)S(1)} %reshape.322, s32[204]{0:T(256)S(1)} %copy-done.11, s32[204]{0:T(256)S(1)} %get-tuple-element.45, s32[3264]{0:T(1024)S(1)} %get-tuple-element.28, s32[3264]{0:T(1024)S(1)} %get-tuple-element.29, s32[204]{0:T(256)S(1)} %copy-done.10, s32[204]{0:T(256)S(1)} %get-tuple-element.46, ...), kind=kOutput, calls=%fused_computation.10 | convolution fusion | flops 58595328 | bytes 145657 | tf_op jit(solution)/shard_map/dot_general | solution.py:120
  86.8 0.8 slice.345
  (101 shorter events, 13.2 us)
Async XLA Ops:
  1.7 7.3 %copy-start.9 = (s32[8,4]{0,1:T(4,128)S(1)}, s32[8,4]{0,1:T(4,128)}, u32[]{:S(2)}) copy-start(s32[8,4]{0,1:T(4,128)} %param.11) | copy-start | bytes 388
  1.7 8.6 %copy-start = (f32[8,64,256]{2,1,0:T(8,128)S(1)}, f32[8,64,256]{2,1,0:T(8,128)}, u32[]{:S(2)}) copy-start(f32[8,64,256]{2,1,0:T(8,128)} %param.10) | copy-start | bytes 1572868
  1.9 9.5 %copy-start.3 = (f32[16,16,128]{2,1,0:T(8,128)S(1)}, f32[16,16,128]{2,1,0:T(8,128)}, u32[]{:S(2)}) copy-start(f32[16,16,128]{2,1,0:T(8,128)} %param.8) | copy-start | bytes 393220
  1.9 9.5 %copy-start.4 = (f32[16,16,128]{2,1,0:T(8,128)S(1)}, f32[16,16,128]{2,1,0:T(8,128)}, u32[]{:S(2)}) copy-start(f32[16,16,128]{2,1,0:T(8,128)} %param.7) | copy-start | bytes 393220
  1.9 9.5 %copy-start.5 = (f32[16,16,128]{2,1,0:T(8,128)S(1)}, f32[16,16,128]{2,1,0:T(8,128)}, u32[]{:S(2)}) copy-start(f32[16,16,128]{2,1,0:T(8,128)} %param.6) | copy-start | bytes 393220
  2.2 8.4 %collective-permute-start = (f32[24,128]{1,0:T(8,128)S(1)}, f32[24,128]{1,0:T(8,128)S(1)}, u32[]{:S(2)}, u32[]{:S(2)}) collective-permute-start(f32[24,128]{1,0:T(8,128)S(1)} %reshape.308), channel_id=1, source_target_pairs={{8,16},{16,8},{9,17},{17,9},{10,18},{18,10},{11,19},{19,11},{12,20... | collective-permute-start | bytes 36872 | tf_op jit(solution)/shard_map/ppermute | solution.py:28
  3.0 7.6 %collective-permute-start.1 = (f32[24,128]{1,0:T(8,128)S(1)}, f32[24,128]{1,0:T(8,128)S(1)}, u32[]{:S(2)}, u32[]{:S(2)}) collective-permute-start(f32[24,128]{1,0:T(8,128)S(1)} %reshape.309), channel_id=1, source_target_pairs={{0,8},{8,0},{16,24},{24,16},{1,9},{9,1},{17,25},{25,17},{2,10},{10... | collective-permute-start | bytes 36872 | tf_op jit(solution)/shard_map/ppermute | solution.py:28
  9.2 2.6 %copy-start.12 = (s32[32]{0:T(128)}, s32[32]{0:T(128)S(1)}, u32[]{:S(2)}) copy-start(s32[32]{0:T(128)S(1)} %reshape.314) | copy-start | bytes 388
  12.4 4.9 %collective-permute-start.2 = (f32[3,16,544]{2,1,0:T(8,128)S(1)}, f32[3,16,544]{2,1,0:T(8,128)S(1)}, u32[]{:S(2)}, u32[]{:S(2)}) collective-permute-start(f32[3,16,544]{2,1,0:T(8,128)S(1)} %slice_select_fusion.4), channel_id=1, source_target_pairs={{0,1},{1,0},{2,3},{3,2},{4,5},{5,4},{6,7},{7,6},{8,9},{9,8},{10,11... | collective-permute-start | bytes 313352 | tf_op jit(solution)/shard_map/ppermute | solution.py:29
  17.8 5.8 %collective-permute-start.3 = (f32[306,128]{1,0:T(8,128)S(1)}, f32[306,128]{1,0:T(8,128)S(1)}, u32[]{:S(2)}, u32[]{:S(2)}) collective-permute-start(f32[306,128]{1,0:T(8,128)S(1)} %reshape.311), channel_id=1, source_target_pairs={{2,4},{4,2},{3,5},{5,3},{10,12},{12,10},{11,13},{13,11},{18,20},{2... | collective-permute-start | bytes 470024 | tf_op jit(solution)/shard_map/ppermute | solution.py:28
  18.7 5.0 %collective-permute-start.4 = (f32[306,128]{1,0:T(8,128)S(1)}, f32[306,128]{1,0:T(8,128)S(1)}, u32[]{:S(2)}, u32[]{:S(2)}) collective-permute-start(f32[306,128]{1,0:T(8,128)S(1)} %reshape.312), channel_id=1, source_target_pairs={{0,2},{2,0},{4,6},{6,4},{1,3},{3,1},{5,7},{7,5},{8,10},{10,8},{12,... | collective-permute-start | bytes 470024 | tf_op jit(solution)/shard_map/ppermute | solution.py:28
  25.2 0.7 copy-start.1
  28.6 0.7 copy-start.7
  29.3 12.6 %all-to-all-start = ((f32[32,1,512]{2,1,0:T(1,128)}), f32[32,1,512]{2,1,0:T(1,128)S(1)}, u32[]{:S(2)}, u32[]{:S(2)}) async-start(f32[32,1,512]{2,1,0:T(1,128)} %broadcast_in_dim.164), calls=%async_computation | async-start | bytes 131072 | tf_op jit(solution)/shard_map/all_to_all | solution.py:139
  56.6 0.7 copy-start.6
  57.3 10.2 %all-to-all-start.2 = ((f32[32,1,512]{2,1,0:T(1,128)}), f32[32,1,512]{2,1,0:T(1,128)S(1)}, u32[]{:S(2)}, u32[]{:S(2)}) async-start(f32[32,1,512]{2,1,0:T(1,128)} %broadcast_in_dim.172), calls=%async_computation.2 | async-start | bytes 131072 | tf_op jit(solution)/shard_map/all_to_all | solution.py:139
  69.7 12.8 %copy-start.10 = (s32[204]{0:T(256)S(1)}, s32[204]{0:T(256)}, u32[]{:S(2)}) copy-start(s32[204]{0:T(256)} %get-tuple-element.41) | copy-start | bytes 2452
  69.7 12.8 %copy-start.11 = (s32[204]{0:T(256)S(1)}, s32[204]{0:T(256)}, u32[]{:S(2)}) copy-start(s32[204]{0:T(256)} %get-tuple-element.42) | copy-start | bytes 2452
  69.7 12.8 %copy-start.13 = (pred[204]{0:T(512)(128)(4,1)S(1)}, pred[204]{0:T(512)(128)(4,1)}, u32[]{:S(2)}) copy-start(pred[204]{0:T(512)(128)(4,1)} %get-tuple-element.43) | copy-start | bytes 616
  69.7 12.8 %copy-start.14 = (pred[204]{0:T(512)(128)(4,1)S(1)}, pred[204]{0:T(512)(128)(4,1)}, u32[]{:S(2)}) copy-start(pred[204]{0:T(512)(128)(4,1)} %get-tuple-element.44) | copy-start | bytes 616
  70.4 13.8 %copy-start.8 = (f32[512]{0:T(512)}, f32[512]{0:T(512)S(1)}, u32[]{:S(2)}) copy-start(f32[512]{0:T(512)S(1)} %divide_add_fusion) | copy-start | bytes 6148
  71.4 10.2 %all-to-all-start.3 = ((f32[32,1,512]{2,1,0:T(1,128)}), f32[32,1,512]{2,1,0:T(1,128)S(1)}, u32[]{:S(2)}, u32[]{:S(2)}) async-start(f32[32,1,512]{2,1,0:T(1,128)} %broadcast_in_dim.174), calls=%async_computation.3 | async-start | bytes 131072 | tf_op jit(solution)/shard_map/all_to_all | solution.py:139
  82.5 2.3 %copy-start.2 = (f32[24,3264]{1,0:T(8,128)S(1)}, f32[24,3264]{1,0:T(8,128)}, u32[]{:S(2)}) copy-start(f32[24,3264]{1,0:T(8,128)} %copy-done.1) | copy-start | bytes 940036

commit v16 on v15

--- a/solution.py
+++ b/solution.py
@@ -173,7 +173,9 @@
     pick_x = box_matrix(bx, rows, 1, HALO, live)
     pick_yz = box_matrix(by * bz, span_y * span_z, span_z, HALO, live, bz).T
     box_totals = dot(pick_x, dot(smoothed, pick_yz)).reshape(-1)
-    box_labels = aggregate_ids[::BOX, ::BOX, ::BOX].reshape(-1)
+    corner_ids = aggregate_ids[::BOX, ::BOX].reshape(bx * by, size_z).astype(source.dtype)
+    first_z = lax.broadcasted_iota(jnp.int32, (size_z, bz), 0) == BOX * lax.broadcasted_iota(jnp.int32, (size_z, bz), 1)
+    box_labels = dot(corner_ids, first_z.astype(source.dtype)).astype(jnp.int32).reshape(-1)
     placed = box_labels[:, None] == lax.broadcasted_iota(jnp.int32, (box_labels.shape[0],) * 2, 1)
     coarse_rhs = jnp.sum(jnp.where(placed, box_totals[:, None], 0.0), axis=0)
     eye = lax.broadcasted_iota(jnp.int32, (64, 64), 0) == lax.broadcasted_iota(jnp.int32, (64, 64), 1)

time: 88.2 us -> 91.2 us (1.034)
  other arithmetic: 13.3 us -> 15.2 us
    dot_general x7 -> x8, matrix products: 7.08 us -> 7.39 us  [dot(): return jnp.dot(left, right, precision=lax.Precision.HIGHEST)]
  transfers between devices with their start and end apart: 8 -> 8, of which waited for: 5 -> 5; matrix products, arithmetic and copies ran while one was open for 7% -> 9% of each run, Pallas kernels for 0% -> 0%
where the time goes in v16:
time: 91.2 us; the launch traced here: 90.6 us
  waiting for transfers between devices  24.4 us (27%)
  starting transfers between devices  22.6 us (25%)
  other arithmetic  15.2 us (17%)
  blocking collectives  9.3 us (10%)
  local copies, waits for them, and re-layouts  9.02 us (10%)
  matrix products  8.95 us (10%)
  between operations  1.12 us (1%)
    all_to_all x3, waiting for transfers between devices, everyone(): return lax.all_to_all(copies, ALL_AXES, 0, 0, tiled=True).reshape(-1)  20.2 us
    all_to_all x3, starting transfers between devices, everyone(): return lax.all_to_all(copies, ALL_AXES, 0, 0, tiled=True).reshape(-1)  10.7 us
    ppermute x4, starting transfers between devices, permute(): return lax.ppermute(slab.reshape(-1, 128), axis, pairs).reshape(slab.shape)  10.3 us
    all_to_all x1, blocking collectives, everyone(): return lax.all_to_all(copies, ALL_AXES, 0, 0, tiled=True).reshape(-1)  9.3 us
    dot_general x8, matrix products, dot(): return jnp.dot(left, right, precision=lax.Precision.HIGHEST)  7.39 us
    ppermute x1, waiting for transfers between devices, permute(): return lax.ppermute(slab, axis, pairs)  3.38 us
    select_n x3, other arithmetic, local(): jnp.where(within == part, rows_of[:, part * 64:(part + 1) * 64], blocks)  2.43 us
    broadcast_in_dim x4, local copies, waits for them, and re-layouts, everyone(): copies = jnp.broadcast_to(vector[None], (count,) + vector.shape)  2.06 us
  transfers between devices with their start and end apart: 8, of which 5 were waited for; matrix products, arithmetic and copies ran while one was open for 9% of the time, Pallas kernels for 0%

profile of v16, /device:TPU:0, one launch (start us, length us, event | category | flops | bytes accessed | tf_op | source)
XLA Modules:
  0.0 90.6 jit_solution(6316170505797165717)
XLA Ops:
  0.6 1.1 %pad_maximum_fusion.2 = f32[3,16,16,128]{3,2,1,0:T(8,128)S(1)} fusion(f32[1,16,16,128]{3,2,1,0:T(8,128)} %bitcast.84, f32[1,16,16,128]{3,2,1,0:T(8,128)} %bitcast.86, f32[1,16,16,128]{3,2,1,0:T(8,128)} %bitcast.88), kind=kLoop, calls=%fused_computation.103 | loop fusion | flops 196608 | bytes 786432 | tf_op jit(solution)/shard_map/stack | solution.py:145
  2.2 0.8 collective-permute-start
  3.2 5.9 %collective-permute-start.1 = (f32[24,128]{1,0:T(8,128)S(1)}, f32[24,128]{1,0:T(8,128)S(1)}, u32[]{:S(2)}, u32[]{:S(2)}) collective-permute-start(f32[24,128]{1,0:T(8,128)S(1)} %reshape.311), channel_id=1, source_target_pairs={{0,8},{8,0},{16,24},{24,16},{1,9},{9,1},{17,25},{25,17},{2,10},{10... | collective-permute-start | bytes 36872 | tf_op jit(solution)/shard_map/ppermute | solution.py:28
  10.2 1.6 %slice.255 = s32[4,4,128]{2,1,0:T(4,128)S(1)} slice(s32[16,16,128]{2,1,0:T(8,128)} %param.9), slice={[0:16:4], [0:16:4], [0:128:1]} | slice | bytes 16384 | tf_op jit(solution)/shard_map/slice | solution.py:176
  12.5 0.6 broadcast_compare_fusion.2
  15.8 1.6 %collective-permute-start.2 = (f32[3,16,544]{2,1,0:T(8,128)S(1)}, f32[3,16,544]{2,1,0:T(8,128)S(1)}, u32[]{:S(2)}, u32[]{:S(2)}) collective-permute-start(f32[3,16,544]{2,1,0:T(8,128)S(1)} %slice_select_fusion.4), channel_id=1, source_target_pairs={{0,1},{1,0},{2,3},{3,2},{4,5},{5,4},{6,7},{7,6},{8,9},{9,8},{10,11... | collective-permute-start | bytes 313352 | tf_op jit(solution)/shard_map/ppermute | solution.py:29
  17.3 3.4 %collective-permute-done.2 = f32[3,16,544]{2,1,0:T(8,128)S(1)} collective-permute-done((f32[3,16,544]{2,1,0:T(8,128)S(1)}, f32[3,16,544]{2,1,0:T(8,128)S(1)}, u32[]{:S(2)}, u32[]{:S(2)}) %collective-permute-start.2) | collective-permute-done | bytes 104480 | tf_op jit(solution)/shard_map/ppermute | solution.py:29
  21.2 0.7 collective-permute-start.3
  22.1 2.9 %collective-permute-start.4 = (f32[306,128]{1,0:T(8,128)S(1)}, f32[306,128]{1,0:T(8,128)S(1)}, u32[]{:S(2)}, u32[]{:S(2)}) collective-permute-start(f32[306,128]{1,0:T(8,128)S(1)} %reshape.314), channel_id=1, source_target_pairs={{0,2},{2,0},{4,6},{6,4},{1,3},{3,1},{5,7},{7,5},{8,10},{10,8},{12,... | collective-permute-start | bytes 470024 | tf_op jit(solution)/shard_map/ppermute | solution.py:28
  25.2 0.8 collective-permute-done.4
  28.4 2.2 %fusion.12 = f32[24,128]{1,0:T(8,128)S(1)} fusion(s32[128]{0:T(128)S(1)} %copy-done.13, s32[128]{0:T(128)S(1)} %copy-done.14, s32[3264]{0:T(1024)S(1)} %get-tuple-element.28, s32[3264]{0:T(1024)S(1)} %get-tuple-element.29, s32[128]{0:T(128)S(1)} %get-tuple-element.35, s32[128]{0:T(128)S(1)} %copy-done.15, s32[3264]{0:T(1024)S(1)} %get-tuple-element.27, ...), kind=kOutput, calls=%fused_computation.23 | convolution fusion | flops 131056128 | bytes 3283969 | tf_op jit(solution)/shard_map/dot_general | solution.py:120
  31.0 0.7 broadcast_in_dim.164
  31.7 5.4 %all-to-all-start = ((f32[32,1,512]{2,1,0:T(1,128)}), f32[32,1,512]{2,1,0:T(1,128)S(1)}, u32[]{:S(2)}, u32[]{:S(2)}) async-start(f32[32,1,512]{2,1,0:T(1,128)} %broadcast_in_dim.164), calls=%async_computation | async-start | bytes 131072 | tf_op jit(solution)/shard_map/all_to_all | solution.py:139
  37.1 1.3 %and_select_fusion = s32[32]{0:T(128)} fusion(s32[32]{0:T(128)} %copy-done.12), kind=kLoop, calls=%fused_computation.341 | loop fusion | flops 480 | bytes 256 | tf_op jit(solution)/shard_map/jit(floor_divide)/jit(_where)/select_n | solution.py:190
  38.3 6.4 %all-to-all-done = f32[32,1,512]{2,1,0:T(1,128)S(1)} async-done(((f32[32,1,512]{2,1,0:T(1,128)}), f32[32,1,512]{2,1,0:T(1,128)S(1)}, u32[]{:S(2)}, u32[]{:S(2)}) %all-to-all-start) | async-done | bytes 65568 | tf_op jit(solution)/shard_map/all_to_all | solution.py:139
  44.7 0.9 fusion.203
  45.6 0.8 fusion.230
  47.1 0.7 divide_add_fusion.2
  47.8 9.3 %all_to_all.33 = f32[32,1,512]{2,1,0:T(1,128)S(1)} all-to-all(f32[32,1,512]{2,1,0:T(1,128)S(1)} %broadcast_in_dim.171), channel_id=1, replica_groups=mesh['grp'=4,'gx'=4,'gy'=2] {'grp','gx','gy'}, dimensions={0} | all-to-all | bytes 131072 | tf_op jit(solution)/shard_map/all_to_all | solution.py:139
  57.1 0.9 fusion.200
  58.0 0.8 fusion.224
  59.5 0.7 broadcast_in_dim.172
  60.2 2.6 %all-to-all-start.2 = ((f32[32,1,512]{2,1,0:T(1,128)}), f32[32,1,512]{2,1,0:T(1,128)S(1)}, u32[]{:S(2)}, u32[]{:S(2)}) async-start(f32[32,1,512]{2,1,0:T(1,128)} %broadcast_in_dim.172), calls=%async_computation.2 | async-start | bytes 131072 | tf_op jit(solution)/shard_map/all_to_all | solution.py:139
  64.0 6.4 %all-to-all-done.2 = f32[32,1,512]{2,1,0:T(1,128)S(1)} async-done(((f32[32,1,512]{2,1,0:T(1,128)}), f32[32,1,512]{2,1,0:T(1,128)S(1)}, u32[]{:S(2)}, u32[]{:S(2)}) %all-to-all-start.2) | async-done | bytes 65568 | tf_op jit(solution)/shard_map/all_to_all | solution.py:139
  70.4 0.9 fusion.197
  71.3 0.8 fusion.218
  72.8 0.7 divide_add_fusion
  73.7 0.7 broadcast_in_dim.174
  74.4 2.8 %all-to-all-start.3 = ((f32[32,1,512]{2,1,0:T(1,128)}), f32[32,1,512]{2,1,0:T(1,128)S(1)}, u32[]{:S(2)}, u32[]{:S(2)}) async-start(f32[32,1,512]{2,1,0:T(1,128)} %broadcast_in_dim.174), calls=%async_computation.3 | async-start | bytes 131072 | tf_op jit(solution)/shard_map/all_to_all | solution.py:139
  77.2 7.4 %all-to-all-done.3 = f32[32,1,512]{2,1,0:T(1,128)S(1)} async-done(((f32[32,1,512]{2,1,0:T(1,128)}), f32[32,1,512]{2,1,0:T(1,128)S(1)}, u32[]{:S(2)}, u32[]{:S(2)}) %all-to-all-start.3) | async-done | bytes 65568 | tf_op jit(solution)/shard_map/all_to_all | solution.py:139
  85.5 1.8 %fusion.4 = f32[6,3264]{1,0:T(8,128)S(1)} fusion(f32[6,204]{1,0:T(8,128)S(1)} %reshape.324, s32[204]{0:T(256)S(1)} %copy-done.11, s32[204]{0:T(256)S(1)} %get-tuple-element.45, s32[3264]{0:T(1024)S(1)} %get-tuple-element.28, s32[3264]{0:T(1024)S(1)} %get-tuple-element.29, s32[204]{0:T(256)S(1)} %copy-done.10, s32[204]{0:T(256)S(1)} %get-tuple-element.46, ...), kind=kOutput, calls=%fused_computation.10 | convolution fusion | flops 58595328 | bytes 145657 | tf_op jit(solution)/shard_map/dot_general | solution.py:120
  89.9 0.8 slice.345
  (112 shorter events, 15.5 us)
Async XLA Ops:
  1.7 10.1 %copy-start.9 = (s32[8,4]{0,1:T(4,128)S(1)}, s32[8,4]{0,1:T(4,128)}, u32[]{:S(2)}) copy-start(s32[8,4]{0,1:T(4,128)} %param.11) | copy-start | bytes 388
  1.7 11.6 %copy-start = (f32[8,64,256]{2,1,0:T(8,128)S(1)}, f32[8,64,256]{2,1,0:T(8,128)}, u32[]{:S(2)}) copy-start(f32[8,64,256]{2,1,0:T(8,128)} %param.10) | copy-start | bytes 1572868
  2.1 12.7 %copy-start.3 = (f32[16,16,128]{2,1,0:T(8,128)S(1)}, f32[16,16,128]{2,1,0:T(8,128)}, u32[]{:S(2)}) copy-start(f32[16,16,128]{2,1,0:T(8,128)} %param.8) | copy-start | bytes 393220
  2.1 12.7 %copy-start.4 = (f32[16,16,128]{2,1,0:T(8,128)S(1)}, f32[16,16,128]{2,1,0:T(8,128)}, u32[]{:S(2)}) copy-start(f32[16,16,128]{2,1,0:T(8,128)} %param.7) | copy-start | bytes 393220
  2.1 12.7 %copy-start.5 = (f32[16,16,128]{2,1,0:T(8,128)S(1)}, f32[16,16,128]{2,1,0:T(8,128)}, u32[]{:S(2)}) copy-start(f32[16,16,128]{2,1,0:T(8,128)} %param.6) | copy-start | bytes 393220
  2.2 11.9 %collective-permute-start = (f32[24,128]{1,0:T(8,128)S(1)}, f32[24,128]{1,0:T(8,128)S(1)}, u32[]{:S(2)}, u32[]{:S(2)}) collective-permute-start(f32[24,128]{1,0:T(8,128)S(1)} %reshape.310), channel_id=1, source_target_pairs={{8,16},{16,8},{9,17},{17,9},{10,18},{18,10},{11,19},{19,11},{12,20... | collective-permute-start | bytes 36872 | tf_op jit(solution)/shard_map/ppermute | solution.py:28
  3.2 10.9 %collective-permute-start.1 = (f32[24,128]{1,0:T(8,128)S(1)}, f32[24,128]{1,0:T(8,128)S(1)}, u32[]{:S(2)}, u32[]{:S(2)}) collective-permute-start(f32[24,128]{1,0:T(8,128)S(1)} %reshape.311), channel_id=1, source_target_pairs={{0,8},{8,0},{16,24},{24,16},{1,9},{9,1},{17,25},{25,17},{2,10},{10... | collective-permute-start | bytes 36872 | tf_op jit(solution)/shard_map/ppermute | solution.py:28
  11.9 2.1 %copy-start.12 = (s32[32]{0:T(128)}, s32[32]{0:T(128)S(1)}, u32[]{:S(2)}) copy-start(s32[32]{0:T(128)S(1)} %reshape.316) | copy-start | bytes 388
  15.8 4.9 %collective-permute-start.2 = (f32[3,16,544]{2,1,0:T(8,128)S(1)}, f32[3,16,544]{2,1,0:T(8,128)S(1)}, u32[]{:S(2)}, u32[]{:S(2)}) collective-permute-start(f32[3,16,544]{2,1,0:T(8,128)S(1)} %slice_select_fusion.4), channel_id=1, source_target_pairs={{0,1},{1,0},{2,3},{3,2},{4,5},{5,4},{6,7},{7,6},{8,9},{9,8},{10,11... | collective-permute-start | bytes 313352 | tf_op jit(solution)/shard_map/ppermute | solution.py:29
  21.2 4.0 %collective-permute-start.3 = (f32[306,128]{1,0:T(8,128)S(1)}, f32[306,128]{1,0:T(8,128)S(1)}, u32[]{:S(2)}, u32[]{:S(2)}) collective-permute-start(f32[306,128]{1,0:T(8,128)S(1)} %reshape.313), channel_id=1, source_target_pairs={{2,4},{4,2},{3,5},{5,3},{10,12},{12,10},{11,13},{13,11},{18,20},{2... | collective-permute-start | bytes 470024 | tf_op jit(solution)/shard_map/ppermute | solution.py:28
  22.1 4.0 %collective-permute-start.4 = (f32[306,128]{1,0:T(8,128)S(1)}, f32[306,128]{1,0:T(8,128)S(1)}, u32[]{:S(2)}, u32[]{:S(2)}) collective-permute-start(f32[306,128]{1,0:T(8,128)S(1)} %reshape.314), channel_id=1, source_target_pairs={{0,2},{2,0},{4,6},{6,4},{1,3},{3,1},{5,7},{7,5},{8,10},{10,8},{12,... | collective-permute-start | bytes 470024 | tf_op jit(solution)/shard_map/ppermute | solution.py:28
  27.6 0.7 copy-start.1
  27.6 0.7 copy-start.13
  27.6 0.7 copy-start.14
  27.6 0.7 copy-start.15
  28.4 2.2 %copy-start.16 = (s32[4]{0:T(128)S(1)}, s32[4]{0:T(128)}, u32[]{:S(2)}) copy-start(s32[4]{0:T(128)} %get-tuple-element.40) | copy-start | bytes 52
  31.0 0.7 copy-start.7
  31.7 13.0 %all-to-all-start = ((f32[32,1,512]{2,1,0:T(1,128)}), f32[32,1,512]{2,1,0:T(1,128)S(1)}, u32[]{:S(2)}, u32[]{:S(2)}) async-start(f32[32,1,512]{2,1,0:T(1,128)} %broadcast_in_dim.164), calls=%async_computation | async-start | bytes 131072 | tf_op jit(solution)/shard_map/all_to_all | solution.py:139
  59.5 0.7 copy-start.6
  60.2 10.2 %all-to-all-start.2 = ((f32[32,1,512]{2,1,0:T(1,128)}), f32[32,1,512]{2,1,0:T(1,128)S(1)}, u32[]{:S(2)}, u32[]{:S(2)}) async-start(f32[32,1,512]{2,1,0:T(1,128)} %broadcast_in_dim.172), calls=%async_computation.2 | async-start | bytes 131072 | tf_op jit(solution)/shard_map/all_to_all | solution.py:139
  72.7 12.8 %copy-start.10 = (s32[204]{0:T(256)S(1)}, s32[204]{0:T(256)}, u32[]{:S(2)}) copy-start(s32[204]{0:T(256)} %get-tuple-element.41) | copy-start | bytes 2452
  72.7 12.8 %copy-start.11 = (s32[204]{0:T(256)S(1)}, s32[204]{0:T(256)}, u32[]{:S(2)}) copy-start(s32[204]{0:T(256)} %get-tuple-element.42) | copy-start | bytes 2452
  72.7 12.8 %copy-start.17 = (pred[204]{0:T(512)(128)(4,1)S(1)}, pred[204]{0:T(512)(128)(4,1)}, u32[]{:S(2)}) copy-start(pred[204]{0:T(512)(128)(4,1)} %get-tuple-element.43) | copy-start | bytes 616
  72.7 12.8 %copy-start.18 = (pred[204]{0:T(512)(128)(4,1)S(1)}, pred[204]{0:T(512)(128)(4,1)}, u32[]{:S(2)}) copy-start(pred[204]{0:T(512)(128)(4,1)} %get-tuple-element.44) | copy-start | bytes 616
  73.5 13.8 %copy-start.8 = (f32[512]{0:T(512)}, f32[512]{0:T(512)S(1)}, u32[]{:S(2)}) copy-start(f32[512]{0:T(512)S(1)} %divide_add_fusion) | copy-start | bytes 6148
  74.4 10.2 %all-to-all-start.3 = ((f32[32,1,512]{2,1,0:T(1,128)}), f32[32,1,512]{2,1,0:T(1,128)S(1)}, u32[]{:S(2)}, u32[]{:S(2)}) async-start(f32[32,1,512]{2,1,0:T(1,128)} %broadcast_in_dim.174), calls=%async_computation.3 | async-start | bytes 131072 | tf_op jit(solution)/shard_map/all_to_all | solution.py:139
  85.5 2.3 %copy-start.2 = (f32[24,3264]{1,0:T(8,128)S(1)}, f32[24,3264]{1,0:T(8,128)}, u32[]{:S(2)}) copy-start(f32[24,3264]{1,0:T(8,128)} %copy-done.1) | copy-start | bytes 940036

commit v17 on v15

--- a/solution.py
+++ b/solution.py
@@ -121,16 +121,17 @@
 
 
 def box_matrix(boxes, cells, stride, offset, live, inner=None):
-    box = lax.broadcasted_iota(jnp.int32, (boxes, cells), 0)
-    cell = lax.broadcasted_iota(jnp.int32, (boxes, cells), 1)
+    cell = lax.broadcasted_iota(jnp.int32, (1, cells), 1)
     if inner is None:
-        hit = (cell - offset >= box * BOX) & (cell - offset < box * BOX + BOX)
+        local = cell - offset
+        owner = jnp.where((local >= 0) & (local < boxes * BOX), local // BOX, -1)
     else:
         outer_cell, inner_cell = cell // stride - offset, cell % stride - offset
-        outer_box, inner_box = box // inner, box % inner
-        hit = (outer_cell >= outer_box * BOX) & (outer_cell < outer_box * BOX + BOX)
-        hit = hit & (inner_cell >= inner_box * BOX) & (inner_cell < inner_box * BOX + BOX)
-    return (hit & live).astype(jnp.float32)
+        inside = (outer_cell >= 0) & (outer_cell < (boxes // inner) * BOX)
+        inside = inside & (inner_cell >= 0) & (inner_cell < inner * BOX)
+        owner = jnp.where(inside, (outer_cell // BOX) * inner + inner_cell // BOX, -1)
+    box = lax.broadcasted_iota(jnp.int32, (boxes, cells), 0)
+    return ((box == owner) & live).astype(jnp.float32)
 
 
 def everyone(vector):

time: 88.2 us -> 84.6 us (0.959)
  blocking collectives: 9.3 us -> 18.6 us
  waiting for transfers between devices: 23.8 us -> 16.7 us
  starting transfers between devices: 22.1 us -> 19.5 us
  other arithmetic: 13.3 us -> 11.5 us
    all_to_all x1 -> x2, blocking collectives: 9.3 us -> 18.6 us  [everyone(): return lax.all_to_all(copies, ALL_AXES, 0, 0, tiled=True).reshape(-1)]
    all_to_all x3 -> x2, waiting for transfers between devices: 20.3 us -> 13.3 us  [everyone(): return lax.all_to_all(copies, ALL_AXES, 0, 0, tiled=True).reshape(-1)]
    all_to_all x3 -> x2, starting transfers between devices: 10.3 us -> 7.76 us  [everyone(): return lax.all_to_all(copies, ALL_AXES, 0, 0, tiled=True).reshape(-1)]
  transfers between devices with their start and end apart: 8 -> 7, of which waited for: 5 -> 4; matrix products, arithmetic and copies ran while one was open for 7% -> 7% of each run, Pallas kernels for 0% -> 0%
where the time goes in v17:
time: 84.6 us; the launch traced here: 84.1 us
  starting transfers between devices  19.5 us (23%)
  blocking collectives  18.6 us (22%)
  waiting for transfers between devices  16.7 us (20%)
  other arithmetic  11.5 us (14%)
  local copies, waits for them, and re-layouts  8.69 us (10%)
  matrix products  7.82 us (9%)
  between operations  1.21 us (1%)
    all_to_all x2, blocking collectives, everyone(): return lax.all_to_all(copies, ALL_AXES, 0, 0, tiled=True).reshape(-1)  18.6 us
    all_to_all x2, waiting for transfers between devices, everyone(): return lax.all_to_all(copies, ALL_AXES, 0, 0, tiled=True).reshape(-1)  13.3 us
    ppermute x4, starting transfers between devices, permute(): return lax.ppermute(slab.reshape(-1, 128), axis, pairs).reshape(slab.shape)  10.2 us
    all_to_all x2, starting transfers between devices, everyone(): return lax.all_to_all(copies, ALL_AXES, 0, 0, tiled=True).reshape(-1)  7.76 us
    dot_general x7, matrix products, dot(): return jnp.dot(left, right, precision=lax.Precision.HIGHEST)  6.26 us
    ppermute x1, waiting for transfers between devices, permute(): return lax.ppermute(slab, axis, pairs)  3.38 us
    slice x1, local copies, waits for them, and re-layouts, local(): box_labels = aggregate_ids[::BOX, ::BOX, ::BOX].reshape(-1)  1.87 us
    select_n x3, other arithmetic, local(): jnp.where(within == part, rows_of[:, part * 64:(part + 1) * 64], blocks)  1.72 us
  transfers between devices with their start and end apart: 7, of which 4 were waited for; matrix products, arithmetic and copies ran while one was open for 7% of the time, Pallas kernels for 0%

profile of v17, /device:TPU:0, one launch (start us, length us, event | category | flops | bytes accessed | tf_op | source)
XLA Modules:
  0.0 84.1 jit_solution(13483024388001430247)
XLA Ops:
  0.6 1.1 %pad_maximum_fusion.2 = f32[3,16,16,128]{3,2,1,0:T(8,128)S(1)} fusion(f32[1,16,16,128]{3,2,1,0:T(8,128)} %bitcast.80, f32[1,16,16,128]{3,2,1,0:T(8,128)} %bitcast.82, f32[1,16,16,128]{3,2,1,0:T(8,128)} %bitcast.84), kind=kLoop, calls=%fused_computation.58 | loop fusion | flops 196608 | bytes 786432 | tf_op jit(solution)/shard_map/stack | solution.py:146
  2.2 0.7 collective-permute-start
  3.0 5.9 %collective-permute-start.1 = (f32[24,128]{1,0:T(8,128)S(1)}, f32[24,128]{1,0:T(8,128)S(1)}, u32[]{:S(2)}, u32[]{:S(2)}) collective-permute-start(f32[24,128]{1,0:T(8,128)S(1)} %reshape.609), channel_id=1, source_target_pairs={{0,8},{8,0},{16,24},{24,16},{1,9},{9,1},{17,25},{25,17},{2,10},{10... | collective-permute-start | bytes 36872 | tf_op jit(solution)/shard_map/ppermute | solution.py:28
  9.2 0.6 broadcast_compare_fusion.6
  9.8 0.6 broadcast_compare_fusion.3
  12.4 1.6 %collective-permute-start.2 = (f32[3,16,544]{2,1,0:T(8,128)S(1)}, f32[3,16,544]{2,1,0:T(8,128)S(1)}, u32[]{:S(2)}, u32[]{:S(2)}) collective-permute-start(f32[3,16,544]{2,1,0:T(8,128)S(1)} %slice_select_fusion.4), channel_id=1, source_target_pairs={{0,1},{1,0},{2,3},{3,2},{4,5},{5,4},{6,7},{7,6},{8,9},{9,8},{10,11... | collective-permute-start | bytes 313352 | tf_op jit(solution)/shard_map/ppermute | solution.py:29
  13.9 3.4 %collective-permute-done.2 = f32[3,16,544]{2,1,0:T(8,128)S(1)} collective-permute-done((f32[3,16,544]{2,1,0:T(8,128)S(1)}, f32[3,16,544]{2,1,0:T(8,128)S(1)}, u32[]{:S(2)}, u32[]{:S(2)}) %collective-permute-start.2) | collective-permute-done | bytes 104480 | tf_op jit(solution)/shard_map/ppermute | solution.py:29
  17.8 0.7 collective-permute-start.3
  18.7 2.9 %collective-permute-start.4 = (f32[306,128]{1,0:T(8,128)S(1)}, f32[306,128]{1,0:T(8,128)S(1)}, u32[]{:S(2)}, u32[]{:S(2)}) collective-permute-start(f32[306,128]{1,0:T(8,128)S(1)} %reshape.612), channel_id=1, source_target_pairs={{0,2},{2,0},{4,6},{6,4},{1,3},{3,1},{5,7},{7,5},{8,10},{10,8},{12,... | collective-permute-start | bytes 470024 | tf_op jit(solution)/shard_map/ppermute | solution.py:28
  21.6 1.9 %slice.255 = s32[4,4,32]{2,1,0:T(4,128)S(1)} slice(s32[16,16,128]{2,1,0:T(8,128)} %param.9), slice={[0:16:4], [0:16:4], [0:128:4]} | slice | bytes 4096 | tf_op jit(solution)/shard_map/slice | solution.py:177
  24.7 0.6 fusion.161
  26.0 1.6 %fusion.4 = f32[24,128]{1,0:T(8,128)S(1)} fusion(s32[3264]{0:T(1024)S(1)} %fusion.181, pred[]{:T(512)S(6)} %ge.57, f32[24,3264]{1,0:T(8,128)S(1)} %get-tuple-element.5, f32[24,3264]{1,0:T(8,128)S(1)} %divide_select_fusion, f32[24,3264]{1,0:T(8,128)S(1)} %get-tuple-element.6, f32[24,3264]{1,0:T(8,128)S(1)} %get-tuple-element.7, ...), kind=kOutput, calls=%fused_computation.5 | convolution fusion | flops 124371456 | bytes 3223553 | tf_op jit(solution)/shard_map/dot_general | solution.py:120
  27.9 0.7 broadcast_in_dim.170
  28.6 5.0 %all-to-all-start = ((f32[32,1,512]{2,1,0:T(1,128)}), f32[32,1,512]{2,1,0:T(1,128)S(1)}, u32[]{:S(2)}, u32[]{:S(2)}) async-start(f32[32,1,512]{2,1,0:T(1,128)} %broadcast_in_dim.170), calls=%async_computation | async-start | bytes 131072 | tf_op jit(solution)/shard_map/all_to_all | solution.py:140
  33.6 1.1 %and_select_fusion = s32[32]{0:T(128)} fusion(s32[32]{0:T(128)} %copy-done.16), kind=kLoop, calls=%fused_computation.324 | loop fusion | flops 480 | bytes 256 | tf_op jit(solution)/shard_map/jit(floor_divide)/jit(_where)/select_n | solution.py:189
  34.7 6.5 %all-to-all-done = f32[32,1,512]{2,1,0:T(1,128)S(1)} async-done(((f32[32,1,512]{2,1,0:T(1,128)}), f32[32,1,512]{2,1,0:T(1,128)S(1)}, u32[]{:S(2)}, u32[]{:S(2)}) %all-to-all-start) | async-done | bytes 65568 | tf_op jit(solution)/shard_map/all_to_all | solution.py:140
  41.2 0.8 fusion.169
  42.0 0.8 fusion.206
  43.6 0.7 divide_add_fusion.2
  44.3 9.3 %all_to_all.33 = f32[32,1,512]{2,1,0:T(1,128)S(1)} all-to-all(f32[32,1,512]{2,1,0:T(1,128)S(1)} %broadcast_in_dim.177), channel_id=1, replica_groups=mesh['grp'=4,'gx'=4,'gy'=2] {'grp','gx','gy'}, dimensions={0} | all-to-all | bytes 131072 | tf_op jit(solution)/shard_map/all_to_all | solution.py:140
  53.6 0.8 fusion.166
  54.5 0.8 fusion.200
  56.0 9.3 %all_to_all.34 = f32[32,1,512]{2,1,0:T(1,128)S(1)} all-to-all(f32[32,1,512]{2,1,0:T(1,128)S(1)} %broadcast_in_dim.178), channel_id=1, replica_groups=mesh['grp'=4,'gx'=4,'gy'=2] {'grp','gx','gy'}, dimensions={0} | all-to-all | bytes 131072 | tf_op jit(solution)/shard_map/all_to_all | solution.py:140
  65.3 0.8 fusion.163
  67.3 0.7 broadcast_in_dim.180
  68.0 2.8 %all-to-all-start.3 = ((f32[32,1,512]{2,1,0:T(1,128)}), f32[32,1,512]{2,1,0:T(1,128)S(1)}, u32[]{:S(2)}, u32[]{:S(2)}) async-start(f32[32,1,512]{2,1,0:T(1,128)} %broadcast_in_dim.180), calls=%async_computation.3 | async-start | bytes 131072 | tf_op jit(solution)/shard_map/all_to_all | solution.py:140
  70.7 0.6 fusion.186
  71.4 6.8 %all-to-all-done.3 = f32[32,1,512]{2,1,0:T(1,128)S(1)} async-done(((f32[32,1,512]{2,1,0:T(1,128)}), f32[32,1,512]{2,1,0:T(1,128)S(1)}, u32[]{:S(2)}, u32[]{:S(2)}) %all-to-all-start.3) | async-done | bytes 65568 | tf_op jit(solution)/shard_map/all_to_all | solution.py:140
  79.0 1.8 %fusion.1 = f32[6,3264]{1,0:T(8,128)S(1)} fusion(f32[6,204]{1,0:T(8,128)S(1)} %reshape.622, s32[3264]{0:T(1024)} %fusion.186, pred[]{:T(512)S(6)} %ge.57), kind=kOutput, calls=%fused_computation.2 | convolution fusion | flops 49273344 | bytes 96289 | tf_op jit(solution)/shard_map/dot_general | solution.py:120
  81.2 0.6 fusion.160
  82.3 0.6 fusion.158
  83.3 0.8 slice.345
  (99 shorter events, 10.4 us)
Async XLA Ops:
  1.7 7.3 %copy-start.15 = (s32[8,4]{0,1:T(4,128)S(1)}, s32[8,4]{0,1:T(4,128)}, u32[]{:S(2)}) copy-start(s32[8,4]{0,1:T(4,128)} %param.11) | copy-start | bytes 388
  1.7 8.7 %copy-start = (f32[8,64,256]{2,1,0:T(8,128)S(1)}, f32[8,64,256]{2,1,0:T(8,128)}, u32[]{:S(2)}) copy-start(f32[8,64,256]{2,1,0:T(8,128)} %param.10) | copy-start | bytes 1572868
  1.9 9.5 %copy-start.3 = (f32[16,16,128]{2,1,0:T(8,128)S(1)}, f32[16,16,128]{2,1,0:T(8,128)}, u32[]{:S(2)}) copy-start(f32[16,16,128]{2,1,0:T(8,128)} %param.8) | copy-start | bytes 393220
  1.9 9.5 %copy-start.4 = (f32[16,16,128]{2,1,0:T(8,128)S(1)}, f32[16,16,128]{2,1,0:T(8,128)}, u32[]{:S(2)}) copy-start(f32[16,16,128]{2,1,0:T(8,128)} %param.7) | copy-start | bytes 393220
  1.9 9.5 %copy-start.5 = (f32[16,16,128]{2,1,0:T(8,128)S(1)}, f32[16,16,128]{2,1,0:T(8,128)}, u32[]{:S(2)}) copy-start(f32[16,16,128]{2,1,0:T(8,128)} %param.6) | copy-start | bytes 393220
  2.2 8.4 %collective-permute-start = (f32[24,128]{1,0:T(8,128)S(1)}, f32[24,128]{1,0:T(8,128)S(1)}, u32[]{:S(2)}, u32[]{:S(2)}) collective-permute-start(f32[24,128]{1,0:T(8,128)S(1)} %reshape.608), channel_id=1, source_target_pairs={{8,16},{16,8},{9,17},{17,9},{10,18},{18,10},{11,19},{19,11},{12,20... | collective-permute-start | bytes 36872 | tf_op jit(solution)/shard_map/ppermute | solution.py:28
  3.0 7.6 %collective-permute-start.1 = (f32[24,128]{1,0:T(8,128)S(1)}, f32[24,128]{1,0:T(8,128)S(1)}, u32[]{:S(2)}, u32[]{:S(2)}) collective-permute-start(f32[24,128]{1,0:T(8,128)S(1)} %reshape.609), channel_id=1, source_target_pairs={{0,8},{8,0},{16,24},{24,16},{1,9},{9,1},{17,25},{25,17},{2,10},{10... | collective-permute-start | bytes 36872 | tf_op jit(solution)/shard_map/ppermute | solution.py:28
  9.2 2.6 %copy-start.16 = (s32[32]{0:T(128)}, s32[32]{0:T(128)S(1)}, u32[]{:S(2)}) copy-start(s32[32]{0:T(128)S(1)} %reshape.614) | copy-start | bytes 388
  12.4 4.9 %collective-permute-start.2 = (f32[3,16,544]{2,1,0:T(8,128)S(1)}, f32[3,16,544]{2,1,0:T(8,128)S(1)}, u32[]{:S(2)}, u32[]{:S(2)}) collective-permute-start(f32[3,16,544]{2,1,0:T(8,128)S(1)} %slice_select_fusion.4), channel_id=1, source_target_pairs={{0,1},{1,0},{2,3},{3,2},{4,5},{5,4},{6,7},{7,6},{8,9},{9,8},{10,11... | collective-permute-start | bytes 313352 | tf_op jit(solution)/shard_map/ppermute | solution.py:29
  17.8 5.8 %collective-permute-start.3 = (f32[306,128]{1,0:T(8,128)S(1)}, f32[306,128]{1,0:T(8,128)S(1)}, u32[]{:S(2)}, u32[]{:S(2)}) collective-permute-start(f32[306,128]{1,0:T(8,128)S(1)} %reshape.611), channel_id=1, source_target_pairs={{2,4},{4,2},{3,5},{5,3},{10,12},{12,10},{11,13},{13,11},{18,20},{2... | collective-permute-start | bytes 470024 | tf_op jit(solution)/shard_map/ppermute | solution.py:28
  18.7 5.0 %collective-permute-start.4 = (f32[306,128]{1,0:T(8,128)S(1)}, f32[306,128]{1,0:T(8,128)S(1)}, u32[]{:S(2)}, u32[]{:S(2)}) collective-permute-start(f32[306,128]{1,0:T(8,128)S(1)} %reshape.612), channel_id=1, source_target_pairs={{0,2},{2,0},{4,6},{6,4},{1,3},{3,1},{5,7},{7,5},{8,10},{10,8},{12,... | collective-permute-start | bytes 470024 | tf_op jit(solution)/shard_map/ppermute | solution.py:28
  25.2 0.7 copy-start.1
  27.9 0.7 copy-start.6
  28.6 12.6 %all-to-all-start = ((f32[32,1,512]{2,1,0:T(1,128)}), f32[32,1,512]{2,1,0:T(1,128)S(1)}, u32[]{:S(2)}, u32[]{:S(2)}) async-start(f32[32,1,512]{2,1,0:T(1,128)} %broadcast_in_dim.170), calls=%async_computation | async-start | bytes 131072 | tf_op jit(solution)/shard_map/all_to_all | solution.py:140
  42.9 23.2 %copy-start.7 = (pred[32]{0:T(512)(128)(4,1)S(1)}, pred[32]{0:T(512)(128)(4,1)}, u32[]{:S(2)}) copy-start(pred[32]{0:T(512)(128)(4,1)} %get-tuple-element.21) | copy-start | bytes 100
  42.9 23.2 %copy-start.8 = (pred[32]{0:T(512)(128)(4,1)S(1)}, pred[32]{0:T(512)(128)(4,1)}, u32[]{:S(2)}) copy-start(pred[32]{0:T(512)(128)(4,1)} %get-tuple-element.22) | copy-start | bytes 100
  42.9 23.2 %copy-start.9 = (pred[32]{0:T(512)(128)(4,1)S(1)}, pred[32]{0:T(512)(128)(4,1)}, u32[]{:S(2)}) copy-start(pred[32]{0:T(512)(128)(4,1)} %get-tuple-element.23) | copy-start | bytes 100
  43.0 23.2 %copy-start.10 = (pred[32]{0:T(512)(128)(4,1)S(1)}, pred[32]{0:T(512)(128)(4,1)}, u32[]{:S(2)}) copy-start(pred[32]{0:T(512)(128)(4,1)} %get-tuple-element.24) | copy-start | bytes 100
  43.0 23.2 %copy-start.11 = (pred[32]{0:T(512)(128)(4,1)S(1)}, pred[32]{0:T(512)(128)(4,1)}, u32[]{:S(2)}) copy-start(pred[32]{0:T(512)(128)(4,1)} %get-tuple-element.25) | copy-start | bytes 100
  43.0 23.2 %copy-start.12 = (pred[32]{0:T(512)(128)(4,1)S(1)}, pred[32]{0:T(512)(128)(4,1)}, u32[]{:S(2)}) copy-start(pred[32]{0:T(512)(128)(4,1)} %get-tuple-element.26) | copy-start | bytes 100
  43.0 23.2 %copy-start.14 = (pred[32]{0:T(512)(128)(4,1)S(1)}, pred[32]{0:T(512)(128)(4,1)}, u32[]{:S(2)}) copy-start(pred[32]{0:T(512)(128)(4,1)} %get-tuple-element.2) | copy-start | bytes 100
  67.0 11.5 %copy-start.13 = (f32[512]{0:T(512)}, f32[512]{0:T(512)S(1)}, u32[]{:S(2)}) copy-start(f32[512]{0:T(512)S(1)} %divide_add_fusion) | copy-start | bytes 6148
  68.0 10.2 %all-to-all-start.3 = ((f32[32,1,512]{2,1,0:T(1,128)}), f32[32,1,512]{2,1,0:T(1,128)S(1)}, u32[]{:S(2)}, u32[]{:S(2)}) async-start(f32[32,1,512]{2,1,0:T(1,128)} %broadcast_in_dim.180), calls=%async_computation.3 | async-start | bytes 131072 | tf_op jit(solution)/shard_map/all_to_all | solution.py:140
  78.8 2.3 %copy-start.2 = (f32[24,3264]{1,0:T(8,128)S(1)}, f32[24,3264]{1,0:T(8,128)}, u32[]{:S(2)}) copy-start(f32[24,3264]{1,0:T(8,128)} %copy-done.1) | copy-start | bytes 940036

commit v18 on v17

--- a/solution.py
+++ b/solution.py
@@ -145,6 +145,9 @@
     assert HALO == BOX and HALO >= 2 * NU and HALO >= NU + 2
     stacked = jnp.stack([source, conductance, storage])
     wide = exchange(stacked, (("grp", 3),), HALO)
+    wide, box_labels = lax.optimization_barrier(
+        (wide, aggregate_ids[::BOX, ::BOX, ::BOX].reshape(-1))
+    )
     span_z = wide.shape[3]
     stride = span_z
     wide = wide.reshape(3, size_x, size_y * span_z)
@@ -174,7 +177,6 @@
     pick_x = box_matrix(bx, rows, 1, HALO, live)
     pick_yz = box_matrix(by * bz, span_y * span_z, span_z, HALO, live, bz).T
     box_totals = dot(pick_x, dot(smoothed, pick_yz)).reshape(-1)
-    box_labels = aggregate_ids[::BOX, ::BOX, ::BOX].reshape(-1)
     placed = box_labels[:, None] == lax.broadcasted_iota(jnp.int32, (box_labels.shape[0],) * 2, 1)
     coarse_rhs = jnp.sum(jnp.where(placed, box_totals[:, None], 0.0), axis=0)
     eye = lax.broadcasted_iota(jnp.int32, (64, 64), 0) == lax.broadcasted_iota(jnp.int32, (64, 64), 1)

time: 84.6 us -> 85.8 us (1.014)
  waiting for transfers between devices: 16.7 us -> 17.6 us
    ppermute x4, waiting for transfers between devices: 0.06 us -> 0.93 us  [permute(): return lax.ppermute(slab.reshape(-1, 128), axis, pairs).reshape(slab.shape)]
where the time goes in v18:
time: 85.8 us; the launch traced here: 85.3 us
  starting transfers between devices  19.9 us (23%)
  blocking collectives  18.6 us (22%)
  waiting for transfers between devices  17.6 us (21%)
  other arithmetic  11.5 us (13%)
  local copies, waits for them, and re-layouts  8.7 us (10%)
  matrix products  7.81 us (9%)
  between operations  1.19 us (1%)
    all_to_all x2, blocking collectives, everyone(): return lax.all_to_all(copies, ALL_AXES, 0, 0, tiled=True).reshape(-1)  18.6 us
    all_to_all x2, waiting for transfers between devices, everyone(): return lax.all_to_all(copies, ALL_AXES, 0, 0, tiled=True).reshape(-1)  13.3 us
    ppermute x4, starting transfers between devices, permute(): return lax.ppermute(slab.reshape(-1, 128), axis, pairs).reshape(slab.shape)  10.2 us
    all_to_all x2, starting transfers between devices, everyone(): return lax.all_to_all(copies, ALL_AXES, 0, 0, tiled=True).reshape(-1)  8.15 us
    dot_general x7, matrix products, dot(): return jnp.dot(left, right, precision=lax.Precision.HIGHEST)  6.26 us
    ppermute x1, waiting for transfers between devices, permute(): return lax.ppermute(slab, axis, pairs)  3.38 us
    slice x1, local copies, waits for them, and re-layouts, local(): aggregate_ids[::BOX, ::BOX, ::BOX].reshape(-1)  1.88 us
    select_n x3, other arithmetic, local(): jnp.where(within == part, rows_of[:, part * 64:(part + 1) * 64], blocks)  1.72 us
  transfers between devices with their start and end apart: 7, of which 4 were waited for; matrix products, arithmetic and copies ran while one was open for 7% of the time, Pallas kernels for 0%

profile of v18, /device:TPU:0, one launch (start us, length us, event | category | flops | bytes accessed | tf_op | source)
XLA Modules:
  0.0 85.3 jit_solution(861092572294410797)
XLA Ops:
  0.6 1.1 %pad_maximum_fusion.2 = f32[3,16,16,128]{3,2,1,0:T(8,128)S(1)} fusion(f32[1,16,16,128]{3,2,1,0:T(8,128)} %bitcast.80, f32[1,16,16,128]{3,2,1,0:T(8,128)} %bitcast.82, f32[1,16,16,128]{3,2,1,0:T(8,128)} %bitcast.84), kind=kLoop, calls=%fused_computation.58 | loop fusion | flops 196608 | bytes 786432 | tf_op jit(solution)/shard_map/stack | solution.py:146
  2.2 0.7 collective-permute-start
  3.0 5.9 %collective-permute-start.1 = (f32[24,128]{1,0:T(8,128)S(1)}, f32[24,128]{1,0:T(8,128)S(1)}, u32[]{:S(2)}, u32[]{:S(2)}) collective-permute-start(f32[24,128]{1,0:T(8,128)S(1)} %reshape.612), channel_id=1, source_target_pairs={{0,8},{8,0},{16,24},{24,16},{1,9},{9,1},{17,25},{25,17},{2,10},{10... | collective-permute-start | bytes 36872 | tf_op jit(solution)/shard_map/ppermute | solution.py:28
  9.2 0.6 broadcast_compare_fusion.6
  9.8 0.6 broadcast_compare_fusion.3
  10.6 1.9 %slice.236 = s32[4,4,32]{2,1,0:T(4,128)S(1)} slice(s32[16,16,128]{2,1,0:T(8,128)} %param.9), slice={[0:16:4], [0:16:4], [0:128:4]} | slice | bytes 4096 | tf_op jit(solution)/shard_map/slice | solution.py:149
  14.3 1.6 %collective-permute-start.2 = (f32[3,16,544]{2,1,0:T(8,128)S(1)}, f32[3,16,544]{2,1,0:T(8,128)S(1)}, u32[]{:S(2)}, u32[]{:S(2)}) collective-permute-start(f32[3,16,544]{2,1,0:T(8,128)S(1)} %slice_select_fusion.4), channel_id=1, source_target_pairs={{0,1},{1,0},{2,3},{3,2},{4,5},{5,4},{6,7},{7,6},{8,9},{9,8},{10,11... | collective-permute-start | bytes 313352 | tf_op jit(solution)/shard_map/ppermute | solution.py:29
  15.8 3.4 %collective-permute-done.2 = f32[3,16,544]{2,1,0:T(8,128)S(1)} collective-permute-done((f32[3,16,544]{2,1,0:T(8,128)S(1)}, f32[3,16,544]{2,1,0:T(8,128)S(1)}, u32[]{:S(2)}, u32[]{:S(2)}) %collective-permute-start.2) | collective-permute-done | bytes 104480 | tf_op jit(solution)/shard_map/ppermute | solution.py:29
  19.7 0.7 collective-permute-start.3
  20.6 2.9 %collective-permute-start.4 = (f32[306,128]{1,0:T(8,128)S(1)}, f32[306,128]{1,0:T(8,128)S(1)}, u32[]{:S(2)}, u32[]{:S(2)}) collective-permute-start(f32[306,128]{1,0:T(8,128)S(1)} %reshape.616), channel_id=1, source_target_pairs={{0,2},{2,0},{4,6},{6,4},{1,3},{3,1},{5,7},{7,5},{8,10},{10,8},{12,... | collective-permute-start | bytes 470024 | tf_op jit(solution)/shard_map/ppermute | solution.py:28
  23.6 0.9 %collective-permute-done.4 = f32[306,128]{1,0:T(8,128)S(1)} collective-permute-done((f32[306,128]{1,0:T(8,128)S(1)}, f32[306,128]{1,0:T(8,128)S(1)}, u32[]{:S(2)}, u32[]{:S(2)}) %collective-permute-start.4) | collective-permute-done | bytes 156704 | tf_op jit(solution)/shard_map/ppermute | solution.py:28
  26.8 1.6 %fusion.4 = f32[24,128]{1,0:T(8,128)S(1)} fusion(s32[3264]{0:T(1024)S(1)} %fusion.181, pred[]{:T(512)S(6)} %ge.57, f32[24,3264]{1,0:T(8,128)S(1)} %get-tuple-element.9, f32[24,3264]{1,0:T(8,128)S(1)} %divide_select_fusion, f32[24,3264]{1,0:T(8,128)S(1)} %get-tuple-element.10, f32[24,3264]{1,0:T(8,128)S(1)} %get-tuple-element.11, ...), kind=kOutput, calls=%fused_computation.5 | convolution fusion | flops 124371456 | bytes 3223553 | tf_op jit(solution)/shard_map/dot_general | solution.py:120
  28.8 0.7 broadcast_in_dim.171
  29.4 5.4 %all-to-all-start = ((f32[32,1,512]{2,1,0:T(1,128)}), f32[32,1,512]{2,1,0:T(1,128)S(1)}, u32[]{:S(2)}, u32[]{:S(2)}) async-start(f32[32,1,512]{2,1,0:T(1,128)} %broadcast_in_dim.171), calls=%async_computation | async-start | bytes 131072 | tf_op jit(solution)/shard_map/all_to_all | solution.py:140
  34.9 1.1 %and_select_fusion = s32[32]{0:T(128)} fusion(s32[32]{0:T(128)} %copy-done.16), kind=kLoop, calls=%fused_computation.324 | loop fusion | flops 480 | bytes 256 | tf_op jit(solution)/shard_map/jit(floor_divide)/jit(_where)/select_n | solution.py:191
  35.9 6.5 %all-to-all-done = f32[32,1,512]{2,1,0:T(1,128)S(1)} async-done(((f32[32,1,512]{2,1,0:T(1,128)}), f32[32,1,512]{2,1,0:T(1,128)S(1)}, u32[]{:S(2)}, u32[]{:S(2)}) %all-to-all-start) | async-done | bytes 65568 | tf_op jit(solution)/shard_map/all_to_all | solution.py:140
  42.5 0.8 fusion.169
  43.3 0.8 fusion.206
  44.8 0.7 divide_add_fusion.2
  45.6 9.3 %all_to_all.33 = f32[32,1,512]{2,1,0:T(1,128)S(1)} all-to-all(f32[32,1,512]{2,1,0:T(1,128)S(1)} %broadcast_in_dim.178), channel_id=1, replica_groups=mesh['grp'=4,'gx'=4,'gy'=2] {'grp','gx','gy'}, dimensions={0} | all-to-all | bytes 131072 | tf_op jit(solution)/shard_map/all_to_all | solution.py:140
  54.9 0.8 fusion.166
  55.7 0.8 fusion.200
  57.3 9.3 %all_to_all.34 = f32[32,1,512]{2,1,0:T(1,128)S(1)} all-to-all(f32[32,1,512]{2,1,0:T(1,128)S(1)} %broadcast_in_dim.179), channel_id=1, replica_groups=mesh['grp'=4,'gx'=4,'gy'=2] {'grp','gx','gy'}, dimensions={0} | all-to-all | bytes 131072 | tf_op jit(solution)/shard_map/all_to_all | solution.py:140
  66.6 0.8 fusion.163
  68.5 0.7 broadcast_in_dim.181
  69.2 2.8 %all-to-all-start.3 = ((f32[32,1,512]{2,1,0:T(1,128)}), f32[32,1,512]{2,1,0:T(1,128)S(1)}, u32[]{:S(2)}, u32[]{:S(2)}) async-start(f32[32,1,512]{2,1,0:T(1,128)} %broadcast_in_dim.181), calls=%async_computation.3 | async-start | bytes 131072 | tf_op jit(solution)/shard_map/all_to_all | solution.py:140
  72.0 0.6 fusion.186
  72.6 6.8 %all-to-all-done.3 = f32[32,1,512]{2,1,0:T(1,128)S(1)} async-done(((f32[32,1,512]{2,1,0:T(1,128)}), f32[32,1,512]{2,1,0:T(1,128)S(1)}, u32[]{:S(2)}, u32[]{:S(2)}) %all-to-all-start.3) | async-done | bytes 65568 | tf_op jit(solution)/shard_map/all_to_all | solution.py:140
  80.3 1.8 %fusion.1 = f32[6,3264]{1,0:T(8,128)S(1)} fusion(f32[6,204]{1,0:T(8,128)S(1)} %reshape.626, s32[3264]{0:T(1024)} %fusion.186, pred[]{:T(512)S(6)} %ge.57), kind=kOutput, calls=%fused_computation.2 | convolution fusion | flops 49273344 | bytes 96289 | tf_op jit(solution)/shard_map/dot_general | solution.py:120
  82.4 0.6 fusion.160
  83.6 0.6 fusion.158
  84.5 0.8 slice.345
  (99 shorter events, 10.9 us)
Async XLA Ops:
  1.7 7.3 %copy-start.15 = (s32[8,4]{0,1:T(4,128)S(1)}, s32[8,4]{0,1:T(4,128)}, u32[]{:S(2)}) copy-start(s32[8,4]{0,1:T(4,128)} %param.11) | copy-start | bytes 388
  1.7 8.7 %copy-start = (f32[8,64,256]{2,1,0:T(8,128)S(1)}, f32[8,64,256]{2,1,0:T(8,128)}, u32[]{:S(2)}) copy-start(f32[8,64,256]{2,1,0:T(8,128)} %param.10) | copy-start | bytes 1572868
  1.9 11.4 %copy-start.3 = (f32[16,16,128]{2,1,0:T(8,128)S(1)}, f32[16,16,128]{2,1,0:T(8,128)}, u32[]{:S(2)}) copy-start(f32[16,16,128]{2,1,0:T(8,128)} %param.8) | copy-start | bytes 393220
  1.9 11.4 %copy-start.4 = (f32[16,16,128]{2,1,0:T(8,128)S(1)}, f32[16,16,128]{2,1,0:T(8,128)}, u32[]{:S(2)}) copy-start(f32[16,16,128]{2,1,0:T(8,128)} %param.7) | copy-start | bytes 393220
  1.9 11.4 %copy-start.5 = (f32[16,16,128]{2,1,0:T(8,128)S(1)}, f32[16,16,128]{2,1,0:T(8,128)}, u32[]{:S(2)}) copy-start(f32[16,16,128]{2,1,0:T(8,128)} %param.6) | copy-start | bytes 393220
  2.2 10.4 %collective-permute-start = (f32[24,128]{1,0:T(8,128)S(1)}, f32[24,128]{1,0:T(8,128)S(1)}, u32[]{:S(2)}, u32[]{:S(2)}) collective-permute-start(f32[24,128]{1,0:T(8,128)S(1)} %reshape.611), channel_id=1, source_target_pairs={{8,16},{16,8},{9,17},{17,9},{10,18},{18,10},{11,19},{19,11},{12,20... | collective-permute-start | bytes 36872 | tf_op jit(solution)/shard_map/ppermute | solution.py:28
  3.0 9.5 %collective-permute-start.1 = (f32[24,128]{1,0:T(8,128)S(1)}, f32[24,128]{1,0:T(8,128)S(1)}, u32[]{:S(2)}, u32[]{:S(2)}) collective-permute-start(f32[24,128]{1,0:T(8,128)S(1)} %reshape.612), channel_id=1, source_target_pairs={{0,8},{8,0},{16,24},{24,16},{1,9},{9,1},{17,25},{25,17},{2,10},{10... | collective-permute-start | bytes 36872 | tf_op jit(solution)/shard_map/ppermute | solution.py:28
  9.2 1.4 %copy-start.16 = (s32[32]{0:T(128)}, s32[32]{0:T(128)S(1)}, u32[]{:S(2)}) copy-start(s32[32]{0:T(128)S(1)} %reshape.618) | copy-start | bytes 388
  14.3 4.9 %collective-permute-start.2 = (f32[3,16,544]{2,1,0:T(8,128)S(1)}, f32[3,16,544]{2,1,0:T(8,128)S(1)}, u32[]{:S(2)}, u32[]{:S(2)}) collective-permute-start(f32[3,16,544]{2,1,0:T(8,128)S(1)} %slice_select_fusion.4), channel_id=1, source_target_pairs={{0,1},{1,0},{2,3},{3,2},{4,5},{5,4},{6,7},{7,6},{8,9},{9,8},{10,11... | collective-permute-start | bytes 313352 | tf_op jit(solution)/shard_map/ppermute | solution.py:29
  19.7 3.9 %collective-permute-start.3 = (f32[306,128]{1,0:T(8,128)S(1)}, f32[306,128]{1,0:T(8,128)S(1)}, u32[]{:S(2)}, u32[]{:S(2)}) collective-permute-start(f32[306,128]{1,0:T(8,128)S(1)} %reshape.615), channel_id=1, source_target_pairs={{2,4},{4,2},{3,5},{5,3},{10,12},{12,10},{11,13},{13,11},{18,20},{2... | collective-permute-start | bytes 470024 | tf_op jit(solution)/shard_map/ppermute | solution.py:28
  20.6 4.0 %collective-permute-start.4 = (f32[306,128]{1,0:T(8,128)S(1)}, f32[306,128]{1,0:T(8,128)S(1)}, u32[]{:S(2)}, u32[]{:S(2)}) collective-permute-start(f32[306,128]{1,0:T(8,128)S(1)} %reshape.616), channel_id=1, source_target_pairs={{0,2},{2,0},{4,6},{6,4},{1,3},{3,1},{5,7},{7,5},{8,10},{10,8},{12,... | collective-permute-start | bytes 470024 | tf_op jit(solution)/shard_map/ppermute | solution.py:28
  26.1 0.7 copy-start.1
  28.8 0.7 copy-start.6
  29.4 13.0 %all-to-all-start = ((f32[32,1,512]{2,1,0:T(1,128)}), f32[32,1,512]{2,1,0:T(1,128)S(1)}, u32[]{:S(2)}, u32[]{:S(2)}) async-start(f32[32,1,512]{2,1,0:T(1,128)} %broadcast_in_dim.171), calls=%async_computation | async-start | bytes 131072 | tf_op jit(solution)/shard_map/all_to_all | solution.py:140
  44.2 23.2 %copy-start.7 = (pred[32]{0:T(512)(128)(4,1)S(1)}, pred[32]{0:T(512)(128)(4,1)}, u32[]{:S(2)}) copy-start(pred[32]{0:T(512)(128)(4,1)} %get-tuple-element.25) | copy-start | bytes 100
  44.2 23.2 %copy-start.8 = (pred[32]{0:T(512)(128)(4,1)S(1)}, pred[32]{0:T(512)(128)(4,1)}, u32[]{:S(2)}) copy-start(pred[32]{0:T(512)(128)(4,1)} %get-tuple-element.26) | copy-start | bytes 100
  44.2 23.2 %copy-start.9 = (pred[32]{0:T(512)(128)(4,1)S(1)}, pred[32]{0:T(512)(128)(4,1)}, u32[]{:S(2)}) copy-start(pred[32]{0:T(512)(128)(4,1)} %get-tuple-element.27) | copy-start | bytes 100
  44.2 23.2 %copy-start.10 = (pred[32]{0:T(512)(128)(4,1)S(1)}, pred[32]{0:T(512)(128)(4,1)}, u32[]{:S(2)}) copy-start(pred[32]{0:T(512)(128)(4,1)} %get-tuple-element.28) | copy-start | bytes 100
  44.2 23.2 %copy-start.11 = (pred[32]{0:T(512)(128)(4,1)S(1)}, pred[32]{0:T(512)(128)(4,1)}, u32[]{:S(2)}) copy-start(pred[32]{0:T(512)(128)(4,1)} %get-tuple-element.29) | copy-start | bytes 100
  44.2 23.2 %copy-start.12 = (pred[32]{0:T(512)(128)(4,1)S(1)}, pred[32]{0:T(512)(128)(4,1)}, u32[]{:S(2)}) copy-start(pred[32]{0:T(512)(128)(4,1)} %get-tuple-element.30) | copy-start | bytes 100
  44.2 23.2 %copy-start.14 = (pred[32]{0:T(512)(128)(4,1)S(1)}, pred[32]{0:T(512)(128)(4,1)}, u32[]{:S(2)}) copy-start(pred[32]{0:T(512)(128)(4,1)} %get-tuple-element.6) | copy-start | bytes 100
  68.3 11.5 %copy-start.13 = (f32[512]{0:T(512)}, f32[512]{0:T(512)S(1)}, u32[]{:S(2)}) copy-start(f32[512]{0:T(512)S(1)} %divide_add_fusion) | copy-start | bytes 6148
  69.2 10.2 %all-to-all-start.3 = ((f32[32,1,512]{2,1,0:T(1,128)}), f32[32,1,512]{2,1,0:T(1,128)S(1)}, u32[]{:S(2)}, u32[]{:S(2)}) async-start(f32[32,1,512]{2,1,0:T(1,128)} %broadcast_in_dim.181), calls=%async_computation.3 | async-start | bytes 131072 | tf_op jit(solution)/shard_map/all_to_all | solution.py:140
  80.1 2.3 %copy-start.2 = (f32[24,3264]{1,0:T(8,128)S(1)}, f32[24,3264]{1,0:T(8,128)}, u32[]{:S(2)}) copy-start(f32[24,3264]{1,0:T(8,128)} %copy-done.1) | copy-start | bytes 940036

commit v19 on v17

--- a/solution.py
+++ b/solution.py
@@ -190,9 +190,11 @@
     ).astype(source.dtype)
     within = column_list % block_rows
     coarse_error = coarse_rhs / coarse_diag
+    me = lax.axis_index(ALL_AXES)
     for sweep_number in range(CITER - 1):
-        pooled = everyone(coarse_error)
-        rows_of = dot(pick, pooled.reshape(devices, -1))
+        pooled = everyone(coarse_error).reshape(devices, -1)
+        coarse_error = lax.dynamic_index_in_dim(pooled, me, axis=0, keepdims=False)
+        rows_of = dot(pick, pooled)
         blocks = rows_of[:, :64]
         for part in range(1, block_rows):
             blocks = jnp.where(within == part, rows_of[:, part * 64:(part + 1) * 64], blocks)

time: 84.6 us -> 90 us (1.064)
  local copies, waits for them, and re-layouts: 8.69 us -> 10.5 us
  other arithmetic: 11.5 us -> 13 us
  waiting for transfers between devices: 16.7 us -> 17.9 us
    dot_general x3, matrix products: 1.55 us -> 3.63 us  [local(): jnp.einsum('bim,bm->bi', coarse_values, blocks, precision=lax.Precision.H...]
    reshape x3, local copies, waits for them, and re-layouts: 0.24 us -> 2.03 us  [local(): blocks = blocks.reshape(block_rows, -1)]
    all_to_all x2, waiting for transfers between devices: 13.3 us -> 15 us  [everyone(): return lax.all_to_all(copies, ALL_AXES, 0, 0, tiled=True).reshape(-1)]
    add x3, other arithmetic: 0.72 us -> 2.11 us  [local(): coarse_error = coarse_error + (coarse_rhs - applied) / coarse_diag]
    dot_general x7, matrix products: 6.26 us -> 5.01 us  [dot(): return jnp.dot(left, right, precision=lax.Precision.HIGHEST)]
    select_n x1, other arithmetic: 1.08 us -> 0.01 us  [local(): column_list // block_rows]
  transfers between devices with their start and end apart: 7 -> 7, of which waited for: 4 -> 4; matrix products, arithmetic and copies ran while one was open for 7% -> 5% of each run, Pallas kernels for 0% -> 0%
where the time goes in v19:
time: 90 us; the launch traced here: 89.3 us
  starting transfers between devices  19.5 us (22%)
  blocking collectives  18.6 us (21%)
  waiting for transfers between devices  17.9 us (20%)
  other arithmetic  13 us (14%)
  local copies, waits for them, and re-layouts  10.5 us (12%)
  matrix products  8.65 us (10%)
  between operations  1.17 us (1%)
    all_to_all x2, blocking collectives, everyone(): return lax.all_to_all(copies, ALL_AXES, 0, 0, tiled=True).reshape(-1)  18.6 us
    all_to_all x2, waiting for transfers between devices, everyone(): return lax.all_to_all(copies, ALL_AXES, 0, 0, tiled=True).reshape(-1)  15 us
    ppermute x4, starting transfers between devices, permute(): return lax.ppermute(slab.reshape(-1, 128), axis, pairs).reshape(slab.shape)  10.2 us
    all_to_all x2, starting transfers between devices, everyone(): return lax.all_to_all(copies, ALL_AXES, 0, 0, tiled=True).reshape(-1)  7.75 us
    dot_general x7, matrix products, dot(): return jnp.dot(left, right, precision=lax.Precision.HIGHEST)  5.01 us
    dot_general x3, matrix products, local(): jnp.einsum('bim,bm->bi', coarse_values, blocks, precision=lax.Precision.H...  3.63 us
    ppermute x1, waiting for transfers between devices, permute(): return lax.ppermute(slab, axis, pairs)  2.81 us
    select_n x3, other arithmetic, local(): jnp.where(within == part, rows_of[:, part * 64:(part + 1) * 64], blocks)  2.39 us
  transfers between devices with their start and end apart: 7, of which 4 were waited for; matrix products, arithmetic and copies ran while one was open for 5% of the time, Pallas kernels for 0%

profile of v19, /device:TPU:0, one launch (start us, length us, event | category | flops | bytes accessed | tf_op | source)
XLA Modules:
  0.0 89.3 jit_solution(7787847938122693860)
XLA Ops:
  0.6 1.1 %pad_maximum_fusion.2 = f32[3,16,16,128]{3,2,1,0:T(8,128)S(1)} fusion(f32[1,16,16,128]{3,2,1,0:T(8,128)} %bitcast.83, f32[1,16,16,128]{3,2,1,0:T(8,128)} %bitcast.85, f32[1,16,16,128]{3,2,1,0:T(8,128)} %bitcast.87), kind=kLoop, calls=%fused_computation.58 | loop fusion | flops 196608 | bytes 786432 | tf_op jit(solution)/shard_map/stack | solution.py:146
  3.0 5.9 %collective-permute-start.1 = (f32[24,128]{1,0:T(8,128)S(1)}, f32[24,128]{1,0:T(8,128)S(1)}, u32[]{:S(2)}, u32[]{:S(2)}) collective-permute-start(f32[24,128]{1,0:T(8,128)S(1)} %reshape.601), channel_id=1, source_target_pairs={{0,8},{8,0},{16,24},{24,16},{1,9},{9,1},{17,25},{25,17},{2,10},{10... | collective-permute-start | bytes 36872 | tf_op jit(solution)/shard_map/ppermute | solution.py:28
  12.3 1.6 %collective-permute-start.2 = (f32[3,16,544]{2,1,0:T(8,128)S(1)}, f32[3,16,544]{2,1,0:T(8,128)S(1)}, u32[]{:S(2)}, u32[]{:S(2)}) collective-permute-start(f32[3,16,544]{2,1,0:T(8,128)S(1)} %slice_select_fusion.4), channel_id=1, source_target_pairs={{0,1},{1,0},{2,3},{3,2},{4,5},{5,4},{6,7},{7,6},{8,9},{9,8},{10,11... | collective-permute-start | bytes 313352 | tf_op jit(solution)/shard_map/ppermute | solution.py:29
  14.5 2.8 %collective-permute-done.2 = f32[3,16,544]{2,1,0:T(8,128)S(1)} collective-permute-done((f32[3,16,544]{2,1,0:T(8,128)S(1)}, f32[3,16,544]{2,1,0:T(8,128)S(1)}, u32[]{:S(2)}, u32[]{:S(2)}) %collective-permute-start.2) | collective-permute-done | bytes 104480 | tf_op jit(solution)/shard_map/ppermute | solution.py:29
  17.8 0.7 collective-permute-start.3
  18.7 2.9 %collective-permute-start.4 = (f32[306,128]{1,0:T(8,128)S(1)}, f32[306,128]{1,0:T(8,128)S(1)}, u32[]{:S(2)}, u32[]{:S(2)}) collective-permute-start(f32[306,128]{1,0:T(8,128)S(1)} %reshape.604), channel_id=1, source_target_pairs={{0,2},{2,0},{4,6},{6,4},{1,3},{3,1},{5,7},{7,5},{8,10},{10,8},{12,... | collective-permute-start | bytes 470024 | tf_op jit(solution)/shard_map/ppermute | solution.py:28
  21.6 1.9 %slice.255 = s32[4,4,32]{2,1,0:T(4,128)S(1)} slice(s32[16,16,128]{2,1,0:T(8,128)} %param.9), slice={[0:16:4], [0:16:4], [0:128:4]} | slice | bytes 4096 | tf_op jit(solution)/shard_map/slice | solution.py:177
  26.0 1.6 %fusion.4 = f32[24,128]{1,0:T(8,128)S(1)} fusion(s32[3264]{0:T(1024)S(1)} %fusion.181, pred[]{:T(512)S(6)} %ge.57, f32[24,3264]{1,0:T(8,128)S(1)} %get-tuple-element.5, f32[24,3264]{1,0:T(8,128)S(1)} %divide_select_fusion, f32[24,3264]{1,0:T(8,128)S(1)} %get-tuple-element.6, f32[24,3264]{1,0:T(8,128)S(1)} %get-tuple-element.7, ...), kind=kOutput, calls=%fused_computation.5 | convolution fusion | flops 124371456 | bytes 3223553 | tf_op jit(solution)/shard_map/dot_general | solution.py:120
  28.6 5.0 %all-to-all-start = ((f32[32,1,512]{2,1,0:T(1,128)}), f32[32,1,512]{2,1,0:T(1,128)S(1)}, u32[]{:S(2)}, u32[]{:S(2)}) async-start(f32[32,1,512]{2,1,0:T(1,128)} %broadcast_in_dim.169), calls=%async_computation | async-start | bytes 131072 | tf_op jit(solution)/shard_map/all_to_all | solution.py:140
  33.6 7.6 %all-to-all-done = f32[32,1,512]{2,1,0:T(1,128)S(1)} async-done(((f32[32,1,512]{2,1,0:T(1,128)}), f32[32,1,512]{2,1,0:T(1,128)S(1)}, u32[]{:S(2)}, u32[]{:S(2)}) %all-to-all-start) | async-done | bytes 65568 | tf_op jit(solution)/shard_map/all_to_all | solution.py:140
  41.5 0.8 fusion.206
  42.3 0.7 reshape.623
  42.9 1.2 %fusion.233 = f32[8,1,64]{2,1,0:T(1,128)S(1)} fusion(f32[8,256,1]{1,2,0:T(1,128)} %reshape.623, f32[8,64,256]{2,1,0:T(8,128)S(1)} %copy-done), kind=kOutput, calls=%fused_computation.355 | convolution fusion | flops 1572864 | bytes 534528 | tf_op jit(solution)/shard_map/bim,bm->bi/dot_general | solution.py:202
  44.2 0.7 divide_add_fusion.2
  45.0 9.3 %all_to_all.33 = f32[32,1,512]{2,1,0:T(1,128)S(1)} all-to-all(f32[32,1,512]{2,1,0:T(1,128)S(1)} %broadcast_in_dim.177), channel_id=1, replica_groups=mesh['grp'=4,'gx'=4,'gy'=2] {'grp','gx','gy'}, dimensions={0} | all-to-all | bytes 131072 | tf_op jit(solution)/shard_map/all_to_all | solution.py:140
  54.3 0.8 fusion.166
  55.1 0.8 fusion.200
  55.9 0.7 reshape.625
  56.6 1.2 %fusion.234 = f32[8,1,64]{2,1,0:T(1,128)S(1)} fusion(f32[8,256,1]{1,2,0:T(1,128)} %reshape.625, f32[8,64,256]{2,1,0:T(8,128)S(1)} %copy-done), kind=kOutput, calls=%fused_computation.356 | convolution fusion | flops 1572864 | bytes 534528 | tf_op jit(solution)/shard_map/bim,bm->bi/dot_general | solution.py:202
  57.9 0.7 divide_add_fusion.1
  58.7 9.3 %all_to_all.34 = f32[32,1,512]{2,1,0:T(1,128)S(1)} all-to-all(f32[32,1,512]{2,1,0:T(1,128)S(1)} %broadcast_in_dim.178), channel_id=1, replica_groups=mesh['grp'=4,'gx'=4,'gy'=2] {'grp','gx','gy'}, dimensions={0} | all-to-all | bytes 131072 | tf_op jit(solution)/shard_map/all_to_all | solution.py:140
  68.0 0.8 fusion.163
  68.8 0.8 fusion.194
  69.6 0.7 reshape.627
  70.3 1.2 %fusion.235 = f32[8,1,64]{2,1,0:T(1,128)S(1)} fusion(f32[8,256,1]{1,2,0:T(1,128)} %reshape.627, f32[8,64,256]{2,1,0:T(8,128)S(1)} %copy-done), kind=kOutput, calls=%fused_computation.357 | convolution fusion | flops 1572864 | bytes 534528 | tf_op jit(solution)/shard_map/bim,bm->bi/dot_general | solution.py:202
  71.6 0.7 divide_add_fusion
  72.3 0.9 %select_reduce_fusion = f32[512]{0:T(512)S(1)} fusion(f32[512]{0:T(512)S(1)} %divide_add_fusion, s32[512]{0:T(512)} %copy-done.10), kind=kLoop, calls=%fused_computation.9 | loop fusion | flops 785920 | bytes 6144 | tf_op jit(solution)/shard_map/reduce_sum | solution.py:207
  73.2 0.7 broadcast_in_dim.180
  73.9 2.8 %all-to-all-start.3 = ((f32[32,1,512]{2,1,0:T(1,128)}), f32[32,1,512]{2,1,0:T(1,128)S(1)}, u32[]{:S(2)}, u32[]{:S(2)}) async-start(f32[32,1,512]{2,1,0:T(1,128)} %broadcast_in_dim.180), calls=%async_computation.3 | async-start | bytes 131072 | tf_op jit(solution)/shard_map/all_to_all | solution.py:140
  76.7 7.4 %all-to-all-done.3 = f32[32,1,512]{2,1,0:T(1,128)S(1)} async-done(((f32[32,1,512]{2,1,0:T(1,128)}), f32[32,1,512]{2,1,0:T(1,128)S(1)}, u32[]{:S(2)}, u32[]{:S(2)}) %all-to-all-start.3) | async-done | bytes 65568 | tf_op jit(solution)/shard_map/all_to_all | solution.py:140
  85.0 1.0 %fusion.1 = f32[6,3264]{1,0:T(8,128)S(1)} fusion(f32[6,204]{1,0:T(8,128)S(1)} %reshape.614, s32[3264]{0:T(1024)S(1)} %fusion.186, pred[]{:T(512)S(6)} %ge.57), kind=kOutput, calls=%fused_computation.2 | convolution fusion | flops 49273344 | bytes 96289 | tf_op jit(solution)/shard_map/dot_general | solution.py:120
  88.5 0.8 slice.345
  (97 shorter events, 13.2 us)
Async XLA Ops:
  1.7 7.3 %copy-start.13 = (s32[8,4]{0,1:T(4,128)S(1)}, s32[8,4]{0,1:T(4,128)}, u32[]{:S(2)}) copy-start(s32[8,4]{0,1:T(4,128)} %param.11) | copy-start | bytes 388
  1.7 8.6 %copy-start = (f32[8,64,256]{2,1,0:T(8,128)S(1)}, f32[8,64,256]{2,1,0:T(8,128)}, u32[]{:S(2)}) copy-start(f32[8,64,256]{2,1,0:T(8,128)} %param.10) | copy-start | bytes 1572868
  1.9 9.5 %copy-start.3 = (f32[16,16,128]{2,1,0:T(8,128)S(1)}, f32[16,16,128]{2,1,0:T(8,128)}, u32[]{:S(2)}) copy-start(f32[16,16,128]{2,1,0:T(8,128)} %param.8) | copy-start | bytes 393220
  1.9 9.5 %copy-start.4 = (f32[16,16,128]{2,1,0:T(8,128)S(1)}, f32[16,16,128]{2,1,0:T(8,128)}, u32[]{:S(2)}) copy-start(f32[16,16,128]{2,1,0:T(8,128)} %param.7) | copy-start | bytes 393220
  1.9 9.5 %copy-start.5 = (f32[16,16,128]{2,1,0:T(8,128)S(1)}, f32[16,16,128]{2,1,0:T(8,128)}, u32[]{:S(2)}) copy-start(f32[16,16,128]{2,1,0:T(8,128)} %param.6) | copy-start | bytes 393220
  2.2 8.3 %collective-permute-start = (f32[24,128]{1,0:T(8,128)S(1)}, f32[24,128]{1,0:T(8,128)S(1)}, u32[]{:S(2)}, u32[]{:S(2)}) collective-permute-start(f32[24,128]{1,0:T(8,128)S(1)} %reshape.600), channel_id=1, source_target_pairs={{8,16},{16,8},{9,17},{17,9},{10,18},{18,10},{11,19},{19,11},{12,20... | collective-permute-start | bytes 36872 | tf_op jit(solution)/shard_map/ppermute | solution.py:28
  3.0 7.6 %collective-permute-start.1 = (f32[24,128]{1,0:T(8,128)S(1)}, f32[24,128]{1,0:T(8,128)S(1)}, u32[]{:S(2)}, u32[]{:S(2)}) collective-permute-start(f32[24,128]{1,0:T(8,128)S(1)} %reshape.601), channel_id=1, source_target_pairs={{0,8},{8,0},{16,24},{24,16},{1,9},{9,1},{17,25},{25,17},{2,10},{10... | collective-permute-start | bytes 36872 | tf_op jit(solution)/shard_map/ppermute | solution.py:28
  12.3 4.9 %collective-permute-start.2 = (f32[3,16,544]{2,1,0:T(8,128)S(1)}, f32[3,16,544]{2,1,0:T(8,128)S(1)}, u32[]{:S(2)}, u32[]{:S(2)}) collective-permute-start(f32[3,16,544]{2,1,0:T(8,128)S(1)} %slice_select_fusion.4), channel_id=1, source_target_pairs={{0,1},{1,0},{2,3},{3,2},{4,5},{5,4},{6,7},{7,6},{8,9},{9,8},{10,11... | collective-permute-start | bytes 313352 | tf_op jit(solution)/shard_map/ppermute | solution.py:29
  17.8 5.8 %collective-permute-start.3 = (f32[306,128]{1,0:T(8,128)S(1)}, f32[306,128]{1,0:T(8,128)S(1)}, u32[]{:S(2)}, u32[]{:S(2)}) collective-permute-start(f32[306,128]{1,0:T(8,128)S(1)} %reshape.603), channel_id=1, source_target_pairs={{2,4},{4,2},{3,5},{5,3},{10,12},{12,10},{11,13},{13,11},{18,20},{2... | collective-permute-start | bytes 470024 | tf_op jit(solution)/shard_map/ppermute | solution.py:28
  18.7 5.0 %collective-permute-start.4 = (f32[306,128]{1,0:T(8,128)S(1)}, f32[306,128]{1,0:T(8,128)S(1)}, u32[]{:S(2)}, u32[]{:S(2)}) collective-permute-start(f32[306,128]{1,0:T(8,128)S(1)} %reshape.604), channel_id=1, source_target_pairs={{0,2},{2,0},{4,6},{6,4},{1,3},{3,1},{5,7},{7,5},{8,10},{10,8},{12,... | collective-permute-start | bytes 470024 | tf_op jit(solution)/shard_map/ppermute | solution.py:28
  21.6 3.7 %copy-start.8 = (pred[24]{0:T(512)(128)(4,1)}, pred[24]{0:T(512)(128)(4,1)S(1)}, u32[]{:S(2)}) copy-start(pred[24]{0:T(512)(128)(4,1)S(1)} %compare_and_fusion) | copy-start | bytes 76
  23.6 4.1 %copy-start.10 = (s32[512]{0:T(512)}, s32[512]{0:T(512)S(1)}, u32[]{:S(2)}) copy-start(s32[512]{0:T(512)S(1)} %eq.156) | copy-start | bytes 6148
  23.6 4.3 %copy-start.6 = (f32[512]{0:T(512)}, f32[512]{0:T(512)S(1)}, u32[]{:S(2)}) copy-start(f32[512]{0:T(512)S(1)} %reshape.605) | copy-start | bytes 6148
  25.3 0.7 copy-start.1
  27.9 0.7 copy-start.7
  28.6 12.6 %all-to-all-start = ((f32[32,1,512]{2,1,0:T(1,128)}), f32[32,1,512]{2,1,0:T(1,128)S(1)}, u32[]{:S(2)}, u32[]{:S(2)}) async-start(f32[32,1,512]{2,1,0:T(1,128)} %broadcast_in_dim.169), calls=%async_computation | async-start | bytes 131072 | tf_op jit(solution)/shard_map/all_to_all | solution.py:140
  33.6 7.8 %copy-start.12 = (s32[32]{0:T(128)}, s32[32]{0:T(128)S(1)}, u32[]{:S(2)}) copy-start(s32[32]{0:T(128)S(1)} %and_select_fusion) | copy-start | bytes 388
  72.3 12.1 %copy-start.11 = (f32[512]{0:T(512)}, f32[512]{0:T(512)S(1)}, u32[]{:S(2)}) copy-start(f32[512]{0:T(512)S(1)} %divide_add_fusion) | copy-start | bytes 6148
  73.9 10.2 %all-to-all-start.3 = ((f32[32,1,512]{2,1,0:T(1,128)}), f32[32,1,512]{2,1,0:T(1,128)S(1)}, u32[]{:S(2)}, u32[]{:S(2)}) async-start(f32[32,1,512]{2,1,0:T(1,128)} %broadcast_in_dim.180), calls=%async_computation.3 | async-start | bytes 131072 | tf_op jit(solution)/shard_map/all_to_all | solution.py:140
  84.8 1.3 %copy-start.14 = (s32[24]{0:T(128)S(1)}, s32[24]{0:T(128)}, u32[]{:S(2)}) copy-start(s32[24]{0:T(128)} %get-tuple-element.28) | copy-start | bytes 292
  84.8 1.6 %copy-start.2 = (f32[24,3264]{1,0:T(8,128)S(1)}, f32[24,3264]{1,0:T(8,128)}, u32[]{:S(2)}) copy-start(f32[24,3264]{1,0:T(8,128)} %copy-done.1) | copy-start | bytes 940036
  84.8 1.6 %copy-start.9 = (pred[24]{0:T(512)(128)(4,1)S(1)}, pred[24]{0:T(512)(128)(4,1)}, u32[]{:S(2)}) copy-start(pred[24]{0:T(512)(128)(4,1)} %copy-done.8) | copy-start | bytes 76

commit v20 on v17

--- a/solution.py
+++ b/solution.py
@@ -84,10 +84,9 @@
 
 
 def inside_mask(rows, span_y, span_z):
-    shape = (rows, span_y * span_z)
-    column = lax.broadcasted_iota(jnp.int32, shape, 1)
+    column = lax.broadcasted_iota(jnp.int32, (1, span_y * span_z), 1)
     coords = (
-        (lax.broadcasted_iota(jnp.int32, shape, 0), rows, "gx"),
+        (lax.broadcasted_iota(jnp.int32, (rows, 1), 0), rows, "gx"),
         (column // span_z, span_y, "gy"),
         (column % span_z, span_z, "grp"),
     )
@@ -97,7 +96,7 @@
         where = lax.axis_index(axis) * block - HALO + local_index
         ok = (where >= 0) & (where < block * lax.axis_size(axis))
         mask = ok if mask is None else mask & ok
-    return mask
+    return jnp.broadcast_to(mask, (rows, span_y * span_z))
 
 
 def trimmed(flat, span_y, span_z):

time: 84.6 us -> 80.2 us (0.948)
  other arithmetic: 11.5 us -> 7.14 us
  waiting for transfers between devices: 16.7 us -> 19.6 us
  matrix products: 7.82 us -> 5.31 us
    dot_general x7, matrix products: 6.26 us -> 3.76 us  [dot(): return jnp.dot(left, right, precision=lax.Precision.HIGHEST)]
    all_to_all x2, waiting for transfers between devices: 13.3 us -> 15 us  [everyone(): return lax.all_to_all(copies, ALL_AXES, 0, 0, tiled=True).reshape(-1)]
    select_n x3, other arithmetic: 1.72 us -> 0.35 us  [local(): jnp.where(within == part, rows_of[:, part * 64:(part + 1) * 64], blocks)]
    ppermute x4, waiting for transfers between devices: 0.06 us -> 1.24 us  [permute(): return lax.ppermute(slab.reshape(-1, 128), axis, pairs).reshape(slab.shape)]
    eq x2, other arithmetic: 1.18 us -> 0.02 us  [local(): within == part]
    select_n x1, other arithmetic: 1.08 us -> 0.01 us  [local(): column_list // block_rows]
  transfers between devices with their start and end apart: 7 -> 7, of which waited for: 4 -> 4; matrix products, arithmetic and copies ran while one was open for 7% -> 4% of each run, Pallas kernels for 0% -> 0%
where the time goes in v20:
time: 80.2 us; the launch traced here: 79.7 us
  waiting for transfers between devices  19.6 us (24%)
  starting transfers between devices  19.5 us (24%)
  blocking collectives  18.6 us (23%)
  local copies, waits for them, and re-layouts  8.53 us (11%)
  other arithmetic  7.14 us (9%)
  matrix products  5.31 us (7%)
  between operations  1.11 us (1%)
    all_to_all x2, blocking collectives, everyone(): return lax.all_to_all(copies, ALL_AXES, 0, 0, tiled=True).reshape(-1)  18.6 us
    all_to_all x2, waiting for transfers between devices, everyone(): return lax.all_to_all(copies, ALL_AXES, 0, 0, tiled=True).reshape(-1)  15 us
    ppermute x4, starting transfers between devices, permute(): return lax.ppermute(slab.reshape(-1, 128), axis, pairs).reshape(slab.shape)  10.2 us
    all_to_all x2, starting transfers between devices, everyone(): return lax.all_to_all(copies, ALL_AXES, 0, 0, tiled=True).reshape(-1)  7.73 us
    dot_general x7, matrix products, dot(): return jnp.dot(left, right, precision=lax.Precision.HIGHEST)  3.76 us
    ppermute x1, waiting for transfers between devices, permute(): return lax.ppermute(slab, axis, pairs)  3.38 us
    select_n x3, other arithmetic, local(): jnp.where(mask, solution + WEIGHT * (src - op(solution)) / diagonal, 0.0)  2.31 us
    slice x1, local copies, waits for them, and re-layouts, local(): box_labels = aggregate_ids[::BOX, ::BOX, ::BOX].reshape(-1)  1.87 us
  transfers between devices with their start and end apart: 7, of which 4 were waited for; matrix products, arithmetic and copies ran while one was open for 4% of the time, Pallas kernels for 0%

profile of v20, /device:TPU:0, one launch (start us, length us, event | category | flops | bytes accessed | tf_op | source)
XLA Modules:
  0.0 79.7 jit_solution(6402692222321017625)
XLA Ops:
  0.6 1.1 %pad_maximum_fusion.2 = f32[3,16,16,128]{3,2,1,0:T(8,128)S(1)} fusion(f32[1,16,16,128]{3,2,1,0:T(8,128)} %bitcast.82, f32[1,16,16,128]{3,2,1,0:T(8,128)} %bitcast.84, f32[1,16,16,128]{3,2,1,0:T(8,128)} %bitcast.86), kind=kLoop, calls=%fused_computation.58 | loop fusion | flops 196608 | bytes 786432 | tf_op jit(solution)/shard_map/stack | solution.py:145
  2.2 0.7 collective-permute-start
  3.0 5.9 %collective-permute-start.1 = (f32[24,128]{1,0:T(8,128)S(1)}, f32[24,128]{1,0:T(8,128)S(1)}, u32[]{:S(2)}, u32[]{:S(2)}) collective-permute-start(f32[24,128]{1,0:T(8,128)S(1)} %reshape.638), channel_id=1, source_target_pairs={{0,8},{8,0},{16,24},{24,16},{1,9},{9,1},{17,25},{25,17},{2,10},{10... | collective-permute-start | bytes 36872 | tf_op jit(solution)/shard_map/ppermute | solution.py:28
  9.4 1.2 %collective-permute-done.1 = f32[24,128]{1,0:T(8,128)S(1)} collective-permute-done((f32[24,128]{1,0:T(8,128)S(1)}, f32[24,128]{1,0:T(8,128)S(1)}, u32[]{:S(2)}, u32[]{:S(2)}) %collective-permute-start.1) | collective-permute-done | bytes 12320 | tf_op jit(solution)/shard_map/ppermute | solution.py:28
  10.6 0.4 select_n.374
  11.0 0.4 select_n.376
  11.8 0.4 reshape.639
  12.3 1.6 %collective-permute-start.2 = (f32[3,16,544]{2,1,0:T(8,128)S(1)}, f32[3,16,544]{2,1,0:T(8,128)S(1)}, u32[]{:S(2)}, u32[]{:S(2)}) collective-permute-start(f32[3,16,544]{2,1,0:T(8,128)S(1)} %slice_select_fusion.4), channel_id=1, source_target_pairs={{0,1},{1,0},{2,3},{3,2},{4,5},{5,4},{6,7},{7,6},{8,9},{9,8},{10,11... | collective-permute-start | bytes 313352 | tf_op jit(solution)/shard_map/ppermute | solution.py:29
  13.9 3.4 %collective-permute-done.2 = f32[3,16,544]{2,1,0:T(8,128)S(1)} collective-permute-done((f32[3,16,544]{2,1,0:T(8,128)S(1)}, f32[3,16,544]{2,1,0:T(8,128)S(1)}, u32[]{:S(2)}, u32[]{:S(2)}) %collective-permute-start.2) | collective-permute-done | bytes 104480 | tf_op jit(solution)/shard_map/ppermute | solution.py:29
  17.8 0.7 collective-permute-start.3
  18.7 2.9 %collective-permute-start.4 = (f32[306,128]{1,0:T(8,128)S(1)}, f32[306,128]{1,0:T(8,128)S(1)}, u32[]{:S(2)}, u32[]{:S(2)}) collective-permute-start(f32[306,128]{1,0:T(8,128)S(1)} %reshape.641), channel_id=1, source_target_pairs={{0,2},{2,0},{4,6},{6,4},{1,3},{3,1},{5,7},{7,5},{8,10},{10,8},{12,... | collective-permute-start | bytes 470024 | tf_op jit(solution)/shard_map/ppermute | solution.py:28
  21.6 1.9 %slice.255 = s32[4,4,32]{2,1,0:T(4,128)S(1)} slice(s32[16,16,128]{2,1,0:T(8,128)} %param.9), slice={[0:16:4], [0:16:4], [0:128:4]} | slice | bytes 4096 | tf_op jit(solution)/shard_map/slice | solution.py:176
  24.2 0.5 divide_select_fusion.1
  24.7 1.2 %fusion.152 = (f32[24,3264]{1,0:T(8,128)S(1)}, f32[24,3264]{1,0:T(8,128)}) fusion(pred[3264]{0:T(1024)(128)(4,1)S(1)} %get-tuple-element.29, pred[3264]{0:T(1024)(128)(4,1)S(1)} %get-tuple-element.30, pred[24]{0:T(512)(128)(4,1)S(1)} %compare_and_fusion.1, f32[24,3264]{1,0:T(8,128)S(1)} %get-tuple-element.6, f32[24,3264]{1,0:T(8,128)S(1)} %get-tuple-element.11, ...), kind=kLoop, calls=%fused_computation.212 | loop fusion | flops 2506752 | bytes 3453336 | tf_op jit(solution)/shard_map/jit(_where)/select_n | solution.py:166
  25.9 0.5 divide_select_fusion
  26.5 1.6 %fusion.4 = f32[24,128]{1,0:T(8,128)S(1)} fusion(s32[3264]{0:T(1024)S(1)} %fusion.173, pred[]{:T(512)S(6)} %ge.71, f32[24,3264]{1,0:T(8,128)S(1)} %get-tuple-element.12, f32[24,3264]{1,0:T(8,128)S(1)} %divide_select_fusion, f32[24,3264]{1,0:T(8,128)S(1)} %get-tuple-element.7, f32[24,3264]{1,0:T(8,128)S(1)} %get-tuple-element.8, ...), kind=kOutput, calls=%fused_computation.5 | convolution fusion | flops 124371456 | bytes 3223553 | tf_op jit(solution)/shard_map/dot_general | solution.py:119
  28.4 0.7 broadcast_in_dim.170
  29.1 5.0 %all-to-all-start = ((f32[32,1,512]{2,1,0:T(1,128)}), f32[32,1,512]{2,1,0:T(1,128)S(1)}, u32[]{:S(2)}, u32[]{:S(2)}) async-start(f32[32,1,512]{2,1,0:T(1,128)} %broadcast_in_dim.170), calls=%async_computation | async-start | bytes 131072 | tf_op jit(solution)/shard_map/all_to_all | solution.py:139
  34.1 7.6 %all-to-all-done = f32[32,1,512]{2,1,0:T(1,128)S(1)} async-done(((f32[32,1,512]{2,1,0:T(1,128)}), f32[32,1,512]{2,1,0:T(1,128)S(1)}, u32[]{:S(2)}, u32[]{:S(2)}) %all-to-all-start) | async-done | bytes 65568 | tf_op jit(solution)/shard_map/all_to_all | solution.py:139
  42.1 0.5 fusion.244
  42.8 9.3 %all_to_all.33 = f32[32,1,512]{2,1,0:T(1,128)S(1)} all-to-all(f32[32,1,512]{2,1,0:T(1,128)S(1)} %broadcast_in_dim.177), channel_id=1, replica_groups=mesh['grp'=4,'gx'=4,'gy'=2] {'grp','gx','gy'}, dimensions={0} | all-to-all | bytes 131072 | tf_op jit(solution)/shard_map/all_to_all | solution.py:139
  52.5 0.5 fusion.245
  53.2 9.3 %all_to_all.34 = f32[32,1,512]{2,1,0:T(1,128)S(1)} all-to-all(f32[32,1,512]{2,1,0:T(1,128)S(1)} %broadcast_in_dim.178), channel_id=1, replica_groups=mesh['grp'=4,'gx'=4,'gy'=2] {'grp','gx','gy'}, dimensions={0} | all-to-all | bytes 131072 | tf_op jit(solution)/shard_map/all_to_all | solution.py:139
  62.9 0.5 fusion.246
  63.8 0.7 broadcast_in_dim.180
  64.5 2.8 %all-to-all-start.3 = ((f32[32,1,512]{2,1,0:T(1,128)}), f32[32,1,512]{2,1,0:T(1,128)S(1)}, u32[]{:S(2)}, u32[]{:S(2)}) async-start(f32[32,1,512]{2,1,0:T(1,128)} %broadcast_in_dim.180), calls=%async_computation.3 | async-start | bytes 131072 | tf_op jit(solution)/shard_map/all_to_all | solution.py:139
  67.3 7.4 %all-to-all-done.3 = f32[32,1,512]{2,1,0:T(1,128)S(1)} async-done(((f32[32,1,512]{2,1,0:T(1,128)}), f32[32,1,512]{2,1,0:T(1,128)S(1)}, u32[]{:S(2)}, u32[]{:S(2)}) %all-to-all-start.3) | async-done | bytes 65568 | tf_op jit(solution)/shard_map/all_to_all | solution.py:139
  75.5 1.0 %fusion.1 = f32[6,3264]{1,0:T(8,128)S(1)} fusion(f32[6,204]{1,0:T(8,128)S(1)} %reshape.651, s32[3264]{0:T(1024)S(1)} %fusion.178, pred[]{:T(512)S(6)} %ge.71), kind=kOutput, calls=%fused_computation.2 | convolution fusion | flops 49273344 | bytes 96289 | tf_op jit(solution)/shard_map/dot_general | solution.py:119
  77.0 0.6 fusion.151
  77.5 0.5 fusion.150
  78.0 0.5 fusion.149
  79.0 0.8 slice.345
  (77 shorter events, 6.7 us)
Async XLA Ops:
  1.7 7.3 %copy-start.6 = (s32[8,4]{0,1:T(4,128)S(1)}, s32[8,4]{0,1:T(4,128)}, u32[]{:S(2)}) copy-start(s32[8,4]{0,1:T(4,128)} %param.11) | copy-start | bytes 388
  1.7 7.5 %copy-start = (f32[8,64,256]{2,1,0:T(8,128)S(1)}, f32[8,64,256]{2,1,0:T(8,128)}, u32[]{:S(2)}) copy-start(f32[8,64,256]{2,1,0:T(8,128)} %param.10) | copy-start | bytes 1572868
  1.9 9.5 %copy-start.2 = (f32[16,16,128]{2,1,0:T(8,128)S(1)}, f32[16,16,128]{2,1,0:T(8,128)}, u32[]{:S(2)}) copy-start(f32[16,16,128]{2,1,0:T(8,128)} %param.8) | copy-start | bytes 393220
  1.9 9.5 %copy-start.3 = (f32[16,16,128]{2,1,0:T(8,128)S(1)}, f32[16,16,128]{2,1,0:T(8,128)}, u32[]{:S(2)}) copy-start(f32[16,16,128]{2,1,0:T(8,128)} %param.7) | copy-start | bytes 393220
  1.9 9.5 %copy-start.4 = (f32[16,16,128]{2,1,0:T(8,128)S(1)}, f32[16,16,128]{2,1,0:T(8,128)}, u32[]{:S(2)}) copy-start(f32[16,16,128]{2,1,0:T(8,128)} %param.6) | copy-start | bytes 393220
  2.2 7.2 %collective-permute-start = (f32[24,128]{1,0:T(8,128)S(1)}, f32[24,128]{1,0:T(8,128)S(1)}, u32[]{:S(2)}, u32[]{:S(2)}) collective-permute-start(f32[24,128]{1,0:T(8,128)S(1)} %reshape.637), channel_id=1, source_target_pairs={{8,16},{16,8},{9,17},{17,9},{10,18},{18,10},{11,19},{19,11},{12,20... | collective-permute-start | bytes 36872 | tf_op jit(solution)/shard_map/ppermute | solution.py:28
  3.0 7.6 %collective-permute-start.1 = (f32[24,128]{1,0:T(8,128)S(1)}, f32[24,128]{1,0:T(8,128)S(1)}, u32[]{:S(2)}, u32[]{:S(2)}) collective-permute-start(f32[24,128]{1,0:T(8,128)S(1)} %reshape.638), channel_id=1, source_target_pairs={{0,8},{8,0},{16,24},{24,16},{1,9},{9,1},{17,25},{25,17},{2,10},{10... | collective-permute-start | bytes 36872 | tf_op jit(solution)/shard_map/ppermute | solution.py:28
  12.3 4.9 %collective-permute-start.2 = (f32[3,16,544]{2,1,0:T(8,128)S(1)}, f32[3,16,544]{2,1,0:T(8,128)S(1)}, u32[]{:S(2)}, u32[]{:S(2)}) collective-permute-start(f32[3,16,544]{2,1,0:T(8,128)S(1)} %slice_select_fusion.4), channel_id=1, source_target_pairs={{0,1},{1,0},{2,3},{3,2},{4,5},{5,4},{6,7},{7,6},{8,9},{9,8},{10,11... | collective-permute-start | bytes 313352 | tf_op jit(solution)/shard_map/ppermute | solution.py:29
  17.8 5.9 %collective-permute-start.3 = (f32[306,128]{1,0:T(8,128)S(1)}, f32[306,128]{1,0:T(8,128)S(1)}, u32[]{:S(2)}, u32[]{:S(2)}) collective-permute-start(f32[306,128]{1,0:T(8,128)S(1)} %reshape.640), channel_id=1, source_target_pairs={{2,4},{4,2},{3,5},{5,3},{10,12},{12,10},{11,13},{13,11},{18,20},{2... | collective-permute-start | bytes 470024 | tf_op jit(solution)/shard_map/ppermute | solution.py:28
  18.7 5.0 %collective-permute-start.4 = (f32[306,128]{1,0:T(8,128)S(1)}, f32[306,128]{1,0:T(8,128)S(1)}, u32[]{:S(2)}, u32[]{:S(2)}) collective-permute-start(f32[306,128]{1,0:T(8,128)S(1)} %reshape.641), channel_id=1, source_target_pairs={{0,2},{2,0},{4,6},{6,4},{1,3},{3,1},{5,7},{7,5},{8,10},{10,8},{12,... | collective-permute-start | bytes 470024 | tf_op jit(solution)/shard_map/ppermute | solution.py:28
  29.1 12.6 %all-to-all-start = ((f32[32,1,512]{2,1,0:T(1,128)}), f32[32,1,512]{2,1,0:T(1,128)S(1)}, u32[]{:S(2)}, u32[]{:S(2)}) async-start(f32[32,1,512]{2,1,0:T(1,128)} %broadcast_in_dim.170), calls=%async_computation | async-start | bytes 131072 | tf_op jit(solution)/shard_map/all_to_all | solution.py:139
  63.5 13.1 %copy-start.5 = (f32[512]{0:T(512)}, f32[512]{0:T(512)S(1)}, u32[]{:S(2)}) copy-start(f32[512]{0:T(512)S(1)} %divide_add_fusion) | copy-start | bytes 6148
  64.5 10.2 %all-to-all-start.3 = ((f32[32,1,512]{2,1,0:T(1,128)}), f32[32,1,512]{2,1,0:T(1,128)S(1)}, u32[]{:S(2)}, u32[]{:S(2)}) async-start(f32[32,1,512]{2,1,0:T(1,128)} %broadcast_in_dim.180), calls=%async_computation.3 | async-start | bytes 131072 | tf_op jit(solution)/shard_map/all_to_all | solution.py:139
  75.3 1.6 %copy-start.1 = (f32[24,3264]{1,0:T(8,128)S(1)}, f32[24,3264]{1,0:T(8,128)}, u32[]{:S(2)}) copy-start(f32[24,3264]{1,0:T(8,128)} %get-tuple-element.5) | copy-start | bytes 940036

commit v21 on v20

--- a/solution.py
+++ b/solution.py
@@ -173,7 +173,7 @@
     pick_x = box_matrix(bx, rows, 1, HALO, live)
     pick_yz = box_matrix(by * bz, span_y * span_z, span_z, HALO, live, bz).T
     box_totals = dot(pick_x, dot(smoothed, pick_yz)).reshape(-1)
-    box_labels = aggregate_ids[::BOX, ::BOX, ::BOX].reshape(-1)
+    box_labels = aggregate_ids[::BOX, ::BOX].reshape(bx, by, bz, BOX)[:, :, :, 0].reshape(-1)
     placed = box_labels[:, None] == lax.broadcasted_iota(jnp.int32, (box_labels.shape[0],) * 2, 1)
     coarse_rhs = jnp.sum(jnp.where(placed, box_totals[:, None], 0.0), axis=0)
     eye = lax.broadcasted_iota(jnp.int32, (64, 64), 0) == lax.broadcasted_iota(jnp.int32, (64, 64), 1)

time: 80.2 us -> 80.5 us (level)
    slice x1 -> x2, local copies, waits for them, and re-layouts: 1.87 us -> 1.94 us  [local(): aggregate_ids[::BOX, ::BOX].reshape(bx, by, bz, BOX)[:, :, :, 0].reshape(-1)]
where the time goes in v21:
time: 80.5 us; the launch traced here: 80.1 us
  starting transfers between devices  19.9 us (25%)
  waiting for transfers between devices  19.2 us (24%)
  blocking collectives  18.6 us (23%)
  local copies, waits for them, and re-layouts  8.85 us (11%)
  other arithmetic  7.15 us (9%)
  matrix products  5.31 us (7%)
  between operations  1.11 us (1%)
    all_to_all x2, blocking collectives, everyone(): return lax.all_to_all(copies, ALL_AXES, 0, 0, tiled=True).reshape(-1)  18.6 us
    all_to_all x2, waiting for transfers between devices, everyone(): return lax.all_to_all(copies, ALL_AXES, 0, 0, tiled=True).reshape(-1)  15 us
    ppermute x4, starting transfers between devices, permute(): return lax.ppermute(slab.reshape(-1, 128), axis, pairs).reshape(slab.shape)  10.2 us
    all_to_all x2, starting transfers between devices, everyone(): return lax.all_to_all(copies, ALL_AXES, 0, 0, tiled=True).reshape(-1)  8.15 us
    dot_general x7, matrix products, dot(): return jnp.dot(left, right, precision=lax.Precision.HIGHEST)  3.75 us
    ppermute x1, waiting for transfers between devices, permute(): return lax.ppermute(slab, axis, pairs)  3.38 us
    select_n x3, other arithmetic, local(): jnp.where(mask, solution + WEIGHT * (src - op(solution)) / diagonal, 0.0)  2.32 us
    slice x2, local copies, waits for them, and re-layouts, local(): aggregate_ids[::BOX, ::BOX].reshape(bx, by, bz, BOX)[:, :, :, 0].reshape(-1)  1.94 us
  transfers between devices with their start and end apart: 7, of which 4 were waited for; matrix products, arithmetic and copies ran while one was open for 4% of the time, Pallas kernels for 0%

profile of v21, /device:TPU:0, one launch (start us, length us, event | category | flops | bytes accessed | tf_op | source)
XLA Modules:
  0.0 80.1 jit_solution(15615072312431293898)
XLA Ops:
  0.6 1.1 %pad_maximum_fusion.2 = f32[3,16,16,128]{3,2,1,0:T(8,128)S(1)} fusion(f32[1,16,16,128]{3,2,1,0:T(8,128)} %bitcast.82, f32[1,16,16,128]{3,2,1,0:T(8,128)} %bitcast.84, f32[1,16,16,128]{3,2,1,0:T(8,128)} %bitcast.86), kind=kLoop, calls=%fused_computation.58 | loop fusion | flops 196608 | bytes 786432 | tf_op jit(solution)/shard_map/stack | solution.py:145
  2.1 0.7 collective-permute-start
  3.0 5.9 %collective-permute-start.1 = (f32[24,128]{1,0:T(8,128)S(1)}, f32[24,128]{1,0:T(8,128)S(1)}, u32[]{:S(2)}, u32[]{:S(2)}) collective-permute-start(f32[24,128]{1,0:T(8,128)S(1)} %reshape.641), channel_id=1, source_target_pairs={{0,8},{8,0},{16,24},{24,16},{1,9},{9,1},{17,25},{25,17},{2,10},{10... | collective-permute-start | bytes 36872 | tf_op jit(solution)/shard_map/ppermute | solution.py:28
  9.0 1.6 %slice.258 = s32[4,4,128]{2,1,0:T(4,128)S(1)} slice(s32[16,16,128]{2,1,0:T(8,128)} %param.9), slice={[0:16:4], [0:16:4], [0:128:1]} | slice | bytes 16384 | tf_op jit(solution)/shard_map/slice | solution.py:176
  11.6 0.4 select_n.374
  12.0 0.4 select_n.376
  12.8 0.4 reshape.642
  13.3 1.6 %collective-permute-start.2 = (f32[3,16,544]{2,1,0:T(8,128)S(1)}, f32[3,16,544]{2,1,0:T(8,128)S(1)}, u32[]{:S(2)}, u32[]{:S(2)}) collective-permute-start(f32[3,16,544]{2,1,0:T(8,128)S(1)} %slice_select_fusion.4), channel_id=1, source_target_pairs={{0,1},{1,0},{2,3},{3,2},{4,5},{5,4},{6,7},{7,6},{8,9},{9,8},{10,11... | collective-permute-start | bytes 313352 | tf_op jit(solution)/shard_map/ppermute | solution.py:29
  14.9 3.4 %collective-permute-done.2 = f32[3,16,544]{2,1,0:T(8,128)S(1)} collective-permute-done((f32[3,16,544]{2,1,0:T(8,128)S(1)}, f32[3,16,544]{2,1,0:T(8,128)S(1)}, u32[]{:S(2)}, u32[]{:S(2)}) %collective-permute-start.2) | collective-permute-done | bytes 104480 | tf_op jit(solution)/shard_map/ppermute | solution.py:29
  18.8 0.7 collective-permute-start.3
  19.6 2.9 %collective-permute-start.4 = (f32[306,128]{1,0:T(8,128)S(1)}, f32[306,128]{1,0:T(8,128)S(1)}, u32[]{:S(2)}, u32[]{:S(2)}) collective-permute-start(f32[306,128]{1,0:T(8,128)S(1)} %reshape.644), channel_id=1, source_target_pairs={{0,2},{2,0},{4,6},{6,4},{1,3},{3,1},{5,7},{7,5},{8,10},{10,8},{12,... | collective-permute-start | bytes 470024 | tf_op jit(solution)/shard_map/ppermute | solution.py:28
  22.8 0.8 %collective-permute-done.4 = f32[306,128]{1,0:T(8,128)S(1)} collective-permute-done((f32[306,128]{1,0:T(8,128)S(1)}, f32[306,128]{1,0:T(8,128)S(1)}, u32[]{:S(2)}, u32[]{:S(2)}) %collective-permute-start.4) | collective-permute-done | bytes 156704 | tf_op jit(solution)/shard_map/ppermute | solution.py:28
  24.1 0.5 divide_select_fusion.1
  24.6 1.3 %fusion.152 = (f32[24,3264]{1,0:T(8,128)S(1)}, f32[24,3264]{1,0:T(8,128)}) fusion(pred[3264]{0:T(1024)(128)(4,1)S(1)} %get-tuple-element.29, pred[3264]{0:T(1024)(128)(4,1)S(1)} %get-tuple-element.30, pred[24]{0:T(512)(128)(4,1)S(1)} %compare_and_fusion.1, f32[24,3264]{1,0:T(8,128)S(1)} %get-tuple-element.6, f32[24,3264]{1,0:T(8,128)S(1)} %get-tuple-element.11, ...), kind=kLoop, calls=%fused_computation.212 | loop fusion | flops 2506752 | bytes 3453336 | tf_op jit(solution)/shard_map/jit(_where)/select_n | solution.py:166
  25.8 0.5 divide_select_fusion
  26.4 1.6 %fusion.4 = f32[24,128]{1,0:T(8,128)S(1)} fusion(s32[3264]{0:T(1024)S(1)} %fusion.173, pred[]{:T(512)S(6)} %ge.71, f32[24,3264]{1,0:T(8,128)S(1)} %get-tuple-element.12, f32[24,3264]{1,0:T(8,128)S(1)} %divide_select_fusion, f32[24,3264]{1,0:T(8,128)S(1)} %get-tuple-element.7, f32[24,3264]{1,0:T(8,128)S(1)} %get-tuple-element.8, ...), kind=kOutput, calls=%fused_computation.5 | convolution fusion | flops 124371456 | bytes 3223553 | tf_op jit(solution)/shard_map/dot_general | solution.py:119
  28.3 0.7 broadcast_in_dim.170
  29.0 5.4 %all-to-all-start = ((f32[32,1,512]{2,1,0:T(1,128)}), f32[32,1,512]{2,1,0:T(1,128)S(1)}, u32[]{:S(2)}, u32[]{:S(2)}) async-start(f32[32,1,512]{2,1,0:T(1,128)} %broadcast_in_dim.170), calls=%async_computation | async-start | bytes 131072 | tf_op jit(solution)/shard_map/all_to_all | solution.py:139
  34.4 7.6 %all-to-all-done = f32[32,1,512]{2,1,0:T(1,128)S(1)} async-done(((f32[32,1,512]{2,1,0:T(1,128)}), f32[32,1,512]{2,1,0:T(1,128)S(1)}, u32[]{:S(2)}, u32[]{:S(2)}) %all-to-all-start) | async-done | bytes 65568 | tf_op jit(solution)/shard_map/all_to_all | solution.py:139
  42.4 0.5 fusion.244
  43.1 9.3 %all_to_all.33 = f32[32,1,512]{2,1,0:T(1,128)S(1)} all-to-all(f32[32,1,512]{2,1,0:T(1,128)S(1)} %broadcast_in_dim.177), channel_id=1, replica_groups=mesh['grp'=4,'gx'=4,'gy'=2] {'grp','gx','gy'}, dimensions={0} | all-to-all | bytes 131072 | tf_op jit(solution)/shard_map/all_to_all | solution.py:139
  52.8 0.5 fusion.245
  53.5 9.3 %all_to_all.34 = f32[32,1,512]{2,1,0:T(1,128)S(1)} all-to-all(f32[32,1,512]{2,1,0:T(1,128)S(1)} %broadcast_in_dim.178), channel_id=1, replica_groups=mesh['grp'=4,'gx'=4,'gy'=2] {'grp','gx','gy'}, dimensions={0} | all-to-all | bytes 131072 | tf_op jit(solution)/shard_map/all_to_all | solution.py:139
  63.2 0.5 fusion.246
  64.1 0.7 broadcast_in_dim.180
  64.8 2.8 %all-to-all-start.3 = ((f32[32,1,512]{2,1,0:T(1,128)}), f32[32,1,512]{2,1,0:T(1,128)S(1)}, u32[]{:S(2)}, u32[]{:S(2)}) async-start(f32[32,1,512]{2,1,0:T(1,128)} %broadcast_in_dim.180), calls=%async_computation.3 | async-start | bytes 131072 | tf_op jit(solution)/shard_map/all_to_all | solution.py:139
  67.6 7.4 %all-to-all-done.3 = f32[32,1,512]{2,1,0:T(1,128)S(1)} async-done(((f32[32,1,512]{2,1,0:T(1,128)}), f32[32,1,512]{2,1,0:T(1,128)S(1)}, u32[]{:S(2)}, u32[]{:S(2)}) %all-to-all-start.3) | async-done | bytes 65568 | tf_op jit(solution)/shard_map/all_to_all | solution.py:139
  75.9 1.0 %fusion.1 = f32[6,3264]{1,0:T(8,128)S(1)} fusion(f32[6,204]{1,0:T(8,128)S(1)} %reshape.655, s32[3264]{0:T(1024)S(1)} %fusion.178, pred[]{:T(512)S(6)} %ge.71), kind=kOutput, calls=%fused_computation.2 | convolution fusion | flops 49273344 | bytes 96289 | tf_op jit(solution)/shard_map/dot_general | solution.py:119
  77.3 0.6 fusion.151
  77.8 0.5 fusion.150
  78.4 0.5 fusion.149
  79.3 0.8 slice.350
  (79 shorter events, 7.3 us)
Async XLA Ops:
  1.9 9.3 %copy-start.6 = (s32[8,4]{0,1:T(4,128)S(1)}, s32[8,4]{0,1:T(4,128)}, u32[]{:S(2)}) copy-start(s32[8,4]{0,1:T(4,128)} %param.11) | copy-start | bytes 388
  1.9 9.5 %copy-start = (f32[8,64,256]{2,1,0:T(8,128)S(1)}, f32[8,64,256]{2,1,0:T(8,128)}, u32[]{:S(2)}) copy-start(f32[8,64,256]{2,1,0:T(8,128)} %param.10) | copy-start | bytes 1572868
  2.1 9.5 %collective-permute-start = (f32[24,128]{1,0:T(8,128)S(1)}, f32[24,128]{1,0:T(8,128)S(1)}, u32[]{:S(2)}, u32[]{:S(2)}) collective-permute-start(f32[24,128]{1,0:T(8,128)S(1)} %reshape.640), channel_id=1, source_target_pairs={{8,16},{16,8},{9,17},{17,9},{10,18},{18,10},{11,19},{19,11},{12,20... | collective-permute-start | bytes 36872 | tf_op jit(solution)/shard_map/ppermute | solution.py:28
  3.0 9.4 %copy-start.2 = (f32[16,16,128]{2,1,0:T(8,128)S(1)}, f32[16,16,128]{2,1,0:T(8,128)}, u32[]{:S(2)}) copy-start(f32[16,16,128]{2,1,0:T(8,128)} %param.8) | copy-start | bytes 393220
  3.0 9.4 %copy-start.3 = (f32[16,16,128]{2,1,0:T(8,128)S(1)}, f32[16,16,128]{2,1,0:T(8,128)}, u32[]{:S(2)}) copy-start(f32[16,16,128]{2,1,0:T(8,128)} %param.7) | copy-start | bytes 393220
  3.0 9.4 %copy-start.4 = (f32[16,16,128]{2,1,0:T(8,128)S(1)}, f32[16,16,128]{2,1,0:T(8,128)}, u32[]{:S(2)}) copy-start(f32[16,16,128]{2,1,0:T(8,128)} %param.6) | copy-start | bytes 393220
  3.0 8.6 %collective-permute-start.1 = (f32[24,128]{1,0:T(8,128)S(1)}, f32[24,128]{1,0:T(8,128)S(1)}, u32[]{:S(2)}, u32[]{:S(2)}) collective-permute-start(f32[24,128]{1,0:T(8,128)S(1)} %reshape.641), channel_id=1, source_target_pairs={{0,8},{8,0},{16,24},{24,16},{1,9},{9,1},{17,25},{25,17},{2,10},{10... | collective-permute-start | bytes 36872 | tf_op jit(solution)/shard_map/ppermute | solution.py:28
  13.3 4.9 %collective-permute-start.2 = (f32[3,16,544]{2,1,0:T(8,128)S(1)}, f32[3,16,544]{2,1,0:T(8,128)S(1)}, u32[]{:S(2)}, u32[]{:S(2)}) collective-permute-start(f32[3,16,544]{2,1,0:T(8,128)S(1)} %slice_select_fusion.4), channel_id=1, source_target_pairs={{0,1},{1,0},{2,3},{3,2},{4,5},{5,4},{6,7},{7,6},{8,9},{9,8},{10,11... | collective-permute-start | bytes 313352 | tf_op jit(solution)/shard_map/ppermute | solution.py:29
  18.8 4.0 %collective-permute-start.3 = (f32[306,128]{1,0:T(8,128)S(1)}, f32[306,128]{1,0:T(8,128)S(1)}, u32[]{:S(2)}, u32[]{:S(2)}) collective-permute-start(f32[306,128]{1,0:T(8,128)S(1)} %reshape.643), channel_id=1, source_target_pairs={{2,4},{4,2},{3,5},{5,3},{10,12},{12,10},{11,13},{13,11},{18,20},{2... | collective-permute-start | bytes 470024 | tf_op jit(solution)/shard_map/ppermute | solution.py:28
  19.6 4.0 %collective-permute-start.4 = (f32[306,128]{1,0:T(8,128)S(1)}, f32[306,128]{1,0:T(8,128)S(1)}, u32[]{:S(2)}, u32[]{:S(2)}) collective-permute-start(f32[306,128]{1,0:T(8,128)S(1)} %reshape.644), channel_id=1, source_target_pairs={{0,2},{2,0},{4,6},{6,4},{1,3},{3,1},{5,7},{7,5},{8,10},{10,8},{12,... | collective-permute-start | bytes 470024 | tf_op jit(solution)/shard_map/ppermute | solution.py:28
  29.0 13.0 %all-to-all-start = ((f32[32,1,512]{2,1,0:T(1,128)}), f32[32,1,512]{2,1,0:T(1,128)S(1)}, u32[]{:S(2)}, u32[]{:S(2)}) async-start(f32[32,1,512]{2,1,0:T(1,128)} %broadcast_in_dim.170), calls=%async_computation | async-start | bytes 131072 | tf_op jit(solution)/shard_map/all_to_all | solution.py:139
  63.8 13.1 %copy-start.5 = (f32[512]{0:T(512)}, f32[512]{0:T(512)S(1)}, u32[]{:S(2)}) copy-start(f32[512]{0:T(512)S(1)} %divide_add_fusion) | copy-start | bytes 6148
  64.8 10.2 %all-to-all-start.3 = ((f32[32,1,512]{2,1,0:T(1,128)}), f32[32,1,512]{2,1,0:T(1,128)S(1)}, u32[]{:S(2)}, u32[]{:S(2)}) async-start(f32[32,1,512]{2,1,0:T(1,128)} %broadcast_in_dim.180), calls=%async_computation.3 | async-start | bytes 131072 | tf_op jit(solution)/shard_map/all_to_all | solution.py:139
  75.7 1.6 %copy-start.1 = (f32[24,3264]{1,0:T(8,128)S(1)}, f32[24,3264]{1,0:T(8,128)}, u32[]{:S(2)}) copy-start(f32[24,3264]{1,0:T(8,128)} %get-tuple-element.5) | copy-start | bytes 940036

commit v22 on v20

--- a/solution.py
+++ b/solution.py
@@ -211,9 +211,8 @@
         (bx + 2, by + 2, bz + 2),
     )
     window = window.reshape(bx + 2, (by + 2) * (bz + 2))
-    spread_x = box_matrix(bx + 2, rows, 1, 0, live).T
     spread_yz = box_matrix((by + 2) * (bz + 2), span_y * span_z, span_z, 0, live, bz + 2)
-    lifted = dot(spread_x, dot(window, spread_yz))
+    lifted = jnp.repeat(dot(window, spread_yz), BOX, axis=0)
     solution = jnp.where(mask, solution + (lifted - WEIGHT * op(lifted) / diagonal), 0.0)
     for sweep_number in range(NU):
         solution = jnp.where(mask, solution + WEIGHT * (src - op(solution)) / diagonal, 0.0)

time: 80.2 us -> 81 us (level)
  other arithmetic: 7.14 us -> 8.09 us
    select_n x1, other arithmetic: 0.55 us -> 1.5 us  [local(): jnp.where(mask, solution + (lifted - WEIGHT * op(lifted) / diagonal), 0.0)]
    dot_general x7 -> x6, matrix products: 3.76 us -> 3.4 us  [dot(): return jnp.dot(left, right, precision=lax.Precision.HIGHEST)]
where the time goes in v22:
time: 81 us; the launch traced here: 80.5 us
  waiting for transfers between devices  19.6 us (24%)
  starting transfers between devices  19.5 us (24%)
  blocking collectives  18.6 us (23%)
  local copies, waits for them, and re-layouts  8.7 us (11%)
  other arithmetic  8.09 us (10%)
  matrix products  4.96 us (6%)
  between operations  1.1 us (1%)
    all_to_all x2, blocking collectives, everyone(): return lax.all_to_all(copies, ALL_AXES, 0, 0, tiled=True).reshape(-1)  18.6 us
    all_to_all x2, waiting for transfers between devices, everyone(): return lax.all_to_all(copies, ALL_AXES, 0, 0, tiled=True).reshape(-1)  15 us
    ppermute x4, starting transfers between devices, permute(): return lax.ppermute(slab.reshape(-1, 128), axis, pairs).reshape(slab.shape)  10.2 us
    all_to_all x2, starting transfers between devices, everyone(): return lax.all_to_all(copies, ALL_AXES, 0, 0, tiled=True).reshape(-1)  7.73 us
    dot_general x6, matrix products, dot(): return jnp.dot(left, right, precision=lax.Precision.HIGHEST)  3.4 us
    ppermute x1, waiting for transfers between devices, permute(): return lax.ppermute(slab, axis, pairs)  3.38 us
    select_n x3, other arithmetic, local(): jnp.where(mask, solution + WEIGHT * (src - op(solution)) / diagonal, 0.0)  2.31 us
    slice x1, local copies, waits for them, and re-layouts, local(): box_labels = aggregate_ids[::BOX, ::BOX, ::BOX].reshape(-1)  1.87 us
  transfers between devices with their start and end apart: 7, of which 4 were waited for; matrix products, arithmetic and copies ran while one was open for 4% of the time, Pallas kernels for 0%

profile of v22, /device:TPU:0, one launch (start us, length us, event | category | flops | bytes accessed | tf_op | source)
XLA Modules:
  0.0 80.5 jit_solution(13823546151712883441)
XLA Ops:
  0.6 1.1 %pad_maximum_fusion.2 = f32[3,16,16,128]{3,2,1,0:T(8,128)S(1)} fusion(f32[1,16,16,128]{3,2,1,0:T(8,128)} %bitcast.81, f32[1,16,16,128]{3,2,1,0:T(8,128)} %bitcast.83, f32[1,16,16,128]{3,2,1,0:T(8,128)} %bitcast.85), kind=kLoop, calls=%fused_computation.58 | loop fusion | flops 196608 | bytes 786432 | tf_op jit(solution)/shard_map/stack | solution.py:145
  2.2 0.7 collective-permute-start
  3.0 5.9 %collective-permute-start.1 = (f32[24,128]{1,0:T(8,128)S(1)}, f32[24,128]{1,0:T(8,128)S(1)}, u32[]{:S(2)}, u32[]{:S(2)}) collective-permute-start(f32[24,128]{1,0:T(8,128)S(1)} %reshape.598), channel_id=1, source_target_pairs={{0,8},{8,0},{16,24},{24,16},{1,9},{9,1},{17,25},{25,17},{2,10},{10... | collective-permute-start | bytes 36872 | tf_op jit(solution)/shard_map/ppermute | solution.py:28
  9.4 1.2 %collective-permute-done.1 = f32[24,128]{1,0:T(8,128)S(1)} collective-permute-done((f32[24,128]{1,0:T(8,128)S(1)}, f32[24,128]{1,0:T(8,128)S(1)}, u32[]{:S(2)}, u32[]{:S(2)}) %collective-permute-start.1) | collective-permute-done | bytes 12320 | tf_op jit(solution)/shard_map/ppermute | solution.py:28
  10.6 0.4 select_n.358
  11.0 0.4 select_n.360
  11.8 0.4 reshape.599
  12.3 1.6 %collective-permute-start.2 = (f32[3,16,544]{2,1,0:T(8,128)S(1)}, f32[3,16,544]{2,1,0:T(8,128)S(1)}, u32[]{:S(2)}, u32[]{:S(2)}) collective-permute-start(f32[3,16,544]{2,1,0:T(8,128)S(1)} %slice_select_fusion.4), channel_id=1, source_target_pairs={{0,1},{1,0},{2,3},{3,2},{4,5},{5,4},{6,7},{7,6},{8,9},{9,8},{10,11... | collective-permute-start | bytes 313352 | tf_op jit(solution)/shard_map/ppermute | solution.py:29
  13.9 3.4 %collective-permute-done.2 = f32[3,16,544]{2,1,0:T(8,128)S(1)} collective-permute-done((f32[3,16,544]{2,1,0:T(8,128)S(1)}, f32[3,16,544]{2,1,0:T(8,128)S(1)}, u32[]{:S(2)}, u32[]{:S(2)}) %collective-permute-start.2) | collective-permute-done | bytes 104480 | tf_op jit(solution)/shard_map/ppermute | solution.py:29
  17.8 0.7 collective-permute-start.3
  18.7 2.9 %collective-permute-start.4 = (f32[306,128]{1,0:T(8,128)S(1)}, f32[306,128]{1,0:T(8,128)S(1)}, u32[]{:S(2)}, u32[]{:S(2)}) collective-permute-start(f32[306,128]{1,0:T(8,128)S(1)} %reshape.601), channel_id=1, source_target_pairs={{0,2},{2,0},{4,6},{6,4},{1,3},{3,1},{5,7},{7,5},{8,10},{10,8},{12,... | collective-permute-start | bytes 470024 | tf_op jit(solution)/shard_map/ppermute | solution.py:28
  21.6 1.9 %slice.255 = s32[4,4,32]{2,1,0:T(4,128)S(1)} slice(s32[16,16,128]{2,1,0:T(8,128)} %param.9), slice={[0:16:4], [0:16:4], [0:128:4]} | slice | bytes 4096 | tf_op jit(solution)/shard_map/slice | solution.py:176
  24.2 0.5 divide_select_fusion.1
  24.7 1.2 %fusion.152 = (f32[24,3264]{1,0:T(8,128)S(1)}, f32[24,3264]{1,0:T(8,128)}) fusion(pred[3264]{0:T(1024)(128)(4,1)S(1)} %get-tuple-element.29, pred[3264]{0:T(1024)(128)(4,1)S(1)} %get-tuple-element.30, pred[24]{0:T(512)(128)(4,1)S(1)} %compare_and_fusion.1, f32[24,3264]{1,0:T(8,128)S(1)} %get-tuple-element.6, f32[24,3264]{1,0:T(8,128)S(1)} %get-tuple-element.11, ...), kind=kLoop, calls=%fused_computation.212 | loop fusion | flops 2506752 | bytes 3453336 | tf_op jit(solution)/shard_map/jit(_where)/select_n | solution.py:166
  25.9 0.5 divide_select_fusion
  26.5 1.6 %fusion.4 = f32[24,128]{1,0:T(8,128)S(1)} fusion(s32[3264]{0:T(1024)S(1)} %fusion.173, pred[]{:T(512)S(6)} %ge.71, f32[24,3264]{1,0:T(8,128)S(1)} %get-tuple-element.12, f32[24,3264]{1,0:T(8,128)S(1)} %divide_select_fusion, f32[24,3264]{1,0:T(8,128)S(1)} %get-tuple-element.7, f32[24,3264]{1,0:T(8,128)S(1)} %get-tuple-element.8, ...), kind=kOutput, calls=%fused_computation.5 | convolution fusion | flops 124371456 | bytes 3223553 | tf_op jit(solution)/shard_map/dot_general | solution.py:119
  28.4 0.7 broadcast_in_dim.172
  29.1 5.0 %all-to-all-start = ((f32[32,1,512]{2,1,0:T(1,128)}), f32[32,1,512]{2,1,0:T(1,128)S(1)}, u32[]{:S(2)}, u32[]{:S(2)}) async-start(f32[32,1,512]{2,1,0:T(1,128)} %broadcast_in_dim.172), calls=%async_computation | async-start | bytes 131072 | tf_op jit(solution)/shard_map/all_to_all | solution.py:139
  34.1 7.6 %all-to-all-done = f32[32,1,512]{2,1,0:T(1,128)S(1)} async-done(((f32[32,1,512]{2,1,0:T(1,128)}), f32[32,1,512]{2,1,0:T(1,128)S(1)}, u32[]{:S(2)}, u32[]{:S(2)}) %all-to-all-start) | async-done | bytes 65568 | tf_op jit(solution)/shard_map/all_to_all | solution.py:139
  42.1 0.5 fusion.239
  42.8 9.3 %all_to_all.33 = f32[32,1,512]{2,1,0:T(1,128)S(1)} all-to-all(f32[32,1,512]{2,1,0:T(1,128)S(1)} %broadcast_in_dim.179), channel_id=1, replica_groups=mesh['grp'=4,'gx'=4,'gy'=2] {'grp','gx','gy'}, dimensions={0} | all-to-all | bytes 131072 | tf_op jit(solution)/shard_map/all_to_all | solution.py:139
  52.5 0.5 fusion.240
  53.2 9.3 %all_to_all.34 = f32[32,1,512]{2,1,0:T(1,128)S(1)} all-to-all(f32[32,1,512]{2,1,0:T(1,128)S(1)} %broadcast_in_dim.180), channel_id=1, replica_groups=mesh['grp'=4,'gx'=4,'gy'=2] {'grp','gx','gy'}, dimensions={0} | all-to-all | bytes 131072 | tf_op jit(solution)/shard_map/all_to_all | solution.py:139
  62.9 0.5 fusion.241
  63.8 0.7 broadcast_in_dim.182
  64.5 2.8 %all-to-all-start.3 = ((f32[32,1,512]{2,1,0:T(1,128)}), f32[32,1,512]{2,1,0:T(1,128)S(1)}, u32[]{:S(2)}, u32[]{:S(2)}) async-start(f32[32,1,512]{2,1,0:T(1,128)} %broadcast_in_dim.182), calls=%async_computation.3 | async-start | bytes 131072 | tf_op jit(solution)/shard_map/all_to_all | solution.py:139
  67.3 7.4 %all-to-all-done.3 = f32[32,1,512]{2,1,0:T(1,128)S(1)} async-done(((f32[32,1,512]{2,1,0:T(1,128)}), f32[32,1,512]{2,1,0:T(1,128)S(1)}, u32[]{:S(2)}, u32[]{:S(2)}) %all-to-all-start.3) | async-done | bytes 65568 | tf_op jit(solution)/shard_map/all_to_all | solution.py:139
  75.5 1.0 %fusion.1 = f32[6,3264]{1,0:T(8,128)S(1)} fusion(f32[6,204]{1,0:T(8,128)S(1)} %reshape.611, s32[3264]{0:T(1024)S(1)} %fusion.178, pred[]{:T(512)S(6)} %ge.71), kind=kOutput, calls=%fused_computation.2 | convolution fusion | flops 49273344 | bytes 96289 | tf_op jit(solution)/shard_map/dot_general | solution.py:119
  76.8 1.5 %fusion.151 = f32[24,3264]{1,0:T(8,128)S(1)} fusion(f32[24,3264]{1,0:T(8,128)S(1)} %reshape.612, f32[24,3264]{1,0:T(8,128)S(1)} %get-tuple-element.11, f32[24,3264]{1,0:T(8,128)S(1)} %get-tuple-element.10, f32[24,3264]{1,0:T(8,128)S(1)} %get-tuple-element.9, f32[24,3264]{1,0:T(8,128)S(1)} %get-tuple-element.8, f32[24,3264]{1,0:T(8,128)S(1)} %get-tuple-element.7, ...), kind=kLoop, calls=%fused_computation.211 | loop fusion | flops 2585088 | bytes 3139992 | tf_op jit(solution)/shard_map/jit(_where)/select_n | solution.py:216
  78.3 0.5 fusion.150
  78.8 0.5 fusion.149
  79.7 0.8 slice.345
  (75 shorter events, 6.5 us)
Async XLA Ops:
  1.7 7.3 %copy-start.5 = (s32[8,4]{0,1:T(4,128)S(1)}, s32[8,4]{0,1:T(4,128)}, u32[]{:S(2)}) copy-start(s32[8,4]{0,1:T(4,128)} %param.11) | copy-start | bytes 388
  1.7 7.5 %copy-start = (f32[8,64,256]{2,1,0:T(8,128)S(1)}, f32[8,64,256]{2,1,0:T(8,128)}, u32[]{:S(2)}) copy-start(f32[8,64,256]{2,1,0:T(8,128)} %param.10) | copy-start | bytes 1572868
  1.9 9.5 %copy-start.1 = (f32[16,16,128]{2,1,0:T(8,128)S(1)}, f32[16,16,128]{2,1,0:T(8,128)}, u32[]{:S(2)}) copy-start(f32[16,16,128]{2,1,0:T(8,128)} %param.8) | copy-start | bytes 393220
  1.9 9.5 %copy-start.2 = (f32[16,16,128]{2,1,0:T(8,128)S(1)}, f32[16,16,128]{2,1,0:T(8,128)}, u32[]{:S(2)}) copy-start(f32[16,16,128]{2,1,0:T(8,128)} %param.7) | copy-start | bytes 393220
  1.9 9.5 %copy-start.3 = (f32[16,16,128]{2,1,0:T(8,128)S(1)}, f32[16,16,128]{2,1,0:T(8,128)}, u32[]{:S(2)}) copy-start(f32[16,16,128]{2,1,0:T(8,128)} %param.6) | copy-start | bytes 393220
  2.2 7.2 %collective-permute-start = (f32[24,128]{1,0:T(8,128)S(1)}, f32[24,128]{1,0:T(8,128)S(1)}, u32[]{:S(2)}, u32[]{:S(2)}) collective-permute-start(f32[24,128]{1,0:T(8,128)S(1)} %reshape.597), channel_id=1, source_target_pairs={{8,16},{16,8},{9,17},{17,9},{10,18},{18,10},{11,19},{19,11},{12,20... | collective-permute-start | bytes 36872 | tf_op jit(solution)/shard_map/ppermute | solution.py:28
  3.0 7.6 %collective-permute-start.1 = (f32[24,128]{1,0:T(8,128)S(1)}, f32[24,128]{1,0:T(8,128)S(1)}, u32[]{:S(2)}, u32[]{:S(2)}) collective-permute-start(f32[24,128]{1,0:T(8,128)S(1)} %reshape.598), channel_id=1, source_target_pairs={{0,8},{8,0},{16,24},{24,16},{1,9},{9,1},{17,25},{25,17},{2,10},{10... | collective-permute-start | bytes 36872 | tf_op jit(solution)/shard_map/ppermute | solution.py:28
  12.3 4.9 %collective-permute-start.2 = (f32[3,16,544]{2,1,0:T(8,128)S(1)}, f32[3,16,544]{2,1,0:T(8,128)S(1)}, u32[]{:S(2)}, u32[]{:S(2)}) collective-permute-start(f32[3,16,544]{2,1,0:T(8,128)S(1)} %slice_select_fusion.4), channel_id=1, source_target_pairs={{0,1},{1,0},{2,3},{3,2},{4,5},{5,4},{6,7},{7,6},{8,9},{9,8},{10,11... | collective-permute-start | bytes 313352 | tf_op jit(solution)/shard_map/ppermute | solution.py:29
  17.8 5.9 %collective-permute-start.3 = (f32[306,128]{1,0:T(8,128)S(1)}, f32[306,128]{1,0:T(8,128)S(1)}, u32[]{:S(2)}, u32[]{:S(2)}) collective-permute-start(f32[306,128]{1,0:T(8,128)S(1)} %reshape.600), channel_id=1, source_target_pairs={{2,4},{4,2},{3,5},{5,3},{10,12},{12,10},{11,13},{13,11},{18,20},{2... | collective-permute-start | bytes 470024 | tf_op jit(solution)/shard_map/ppermute | solution.py:28
  18.7 5.0 %collective-permute-start.4 = (f32[306,128]{1,0:T(8,128)S(1)}, f32[306,128]{1,0:T(8,128)S(1)}, u32[]{:S(2)}, u32[]{:S(2)}) collective-permute-start(f32[306,128]{1,0:T(8,128)S(1)} %reshape.601), channel_id=1, source_target_pairs={{0,2},{2,0},{4,6},{6,4},{1,3},{3,1},{5,7},{7,5},{8,10},{10,8},{12,... | collective-permute-start | bytes 470024 | tf_op jit(solution)/shard_map/ppermute | solution.py:28
  29.1 12.6 %all-to-all-start = ((f32[32,1,512]{2,1,0:T(1,128)}), f32[32,1,512]{2,1,0:T(1,128)S(1)}, u32[]{:S(2)}, u32[]{:S(2)}) async-start(f32[32,1,512]{2,1,0:T(1,128)} %broadcast_in_dim.172), calls=%async_computation | async-start | bytes 131072 | tf_op jit(solution)/shard_map/all_to_all | solution.py:139
  63.5 13.0 %copy-start.4 = (f32[512]{0:T(512)}, f32[512]{0:T(512)S(1)}, u32[]{:S(2)}) copy-start(f32[512]{0:T(512)S(1)} %divide_add_fusion) | copy-start | bytes 6148
  64.5 10.2 %all-to-all-start.3 = ((f32[32,1,512]{2,1,0:T(1,128)}), f32[32,1,512]{2,1,0:T(1,128)S(1)}, u32[]{:S(2)}, u32[]{:S(2)}) async-start(f32[32,1,512]{2,1,0:T(1,128)} %broadcast_in_dim.182), calls=%async_computation.3 | async-start | bytes 131072 | tf_op jit(solution)/shard_map/all_to_all | solution.py:139

commit v23 on v20

--- a/solution.py
+++ b/solution.py
@@ -66,10 +66,14 @@
 
 
 def neighbours(field, stride):
-    rows, width = field.shape
-    padded = jnp.pad(field, ((1, 1), (stride, stride)))
-    steps = ((1, 0, 0), (-1, 0, 0), (0, 1, 0), (0, -1, 0), (0, 0, 1), (0, 0, -1))
-    return [flat_shift(padded, rows, width, stride, *step) for step in steps]
+    return [
+        jnp.roll(field, -1, axis=0),
+        jnp.roll(field, 1, axis=0),
+        jnp.roll(field, -stride, axis=1),
+        jnp.roll(field, stride, axis=1),
+        jnp.roll(field, -1, axis=1),
+        jnp.roll(field, 1, axis=1),
+    ]
 
 
 def face_terms(conductance, stride):

time: 80.2 us -> 88.2 us (1.100)
  local copies, waits for them, and re-layouts: 8.53 us -> 13.9 us
  matrix products: 5.31 us -> 8.43 us
    slice x0 -> x42, local copies, waits for them, and re-layouts: none -> 3.7 us  [the longest x10 1.15 us: neighbours(): jnp.roll(field, -1, axis=1)]
    dot_general x3, matrix products: 1.55 us -> 4.67 us  [local(): jnp.einsum('bim,bm->bi', coarse_values, blocks, precision=lax.Precision.H...]
    reshape x1, local copies, waits for them, and re-layouts: 0.16 us -> 1.11 us  [local(): every.transpose(1, 3, 2, 4, 0, 5)]
where the time goes in v23:
time: 88.2 us; the launch traced here: 87.6 us
  starting transfers between devices  19.5 us (22%)
  waiting for transfers between devices  19 us (22%)
  blocking collectives  18.6 us (21%)
  local copies, waits for them, and re-layouts  13.9 us (16%)
  matrix products  8.43 us (10%)
  other arithmetic  6.95 us (8%)
  between operations  1.21 us (1%)
    all_to_all x2, blocking collectives, everyone(): return lax.all_to_all(copies, ALL_AXES, 0, 0, tiled=True).reshape(-1)  18.6 us
    all_to_all x2, waiting for transfers between devices, everyone(): return lax.all_to_all(copies, ALL_AXES, 0, 0, tiled=True).reshape(-1)  14.4 us
    ppermute x4, starting transfers between devices, permute(): return lax.ppermute(slab.reshape(-1, 128), axis, pairs).reshape(slab.shape)  10.2 us
    all_to_all x2, starting transfers between devices, everyone(): return lax.all_to_all(copies, ALL_AXES, 0, 0, tiled=True).reshape(-1)  7.73 us
    dot_general x3, matrix products, local(): jnp.einsum('bim,bm->bi', coarse_values, blocks, precision=lax.Precision.H...  4.67 us
    dot_general x7, matrix products, dot(): return jnp.dot(left, right, precision=lax.Precision.HIGHEST)  3.75 us
    ppermute x1, waiting for transfers between devices, permute(): return lax.ppermute(slab, axis, pairs)  3.38 us
    slice x1, local copies, waits for them, and re-layouts, local(): box_labels = aggregate_ids[::BOX, ::BOX, ::BOX].reshape(-1)  1.87 us
  transfers between devices with their start and end apart: 7, of which 4 were waited for; matrix products, arithmetic and copies ran while one was open for 4% of the time, Pallas kernels for 0%

profile of v23, /device:TPU:0, one launch (start us, length us, event | category | flops | bytes accessed | tf_op | source)
XLA Modules:
  0.0 87.6 jit_solution(12324695311749764287)
XLA Ops:
  0.6 1.1 %pad_maximum_fusion.2 = f32[3,16,16,128]{3,2,1,0:T(8,128)S(1)} fusion(f32[1,16,16,128]{3,2,1,0:T(8,128)} %bitcast.99, f32[1,16,16,128]{3,2,1,0:T(8,128)} %bitcast.101, f32[1,16,16,128]{3,2,1,0:T(8,128)} %bitcast.103), kind=kLoop, calls=%fused_computation.16 | loop fusion | flops 196608 | bytes 786432 | tf_op jit(solution)/shard_map/stack | solution.py:149
  2.2 0.7 collective-permute-start
  3.0 5.9 %collective-permute-start.1 = (f32[24,128]{1,0:T(8,128)S(1)}, f32[24,128]{1,0:T(8,128)S(1)}, u32[]{:S(2)}, u32[]{:S(2)}) collective-permute-start(f32[24,128]{1,0:T(8,128)S(1)} %reshape.642), channel_id=1, source_target_pairs={{0,8},{8,0},{16,24},{24,16},{1,9},{9,1},{17,25},{25,17},{2,10},{10... | collective-permute-start | bytes 36872 | tf_op jit(solution)/shard_map/ppermute | solution.py:28
  9.4 1.2 %collective-permute-done.1 = f32[24,128]{1,0:T(8,128)S(1)} collective-permute-done((f32[24,128]{1,0:T(8,128)S(1)}, f32[24,128]{1,0:T(8,128)S(1)}, u32[]{:S(2)}, u32[]{:S(2)}) %collective-permute-start.1) | collective-permute-done | bytes 12320 | tf_op jit(solution)/shard_map/ppermute | solution.py:28
  12.3 1.6 %collective-permute-start.2 = (f32[3,16,544]{2,1,0:T(8,128)S(1)}, f32[3,16,544]{2,1,0:T(8,128)S(1)}, u32[]{:S(2)}, u32[]{:S(2)}) collective-permute-start(f32[3,16,544]{2,1,0:T(8,128)S(1)} %slice_select_fusion.4), channel_id=1, source_target_pairs={{0,1},{1,0},{2,3},{3,2},{4,5},{5,4},{6,7},{7,6},{8,9},{9,8},{10,11... | collective-permute-start | bytes 313352 | tf_op jit(solution)/shard_map/ppermute | solution.py:29
  13.9 3.4 %collective-permute-done.2 = f32[3,16,544]{2,1,0:T(8,128)S(1)} collective-permute-done((f32[3,16,544]{2,1,0:T(8,128)S(1)}, f32[3,16,544]{2,1,0:T(8,128)S(1)}, u32[]{:S(2)}, u32[]{:S(2)}) %collective-permute-start.2) | collective-permute-done | bytes 104480 | tf_op jit(solution)/shard_map/ppermute | solution.py:29
  17.8 0.7 collective-permute-start.3
  18.7 2.9 %collective-permute-start.4 = (f32[306,128]{1,0:T(8,128)S(1)}, f32[306,128]{1,0:T(8,128)S(1)}, u32[]{:S(2)}, u32[]{:S(2)}) collective-permute-start(f32[306,128]{1,0:T(8,128)S(1)} %reshape.645), channel_id=1, source_target_pairs={{0,2},{2,0},{4,6},{6,4},{1,3},{3,1},{5,7},{7,5},{8,10},{10,8},{12,... | collective-permute-start | bytes 470024 | tf_op jit(solution)/shard_map/ppermute | solution.py:28
  21.6 1.9 %slice.427 = s32[4,4,32]{2,1,0:T(4,128)S(1)} slice(s32[16,16,128]{2,1,0:T(8,128)} %param.9), slice={[0:16:4], [0:16:4], [0:128:4]} | slice | bytes 4096 | tf_op jit(solution)/shard_map/slice | solution.py:180
  24.8 0.4 divide_select_fusion.1
  25.8 0.5 fusion.110
  26.9 0.5 divide_select_fusion
  27.9 1.6 %fusion.4 = f32[24,128]{1,0:T(8,128)S(1)} fusion(s32[3264]{0:T(1024)S(1)} %fusion.132, pred[]{:T(512)S(6)} %ge.71, f32[24,3264]{1,0:T(8,128)S(1)} %get-tuple-element.5, f32[24,3264]{1,0:T(8,128)S(1)} %divide_select_fusion, f32[1,3264]{1,0:T(1,128)S(1)} %get-tuple-element.62, f32[23,3264]{1,0:T(8,128)S(1)} %get-tuple-element.64, ...), kind=kOutput, calls=%fused_computation.5 | convolution fusion | flops 125311488 | bytes 7208961 | tf_op jit(solution)/shard_map/dot_general | solution.py:123
  29.9 0.7 broadcast_in_dim.170
  30.6 5.0 %all-to-all-start = ((f32[32,1,512]{2,1,0:T(1,128)}), f32[32,1,512]{2,1,0:T(1,128)S(1)}, u32[]{:S(2)}, u32[]{:S(2)}) async-start(f32[32,1,512]{2,1,0:T(1,128)} %broadcast_in_dim.170), calls=%async_computation | async-start | bytes 131072 | tf_op jit(solution)/shard_map/all_to_all | solution.py:143
  35.6 7.6 %all-to-all-done = f32[32,1,512]{2,1,0:T(1,128)S(1)} async-done(((f32[32,1,512]{2,1,0:T(1,128)}), f32[32,1,512]{2,1,0:T(1,128)S(1)}, u32[]{:S(2)}, u32[]{:S(2)}) %all-to-all-start) | async-done | bytes 65568 | tf_op jit(solution)/shard_map/all_to_all | solution.py:143
  43.6 1.6 %fusion.241 = f32[8,1,64]{2,1,0:T(1,128)S(1)} fusion(f32[8,256,1]{1,2,0:T(1,128)S(1)} %reshape.664, f32[8,64,256]{2,1,0:T(8,128)} %param.10), kind=kOutput, calls=%fused_computation.362 | convolution fusion | flops 1572864 | bytes 534528 | tf_op jit(solution)/shard_map/bim,bm->bi/dot_general | solution.py:203
  45.3 9.3 %all_to_all.33 = f32[32,1,512]{2,1,0:T(1,128)S(1)} all-to-all(f32[32,1,512]{2,1,0:T(1,128)S(1)} %broadcast_in_dim.177), channel_id=1, replica_groups=mesh['grp'=4,'gx'=4,'gy'=2] {'grp','gx','gy'}, dimensions={0} | all-to-all | bytes 131072 | tf_op jit(solution)/shard_map/all_to_all | solution.py:143
  55.0 1.6 %fusion.242 = f32[8,1,64]{2,1,0:T(1,128)S(1)} fusion(f32[8,256,1]{1,2,0:T(1,128)S(1)} %reshape.666, f32[8,64,256]{2,1,0:T(8,128)} %param.10), kind=kOutput, calls=%fused_computation.363 | convolution fusion | flops 1572864 | bytes 534528 | tf_op jit(solution)/shard_map/bim,bm->bi/dot_general | solution.py:203
  56.7 9.3 %all_to_all.34 = f32[32,1,512]{2,1,0:T(1,128)S(1)} all-to-all(f32[32,1,512]{2,1,0:T(1,128)S(1)} %broadcast_in_dim.178), channel_id=1, replica_groups=mesh['grp'=4,'gx'=4,'gy'=2] {'grp','gx','gy'}, dimensions={0} | all-to-all | bytes 131072 | tf_op jit(solution)/shard_map/all_to_all | solution.py:143
  66.5 1.6 %fusion.243 = f32[8,1,64]{2,1,0:T(1,128)S(1)} fusion(f32[8,256,1]{1,2,0:T(1,128)S(1)} %reshape.668, f32[8,64,256]{2,1,0:T(8,128)} %param.10), kind=kOutput, calls=%fused_computation.364 | convolution fusion | flops 1572864 | bytes 534528 | tf_op jit(solution)/shard_map/bim,bm->bi/dot_general | solution.py:203
  68.4 0.7 broadcast_in_dim.180
  69.0 2.8 %all-to-all-start.3 = ((f32[32,1,512]{2,1,0:T(1,128)}), f32[32,1,512]{2,1,0:T(1,128)S(1)}, u32[]{:S(2)}, u32[]{:S(2)}) async-start(f32[32,1,512]{2,1,0:T(1,128)} %broadcast_in_dim.180), calls=%async_computation.3 | async-start | bytes 131072 | tf_op jit(solution)/shard_map/all_to_all | solution.py:143
  71.8 0.6 compare_select_fusion
  72.4 6.8 %all-to-all-done.3 = f32[32,1,512]{2,1,0:T(1,128)S(1)} async-done(((f32[32,1,512]{2,1,0:T(1,128)}), f32[32,1,512]{2,1,0:T(1,128)S(1)}, u32[]{:S(2)}, u32[]{:S(2)}) %all-to-all-start.3) | async-done | bytes 65568 | tf_op jit(solution)/shard_map/all_to_all | solution.py:143
  79.6 0.9 copy.15
  80.4 1.1 %reshape.654 = f32[16,8,128]{2,1,0:T(8,128)S(1)} reshape(f32[4,4,2,4,4,32]{5,4,3,2,1,0:T(4,128)} %copy.15) | data formatting | bytes 131072 | tf_op jit(solution)/shard_map/reshape | solution.py:210
  81.7 1.0 %fusion.1 = f32[6,3264]{1,0:T(8,128)S(1)} fusion(f32[6,204]{1,0:T(8,128)S(1)} %reshape.655, s32[3264]{0:T(1024)S(1)} %fusion.137, pred[]{:T(512)S(6)} %ge.71), kind=kOutput, calls=%fused_computation.2 | convolution fusion | flops 49273344 | bytes 96289 | tf_op jit(solution)/shard_map/dot_general | solution.py:123
  83.7 0.5 fusion.109
  84.8 0.5 fusion.108
  85.9 0.5 fusion.107
  86.8 0.8 slice.631
  (119 shorter events, 11.3 us)
Async XLA Ops:
  1.7 7.3 %copy-start.5 = (s32[8,4]{0,1:T(4,128)S(1)}, s32[8,4]{0,1:T(4,128)}, u32[]{:S(2)}) copy-start(s32[8,4]{0,1:T(4,128)} %param.11) | copy-start | bytes 388
  1.7 7.5 %copy-start = (f32[8,64,256]{2,1,0:T(8,128)S(1)}, f32[8,64,256]{2,1,0:T(8,128)}, u32[]{:S(2)}) copy-start(f32[8,64,256]{2,1,0:T(8,128)} %param.10) | copy-start | bytes 1572868
  1.9 9.5 %copy-start.1 = (f32[16,16,128]{2,1,0:T(8,128)S(1)}, f32[16,16,128]{2,1,0:T(8,128)}, u32[]{:S(2)}) copy-start(f32[16,16,128]{2,1,0:T(8,128)} %param.8) | copy-start | bytes 393220
  1.9 9.5 %copy-start.2 = (f32[16,16,128]{2,1,0:T(8,128)S(1)}, f32[16,16,128]{2,1,0:T(8,128)}, u32[]{:S(2)}) copy-start(f32[16,16,128]{2,1,0:T(8,128)} %param.7) | copy-start | bytes 393220
  1.9 9.5 %copy-start.3 = (f32[16,16,128]{2,1,0:T(8,128)S(1)}, f32[16,16,128]{2,1,0:T(8,128)}, u32[]{:S(2)}) copy-start(f32[16,16,128]{2,1,0:T(8,128)} %param.6) | copy-start | bytes 393220
  2.2 7.2 %collective-permute-start = (f32[24,128]{1,0:T(8,128)S(1)}, f32[24,128]{1,0:T(8,128)S(1)}, u32[]{:S(2)}, u32[]{:S(2)}) collective-permute-start(f32[24,128]{1,0:T(8,128)S(1)} %reshape.641), channel_id=1, source_target_pairs={{8,16},{16,8},{9,17},{17,9},{10,18},{18,10},{11,19},{19,11},{12,20... | collective-permute-start | bytes 36872 | tf_op jit(solution)/shard_map/ppermute | solution.py:28
  3.0 7.6 %collective-permute-start.1 = (f32[24,128]{1,0:T(8,128)S(1)}, f32[24,128]{1,0:T(8,128)S(1)}, u32[]{:S(2)}, u32[]{:S(2)}) collective-permute-start(f32[24,128]{1,0:T(8,128)S(1)} %reshape.642), channel_id=1, source_target_pairs={{0,8},{8,0},{16,24},{24,16},{1,9},{9,1},{17,25},{25,17},{2,10},{10... | collective-permute-start | bytes 36872 | tf_op jit(solution)/shard_map/ppermute | solution.py:28
  12.3 4.9 %collective-permute-start.2 = (f32[3,16,544]{2,1,0:T(8,128)S(1)}, f32[3,16,544]{2,1,0:T(8,128)S(1)}, u32[]{:S(2)}, u32[]{:S(2)}) collective-permute-start(f32[3,16,544]{2,1,0:T(8,128)S(1)} %slice_select_fusion.4), channel_id=1, source_target_pairs={{0,1},{1,0},{2,3},{3,2},{4,5},{5,4},{6,7},{7,6},{8,9},{9,8},{10,11... | collective-permute-start | bytes 313352 | tf_op jit(solution)/shard_map/ppermute | solution.py:29
  17.8 5.9 %collective-permute-start.3 = (f32[306,128]{1,0:T(8,128)S(1)}, f32[306,128]{1,0:T(8,128)S(1)}, u32[]{:S(2)}, u32[]{:S(2)}) collective-permute-start(f32[306,128]{1,0:T(8,128)S(1)} %reshape.644), channel_id=1, source_target_pairs={{2,4},{4,2},{3,5},{5,3},{10,12},{12,10},{11,13},{13,11},{18,20},{2... | collective-permute-start | bytes 470024 | tf_op jit(solution)/shard_map/ppermute | solution.py:28
  18.7 5.0 %collective-permute-start.4 = (f32[306,128]{1,0:T(8,128)S(1)}, f32[306,128]{1,0:T(8,128)S(1)}, u32[]{:S(2)}, u32[]{:S(2)}) collective-permute-start(f32[306,128]{1,0:T(8,128)S(1)} %reshape.645), channel_id=1, source_target_pairs={{0,2},{2,0},{4,6},{6,4},{1,3},{3,1},{5,7},{7,5},{8,10},{10,8},{12,... | collective-permute-start | bytes 470024 | tf_op jit(solution)/shard_map/ppermute | solution.py:28
  30.6 12.6 %all-to-all-start = ((f32[32,1,512]{2,1,0:T(1,128)}), f32[32,1,512]{2,1,0:T(1,128)S(1)}, u32[]{:S(2)}, u32[]{:S(2)}) async-start(f32[32,1,512]{2,1,0:T(1,128)} %broadcast_in_dim.170), calls=%async_computation | async-start | bytes 131072 | tf_op jit(solution)/shard_map/all_to_all | solution.py:143
  68.1 14.7 %copy-start.4 = (f32[512]{0:T(512)}, f32[512]{0:T(512)S(1)}, u32[]{:S(2)}) copy-start(f32[512]{0:T(512)S(1)} %divide_add_fusion) | copy-start | bytes 6148
  69.0 10.2 %all-to-all-start.3 = ((f32[32,1,512]{2,1,0:T(1,128)}), f32[32,1,512]{2,1,0:T(1,128)S(1)}, u32[]{:S(2)}, u32[]{:S(2)}) async-start(f32[32,1,512]{2,1,0:T(1,128)} %broadcast_in_dim.180), calls=%async_computation.3 | async-start | bytes 131072 | tf_op jit(solution)/shard_map/all_to_all | solution.py:143
  80.4 2.3 %copy-start.6 = (s32[24]{0:T(128)S(1)}, s32[24]{0:T(128)}, u32[]{:S(2)}) copy-start(s32[24]{0:T(128)} %compare_select_fusion) | copy-start | bytes 292

commit v24 on v20

--- a/solution.py
+++ b/solution.py
@@ -119,8 +119,8 @@
     return jnp.dot(left, right, precision=lax.Precision.HIGHEST)
 
 
-def box_matrix(boxes, cells, stride, offset, live, inner=None):
-    cell = lax.broadcasted_iota(jnp.int32, (1, cells), 1)
+def box_matrix(boxes, cells, stride, offset, live, inner=None, cells_first=False):
+    cell = lax.broadcasted_iota(jnp.int32, (cells, 1), 0) if cells_first else lax.broadcasted_iota(jnp.int32, (1, cells), 1)
     if inner is None:
         local = cell - offset
         owner = jnp.where((local >= 0) & (local < boxes * BOX), local // BOX, -1)
@@ -129,7 +129,10 @@
         inside = (outer_cell >= 0) & (outer_cell < (boxes // inner) * BOX)
         inside = inside & (inner_cell >= 0) & (inner_cell < inner * BOX)
         owner = jnp.where(inside, (outer_cell // BOX) * inner + inner_cell // BOX, -1)
-    box = lax.broadcasted_iota(jnp.int32, (boxes, cells), 0)
+    if cells_first:
+        box = lax.broadcasted_iota(jnp.int32, (cells, boxes), 1)
+    else:
+        box = lax.broadcasted_iota(jnp.int32, (boxes, cells), 0)
     return ((box == owner) & live).astype(jnp.float32)
 
 
@@ -171,7 +174,7 @@
     bx, by, bz = size_x // BOX, size_y // BOX, size_z // BOX
     live = lax.axis_index("grp") >= 0
     pick_x = box_matrix(bx, rows, 1, HALO, live)
-    pick_yz = box_matrix(by * bz, span_y * span_z, span_z, HALO, live, bz).T
+    pick_yz = box_matrix(by * bz, span_y * span_z, span_z, HALO, live, bz, cells_first=True)
     box_totals = dot(pick_x, dot(smoothed, pick_yz)).reshape(-1)
     box_labels = aggregate_ids[::BOX, ::BOX, ::BOX].reshape(-1)
     placed = box_labels[:, None] == lax.broadcasted_iota(jnp.int32, (box_labels.shape[0],) * 2, 1)

time: 80.2 us -> 80.1 us (level)
  no operation moved by 1% of the time
where the time goes in v24:
time: 80.1 us; the launch traced here: 79.7 us
  waiting for transfers between devices  19.6 us (24%)
  starting transfers between devices  19.5 us (24%)
  blocking collectives  18.6 us (23%)
  local copies, waits for them, and re-layouts  8.53 us (11%)
  other arithmetic  7.14 us (9%)
  matrix products  5.27 us (7%)
  between operations  1.1 us (1%)
    all_to_all x2, blocking collectives, everyone(): return lax.all_to_all(copies, ALL_AXES, 0, 0, tiled=True).reshape(-1)  18.6 us
    all_to_all x2, waiting for transfers between devices, everyone(): return lax.all_to_all(copies, ALL_AXES, 0, 0, tiled=True).reshape(-1)  15 us
    ppermute x4, starting transfers between devices, permute(): return lax.ppermute(slab.reshape(-1, 128), axis, pairs).reshape(slab.shape)  10.2 us
    all_to_all x2, starting transfers between devices, everyone(): return lax.all_to_all(copies, ALL_AXES, 0, 0, tiled=True).reshape(-1)  7.73 us
    dot_general x7, matrix products, dot(): return jnp.dot(left, right, precision=lax.Precision.HIGHEST)  3.71 us
    ppermute x1, waiting for transfers between devices, permute(): return lax.ppermute(slab, axis, pairs)  3.38 us
    select_n x3, other arithmetic, local(): jnp.where(mask, solution + WEIGHT * (src - op(solution)) / diagonal, 0.0)  2.31 us
    slice x1, local copies, waits for them, and re-layouts, local(): box_labels = aggregate_ids[::BOX, ::BOX, ::BOX].reshape(-1)  1.87 us
  transfers between devices with their start and end apart: 7, of which 4 were waited for; matrix products, arithmetic and copies ran while one was open for 4% of the time, Pallas kernels for 0%

profile of v24, /device:TPU:0, one launch (start us, length us, event | category | flops | bytes accessed | tf_op | source)
XLA Modules:
  0.0 79.7 jit_solution(11206110869631816307)
XLA Ops:
  0.6 1.1 %pad_maximum_fusion.2 = f32[3,16,16,128]{3,2,1,0:T(8,128)S(1)} fusion(f32[1,16,16,128]{3,2,1,0:T(8,128)} %bitcast.82, f32[1,16,16,128]{3,2,1,0:T(8,128)} %bitcast.84, f32[1,16,16,128]{3,2,1,0:T(8,128)} %bitcast.86), kind=kLoop, calls=%fused_computation.58 | loop fusion | flops 196608 | bytes 786432 | tf_op jit(solution)/shard_map/stack | solution.py:148
  2.2 0.7 collective-permute-start
  3.0 5.9 %collective-permute-start.1 = (f32[24,128]{1,0:T(8,128)S(1)}, f32[24,128]{1,0:T(8,128)S(1)}, u32[]{:S(2)}, u32[]{:S(2)}) collective-permute-start(f32[24,128]{1,0:T(8,128)S(1)} %reshape.671), channel_id=1, source_target_pairs={{0,8},{8,0},{16,24},{24,16},{1,9},{9,1},{17,25},{25,17},{2,10},{10... | collective-permute-start | bytes 36872 | tf_op jit(solution)/shard_map/ppermute | solution.py:28
  9.4 1.2 %collective-permute-done.1 = f32[24,128]{1,0:T(8,128)S(1)} collective-permute-done((f32[24,128]{1,0:T(8,128)S(1)}, f32[24,128]{1,0:T(8,128)S(1)}, u32[]{:S(2)}, u32[]{:S(2)}) %collective-permute-start.1) | collective-permute-done | bytes 12320 | tf_op jit(solution)/shard_map/ppermute | solution.py:28
  10.6 0.4 select_n.383
  11.0 0.4 select_n.385
  11.8 0.4 reshape.672
  12.3 1.6 %collective-permute-start.2 = (f32[3,16,544]{2,1,0:T(8,128)S(1)}, f32[3,16,544]{2,1,0:T(8,128)S(1)}, u32[]{:S(2)}, u32[]{:S(2)}) collective-permute-start(f32[3,16,544]{2,1,0:T(8,128)S(1)} %slice_select_fusion.4), channel_id=1, source_target_pairs={{0,1},{1,0},{2,3},{3,2},{4,5},{5,4},{6,7},{7,6},{8,9},{9,8},{10,11... | collective-permute-start | bytes 313352 | tf_op jit(solution)/shard_map/ppermute | solution.py:29
  13.9 3.4 %collective-permute-done.2 = f32[3,16,544]{2,1,0:T(8,128)S(1)} collective-permute-done((f32[3,16,544]{2,1,0:T(8,128)S(1)}, f32[3,16,544]{2,1,0:T(8,128)S(1)}, u32[]{:S(2)}, u32[]{:S(2)}) %collective-permute-start.2) | collective-permute-done | bytes 104480 | tf_op jit(solution)/shard_map/ppermute | solution.py:29
  17.8 0.7 collective-permute-start.3
  18.7 2.9 %collective-permute-start.4 = (f32[306,128]{1,0:T(8,128)S(1)}, f32[306,128]{1,0:T(8,128)S(1)}, u32[]{:S(2)}, u32[]{:S(2)}) collective-permute-start(f32[306,128]{1,0:T(8,128)S(1)} %reshape.674), channel_id=1, source_target_pairs={{0,2},{2,0},{4,6},{6,4},{1,3},{3,1},{5,7},{7,5},{8,10},{10,8},{12,... | collective-permute-start | bytes 470024 | tf_op jit(solution)/shard_map/ppermute | solution.py:28
  21.6 1.9 %slice.255 = s32[4,4,32]{2,1,0:T(4,128)S(1)} slice(s32[16,16,128]{2,1,0:T(8,128)} %param.9), slice={[0:16:4], [0:16:4], [0:128:4]} | slice | bytes 4096 | tf_op jit(solution)/shard_map/slice | solution.py:179
  24.2 0.5 divide_select_fusion.1
  24.7 1.2 %fusion.152 = (f32[24,3264]{1,0:T(8,128)S(1)}, f32[24,3264]{1,0:T(8,128)}) fusion(pred[3264]{0:T(1024)(128)(4,1)S(1)} %get-tuple-element.29, pred[3264]{0:T(1024)(128)(4,1)S(1)} %get-tuple-element.30, pred[24]{0:T(512)(128)(4,1)S(1)} %compare_and_fusion.1, f32[24,3264]{1,0:T(8,128)S(1)} %get-tuple-element.6, f32[24,3264]{1,0:T(8,128)S(1)} %get-tuple-element.11, ...), kind=kLoop, calls=%fused_computation.212 | loop fusion | flops 2506752 | bytes 3453336 | tf_op jit(solution)/shard_map/jit(_where)/select_n | solution.py:169
  25.9 0.5 divide_select_fusion
  26.5 1.5 %fusion.4 = f32[24,128]{1,0:T(8,128)S(1)} fusion(s32[3264]{0:T(1024)S(1)} %fusion.173, pred[]{:T(512)S(6)} %ge.71, f32[24,3264]{1,0:T(8,128)S(1)} %get-tuple-element.12, f32[24,3264]{1,0:T(8,128)S(1)} %divide_select_fusion, f32[24,3264]{1,0:T(8,128)S(1)} %get-tuple-element.7, f32[24,3264]{1,0:T(8,128)S(1)} %get-tuple-element.8, ...), kind=kOutput, calls=%fused_computation.5 | convolution fusion | flops 124371456 | bytes 3223553 | tf_op jit(solution)/shard_map/dot_general | solution.py:119
  28.4 0.7 broadcast_in_dim.171
  29.0 5.0 %all-to-all-start = ((f32[32,1,512]{2,1,0:T(1,128)}), f32[32,1,512]{2,1,0:T(1,128)S(1)}, u32[]{:S(2)}, u32[]{:S(2)}) async-start(f32[32,1,512]{2,1,0:T(1,128)} %broadcast_in_dim.171), calls=%async_computation | async-start | bytes 131072 | tf_op jit(solution)/shard_map/all_to_all | solution.py:142
  34.0 7.6 %all-to-all-done = f32[32,1,512]{2,1,0:T(1,128)S(1)} async-done(((f32[32,1,512]{2,1,0:T(1,128)}), f32[32,1,512]{2,1,0:T(1,128)S(1)}, u32[]{:S(2)}, u32[]{:S(2)}) %all-to-all-start) | async-done | bytes 65568 | tf_op jit(solution)/shard_map/all_to_all | solution.py:142
  42.1 0.5 fusion.244
  42.7 9.3 %all_to_all.33 = f32[32,1,512]{2,1,0:T(1,128)S(1)} all-to-all(f32[32,1,512]{2,1,0:T(1,128)S(1)} %broadcast_in_dim.178), channel_id=1, replica_groups=mesh['grp'=4,'gx'=4,'gy'=2] {'grp','gx','gy'}, dimensions={0} | all-to-all | bytes 131072 | tf_op jit(solution)/shard_map/all_to_all | solution.py:142
  52.5 0.5 fusion.245
  53.1 9.3 %all_to_all.34 = f32[32,1,512]{2,1,0:T(1,128)S(1)} all-to-all(f32[32,1,512]{2,1,0:T(1,128)S(1)} %broadcast_in_dim.179), channel_id=1, replica_groups=mesh['grp'=4,'gx'=4,'gy'=2] {'grp','gx','gy'}, dimensions={0} | all-to-all | bytes 131072 | tf_op jit(solution)/shard_map/all_to_all | solution.py:142
  62.9 0.5 fusion.246
  63.7 0.7 broadcast_in_dim.181
  64.4 2.8 %all-to-all-start.3 = ((f32[32,1,512]{2,1,0:T(1,128)}), f32[32,1,512]{2,1,0:T(1,128)S(1)}, u32[]{:S(2)}, u32[]{:S(2)}) async-start(f32[32,1,512]{2,1,0:T(1,128)} %broadcast_in_dim.181), calls=%async_computation.3 | async-start | bytes 131072 | tf_op jit(solution)/shard_map/all_to_all | solution.py:142
  67.2 7.4 %all-to-all-done.3 = f32[32,1,512]{2,1,0:T(1,128)S(1)} async-done(((f32[32,1,512]{2,1,0:T(1,128)}), f32[32,1,512]{2,1,0:T(1,128)S(1)}, u32[]{:S(2)}, u32[]{:S(2)}) %all-to-all-start.3) | async-done | bytes 65568 | tf_op jit(solution)/shard_map/all_to_all | solution.py:142
  75.5 1.0 %fusion.1 = f32[6,3264]{1,0:T(8,128)S(1)} fusion(f32[6,204]{1,0:T(8,128)S(1)} %reshape.684, s32[3264]{0:T(1024)S(1)} %fusion.178, pred[]{:T(512)S(6)} %ge.71), kind=kOutput, calls=%fused_computation.2 | convolution fusion | flops 49273344 | bytes 96289 | tf_op jit(solution)/shard_map/dot_general | solution.py:119
  76.9 0.6 fusion.151
  77.5 0.5 fusion.150
  78.0 0.5 fusion.149
  78.9 0.8 slice.345
  (77 shorter events, 6.7 us)
Async XLA Ops:
  1.7 7.3 %copy-start.6 = (s32[8,4]{0,1:T(4,128)S(1)}, s32[8,4]{0,1:T(4,128)}, u32[]{:S(2)}) copy-start(s32[8,4]{0,1:T(4,128)} %param.11) | copy-start | bytes 388
  1.7 7.5 %copy-start = (f32[8,64,256]{2,1,0:T(8,128)S(1)}, f32[8,64,256]{2,1,0:T(8,128)}, u32[]{:S(2)}) copy-start(f32[8,64,256]{2,1,0:T(8,128)} %param.10) | copy-start | bytes 1572868
  1.9 9.5 %copy-start.2 = (f32[16,16,128]{2,1,0:T(8,128)S(1)}, f32[16,16,128]{2,1,0:T(8,128)}, u32[]{:S(2)}) copy-start(f32[16,16,128]{2,1,0:T(8,128)} %param.8) | copy-start | bytes 393220
  1.9 9.5 %copy-start.3 = (f32[16,16,128]{2,1,0:T(8,128)S(1)}, f32[16,16,128]{2,1,0:T(8,128)}, u32[]{:S(2)}) copy-start(f32[16,16,128]{2,1,0:T(8,128)} %param.7) | copy-start | bytes 393220
  1.9 9.5 %copy-start.4 = (f32[16,16,128]{2,1,0:T(8,128)S(1)}, f32[16,16,128]{2,1,0:T(8,128)}, u32[]{:S(2)}) copy-start(f32[16,16,128]{2,1,0:T(8,128)} %param.6) | copy-start | bytes 393220
  2.2 7.2 %collective-permute-start = (f32[24,128]{1,0:T(8,128)S(1)}, f32[24,128]{1,0:T(8,128)S(1)}, u32[]{:S(2)}, u32[]{:S(2)}) collective-permute-start(f32[24,128]{1,0:T(8,128)S(1)} %reshape.670), channel_id=1, source_target_pairs={{8,16},{16,8},{9,17},{17,9},{10,18},{18,10},{11,19},{19,11},{12,20... | collective-permute-start | bytes 36872 | tf_op jit(solution)/shard_map/ppermute | solution.py:28
  3.0 7.6 %collective-permute-start.1 = (f32[24,128]{1,0:T(8,128)S(1)}, f32[24,128]{1,0:T(8,128)S(1)}, u32[]{:S(2)}, u32[]{:S(2)}) collective-permute-start(f32[24,128]{1,0:T(8,128)S(1)} %reshape.671), channel_id=1, source_target_pairs={{0,8},{8,0},{16,24},{24,16},{1,9},{9,1},{17,25},{25,17},{2,10},{10... | collective-permute-start | bytes 36872 | tf_op jit(solution)/shard_map/ppermute | solution.py:28
  12.3 4.9 %collective-permute-start.2 = (f32[3,16,544]{2,1,0:T(8,128)S(1)}, f32[3,16,544]{2,1,0:T(8,128)S(1)}, u32[]{:S(2)}, u32[]{:S(2)}) collective-permute-start(f32[3,16,544]{2,1,0:T(8,128)S(1)} %slice_select_fusion.4), channel_id=1, source_target_pairs={{0,1},{1,0},{2,3},{3,2},{4,5},{5,4},{6,7},{7,6},{8,9},{9,8},{10,11... | collective-permute-start | bytes 313352 | tf_op jit(solution)/shard_map/ppermute | solution.py:29
  17.8 5.9 %collective-permute-start.3 = (f32[306,128]{1,0:T(8,128)S(1)}, f32[306,128]{1,0:T(8,128)S(1)}, u32[]{:S(2)}, u32[]{:S(2)}) collective-permute-start(f32[306,128]{1,0:T(8,128)S(1)} %reshape.673), channel_id=1, source_target_pairs={{2,4},{4,2},{3,5},{5,3},{10,12},{12,10},{11,13},{13,11},{18,20},{2... | collective-permute-start | bytes 470024 | tf_op jit(solution)/shard_map/ppermute | solution.py:28
  18.7 5.0 %collective-permute-start.4 = (f32[306,128]{1,0:T(8,128)S(1)}, f32[306,128]{1,0:T(8,128)S(1)}, u32[]{:S(2)}, u32[]{:S(2)}) collective-permute-start(f32[306,128]{1,0:T(8,128)S(1)} %reshape.674), channel_id=1, source_target_pairs={{0,2},{2,0},{4,6},{6,4},{1,3},{3,1},{5,7},{7,5},{8,10},{10,8},{12,... | collective-permute-start | bytes 470024 | tf_op jit(solution)/shard_map/ppermute | solution.py:28
  29.0 12.6 %all-to-all-start = ((f32[32,1,512]{2,1,0:T(1,128)}), f32[32,1,512]{2,1,0:T(1,128)S(1)}, u32[]{:S(2)}, u32[]{:S(2)}) async-start(f32[32,1,512]{2,1,0:T(1,128)} %broadcast_in_dim.171), calls=%async_computation | async-start | bytes 131072 | tf_op jit(solution)/shard_map/all_to_all | solution.py:142
  63.5 13.1 %copy-start.5 = (f32[512]{0:T(512)}, f32[512]{0:T(512)S(1)}, u32[]{:S(2)}) copy-start(f32[512]{0:T(512)S(1)} %divide_add_fusion) | copy-start | bytes 6148
  64.4 10.2 %all-to-all-start.3 = ((f32[32,1,512]{2,1,0:T(1,128)}), f32[32,1,512]{2,1,0:T(1,128)S(1)}, u32[]{:S(2)}, u32[]{:S(2)}) async-start(f32[32,1,512]{2,1,0:T(1,128)} %broadcast_in_dim.181), calls=%async_computation.3 | async-start | bytes 131072 | tf_op jit(solution)/shard_map/all_to_all | solution.py:142
  75.3 1.6 %copy-start.1 = (f32[24,3264]{1,0:T(8,128)S(1)}, f32[24,3264]{1,0:T(8,128)}, u32[]{:S(2)}) copy-start(f32[24,3264]{1,0:T(8,128)} %get-tuple-element.5) | copy-start | bytes 940036

commit v25 on v20

--- a/solution.py
+++ b/solution.py
@@ -100,8 +100,8 @@
 
 
 def trimmed(flat, span_y, span_z):
-    cube = flat.reshape(flat.shape[0], span_y, span_z)
-    return cube[HALO:-HALO, HALO:-HALO, HALO:-HALO]
+    cube = flat[HALO:-HALO].reshape(flat.shape[0] - 2 * HALO, span_y, span_z)
+    return cube[:, HALO:-HALO, HALO:-HALO]
 
 
 def grp_pool(vector):

time: 80.2 us -> 103 us (1.28)
  other arithmetic: 7.14 us -> 17.5 us
  blocking collectives: 18.6 us -> 9.3 us
  local copies, waits for them, and re-layouts: 8.53 us -> 16.6 us
  matrix products: 5.31 us -> 11.9 us
  starting transfers between devices: 19.5 us -> 23 us
  waiting for transfers between devices: 19.6 us -> 22.7 us
    all_to_all x2 -> x1, blocking collectives: 18.6 us -> 9.3 us  [everyone(): return lax.all_to_all(copies, ALL_AXES, 0, 0, tiled=True).reshape(-1)]
    all_to_all x2 -> x3, waiting for transfers between devices: 15 us -> 19.3 us  [everyone(): return lax.all_to_all(copies, ALL_AXES, 0, 0, tiled=True).reshape(-1)]
    all_to_all x2 -> x3, starting transfers between devices: 7.73 us -> 11.2 us  [everyone(): return lax.all_to_all(copies, ALL_AXES, 0, 0, tiled=True).reshape(-1)]
    dot_general x7, matrix products: 3.76 us -> 7.2 us  [dot(): return jnp.dot(left, right, precision=lax.Precision.HIGHEST)]
    dot_general x3, matrix products: 1.55 us -> 4.68 us  [local(): jnp.einsum('bim,bm->bi', coarse_values, blocks, precision=lax.Precision.H...]
    select_n x3, other arithmetic: 0.35 us -> 2.42 us  [local(): jnp.where(within == part, rows_of[:, part * 64:(part + 1) * 64], blocks)]
    add x3, other arithmetic: 0.03 us -> 2.1 us  [local(): coarse_error = coarse_error + (coarse_rhs - applied) / coarse_diag]
    transpose x1, local copies, waits for them, and re-layouts: 0.17 us -> 1.82 us  [local(): every.transpose(1, 3, 2, 4, 0, 5)]
  transfers between devices with their start and end apart: 7 -> 8, of which waited for: 4 -> 5; matrix products, arithmetic and copies ran while one was open for 4% -> 8% of each run, Pallas kernels for 0% -> 0%
where the time goes in v25:
time: 103 us; the launch traced here: 102 us
  starting transfers between devices  23 us (22%)
  waiting for transfers between devices  22.7 us (22%)
  other arithmetic  17.5 us (17%)
  local copies, waits for them, and re-layouts  16.6 us (16%)
  matrix products  11.9 us (12%)
  blocking collectives  9.3 us (9%)
  between operations  1.12 us (1%)
    all_to_all x3, waiting for transfers between devices, everyone(): return lax.all_to_all(copies, ALL_AXES, 0, 0, tiled=True).reshape(-1)  19.3 us
    all_to_all x3, starting transfers between devices, everyone(): return lax.all_to_all(copies, ALL_AXES, 0, 0, tiled=True).reshape(-1)  11.2 us
    ppermute x4, starting transfers between devices, permute(): return lax.ppermute(slab.reshape(-1, 128), axis, pairs).reshape(slab.shape)  10.2 us
    all_to_all x1, blocking collectives, everyone(): return lax.all_to_all(copies, ALL_AXES, 0, 0, tiled=True).reshape(-1)  9.3 us
    dot_general x7, matrix products, dot(): return jnp.dot(left, right, precision=lax.Precision.HIGHEST)  7.2 us
    dot_general x3, matrix products, local(): jnp.einsum('bim,bm->bi', coarse_values, blocks, precision=lax.Precision.H...  4.68 us
    ppermute x1, waiting for transfers between devices, permute(): return lax.ppermute(slab, axis, pairs)  3.38 us
    select_n x3, other arithmetic, local(): jnp.where(within == part, rows_of[:, part * 64:(part + 1) * 64], blocks)  2.42 us
  transfers between devices with their start and end apart: 8, of which 5 were waited for; matrix products, arithmetic and copies ran while one was open for 8% of the time, Pallas kernels for 0%

profile of v25, /device:TPU:0, one launch (start us, length us, event | category | flops | bytes accessed | tf_op | source)
XLA Modules:
  0.0 102.1 jit_solution(3387729670415572182)
XLA Ops:
  0.6 1.1 %pad_maximum_fusion.2 = f32[3,16,16,128]{3,2,1,0:T(8,128)S(1)} fusion(f32[1,16,16,128]{3,2,1,0:T(8,128)} %bitcast.69, f32[1,16,16,128]{3,2,1,0:T(8,128)} %bitcast.71, f32[1,16,16,128]{3,2,1,0:T(8,128)} %bitcast.73), kind=kLoop, calls=%fused_computation.58 | loop fusion | flops 196608 | bytes 786432 | tf_op jit(solution)/shard_map/stack | solution.py:145
  3.0 5.9 %collective-permute-start.1 = (f32[24,128]{1,0:T(8,128)S(1)}, f32[24,128]{1,0:T(8,128)S(1)}, u32[]{:S(2)}, u32[]{:S(2)}) collective-permute-start(f32[24,128]{1,0:T(8,128)S(1)} %reshape.638), channel_id=1, source_target_pairs={{0,8},{8,0},{16,24},{24,16},{1,9},{9,1},{17,25},{25,17},{2,10},{10... | collective-permute-start | bytes 36872 | tf_op jit(solution)/shard_map/ppermute | solution.py:28
  12.4 1.6 %collective-permute-start.2 = (f32[3,16,544]{2,1,0:T(8,128)S(1)}, f32[3,16,544]{2,1,0:T(8,128)S(1)}, u32[]{:S(2)}, u32[]{:S(2)}) collective-permute-start(f32[3,16,544]{2,1,0:T(8,128)S(1)} %slice_select_fusion.4), channel_id=1, source_target_pairs={{0,1},{1,0},{2,3},{3,2},{4,5},{5,4},{6,7},{7,6},{8,9},{9,8},{10,11... | collective-permute-start | bytes 313352 | tf_op jit(solution)/shard_map/ppermute | solution.py:29
  13.9 3.4 %collective-permute-done.2 = f32[3,16,544]{2,1,0:T(8,128)S(1)} collective-permute-done((f32[3,16,544]{2,1,0:T(8,128)S(1)}, f32[3,16,544]{2,1,0:T(8,128)S(1)}, u32[]{:S(2)}, u32[]{:S(2)}) %collective-permute-start.2) | collective-permute-done | bytes 104480 | tf_op jit(solution)/shard_map/ppermute | solution.py:29
  18.7 2.9 %collective-permute-start.4 = (f32[306,128]{1,0:T(8,128)S(1)}, f32[306,128]{1,0:T(8,128)S(1)}, u32[]{:S(2)}, u32[]{:S(2)}) collective-permute-start(f32[306,128]{1,0:T(8,128)S(1)} %reshape.641), channel_id=1, source_target_pairs={{0,2},{2,0},{4,6},{6,4},{1,3},{3,1},{5,7},{7,5},{8,10},{10,8},{12,... | collective-permute-start | bytes 470024 | tf_op jit(solution)/shard_map/ppermute | solution.py:28
  21.6 1.9 %slice.258 = s32[4,4,32]{2,1,0:T(4,128)S(1)} slice(s32[16,16,128]{2,1,0:T(8,128)} %param.9), slice={[0:16:4], [0:16:4], [0:128:4]} | slice | bytes 4096 | tf_op jit(solution)/shard_map/slice | solution.py:176
  27.2 1.3 %fusion.4 = f32[24,128]{1,0:T(8,128)S(1)} fusion(s32[3264]{0:T(1024)S(1)} %copy-done.12, pred[]{:T(512)S(6)} %ge.71, f32[24,3264]{1,0:T(8,128)S(1)} %get-tuple-element.5, f32[24,3264]{1,0:T(8,128)S(1)} %get-tuple-element.8, f32[24,3264]{1,0:T(8,128)S(1)} %get-tuple-element.4, f32[24,3264]{1,0:T(8,128)S(1)} %get-tuple-element.9, ...), kind=kOutput, calls=%fused_computation.5 | convolution fusion | flops 122804736 | bytes 2904065 | tf_op jit(solution)/shard_map/dot_general | solution.py:119
  29.6 4.5 %all-to-all-start = ((f32[32,1,512]{2,1,0:T(1,128)}), f32[32,1,512]{2,1,0:T(1,128)}, u32[]{:S(2)}, u32[]{:S(2)}) async-start(f32[32,1,512]{2,1,0:T(1,128)} %broadcast_in_dim.170), calls=%async_computation | async-start | bytes 131072 | tf_op jit(solution)/shard_map/all_to_all | solution.py:139
  34.8 6.9 %all-to-all-done = f32[32,1,512]{2,1,0:T(1,128)} async-done(((f32[32,1,512]{2,1,0:T(1,128)}), f32[32,1,512]{2,1,0:T(1,128)}, u32[]{:S(2)}, u32[]{:S(2)}) %all-to-all-start) | async-done | bytes 65568 | tf_op jit(solution)/shard_map/all_to_all | solution.py:139
  41.7 1.1 %fusion.157 = f32[32,512]{1,0:T(8,128)S(1)} fusion(f32[32,1,512]{2,1,0:T(1,128)} %all-to-all-done, s32[32]{0:T(128)S(1)} %and_select_fusion), kind=kOutput, calls=%fused_computation.225 | convolution fusion | flops 6292480 | bytes 131200 | tf_op jit(solution)/shard_map/dot_general | solution.py:119
  42.8 0.8 fusion.208
  43.7 1.6 %fusion.239 = f32[8,1,64]{2,1,0:T(1,128)S(1)} fusion(f32[8,256,1]{1,2,0:T(1,128)S(1)} %reshape.660, f32[8,64,256]{2,1,0:T(8,128)} %param.10), kind=kOutput, calls=%fused_computation.358 | convolution fusion | flops 1572864 | bytes 534528 | tf_op jit(solution)/shard_map/bim,bm->bi/dot_general | solution.py:199
  46.0 9.3 %all_to_all.33 = f32[32,1,512]{2,1,0:T(1,128)S(1)} all-to-all(f32[32,1,512]{2,1,0:T(1,128)S(1)} %broadcast_in_dim.177), channel_id=1, replica_groups=mesh['grp'=4,'gx'=4,'gy'=2] {'grp','gx','gy'}, dimensions={0} | all-to-all | bytes 131072 | tf_op jit(solution)/shard_map/all_to_all | solution.py:139
  55.3 0.9 fusion.154
  56.2 0.8 fusion.202
  57.1 1.6 %fusion.240 = f32[8,1,64]{2,1,0:T(1,128)S(1)} fusion(f32[8,256,1]{1,2,0:T(1,128)S(1)} %reshape.662, f32[8,64,256]{2,1,0:T(8,128)} %param.10), kind=kOutput, calls=%fused_computation.359 | convolution fusion | flops 1572864 | bytes 534528 | tf_op jit(solution)/shard_map/bim,bm->bi/dot_general | solution.py:199
  60.1 3.3 %all-to-all-start.2 = ((f32[32,1,512]{2,1,0:T(1,128)}), f32[32,1,512]{2,1,0:T(1,128)}, u32[]{:S(2)}, u32[]{:S(2)}) async-start(f32[32,1,512]{2,1,0:T(1,128)} %broadcast_in_dim.178), calls=%async_computation.2 | async-start | bytes 131072 | tf_op jit(solution)/shard_map/all_to_all | solution.py:139
  63.4 1.4 %and_and_fusion = pred[24,3264]{1,0:T(8,128)(4,1)} fusion(pred[3264]{0:T(1024)(128)(4,1)S(1)} %get-tuple-element.34, pred[3264]{0:T(1024)(128)(4,1)S(1)} %get-tuple-element.35, pred[24]{0:T(512)(128)(4,1)} %copy-done.10), kind=kLoop, calls=%fused_computation.201 | loop fusion | flops 156672 | bytes 84888 | tf_op jit(solution)/shard_map/and | solution.py:98
  64.8 6.2 %all-to-all-done.2 = f32[32,1,512]{2,1,0:T(1,128)} async-done(((f32[32,1,512]{2,1,0:T(1,128)}), f32[32,1,512]{2,1,0:T(1,128)}, u32[]{:S(2)}, u32[]{:S(2)}) %all-to-all-start.2) | async-done | bytes 65568 | tf_op jit(solution)/shard_map/all_to_all | solution.py:139
  71.0 1.1 %fusion.151 = f32[32,512]{1,0:T(8,128)S(1)} fusion(f32[32,1,512]{2,1,0:T(1,128)} %all-to-all-done.2, s32[32]{0:T(128)} %copy-done.16), kind=kOutput, calls=%fused_computation.219 | convolution fusion | flops 6292480 | bytes 131200 | tf_op jit(solution)/shard_map/dot_general | solution.py:119
  72.1 0.8 fusion.196
  73.0 1.6 %fusion.241 = f32[8,1,64]{2,1,0:T(1,128)S(1)} fusion(f32[8,256,1]{1,2,0:T(1,128)S(1)} %reshape.664, f32[8,64,256]{2,1,0:T(8,128)} %param.10), kind=kOutput, calls=%fused_computation.360 | convolution fusion | flops 1572864 | bytes 534528 | tf_op jit(solution)/shard_map/bim,bm->bi/dot_general | solution.py:199
  75.3 0.9 select_reduce_fusion
  76.9 3.4 %all-to-all-start.3 = ((f32[32,1,512]{2,1,0:T(1,128)}), f32[32,1,512]{2,1,0:T(1,128)}, u32[]{:S(2)}, u32[]{:S(2)}) async-start(f32[32,1,512]{2,1,0:T(1,128)} %broadcast_in_dim.180), calls=%async_computation.3 | async-start | bytes 131072 | tf_op jit(solution)/shard_map/all_to_all | solution.py:139
  81.5 6.2 %all-to-all-done.3 = f32[32,1,512]{2,1,0:T(1,128)} async-done(((f32[32,1,512]{2,1,0:T(1,128)}), f32[32,1,512]{2,1,0:T(1,128)}, u32[]{:S(2)}, u32[]{:S(2)}) %all-to-all-start.3) | async-done | bytes 65568 | tf_op jit(solution)/shard_map/all_to_all | solution.py:139
  87.7 1.6 %reduce = f32[32,512]{1,0:T(8,128)} reduce(f32[32,1,512]{2,1,0:T(1,128)} %all-to-all-done.3, f32[]{:T(128)} %constant.206), dimensions={1}, to_apply=%all_to_all.28.reduce_sub_computation | reduce | bytes 131076 | tf_op jit(solution)/shard_map/all_to_all | solution.py:139
  89.3 1.7 %reshape_reshape.3 = f32[4,4,2,4,4,32]{5,4,3,2,1,0:T(4,128)} reshape(f32[32,512]{1,0:T(8,128)} %reduce) | data formatting | bytes 131072 | tf_op jit(solution)/shard_map/reshape;reshape | solution.py:205
  91.1 1.8 %copy.15 = f32[4,4,2,4,4,32]{5,4,3,2,1,0:T(4,128)} copy(f32[4,4,2,4,4,32]{5,3,1,2,0,4:T(4,128)} %bitcast.68) | data formatting | bytes 131072 | tf_op jit(solution)/shard_map/transpose | solution.py:206
  92.9 1.7 %reshape.650 = f32[16,8,128]{2,1,0:T(8,128)} reshape(f32[4,4,2,4,4,32]{5,4,3,2,1,0:T(4,128)} %copy.15) | data formatting | bytes 131072 | tf_op jit(solution)/shard_map/reshape | solution.py:206
  94.6 0.8 pad_dynamic-slice_fusion
  96.1 1.8 %fusion.1 = f32[6,3264]{1,0:T(8,128)S(1)} fusion(f32[6,204]{1,0:T(8,128)} %reshape.651, s32[3264]{0:T(1024)} %fusion.174, pred[]{:T(512)S(6)} %ge.71), kind=kOutput, calls=%fused_computation.2 | convolution fusion | flops 49273344 | bytes 96289 | tf_op jit(solution)/shard_map/dot_general | solution.py:119
  97.9 1.0 %fusion.222 = f32[24,3264]{1,0:T(8,128)S(1)} fusion(f32[6,3264]{1,0:T(8,128)S(1)} %fusion.1, s32[24]{0:T(128)} %compare_select_fusion, pred[]{:T(512)S(6)} %ge.71), kind=kOutput, calls=%fused_computation.323 | convolution fusion | flops 5640480 | bytes 391777 | tf_op jit(solution)/shard_map/dot_general | solution.py:119
  (104 shorter events, 20.3 us)
Async XLA Ops:
  1.7 7.3 %copy-start.17 = (s32[8,4]{0,1:T(4,128)S(1)}, s32[8,4]{0,1:T(4,128)}, u32[]{:S(2)}) copy-start(s32[8,4]{0,1:T(4,128)} %param.11) | copy-start | bytes 388
  1.7 8.6 %copy-start = (f32[8,64,256]{2,1,0:T(8,128)S(1)}, f32[8,64,256]{2,1,0:T(8,128)}, u32[]{:S(2)}) copy-start(f32[8,64,256]{2,1,0:T(8,128)} %param.10) | copy-start | bytes 1572868
  1.9 9.5 %copy-start.2 = (f32[16,16,128]{2,1,0:T(8,128)S(1)}, f32[16,16,128]{2,1,0:T(8,128)}, u32[]{:S(2)}) copy-start(f32[16,16,128]{2,1,0:T(8,128)} %param.8) | copy-start | bytes 393220
  1.9 9.5 %copy-start.3 = (f32[16,16,128]{2,1,0:T(8,128)S(1)}, f32[16,16,128]{2,1,0:T(8,128)}, u32[]{:S(2)}) copy-start(f32[16,16,128]{2,1,0:T(8,128)} %param.7) | copy-start | bytes 393220
  1.9 9.5 %copy-start.4 = (f32[16,16,128]{2,1,0:T(8,128)S(1)}, f32[16,16,128]{2,1,0:T(8,128)}, u32[]{:S(2)}) copy-start(f32[16,16,128]{2,1,0:T(8,128)} %param.6) | copy-start | bytes 393220
  2.2 8.4 %collective-permute-start = (f32[24,128]{1,0:T(8,128)S(1)}, f32[24,128]{1,0:T(8,128)S(1)}, u32[]{:S(2)}, u32[]{:S(2)}) collective-permute-start(f32[24,128]{1,0:T(8,128)S(1)} %reshape.637), channel_id=1, source_target_pairs={{8,16},{16,8},{9,17},{17,9},{10,18},{18,10},{11,19},{19,11},{12,20... | collective-permute-start | bytes 36872 | tf_op jit(solution)/shard_map/ppermute | solution.py:28
  3.0 7.6 %collective-permute-start.1 = (f32[24,128]{1,0:T(8,128)S(1)}, f32[24,128]{1,0:T(8,128)S(1)}, u32[]{:S(2)}, u32[]{:S(2)}) collective-permute-start(f32[24,128]{1,0:T(8,128)S(1)} %reshape.638), channel_id=1, source_target_pairs={{0,8},{8,0},{16,24},{24,16},{1,9},{9,1},{17,25},{25,17},{2,10},{10... | collective-permute-start | bytes 36872 | tf_op jit(solution)/shard_map/ppermute | solution.py:28
  9.1 1.9 %copy-start.18 = (s32[32]{0:T(128)}, s32[32]{0:T(128)S(1)}, u32[]{:S(2)}) copy-start(s32[32]{0:T(128)S(1)} %reshape.643) | copy-start | bytes 388
  10.4 32.4 %copy-start.13 = (pred[32]{0:T(512)(128)(4,1)}, pred[32]{0:T(512)(128)(4,1)S(1)}, u32[]{:S(2)}) copy-start(pred[32]{0:T(512)(128)(4,1)S(1)} %get-tuple-element.28) | copy-start | bytes 100
  10.4 32.4 %copy-start.14 = (pred[32]{0:T(512)(128)(4,1)}, pred[32]{0:T(512)(128)(4,1)S(1)}, u32[]{:S(2)}) copy-start(pred[32]{0:T(512)(128)(4,1)S(1)} %get-tuple-element.29) | copy-start | bytes 100
  12.4 4.9 %collective-permute-start.2 = (f32[3,16,544]{2,1,0:T(8,128)S(1)}, f32[3,16,544]{2,1,0:T(8,128)S(1)}, u32[]{:S(2)}, u32[]{:S(2)}) collective-permute-start(f32[3,16,544]{2,1,0:T(8,128)S(1)} %slice_select_fusion.4), channel_id=1, source_target_pairs={{0,1},{1,0},{2,3},{3,2},{4,5},{5,4},{6,7},{7,6},{8,9},{9,8},{10,11... | collective-permute-start | bytes 313352 | tf_op jit(solution)/shard_map/ppermute | solution.py:29
  17.8 6.5 %collective-permute-start.3 = (f32[306,128]{1,0:T(8,128)S(1)}, f32[306,128]{1,0:T(8,128)S(1)}, u32[]{:S(2)}, u32[]{:S(2)}) collective-permute-start(f32[306,128]{1,0:T(8,128)S(1)} %reshape.640), channel_id=1, source_target_pairs={{2,4},{4,2},{3,5},{5,3},{10,12},{12,10},{11,13},{13,11},{18,20},{2... | collective-permute-start | bytes 470024 | tf_op jit(solution)/shard_map/ppermute | solution.py:28
  18.7 5.6 %collective-permute-start.4 = (f32[306,128]{1,0:T(8,128)S(1)}, f32[306,128]{1,0:T(8,128)S(1)}, u32[]{:S(2)}, u32[]{:S(2)}) collective-permute-start(f32[306,128]{1,0:T(8,128)S(1)} %reshape.641), channel_id=1, source_target_pairs={{0,2},{2,0},{4,6},{6,4},{1,3},{3,1},{5,7},{7,5},{8,10},{10,8},{12,... | collective-permute-start | bytes 470024 | tf_op jit(solution)/shard_map/ppermute | solution.py:28
  21.6 4.9 %copy-start.10 = (pred[24]{0:T(512)(128)(4,1)}, pred[24]{0:T(512)(128)(4,1)S(1)}, u32[]{:S(2)}) copy-start(pred[24]{0:T(512)(128)(4,1)S(1)} %compare_and_fusion.1) | copy-start | bytes 76
  23.6 5.1 %copy-start.6 = (s32[512]{0:T(512)}, s32[512]{0:T(512)S(1)}, u32[]{:S(2)}) copy-start(s32[512]{0:T(512)S(1)} %eq.155) | copy-start | bytes 6148
  26.5 0.7 copy-start.12
  28.9 13.8 %copy-start.8 = (f32[512]{0:T(512)}, f32[512]{0:T(512)S(1)}, u32[]{:S(2)}) copy-start(f32[512]{0:T(512)S(1)} %div.167) | copy-start | bytes 6148
  29.6 12.1 %all-to-all-start = ((f32[32,1,512]{2,1,0:T(1,128)}), f32[32,1,512]{2,1,0:T(1,128)}, u32[]{:S(2)}, u32[]{:S(2)}) async-start(f32[32,1,512]{2,1,0:T(1,128)} %broadcast_in_dim.170), calls=%async_computation | async-start | bytes 131072 | tf_op jit(solution)/shard_map/all_to_all | solution.py:139
  34.8 8.0 %copy-start.16 = (s32[32]{0:T(128)}, s32[32]{0:T(128)S(1)}, u32[]{:S(2)}) copy-start(s32[32]{0:T(128)S(1)} %and_select_fusion) | copy-start | bytes 388
  46.0 9.3 %copy-start.9 = (f32[512]{0:T(512)}, f32[512]{0:T(512)S(1)}, u32[]{:S(2)}) copy-start(f32[512]{0:T(512)S(1)} %divide_add_fusion.2) | copy-start | bytes 6148
  59.5 11.5 %copy-start.7 = (f32[512]{0:T(512)}, f32[512]{0:T(512)S(1)}, u32[]{:S(2)}) copy-start(f32[512]{0:T(512)S(1)} %divide_add_fusion.1) | copy-start | bytes 6148
  60.1 10.9 %all-to-all-start.2 = ((f32[32,1,512]{2,1,0:T(1,128)}), f32[32,1,512]{2,1,0:T(1,128)}, u32[]{:S(2)}, u32[]{:S(2)}) async-start(f32[32,1,512]{2,1,0:T(1,128)} %broadcast_in_dim.178), calls=%async_computation.2 | async-start | bytes 131072 | tf_op jit(solution)/shard_map/all_to_all | solution.py:139
  75.3 22.6 %copy-start.15 = (f32[512]{0:T(512)}, f32[512]{0:T(512)S(1)}, u32[]{:S(2)}) copy-start(f32[512]{0:T(512)S(1)} %divide_add_fusion) | copy-start | bytes 6148
  76.9 10.9 %all-to-all-start.3 = ((f32[32,1,512]{2,1,0:T(1,128)}), f32[32,1,512]{2,1,0:T(1,128)}, u32[]{:S(2)}, u32[]{:S(2)}) async-start(f32[32,1,512]{2,1,0:T(1,128)} %broadcast_in_dim.180), calls=%async_computation.3 | async-start | bytes 131072 | tf_op jit(solution)/shard_map/all_to_all | solution.py:139
  94.6 4.3 %copy-start.11 = (pred[24]{0:T(512)(128)(4,1)S(1)}, pred[24]{0:T(512)(128)(4,1)}, u32[]{:S(2)}) copy-start(pred[24]{0:T(512)(128)(4,1)} %copy-done.10) | copy-start | bytes 76
  99.9 1.0 copy-start.1
  99.9 1.0 copy-start.5
